TPU v7x, 32 devices: a whole 2x2x4 slice. The times are simulated.
32 devices in a mesh: parts: 2 (over y), chain: 4 (over x, core), group: 4 (over z).
Axes of the slice: x: 2, y: 2, z: 4, core: 2. Of those that a mesh axis runs over, the one named last changes fastest.
Arguments:
- rhs: float32 [8, 5, 64, 64], P(('parts', 'chain'), None, None, 'group'), parts along dimension 0, may hold values from -6 to 6
- inv_block: float32 [8, 64, 320, 320], P(('parts', 'chain'), 'group'), parts along dimension 0, may hold values from -0.3125 to 0.3125
- flux_jac: float32 [8, 3, 5, 5, 64], P(('parts', 'chain'), None, None, None, 'group'), parts along dimension 0, may hold values from -2.5 to 2.5
- up_elem: int32 [8, 3, 64], P(('parts', 'chain'), None, 'group'), parts along dimension 0, may hold values from 0 to 63, each once within a row
- lift: float32 [3, 64, 16], replicated, may hold values from -0.875 to 0.875
Outputs:
- solution: float32 [8, 5, 64, 64], P(('parts', 'chain'), None, None, 'group'), parts along dimension 0
There are 2 independent parts, one for each index of `parts`. A program takes and returns all parts, laid end to end along the dimension named above; an argument that names none is the same for every part. Nothing has to cross between parts.
Inputs may be any that keep to these rules, and one draw needn't show every extreme that they name: For every section s and face k, up_elem[s, k, :] names each of the 64 elements once; row s = 0 is not read.
All inputs are finite; a program needn't handle non-finite values.
Results may differ from a plain program's by a relative error of at most 0.02.
Values may be sent and summed in bfloat16 or wider, within the bound.
No kernel may reach another device: no remote copies, remote signals or barrier semaphores. Data moves between devices by JAX's collectives and lax.ppermute only.
A program may use at most 64 MiB of HBM per device.

v0:
```python
import jax
import jax.numpy as jnp
from jax import lax
from jax.sharding import PartitionSpec as P

VARS = 5
NP = 4
NODES = 64
FACE = 16


HIGH = lax.Precision.HIGHEST


def passed_along(value, axis, steps):
    count = lax.axis_size(axis)
    initial, last = (max(0, -steps), min(count, count - steps))
    return lax.ppermute(value, axis, [(source, source + steps) for source in range(initial, last)])


def face_traces(solved):
    elements = solved.shape[-1]
    cube = solved.reshape(VARS, NP, NP, NP, elements)
    first = cube[:, NP - 1, :, :, :].reshape(VARS, FACE, elements)
    second = cube[:, :, NP - 1, :, :].reshape(VARS, FACE, elements)
    third = cube[:, :, :, NP - 1, :].reshape(VARS, FACE, elements)
    return jnp.stack([first, second, third]).astype(jnp.bfloat16)


def solve_section(rhs_s, inv_s, jac_s, up_s, prev_full, lift):
    elements = rhs_s.shape[-1]
    picked = jnp.stack([jnp.take(prev_full[k], up_s[k], axis=2) for k in range(3)])
    upstream = picked.astype(jnp.float32)
    mixed = jnp.einsum("kwve,kvfe->kwfe", jac_s, upstream, precision=HIGH)
    coupling = jnp.einsum("kif,kwfe->wie", lift, mixed, precision=HIGH)
    flat = (rhs_s - coupling).reshape(VARS * NODES, elements)
    result = jnp.einsum("eij,je->ie", inv_s, flat, precision=HIGH)
    return result.reshape(VARS, NODES, elements)


def body(rhs, inv_block, flux_jac, up_elem, lift):
    local = rhs.shape[3]
    chains = lax.axis_size("chain")

    def chain_step(turn, carry):
        last_traces, solved_all = carry
        previous = passed_along(last_traces, "chain", 1)
        full_front = lax.all_gather(previous, "group", axis=3, tiled=True)
        solved = solve_section(rhs[0], inv_block[0], flux_jac[0], up_elem[0], full_front, lift)
        solved_list = [solved]
        previous = face_traces(solved)
        return (previous, jnp.stack(solved_list))

    start = (jnp.zeros((3, VARS, FACE, local), jnp.bfloat16), jnp.zeros(rhs.shape, jnp.float32))
    ended, solution = lax.fori_loop(0, chains, chain_step, start)
    return solution


def solution(mesh):
    return jax.shard_map(
        body,
        mesh=mesh,
        in_specs=(
            P(("parts", "chain"), None, None, "group"),
            P(("parts", "chain"), "group", None, None),
            P(("parts", "chain"), None, None, None, "group"),
            P(("parts", "chain"), None, "group"),
            P(),
        ),
        out_specs=P(("parts", "chain"), None, None, "group"),
        check_vma=False,
    )
```

profile of v0, /device:TPU:2, one launch (start us, length us, event | category | flops | bytes accessed | tf_op | source)
XLA Modules:
  0.0 141.2 jit_solution(16525215014715003966)
XLA Ops:
  0.0 0.8 copy.30
  0.8 0.7 copy.29
  1.5 138.2 %while.12 = (s32[]{:T(128)}, bf16[3,5,16,16]{3,2,1,0:T(8,128)(2,1)S(1)}, f32[1,5,64,16]{2,1,3,0:T(8,128)}, f32[1,5,64,16]{2,3,1,0:T(8,128)}, s32[1,3,16]{2,1,0:T...) while((s32[]{:T(128)}, ...), condition=%wide.region_1.3_spmd, body=%wide.region_0.2_spmd.sunk | while | flops 22868000 | bytes 7120933 | solution.py:55
  1.6 1.9 %collective-permute-start = (bf16[3,5,16,16]{2,1,3,0:T(8,128)(2,1)S(1)}, bf16[3,5,16,16]{2,1,3,0:T(8,128)(2,1)S(1)}, u32[]{:S(2)}, u32[]{:S(2)}) collective-permute-start(bf16[3,5,16,16]{2,1,3,0:T(8,128)(2,1)S(1)} %copy.50), channel_id=1, source_target_pairs={{0,4},{4,8},{8,12},{1,5},{5,9},{9,13},{2,6},{6,10},{10,14},{3,7},{... | collective-permute-start | bytes 23048 | tf_op jit(solution)/shard_map/while/body/eval_jaxpr/ppermute | solution.py:18
  3.8 3.8 %collective-permute-done = bf16[3,5,16,16]{2,1,3,0:T(8,128)(2,1)S(1)} collective-permute-done((bf16[3,5,16,16]{2,1,3,0:T(8,128)(2,1)S(1)}, bf16[3,5,16,16]{2,1,3,0:T(8,128)(2,1)S(1)}, u32[]{:S(2)}, u32[]{:S(2)}) %collective-permute-start) | collective-permute-done | bytes 7712 | tf_op jit(solution)/shard_map/while/body/eval_jaxpr/ppermute | solution.py:18
  7.6 15.3 %all_gather.4 = bf16[3,5,16,64]{2,1,3,0:T(8,128)(2,1)S(1)} all-gather(bf16[3,5,16,16]{2,1,3,0:T(8,128)(2,1)S(1)} %collective-permute-done), channel_id=1, replica_groups=mesh['parts'=2,'chain'=4,'group'=4] {'group'}, dimensions={3}, use_global_device_ids=true | all-gather | bytes 38400 | tf_op jit(solution)/shard_map/while/body/eval_jaxpr/all_gather | solution.py:48
  23.0 0.6 gather_fusion.1
  25.2 1.1 fusion.27
  26.4 9.1 %fusion.28 = f32[16,1,320]{2,1,0:T(1,128)S(1)} fusion(f32[320,16,1]{0,2,1:T(1,128)S(1)} %reshape.74, f32[1,16,320,320]{3,2,1,0:T(8,128)} %get-tuple-element.205), kind=kOutput, calls=%fused_computation.3.clone.1 | convolution fusion | flops 19660800 | bytes 6594560 | tf_op jit(solution)/shard_map/while/body/eval_jaxpr/eij,je->ie/dot_general | solution.py:37
  35.8 0.7 reshape.75
  36.7 1.9 %collective-permute-start = (bf16[3,5,16,16]{2,1,3,0:T(8,128)(2,1)S(1)}, bf16[3,5,16,16]{2,1,3,0:T(8,128)(2,1)S(1)}, u32[]{:S(2)}, u32[]{:S(2)}) collective-permute-start(bf16[3,5,16,16]{2,1,3,0:T(8,128)(2,1)S(1)} %copy.50), channel_id=1, source_target_pairs={{0,4},{4,8},{8,12},{1,5},{5,9},{9,13},{2,6},{6,10},{10,14},{3,7},{... | collective-permute-start | bytes 23048 | tf_op jit(solution)/shard_map/while/body/eval_jaxpr/ppermute | solution.py:18
  38.8 3.8 %collective-permute-done = bf16[3,5,16,16]{2,1,3,0:T(8,128)(2,1)S(1)} collective-permute-done((bf16[3,5,16,16]{2,1,3,0:T(8,128)(2,1)S(1)}, bf16[3,5,16,16]{2,1,3,0:T(8,128)(2,1)S(1)}, u32[]{:S(2)}, u32[]{:S(2)}) %collective-permute-start) | collective-permute-done | bytes 7712 | tf_op jit(solution)/shard_map/while/body/eval_jaxpr/ppermute | solution.py:18
  42.6 15.1 %all_gather.4 = bf16[3,5,16,64]{2,1,3,0:T(8,128)(2,1)S(1)} all-gather(bf16[3,5,16,16]{2,1,3,0:T(8,128)(2,1)S(1)} %collective-permute-done), channel_id=1, replica_groups=mesh['parts'=2,'chain'=4,'group'=4] {'group'}, dimensions={3}, use_global_device_ids=true | all-gather | bytes 38400 | tf_op jit(solution)/shard_map/while/body/eval_jaxpr/all_gather | solution.py:48
  57.8 0.6 gather_fusion.1
  60.1 1.1 fusion.27
  61.2 9.1 %fusion.28 = f32[16,1,320]{2,1,0:T(1,128)S(1)} fusion(f32[320,16,1]{0,2,1:T(1,128)S(1)} %reshape.74, f32[1,16,320,320]{3,2,1,0:T(8,128)} %get-tuple-element.205), kind=kOutput, calls=%fused_computation.3.clone.1 | convolution fusion | flops 19660800 | bytes 6594560 | tf_op jit(solution)/shard_map/while/body/eval_jaxpr/eij,je->ie/dot_general | solution.py:37
  70.6 0.7 reshape.75
  71.5 1.9 %collective-permute-start = (bf16[3,5,16,16]{2,1,3,0:T(8,128)(2,1)S(1)}, bf16[3,5,16,16]{2,1,3,0:T(8,128)(2,1)S(1)}, u32[]{:S(2)}, u32[]{:S(2)}) collective-permute-start(bf16[3,5,16,16]{2,1,3,0:T(8,128)(2,1)S(1)} %copy.50), channel_id=1, source_target_pairs={{0,4},{4,8},{8,12},{1,5},{5,9},{9,13},{2,6},{6,10},{10,14},{3,7},{... | collective-permute-start | bytes 23048 | tf_op jit(solution)/shard_map/while/body/eval_jaxpr/ppermute | solution.py:18
  73.7 3.8 %collective-permute-done = bf16[3,5,16,16]{2,1,3,0:T(8,128)(2,1)S(1)} collective-permute-done((bf16[3,5,16,16]{2,1,3,0:T(8,128)(2,1)S(1)}, bf16[3,5,16,16]{2,1,3,0:T(8,128)(2,1)S(1)}, u32[]{:S(2)}, u32[]{:S(2)}) %collective-permute-start) | collective-permute-done | bytes 7712 | tf_op jit(solution)/shard_map/while/body/eval_jaxpr/ppermute | solution.py:18
  77.4 14.5 %all_gather.4 = bf16[3,5,16,64]{2,1,3,0:T(8,128)(2,1)S(1)} all-gather(bf16[3,5,16,16]{2,1,3,0:T(8,128)(2,1)S(1)} %collective-permute-done), channel_id=1, replica_groups=mesh['parts'=2,'chain'=4,'group'=4] {'group'}, dimensions={3}, use_global_device_ids=true | all-gather | bytes 38400 | tf_op jit(solution)/shard_map/while/body/eval_jaxpr/all_gather | solution.py:48
  92.0 0.6 gather_fusion.1
  94.3 1.1 fusion.27
  95.5 9.1 %fusion.28 = f32[16,1,320]{2,1,0:T(1,128)S(1)} fusion(f32[320,16,1]{0,2,1:T(1,128)S(1)} %reshape.74, f32[1,16,320,320]{3,2,1,0:T(8,128)} %get-tuple-element.205), kind=kOutput, calls=%fused_computation.3.clone.1 | convolution fusion | flops 19660800 | bytes 6594560 | tf_op jit(solution)/shard_map/while/body/eval_jaxpr/eij,je->ie/dot_general | solution.py:37
  104.9 0.7 reshape.75
  105.7 1.9 %collective-permute-start = (bf16[3,5,16,16]{2,1,3,0:T(8,128)(2,1)S(1)}, bf16[3,5,16,16]{2,1,3,0:T(8,128)(2,1)S(1)}, u32[]{:S(2)}, u32[]{:S(2)}) collective-permute-start(bf16[3,5,16,16]{2,1,3,0:T(8,128)(2,1)S(1)} %copy.50), channel_id=1, source_target_pairs={{0,4},{4,8},{8,12},{1,5},{5,9},{9,13},{2,6},{6,10},{10,14},{3,7},{... | collective-permute-start | bytes 23048 | tf_op jit(solution)/shard_map/while/body/eval_jaxpr/ppermute | solution.py:18
  107.9 3.8 %collective-permute-done = bf16[3,5,16,16]{2,1,3,0:T(8,128)(2,1)S(1)} collective-permute-done((bf16[3,5,16,16]{2,1,3,0:T(8,128)(2,1)S(1)}, bf16[3,5,16,16]{2,1,3,0:T(8,128)(2,1)S(1)}, u32[]{:S(2)}, u32[]{:S(2)}) %collective-permute-start) | collective-permute-done | bytes 7712 | tf_op jit(solution)/shard_map/while/body/eval_jaxpr/ppermute | solution.py:18
  111.7 14.4 %all_gather.4 = bf16[3,5,16,64]{2,1,3,0:T(8,128)(2,1)S(1)} all-gather(bf16[3,5,16,16]{2,1,3,0:T(8,128)(2,1)S(1)} %collective-permute-done), channel_id=1, replica_groups=mesh['parts'=2,'chain'=4,'group'=4] {'group'}, dimensions={3}, use_global_device_ids=true | all-gather | bytes 38400 | tf_op jit(solution)/shard_map/while/body/eval_jaxpr/all_gather | solution.py:48
  126.2 0.6 gather_fusion.1
  128.4 1.1 fusion.27
  129.6 9.1 %fusion.28 = f32[16,1,320]{2,1,0:T(1,128)S(1)} fusion(f32[320,16,1]{0,2,1:T(1,128)S(1)} %reshape.74, f32[1,16,320,320]{3,2,1,0:T(8,128)} %get-tuple-element.205), kind=kOutput, calls=%fused_computation.3.clone.1 | convolution fusion | flops 19660800 | bytes 6594560 | tf_op jit(solution)/shard_map/while/body/eval_jaxpr/eij,je->ie/dot_general | solution.py:37
  139.0 0.7 reshape.75
  139.7 1.5 %copy.31 = f32[1,5,64,16]{2,3,1,0:T(8,128)} copy(f32[1,5,64,16]{2,1,3,0:T(8,128)} %get-tuple-element.47) | data formatting | bytes 40960 | tf_op jit(solution)/shard_map/while | solution.py:55
  (86 shorter events, 9.6 us)
Async XLA Ops:
  1.6 5.9 %collective-permute-start = (bf16[3,5,16,16]{2,1,3,0:T(8,128)(2,1)S(1)}, bf16[3,5,16,16]{2,1,3,0:T(8,128)(2,1)S(1)}, u32[]{:S(2)}, u32[]{:S(2)}) collective-permute-start(bf16[3,5,16,16]{2,1,3,0:T(8,128)(2,1)S(1)} %copy.50), channel_id=1, source_target_pairs={{0,4},{4,8},{8,12},{1,5},{5,9},{9,13},{2,6},{6,10},{10,14},{3,7},{... | collective-permute-start | bytes 23048 | tf_op jit(solution)/shard_map/while/body/eval_jaxpr/ppermute | solution.py:18
  36.7 5.9 %collective-permute-start = (bf16[3,5,16,16]{2,1,3,0:T(8,128)(2,1)S(1)}, bf16[3,5,16,16]{2,1,3,0:T(8,128)(2,1)S(1)}, u32[]{:S(2)}, u32[]{:S(2)}) collective-permute-start(bf16[3,5,16,16]{2,1,3,0:T(8,128)(2,1)S(1)} %copy.50), channel_id=1, source_target_pairs={{0,4},{4,8},{8,12},{1,5},{5,9},{9,13},{2,6},{6,10},{10,14},{3,7},{... | collective-permute-start | bytes 23048 | tf_op jit(solution)/shard_map/while/body/eval_jaxpr/ppermute | solution.py:18
  71.5 5.9 %collective-permute-start = (bf16[3,5,16,16]{2,1,3,0:T(8,128)(2,1)S(1)}, bf16[3,5,16,16]{2,1,3,0:T(8,128)(2,1)S(1)}, u32[]{:S(2)}, u32[]{:S(2)}) collective-permute-start(bf16[3,5,16,16]{2,1,3,0:T(8,128)(2,1)S(1)} %copy.50), channel_id=1, source_target_pairs={{0,4},{4,8},{8,12},{1,5},{5,9},{9,13},{2,6},{6,10},{10,14},{3,7},{... | collective-permute-start | bytes 23048 | tf_op jit(solution)/shard_map/while/body/eval_jaxpr/ppermute | solution.py:18
  105.7 5.9 %collective-permute-start = (bf16[3,5,16,16]{2,1,3,0:T(8,128)(2,1)S(1)}, bf16[3,5,16,16]{2,1,3,0:T(8,128)(2,1)S(1)}, u32[]{:S(2)}, u32[]{:S(2)}) collective-permute-start(bf16[3,5,16,16]{2,1,3,0:T(8,128)(2,1)S(1)} %copy.50), channel_id=1, source_target_pairs={{0,4},{4,8},{8,12},{1,5},{5,9},{9,13},{2,6},{6,10},{10,14},{3,7},{... | collective-permute-start | bytes 23048 | tf_op jit(solution)/shard_map/while/body/eval_jaxpr/ppermute | solution.py:18
where the time goes:
time: 142 us; the launch traced here: 141 us
  blocking collectives  59.4 us (42%)
  matrix products  42 us (30%)
  local copies, waits for them, and re-layouts  15.4 us (11%)
  waiting for transfers between devices  15.1 us (11%)
  starting transfers between devices  7.68 us (5%)
    all_gather x4, blocking collectives, chain_step(): full_front = lax.all_gather(previous, 'group', axis=3, tiled=True)  59.4 us
    dot_general x4, matrix products, solve_section(): result = jnp.einsum('eij,je->ie', inv_s, flat, precision=HIGH)  36.5 us
    ppermute x4, waiting for transfers between devices, passed_along(): lax.ppermute(value, axis, [(source, source + steps) for source in range(i...  15.1 us
    ppermute x4, starting transfers between devices, passed_along(): lax.ppermute(value, axis, [(source, source + steps) for source in range(i...  7.68 us
    gather x12, local copies, waits for them, and re-layouts, solve_section(): jnp.take(prev_full[k], up_s[k], axis=2)  6.88 us
    dot_general x4, matrix products, solve_section(): coupling = jnp.einsum('kif,kwfe->wie', lift, mixed, precision=HIGH)  4.27 us
    while x3, local copies, waits for them, and re-layouts, body(): ended, solution = lax.fori_loop(0, chains, chain_step, start)  2.94 us
  transfers between devices with their start and end apart: 4, of which 4 were waited for; matrix products, arithmetic and copies ran while one was open for 1% of the time, Pallas kernels for 0%

commit v1 on v0

v1 whole, which is shorter than its diff:
```python
import jax
import jax.numpy as jnp
from jax import lax
from jax.sharding import PartitionSpec as P

VARS = 5
NP = 4
NODES = 64
FACE = 16
BLOCK = VARS * NODES

HIGH = lax.Precision.HIGHEST


def face_traces(sol):
    elements = sol.shape[0]
    cube = sol.reshape(elements, VARS, NP, NP, NP)
    first = cube[:, :, NP - 1, :, :].reshape(elements, VARS, FACE)
    second = cube[:, :, :, NP - 1, :].reshape(elements, VARS, FACE)
    third = cube[:, :, :, :, NP - 1].reshape(elements, VARS, FACE)
    return jnp.transpose(jnp.stack([first, second, third]), (0, 2, 3, 1))


def body(rhs, inv_block, flux_jac, up_elem, lift):
    chains = lax.axis_size("chain")
    groups = lax.axis_size("group")
    local = rhs.shape[3]
    c = lax.axis_index("chain")
    g = lax.axis_index("group")

    inv = inv_block[0]
    jac = flux_jac[0]
    up = up_elem[0]
    rhs_t = jnp.transpose(rhs[0], (2, 0, 1)).reshape(local, BLOCK)

    shift = (g - up // local) % groups
    pos = shift * local + up % local
    onehot = (jnp.arange(groups * local)[None, :, None] == pos[:, None, :]).astype(jnp.bfloat16)

    def solve(traces_in):
        if traces_in is None:
            x = rhs_t
        else:
            upstream = jnp.einsum("kvfp,kpe->kvfe", traces_in, onehot, preferred_element_type=jnp.float32)
            mixed = jnp.einsum("kwve,kvfe->kwfe", jac, upstream, precision=HIGH)
            coupling = jnp.einsum("kwfe,kif->ewi", mixed, lift, precision=HIGH)
            x = rhs_t - coupling.reshape(local, BLOCK)
        return jnp.sum(inv * x[:, None, :], axis=-1)

    out = jnp.zeros((local, BLOCK), jnp.float32)
    traces = None
    for turn in range(chains):
        if turn > 0:
            blocks = []
            for d in range(groups):
                pairs = [((turn - 1) * groups + s, turn * groups + (s + d) % groups) for s in range(groups)]
                blocks.append(lax.ppermute(traces, ("chain", "group"), pairs))
            traces_in = jnp.concatenate(blocks, axis=3)
        else:
            traces_in = None
        sol = solve(traces_in)
        out = jnp.where(c == turn, sol, out)
        if turn + 1 < chains:
            traces = face_traces(sol).astype(jnp.bfloat16)
    return jnp.transpose(out.reshape(local, VARS, NODES), (1, 2, 0))[None]


def solution(mesh):
    return jax.shard_map(
        body,
        mesh=mesh,
        in_specs=(
            P(("parts", "chain"), None, None, "group"),
            P(("parts", "chain"), "group", None, None),
            P(("parts", "chain"), None, None, None, "group"),
            P(("parts", "chain"), None, "group"),
            P(),
        ),
        out_specs=P(("parts", "chain"), None, None, "group"),
        check_vma=False,
    )
```

time: 142 us -> 52.4 us (0.37)
  the two profiles are of different devices: /device:TPU:2 before, /device:TPU:7 now
where the time goes in v1:
time: 52.4 us; the launch traced here: 51.9 us
  waiting for transfers between devices  18.4 us (35%)
  other arithmetic  16.7 us (32%)
  starting transfers between devices  10.5 us (20%)
  local copies, waits for them, and re-layouts  3.09 us (6%)
  matrix products  2.87 us (5%)
    ppermute x12, waiting for transfers between devices, body(): blocks.append(lax.ppermute(traces, ('chain', 'group'), pairs))  18.4 us
    reduce_sum x4, other arithmetic, solve(): return jnp.sum(inv * x[:, None, :], axis=-1)  16.5 us
    ppermute x12, starting transfers between devices, body(): blocks.append(lax.ppermute(traces, ('chain', 'group'), pairs))  10.5 us
    dot_general x3, matrix products, solve(): mixed = jnp.einsum('kwve,kvfe->kwfe', jac, upstream, precision=HIGH)  1.34 us
  transfers between devices with their start and end apart: 12, of which 2 were waited for; matrix products, arithmetic and copies ran while one was open for 0% of the time, Pallas kernels for 0%

profile of v1, /device:TPU:7, one launch (start us, length us, event | category | flops | bytes accessed | tf_op | source)
XLA Modules:
  0.0 51.9 jit_solution(32792771593833466)
XLA Ops:
  0.0 0.8 %copy.13 = f32[16,5,64]{2,1,0:T(8,128)S(1)} copy(f32[16,5,64]{2,0,1:T(8,128)} %bitcast.119) | data formatting | bytes 40960 | tf_op jit(solution)/shard_map/transpose | solution.py:34
  0.9 4.1 %fusion = f32[16,320]{1,0:T(8,128)S(1)} fusion(f32[1,16,320,320]{3,2,1,0:T(8,128)} %param.6, f32[16,320]{1,0:T(8,128)S(1)} %reshape.125), kind=kLoop, calls=%fused_computation.4 | loop fusion | flops 3271680 | bytes 6594560 | tf_op jit(solution)/shard_map/reduce_sum | solution.py:48
  5.3 0.7 %collective-permute-start = (bf16[3,5,16,16]{3,2,1,0:T(8,128)(2,1)S(1)}, bf16[3,5,16,16]{3,2,1,0:T(8,128)(2,1)S(1)}, u32[]{:S(2)}, u32[]{:S(2)}) collective-permute-start(bf16[3,5,16,16]{3,2,1,0:T(8,128)(2,1)S(1)} %maximum_bitcast_fusion), channel_id=1, source_target_pairs={{0,4},{1,5},{2,6},{3,7},{16,20},{17,21},{18,22},{19,23}} | collective-permute-start | bytes 23048 | tf_op jit(solution)/shard_map/ppermute | solution.py:57
  6.0 0.7 %collective-permute-start.1 = (bf16[3,5,16,16]{3,2,1,0:T(8,128)(2,1)S(1)}, bf16[3,5,16,16]{3,2,1,0:T(8,128)(2,1)S(1)}, u32[]{:S(2)}, u32[]{:S(2)}) collective-permute-start(bf16[3,5,16,16]{3,2,1,0:T(8,128)(2,1)S(1)} %maximum_bitcast_fusion), channel_id=1, source_target_pairs={{0,5},{1,6},{2,7},{3,4},{16,21},{17,22},{18,23},{19,20}} | collective-permute-start | bytes 23048 | tf_op jit(solution)/shard_map/ppermute | solution.py:57
  6.7 0.7 %collective-permute-start.2 = (bf16[3,5,16,16]{3,2,1,0:T(8,128)(2,1)S(1)}, bf16[3,5,16,16]{3,2,1,0:T(8,128)(2,1)S(1)}, u32[]{:S(2)}, u32[]{:S(2)}) collective-permute-start(bf16[3,5,16,16]{3,2,1,0:T(8,128)(2,1)S(1)} %maximum_bitcast_fusion), channel_id=1, source_target_pairs={{0,6},{1,7},{2,4},{3,5},{16,22},{17,23},{18,20},{19,21}} | collective-permute-start | bytes 23048 | tf_op jit(solution)/shard_map/ppermute | solution.py:57
  7.4 0.7 %collective-permute-start.3 = (bf16[3,5,16,16]{3,2,1,0:T(8,128)(2,1)S(1)}, bf16[3,5,16,16]{3,2,1,0:T(8,128)(2,1)S(1)}, u32[]{:S(2)}, u32[]{:S(2)}) collective-permute-start(bf16[3,5,16,16]{3,2,1,0:T(8,128)(2,1)S(1)} %maximum_bitcast_fusion), channel_id=1, source_target_pairs={{0,7},{1,4},{2,5},{3,6},{16,23},{17,20},{18,21},{19,22}} | collective-permute-start | bytes 23048 | tf_op jit(solution)/shard_map/ppermute | solution.py:57
  8.1 0.2 copy.17
  8.3 0.2 fusion.7
  8.6 0.1 copy.16
  8.7 0.4 convolution_bitcast_fusion.2
  9.1 0.3 convolution_bitcast_fusion.5
  9.5 4.1 %fusion.1 = f32[16,320]{1,0:T(8,128)S(1)} fusion(f32[1,16,320,320]{3,2,1,0:T(8,128)} %param.6, f32[16,320]{1,0:T(8,128)S(1)} %sub.40), kind=kLoop, calls=%fused_computation.5 | loop fusion | flops 3271680 | bytes 6594560 | tf_op jit(solution)/shard_map/reduce_sum | solution.py:48
  14.0 0.7 %collective-permute-start.4 = (bf16[3,5,16,16]{3,2,1,0:T(8,128)(2,1)S(1)}, bf16[3,5,16,16]{3,2,1,0:T(8,128)(2,1)S(1)}, u32[]{:S(2)}, u32[]{:S(2)}) collective-permute-start(bf16[3,5,16,16]{3,2,1,0:T(8,128)(2,1)S(1)} %maximum_bitcast_fusion.1), channel_id=1, source_target_pairs={{4,8},{5,9},{6,10},{7,11},{20,24},{21,25},{22,26},{23,27}} | collective-permute-start | bytes 23048 | tf_op jit(solution)/shard_map/ppermute | solution.py:57
  14.6 0.7 %collective-permute-start.5 = (bf16[3,5,16,16]{3,2,1,0:T(8,128)(2,1)S(1)}, bf16[3,5,16,16]{3,2,1,0:T(8,128)(2,1)S(1)}, u32[]{:S(2)}, u32[]{:S(2)}) collective-permute-start(bf16[3,5,16,16]{3,2,1,0:T(8,128)(2,1)S(1)} %maximum_bitcast_fusion.1), channel_id=1, source_target_pairs={{4,9},{5,10},{6,11},{7,8},{20,25},{21,26},{22,27},{23,24}} | collective-permute-start | bytes 23048 | tf_op jit(solution)/shard_map/ppermute | solution.py:57
  15.3 0.7 %collective-permute-start.6 = (bf16[3,5,16,16]{3,2,1,0:T(8,128)(2,1)S(1)}, bf16[3,5,16,16]{3,2,1,0:T(8,128)(2,1)S(1)}, u32[]{:S(2)}, u32[]{:S(2)}) collective-permute-start(bf16[3,5,16,16]{3,2,1,0:T(8,128)(2,1)S(1)} %maximum_bitcast_fusion.1), channel_id=1, source_target_pairs={{4,10},{5,11},{6,8},{7,9},{20,26},{21,27},{22,24},{23,25}} | collective-permute-start | bytes 23048 | tf_op jit(solution)/shard_map/ppermute | solution.py:57
  16.0 0.7 %collective-permute-start.7 = (bf16[3,5,16,16]{3,2,1,0:T(8,128)(2,1)S(1)}, bf16[3,5,16,16]{3,2,1,0:T(8,128)(2,1)S(1)}, u32[]{:S(2)}, u32[]{:S(2)}) collective-permute-start(bf16[3,5,16,16]{3,2,1,0:T(8,128)(2,1)S(1)} %maximum_bitcast_fusion.1), channel_id=1, source_target_pairs={{4,11},{5,8},{6,9},{7,10},{20,27},{21,24},{22,25},{23,26}} | collective-permute-start | bytes 23048 | tf_op jit(solution)/shard_map/ppermute | solution.py:57
  16.7 0.2 fusion.15
  16.9 0.1 copy.21
  17.1 0.4 convolution_bitcast_fusion.1
  17.5 0.3 convolution_bitcast_fusion.4
  17.9 4.1 %fusion.2 = f32[16,320]{1,0:T(8,128)S(1)} fusion(f32[1,16,320,320]{3,2,1,0:T(8,128)} %param.6, f32[16,320]{1,0:T(8,128)S(1)} %sub.41), kind=kLoop, calls=%fused_computation.6 | loop fusion | flops 3271680 | bytes 6594560 | tf_op jit(solution)/shard_map/reduce_sum | solution.py:48
  22.3 1.3 %collective-permute-start.10 = (bf16[3,5,16,16]{3,2,1,0:T(8,128)(2,1)S(1)}, bf16[3,5,16,16]{3,2,1,0:T(8,128)(2,1)S(1)}, u32[]{:S(2)}, u32[]{:S(2)}) collective-permute-start(bf16[3,5,16,16]{3,2,1,0:T(8,128)(2,1)S(1)} %maximum_bitcast_fusion.2), channel_id=1, source_target_pairs={{8,14},{9,15},{10,12},{11,13},{24,30},{25,31},{26,28},{27,29}} | collective-permute-start | bytes 23048 | tf_op jit(solution)/shard_map/ppermute | solution.py:57
  23.6 1.3 %collective-permute-start.11 = (bf16[3,5,16,16]{3,2,1,0:T(8,128)(2,1)S(1)}, bf16[3,5,16,16]{3,2,1,0:T(8,128)(2,1)S(1)}, u32[]{:S(2)}, u32[]{:S(2)}) collective-permute-start(bf16[3,5,16,16]{3,2,1,0:T(8,128)(2,1)S(1)} %maximum_bitcast_fusion.2), channel_id=1, source_target_pairs={{8,15},{9,12},{10,13},{11,14},{24,31},{25,28},{26,29},{27,30}} | collective-permute-start | bytes 23048 | tf_op jit(solution)/shard_map/ppermute | solution.py:57
  24.9 1.3 %collective-permute-start.8 = (bf16[3,5,16,16]{3,2,1,0:T(8,128)(2,1)S(1)}, bf16[3,5,16,16]{3,2,1,0:T(8,128)(2,1)S(1)}, u32[]{:S(2)}, u32[]{:S(2)}) collective-permute-start(bf16[3,5,16,16]{3,2,1,0:T(8,128)(2,1)S(1)} %maximum_bitcast_fusion.2), channel_id=1, source_target_pairs={{8,12},{9,13},{10,14},{11,15},{24,28},{25,29},{26,30},{27,31}} | collective-permute-start | bytes 23048 | tf_op jit(solution)/shard_map/ppermute | solution.py:57
  26.2 1.3 %collective-permute-start.9 = (bf16[3,5,16,16]{3,2,1,0:T(8,128)(2,1)S(1)}, bf16[3,5,16,16]{3,2,1,0:T(8,128)(2,1)S(1)}, u32[]{:S(2)}, u32[]{:S(2)}) collective-permute-start(bf16[3,5,16,16]{3,2,1,0:T(8,128)(2,1)S(1)} %maximum_bitcast_fusion.2), channel_id=1, source_target_pairs={{8,13},{9,14},{10,15},{11,12},{24,29},{25,30},{26,31},{27,28}} | collective-permute-start | bytes 23048 | tf_op jit(solution)/shard_map/ppermute | solution.py:57
  27.5 15.1 %collective-permute-done.10 = bf16[3,5,16,16]{3,2,1,0:T(8,128)(2,1)S(1)} collective-permute-done((bf16[3,5,16,16]{3,2,1,0:T(8,128)(2,1)S(1)}, bf16[3,5,16,16]{3,2,1,0:T(8,128)(2,1)S(1)}, u32[]{:S(2)}, u32[]{:S(2)}) %collective-permute-start.10) | collective-permute-done | bytes 7712 | tf_op jit(solution)/shard_map/ppermute | solution.py:57
  42.6 3.2 %collective-permute-done.9 = bf16[3,5,16,16]{3,2,1,0:T(8,128)(2,1)S(1)} collective-permute-done((bf16[3,5,16,16]{3,2,1,0:T(8,128)(2,1)S(1)}, bf16[3,5,16,16]{3,2,1,0:T(8,128)(2,1)S(1)}, u32[]{:S(2)}, u32[]{:S(2)}) %collective-permute-start.9) | collective-permute-done | bytes 7712 | tf_op jit(solution)/shard_map/ppermute | solution.py:57
  45.9 0.2 fusion.23
  46.2 0.4 convolution_bitcast_fusion
  46.7 0.3 convolution_bitcast_fusion.3
  47.1 4.1 %fusion.3 = f32[16,320]{1,0:T(8,128)S(1)} fusion(f32[1,16,320,320]{3,2,1,0:T(8,128)} %param.6, f32[16,320]{1,0:T(8,128)S(1)} %sub.42), kind=kLoop, calls=%fused_computation.7 | loop fusion | flops 3271680 | bytes 6594560 | tf_op jit(solution)/shard_map/reduce_sum | solution.py:48
  51.3 0.6 %copy.30 = f32[1,5,64,16]{2,3,1,0:T(8,128)} copy(f32[1,5,64,16]{2,1,3,0:T(8,128)S(1)} %bitcast.108) | data formatting | bytes 40960 | tf_op jit(solution)/shard_map/broadcast_in_dim | solution.py:65
  (52 shorter events, 1.4 us)
Async XLA Ops:
  0.0 9.1 %copy-start = (f32[3,64,16]{1,2,0:T(8,128)S(1)}, f32[3,64,16]{1,2,0:T(8,128)}, u32[]{:S(2)}) copy-start(f32[3,64,16]{1,2,0:T(8,128)} %param.9) | copy-start | bytes 36868
  0.0 8.0 %copy-start.2 = (s32[1,3,16]{2,0,1:T(1,128)S(1)}, s32[1,3,16]{2,0,1:T(1,128)}, u32[]{:S(2)}) copy-start(s32[1,3,16]{2,0,1:T(1,128)} %param.8) | copy-start | bytes 580
  0.0 8.1 %copy-start.1 = (f32[1,3,5,5,16]{4,0,3,2,1:T(1,128)S(1)}, f32[1,3,5,5,16]{4,0,3,2,1:T(1,128)}, u32[]{:S(2)}) copy-start(f32[1,3,5,5,16]{4,0,3,2,1:T(1,128)} %param.7) | copy-start | bytes 14404
  5.3 2.9 %collective-permute-start = (bf16[3,5,16,16]{3,2,1,0:T(8,128)(2,1)S(1)}, bf16[3,5,16,16]{3,2,1,0:T(8,128)(2,1)S(1)}, u32[]{:S(2)}, u32[]{:S(2)}) collective-permute-start(bf16[3,5,16,16]{3,2,1,0:T(8,128)(2,1)S(1)} %maximum_bitcast_fusion), channel_id=1, source_target_pairs={{0,4},{1,5},{2,6},{3,7},{16,20},{17,21},{18,22},{19,23}} | collective-permute-start | bytes 23048 | tf_op jit(solution)/shard_map/ppermute | solution.py:57
  6.0 2.3 %collective-permute-start.1 = (bf16[3,5,16,16]{3,2,1,0:T(8,128)(2,1)S(1)}, bf16[3,5,16,16]{3,2,1,0:T(8,128)(2,1)S(1)}, u32[]{:S(2)}, u32[]{:S(2)}) collective-permute-start(bf16[3,5,16,16]{3,2,1,0:T(8,128)(2,1)S(1)} %maximum_bitcast_fusion), channel_id=1, source_target_pairs={{0,5},{1,6},{2,7},{3,4},{16,21},{17,22},{18,23},{19,20}} | collective-permute-start | bytes 23048 | tf_op jit(solution)/shard_map/ppermute | solution.py:57
  6.7 1.6 %collective-permute-start.2 = (bf16[3,5,16,16]{3,2,1,0:T(8,128)(2,1)S(1)}, bf16[3,5,16,16]{3,2,1,0:T(8,128)(2,1)S(1)}, u32[]{:S(2)}, u32[]{:S(2)}) collective-permute-start(bf16[3,5,16,16]{3,2,1,0:T(8,128)(2,1)S(1)} %maximum_bitcast_fusion), channel_id=1, source_target_pairs={{0,6},{1,7},{2,4},{3,5},{16,22},{17,23},{18,20},{19,21}} | collective-permute-start | bytes 23048 | tf_op jit(solution)/shard_map/ppermute | solution.py:57
  7.4 1.0 %collective-permute-start.3 = (bf16[3,5,16,16]{3,2,1,0:T(8,128)(2,1)S(1)}, bf16[3,5,16,16]{3,2,1,0:T(8,128)(2,1)S(1)}, u32[]{:S(2)}, u32[]{:S(2)}) collective-permute-start(bf16[3,5,16,16]{3,2,1,0:T(8,128)(2,1)S(1)} %maximum_bitcast_fusion), channel_id=1, source_target_pairs={{0,7},{1,4},{2,5},{3,6},{16,23},{17,20},{18,21},{19,22}} | collective-permute-start | bytes 23048 | tf_op jit(solution)/shard_map/ppermute | solution.py:57
  14.0 2.7 %collective-permute-start.4 = (bf16[3,5,16,16]{3,2,1,0:T(8,128)(2,1)S(1)}, bf16[3,5,16,16]{3,2,1,0:T(8,128)(2,1)S(1)}, u32[]{:S(2)}, u32[]{:S(2)}) collective-permute-start(bf16[3,5,16,16]{3,2,1,0:T(8,128)(2,1)S(1)} %maximum_bitcast_fusion.1), channel_id=1, source_target_pairs={{4,8},{5,9},{6,10},{7,11},{20,24},{21,25},{22,26},{23,27}} | collective-permute-start | bytes 23048 | tf_op jit(solution)/shard_map/ppermute | solution.py:57
  14.6 2.0 %collective-permute-start.5 = (bf16[3,5,16,16]{3,2,1,0:T(8,128)(2,1)S(1)}, bf16[3,5,16,16]{3,2,1,0:T(8,128)(2,1)S(1)}, u32[]{:S(2)}, u32[]{:S(2)}) collective-permute-start(bf16[3,5,16,16]{3,2,1,0:T(8,128)(2,1)S(1)} %maximum_bitcast_fusion.1), channel_id=1, source_target_pairs={{4,9},{5,10},{6,11},{7,8},{20,25},{21,26},{22,27},{23,24}} | collective-permute-start | bytes 23048 | tf_op jit(solution)/shard_map/ppermute | solution.py:57
  15.3 1.4 %collective-permute-start.6 = (bf16[3,5,16,16]{3,2,1,0:T(8,128)(2,1)S(1)}, bf16[3,5,16,16]{3,2,1,0:T(8,128)(2,1)S(1)}, u32[]{:S(2)}, u32[]{:S(2)}) collective-permute-start(bf16[3,5,16,16]{3,2,1,0:T(8,128)(2,1)S(1)} %maximum_bitcast_fusion.1), channel_id=1, source_target_pairs={{4,10},{5,11},{6,8},{7,9},{20,26},{21,27},{22,24},{23,25}} | collective-permute-start | bytes 23048 | tf_op jit(solution)/shard_map/ppermute | solution.py:57
  16.0 0.7 %collective-permute-start.7 = (bf16[3,5,16,16]{3,2,1,0:T(8,128)(2,1)S(1)}, bf16[3,5,16,16]{3,2,1,0:T(8,128)(2,1)S(1)}, u32[]{:S(2)}, u32[]{:S(2)}) collective-permute-start(bf16[3,5,16,16]{3,2,1,0:T(8,128)(2,1)S(1)} %maximum_bitcast_fusion.1), channel_id=1, source_target_pairs={{4,11},{5,8},{6,9},{7,10},{20,27},{21,24},{22,25},{23,26}} | collective-permute-start | bytes 23048 | tf_op jit(solution)/shard_map/ppermute | solution.py:57
  22.3 20.3 %collective-permute-start.10 = (bf16[3,5,16,16]{3,2,1,0:T(8,128)(2,1)S(1)}, bf16[3,5,16,16]{3,2,1,0:T(8,128)(2,1)S(1)}, u32[]{:S(2)}, u32[]{:S(2)}) collective-permute-start(bf16[3,5,16,16]{3,2,1,0:T(8,128)(2,1)S(1)} %maximum_bitcast_fusion.2), channel_id=1, source_target_pairs={{8,14},{9,15},{10,12},{11,13},{24,30},{25,31},{26,28},{27,29}} | collective-permute-start | bytes 23048 | tf_op jit(solution)/shard_map/ppermute | solution.py:57
  23.6 19.0 %collective-permute-start.11 = (bf16[3,5,16,16]{3,2,1,0:T(8,128)(2,1)S(1)}, bf16[3,5,16,16]{3,2,1,0:T(8,128)(2,1)S(1)}, u32[]{:S(2)}, u32[]{:S(2)}) collective-permute-start(bf16[3,5,16,16]{3,2,1,0:T(8,128)(2,1)S(1)} %maximum_bitcast_fusion.2), channel_id=1, source_target_pairs={{8,15},{9,12},{10,13},{11,14},{24,31},{25,28},{26,29},{27,30}} | collective-permute-start | bytes 23048 | tf_op jit(solution)/shard_map/ppermute | solution.py:57
  24.9 17.7 %collective-permute-start.8 = (bf16[3,5,16,16]{3,2,1,0:T(8,128)(2,1)S(1)}, bf16[3,5,16,16]{3,2,1,0:T(8,128)(2,1)S(1)}, u32[]{:S(2)}, u32[]{:S(2)}) collective-permute-start(bf16[3,5,16,16]{3,2,1,0:T(8,128)(2,1)S(1)} %maximum_bitcast_fusion.2), channel_id=1, source_target_pairs={{8,12},{9,13},{10,14},{11,15},{24,28},{25,29},{26,30},{27,31}} | collective-permute-start | bytes 23048 | tf_op jit(solution)/shard_map/ppermute | solution.py:57
  26.2 19.6 %collective-permute-start.9 = (bf16[3,5,16,16]{3,2,1,0:T(8,128)(2,1)S(1)}, bf16[3,5,16,16]{3,2,1,0:T(8,128)(2,1)S(1)}, u32[]{:S(2)}, u32[]{:S(2)}) collective-permute-start(bf16[3,5,16,16]{3,2,1,0:T(8,128)(2,1)S(1)} %maximum_bitcast_fusion.2), channel_id=1, source_target_pairs={{8,13},{9,14},{10,15},{11,12},{24,29},{25,30},{26,31},{27,28}} | collective-permute-start | bytes 23048 | tf_op jit(solution)/shard_map/ppermute | solution.py:57

commit v2 on v1

--- a/solution.py
+++ b/solution.py
@@ -37,31 +37,48 @@
     pos = shift * local + up % local
     onehot = (jnp.arange(groups * local)[None, :, None] == pos[:, None, :]).astype(jnp.bfloat16)
 
-    def solve(traces_in):
-        if traces_in is None:
-            x = rhs_t
-        else:
-            upstream = jnp.einsum("kvfp,kpe->kvfe", traces_in, onehot, preferred_element_type=jnp.float32)
-            mixed = jnp.einsum("kwve,kvfe->kwfe", jac, upstream, precision=HIGH)
-            coupling = jnp.einsum("kwfe,kif->ewi", mixed, lift, precision=HIGH)
-            x = rhs_t - coupling.reshape(local, BLOCK)
+    def coupled(traces_in):
+        upstream = jnp.einsum("kvfp,kpe->kvfe", traces_in, onehot, preferred_element_type=jnp.float32)
+        mixed = jnp.einsum("kwve,kvfe->kwfe", jac, upstream, precision=HIGH)
+        coupling = jnp.einsum("kwfe,kif->ewi", mixed, lift, precision=HIGH)
+        return rhs_t - coupling.reshape(local, BLOCK)
+
+    def full_solve(x):
         return jnp.sum(inv * x[:, None, :], axis=-1)
 
-    out = jnp.zeros((local, BLOCK), jnp.float32)
-    traces = None
-    for turn in range(chains):
-        if turn > 0:
-            blocks = []
-            for d in range(groups):
-                pairs = [((turn - 1) * groups + s, turn * groups + (s + d) % groups) for s in range(groups)]
-                blocks.append(lax.ppermute(traces, ("chain", "group"), pairs))
-            traces_in = jnp.concatenate(blocks, axis=3)
+    def trace_rows(x):
+        rows = jnp.sum(face_inv * x[:, None, :], axis=-1)
+        return jnp.transpose(rows.reshape(local, 3, VARS, FACE), (1, 2, 3, 0))
+
+    def send(traces, turn):
+        blocks = []
+        for d in range(groups):
+            pairs = [((turn - 1) * groups + s, turn * groups + (s + d) % groups) for s in range(groups)]
+            blocks.append(lax.ppermute(traces, ("chain", "group"), pairs))
+        return jnp.concatenate(blocks, axis=3)
+
+    sol = full_solve(rhs_t)
+    out = sol
+    traces = face_traces(sol).astype(jnp.bfloat16)
+    face_inv = None
+    x_prev = None
+    for turn in range(1, chains):
+        received = send(traces, turn)
+        if x_prev is not None:
+            out = jnp.where(c == turn - 1, full_solve(x_prev), out)
+        if face_inv is None and turn + 1 < chains:
+            cube = inv.reshape(local, VARS, NP, NP, NP, BLOCK)
+            face_inv = jnp.stack([
+                cube[:, :, NP - 1, :, :, :].reshape(local, VARS, FACE, BLOCK),
+                cube[:, :, :, NP - 1, :, :].reshape(local, VARS, FACE, BLOCK),
+                cube[:, :, :, :, NP - 1, :].reshape(local, VARS, FACE, BLOCK),
+            ], axis=1).reshape(local, 3 * VARS * FACE, BLOCK)
+        x = coupled(received)
+        if turn + 1 < chains:
+            traces = trace_rows(x).astype(jnp.bfloat16)
+            x_prev = x
         else:
-            traces_in = None
-        sol = solve(traces_in)
-        out = jnp.where(c == turn, sol, out)
-        if turn + 1 < chains:
-            traces = face_traces(sol).astype(jnp.bfloat16)
+            out = jnp.where(c == turn, full_solve(x), out)
     return jnp.transpose(out.reshape(local, VARS, NODES), (1, 2, 0))[None]
 
 

time: 52.4 us -> 107 us (2.04)
  the two profiles are of different devices: /device:TPU:7 before, /device:TPU:11 now
where the time goes in v2:
time: 107 us; the launch traced here: 106 us
  local copies, waits for them, and re-layouts  37.5 us (35%)
  waiting for transfers between devices  27.3 us (26%)
  other arithmetic  26.1 us (24%)
  starting transfers between devices  12.1 us (11%)
  matrix products  2.88 us (3%)
    ppermute x12, waiting for transfers between devices, send(): blocks.append(lax.ppermute(traces, ('chain', 'group'), pairs))  27.3 us
    reduce_sum x2, other arithmetic, trace_rows(): rows = jnp.sum(face_inv * x[:, None, :], axis=-1)  17.1 us
    ppermute x12, starting transfers between devices, send(): blocks.append(lax.ppermute(traces, ('chain', 'group'), pairs))  12.1 us
    another operation x1, local copies, waits for them, and re-layouts, body(): cube = inv.reshape(local, VARS, NP, NP, NP, BLOCK)  9.71 us
    reduce_sum x2, other arithmetic, full_solve(): return jnp.sum(inv * x[:, None, :], axis=-1)  8.9 us
    another operation x2, local copies, waits for them, and re-layouts, body(): jnp.stack([cube[:, :, NP - 1, :, :, :].reshape(local, VARS, FACE, BLOCK),...  8.24 us
    ppermute x8, local copies, waits for them, and re-layouts, send(): blocks.append(lax.ppermute(traces, ('chain', 'group'), pairs))  6.83 us
    slice x1, local copies, waits for them, and re-layouts, body(): cube[:, :, :, :, NP - 1, :].reshape(local, VARS, FACE, BLOCK)  6.73 us
  transfers between devices with their start and end apart: 12, of which 4 were waited for; matrix products, arithmetic and copies ran while one was open for 32% of the time, Pallas kernels for 0%

profile of v2, /device:TPU:11, one launch (start us, length us, event | category | flops | bytes accessed | tf_op | source)
XLA Modules:
  0.0 106.2 jit_solution(16932898510326206170)
XLA Ops:
  0.0 0.8 copy.17
  0.9 4.1 %fusion = f32[16,320]{1,0:T(8,128)S(1)} fusion(f32[1,16,320,320]{3,2,1,0:T(8,128)} %param.6, f32[16,320]{1,0:T(8,128)S(1)} %reshape.123), kind=kLoop, calls=%fused_computation.5 | loop fusion | flops 3271680 | bytes 6594560 | tf_op jit(solution)/shard_map/reduce_sum | solution.py:47
  5.3 0.7 collective-permute-start
  6.0 0.7 collective-permute-start.1
  6.7 0.7 collective-permute-start.2
  7.3 0.7 collective-permute-start.3
  8.0 9.7 %reshape_squeeze.3 = f32[16,5,4,4,4,320]{5,4,3,2,1,0:T(4,128)} reshape(f32[1,16,320,320]{3,2,1,0:T(8,128)} %param.6) | data formatting | bytes 13107200 | tf_op jit(solution)/shard_map/reshape;squeeze | solution.py:70
  17.8 3.3 %slice.28 = f32[16,5,4,1,4,320]{5,4,3,2,1,0:T(4,128)} slice(f32[16,5,4,4,4,320]{5,4,3,2,1,0:T(4,128)} %reshape_squeeze.3), slice={[0:16], [0:5], [0:4], [3:4], [0:4], [0:320]} | slice | bytes 3276800 | tf_op jit(solution)/shard_map/slice | solution.py:73
  21.1 6.7 %slice.29 = f32[16,5,4,4,1,320]{5,4,3,2,1,0:T(1,128)} slice(f32[16,5,4,4,4,320]{5,4,3,2,1,0:T(4,128)} %reshape_squeeze.3), slice={[0:16], [0:5], [0:4], [0:4], [3:4], [0:320]} | slice | bytes 3276800 | tf_op jit(solution)/shard_map/slice | solution.py:74
  28.0 3.6 %stack_reshape_squeeze.21 = f32[16,1,5,16,320]{4,1,3,2,0:T(1,128)} reshape(f32[16,5,1,4,4,320]{5,4,3,2,1,0:T(4,128)S(1)} %slice-done) | data formatting | bytes 3276800 | tf_op jit(solution)/shard_map/stack;reshape;squeeze | solution.py:71
  31.6 4.7 %stack_reshape_squeeze.22 = f32[16,1,5,16,320]{4,1,3,2,0:T(1,128)} reshape(f32[16,5,4,1,4,320]{5,4,3,2,1,0:T(4,128)} %slice.28) | data formatting | bytes 3276800 | tf_op jit(solution)/shard_map/stack;reshape;squeeze | solution.py:71
  37.5 8.4 %multiply_reduce_fusion.1 = bf16[16,3,5,16]{1,3,2,0:T(8,128)(2,1)S(1)} fusion(f32[16,1,5,16,320]{4,1,3,2,0:T(1,128)} %bitcast.96, f32[16,1,5,16,320]{4,1,3,2,0:T(1,128)} %stack_reshape_squeeze.22, f32[16,1,5,16,320]{4,1,3,2,0:T(1,128)} %stack_reshape_squeeze.21, f32[16,320]{1,0:T(8,128)S(1)} %sub.40), kind=kLoop, calls=%fused_computation.10 | loop fusion | flops 4911360 | bytes 4943360 | tf_op jit(solution)/shard_map/reduce_sum | solution.py:50
  45.9 1.4 %collective-permute-start.4 = (bf16[3,5,16,16]{0,2,1,3:T(8,128)(2,1)S(1)}, bf16[3,5,16,16]{0,2,1,3:T(8,128)(2,1)}, u32[]{:S(2)}, u32[]{:S(2)}) collective-permute-start(bf16[3,5,16,16]{0,2,1,3:T(8,128)(2,1)S(1)} %bitcast.102), channel_id=1, source_target_pairs={{4,8},{5,9},{6,10},{7,11},{20,24},{21,25},{22,26},{23,27}} | collective-permute-start | bytes 23048 | tf_op jit(solution)/shard_map/ppermute | solution.py:57
  47.3 1.4 %collective-permute-start.5 = (bf16[3,5,16,16]{0,2,1,3:T(8,128)(2,1)S(1)}, bf16[3,5,16,16]{0,2,1,3:T(8,128)(2,1)}, u32[]{:S(2)}, u32[]{:S(2)}) collective-permute-start(bf16[3,5,16,16]{0,2,1,3:T(8,128)(2,1)S(1)} %bitcast.103), channel_id=1, source_target_pairs={{4,9},{5,10},{6,11},{7,8},{20,25},{21,26},{22,27},{23,24}} | collective-permute-start | bytes 23048 | tf_op jit(solution)/shard_map/ppermute | solution.py:57
  48.7 0.7 collective-permute-start.6
  49.4 0.9 collective-permute-start.7
  50.3 1.6 %copy.24 = bf16[3,5,16,16]{3,2,1,0:T(8,128)(2,1)S(1)} copy(bf16[3,5,16,16]{0,2,1,3:T(8,128)(2,1)} %collective-permute-done.4) | data formatting | bytes 15360 | tf_op jit(solution)/shard_map/ppermute | solution.py:57
  51.8 1.6 %copy.25 = bf16[3,5,16,16]{3,2,1,0:T(8,128)(2,1)S(1)} copy(bf16[3,5,16,16]{0,2,1,3:T(8,128)(2,1)} %collective-permute-done.5) | data formatting | bytes 15360 | tf_op jit(solution)/shard_map/ppermute | solution.py:57
  54.0 0.6 copy.27
  55.9 8.6 %multiply_reduce_fusion = bf16[16,3,5,16]{1,3,2,0:T(8,128)(2,1)S(1)} fusion(f32[16,1,5,16,320]{4,1,3,2,0:T(1,128)S(1)} %bitcast.97, f32[16,1,5,16,320]{4,1,3,2,0:T(1,128)} %stack_reshape_squeeze.22, f32[16,1,5,16,320]{4,1,3,2,0:T(1,128)} %stack_reshape_squeeze.21, f32[16,320]{1,0:T(8,128)S(1)} %sub.41), kind=kLoop, calls=%fused_computation.9 | loop fusion | flops 4911360 | bytes 4943360 | tf_op jit(solution)/shard_map/reduce_sum | solution.py:50
  64.5 1.3 %collective-permute-start.8 = (bf16[3,5,16,16]{0,2,1,3:T(8,128)(2,1)S(1)}, bf16[3,5,16,16]{0,2,1,3:T(8,128)(2,1)S(1)}, u32[]{:S(2)}, u32[]{:S(2)}) collective-permute-start(bf16[3,5,16,16]{0,2,1,3:T(8,128)(2,1)S(1)} %bitcast.98), channel_id=1, source_target_pairs={{8,12},{9,13},{10,14},{11,15},{24,28},{25,29},{26,30},{27,31}} | collective-permute-start | bytes 23048 | tf_op jit(solution)/shard_map/ppermute | solution.py:57
  65.8 1.3 %collective-permute-start.9 = (bf16[3,5,16,16]{0,2,1,3:T(8,128)(2,1)S(1)}, bf16[3,5,16,16]{0,2,1,3:T(8,128)(2,1)S(1)}, u32[]{:S(2)}, u32[]{:S(2)}) collective-permute-start(bf16[3,5,16,16]{0,2,1,3:T(8,128)(2,1)S(1)} %bitcast.99), channel_id=1, source_target_pairs={{8,13},{9,14},{10,15},{11,12},{24,29},{25,30},{26,31},{27,28}} | collective-permute-start | bytes 23048 | tf_op jit(solution)/shard_map/ppermute | solution.py:57
  67.1 1.3 %collective-permute-start.10 = (bf16[3,5,16,16]{0,2,1,3:T(8,128)(2,1)S(1)}, bf16[3,5,16,16]{0,2,1,3:T(8,128)(2,1)S(1)}, u32[]{:S(2)}, u32[]{:S(2)}) collective-permute-start(bf16[3,5,16,16]{0,2,1,3:T(8,128)(2,1)S(1)} %bitcast.100), channel_id=1, source_target_pairs={{8,14},{9,15},{10,12},{11,13},{24,30},{25,31},{26,28},{27,29}} | collective-permute-start | bytes 23048 | tf_op jit(solution)/shard_map/ppermute | solution.py:57
  68.4 1.3 %collective-permute-start.11 = (bf16[3,5,16,16]{0,2,1,3:T(8,128)(2,1)S(1)}, bf16[3,5,16,16]{0,2,1,3:T(8,128)(2,1)S(1)}, u32[]{:S(2)}, u32[]{:S(2)}) collective-permute-start(bf16[3,5,16,16]{0,2,1,3:T(8,128)(2,1)S(1)} %bitcast.101), channel_id=1, source_target_pairs={{8,15},{9,12},{10,13},{11,14},{24,31},{25,28},{26,29},{27,30}} | collective-permute-start | bytes 23048 | tf_op jit(solution)/shard_map/ppermute | solution.py:57
  69.7 12.9 %collective-permute-done.8 = bf16[3,5,16,16]{0,2,1,3:T(8,128)(2,1)S(1)} collective-permute-done((bf16[3,5,16,16]{0,2,1,3:T(8,128)(2,1)S(1)}, bf16[3,5,16,16]{0,2,1,3:T(8,128)(2,1)S(1)}, u32[]{:S(2)}, u32[]{:S(2)}) %collective-permute-start.8) | collective-permute-done | bytes 7712 | tf_op jit(solution)/shard_map/ppermute | solution.py:57
  83.2 2.5 %collective-permute-done.9 = bf16[3,5,16,16]{0,2,1,3:T(8,128)(2,1)S(1)} collective-permute-done((bf16[3,5,16,16]{0,2,1,3:T(8,128)(2,1)S(1)}, bf16[3,5,16,16]{0,2,1,3:T(8,128)(2,1)S(1)}, u32[]{:S(2)}, u32[]{:S(2)}) %collective-permute-start.9) | collective-permute-done | bytes 7712 | tf_op jit(solution)/shard_map/ppermute | solution.py:57
  85.7 0.6 copy.33
  86.3 5.6 %collective-permute-done.10 = bf16[3,5,16,16]{0,2,1,3:T(8,128)(2,1)S(1)} collective-permute-done((bf16[3,5,16,16]{0,2,1,3:T(8,128)(2,1)S(1)}, bf16[3,5,16,16]{0,2,1,3:T(8,128)(2,1)S(1)}, u32[]{:S(2)}, u32[]{:S(2)}) %collective-permute-start.10) | collective-permute-done | bytes 7712 | tf_op jit(solution)/shard_map/ppermute | solution.py:57
  91.9 0.6 copy.34
  92.5 6.3 %collective-permute-done.11 = bf16[3,5,16,16]{0,2,1,3:T(8,128)(2,1)S(1)} collective-permute-done((bf16[3,5,16,16]{0,2,1,3:T(8,128)(2,1)S(1)}, bf16[3,5,16,16]{0,2,1,3:T(8,128)(2,1)S(1)}, u32[]{:S(2)}, u32[]{:S(2)}) %collective-permute-start.11) | collective-permute-done | bytes 7712 | tf_op jit(solution)/shard_map/ppermute | solution.py:57
  100.7 4.8 %fusion.3 = (f32[16,320]{1,0:T(8,128)S(1)}, f32[16,320]{1,0:T(8,128)S(1)}, f32[16,320]{1,0:T(8,128)S(1)}) fusion(f32[1,16,320,320]{3,2,1,0:T(8,128)} %param.6, f32[16,320]{1,0:T(8,128)S(1)} %sub.40, f32[16,320]{1,0:T(8,128)S(1)} %sub.42, f32[16,320]{1,0:T(8,128)S(1)} %sub.41), kind=kLoop, calls=%fused_computation.8 | loop fusion | flops 9815040 | bytes 6676480 | tf_op jit(solution)/shard_map/reduce_sum | solution.py:47
  105.5 0.6 copy.40
  (55 shorter events, 6.0 us)
Async XLA Ops:
  0.0 37.1 %copy-start = (f32[3,64,16]{1,2,0:T(8,128)S(1)}, f32[3,64,16]{1,2,0:T(8,128)}, u32[]{:S(2)}) copy-start(f32[3,64,16]{1,2,0:T(8,128)} %param.9) | copy-start | bytes 36868
  0.0 8.0 %copy-start.3 = (s32[1,3,16]{2,0,1:T(1,128)S(1)}, s32[1,3,16]{2,0,1:T(1,128)}, u32[]{:S(2)}) copy-start(s32[1,3,16]{2,0,1:T(1,128)} %param.8) | copy-start | bytes 580
  5.3 30.9 %collective-permute-start = (bf16[3,5,16,16]{3,2,1,0:T(8,128)(2,1)S(1)}, bf16[3,5,16,16]{3,2,1,0:T(8,128)(2,1)S(1)}, u32[]{:S(2)}, u32[]{:S(2)}) collective-permute-start(bf16[3,5,16,16]{3,2,1,0:T(8,128)(2,1)S(1)} %maximum_bitcast_fusion), channel_id=1, source_target_pairs={{0,4},{1,5},{2,6},{3,7},{16,20},{17,21},{18,22},{19,23}} | collective-permute-start | bytes 23048 | tf_op jit(solution)/shard_map/ppermute | solution.py:57
  6.0 30.3 %collective-permute-start.1 = (bf16[3,5,16,16]{3,2,1,0:T(8,128)(2,1)S(1)}, bf16[3,5,16,16]{3,2,1,0:T(8,128)(2,1)S(1)}, u32[]{:S(2)}, u32[]{:S(2)}) collective-permute-start(bf16[3,5,16,16]{3,2,1,0:T(8,128)(2,1)S(1)} %maximum_bitcast_fusion), channel_id=1, source_target_pairs={{0,5},{1,6},{2,7},{3,4},{16,21},{17,22},{18,23},{19,20}} | collective-permute-start | bytes 23048 | tf_op jit(solution)/shard_map/ppermute | solution.py:57
  6.7 29.6 %collective-permute-start.2 = (bf16[3,5,16,16]{3,2,1,0:T(8,128)(2,1)S(1)}, bf16[3,5,16,16]{3,2,1,0:T(8,128)(2,1)S(1)}, u32[]{:S(2)}, u32[]{:S(2)}) collective-permute-start(bf16[3,5,16,16]{3,2,1,0:T(8,128)(2,1)S(1)} %maximum_bitcast_fusion), channel_id=1, source_target_pairs={{0,6},{1,7},{2,4},{3,5},{16,22},{17,23},{18,20},{19,21}} | collective-permute-start | bytes 23048 | tf_op jit(solution)/shard_map/ppermute | solution.py:57
  7.3 28.9 %collective-permute-start.3 = (bf16[3,5,16,16]{3,2,1,0:T(8,128)(2,1)S(1)}, bf16[3,5,16,16]{3,2,1,0:T(8,128)(2,1)S(1)}, u32[]{:S(2)}, u32[]{:S(2)}) collective-permute-start(bf16[3,5,16,16]{3,2,1,0:T(8,128)(2,1)S(1)} %maximum_bitcast_fusion), channel_id=1, source_target_pairs={{0,7},{1,4},{2,5},{3,6},{16,23},{17,20},{18,21},{19,22}} | collective-permute-start | bytes 23048 | tf_op jit(solution)/shard_map/ppermute | solution.py:57
  17.8 10.0 %copy-start.2 = (f32[1,3,5,5,16]{4,0,3,2,1:T(1,128)S(1)}, f32[1,3,5,5,16]{4,0,3,2,1:T(1,128)}, u32[]{:S(2)}) copy-start(f32[1,3,5,5,16]{4,0,3,2,1:T(1,128)} %param.7) | copy-start | bytes 14404
  17.8 10.2 %slice-start = ((f32[16,5,4,4,4,320]{5,4,3,2,1,0:T(4,128)}), f32[16,5,1,4,4,320]{5,4,3,2,1,0:T(4,128)S(1)}, s32[]{:S(2)}) async-start(f32[16,5,4,4,4,320]{5,4,3,2,1,0:T(4,128)} %reshape_squeeze.3), calls=%async_computation | async-start | bytes 3932160 | tf_op jit(solution)/shard_map/slice | solution.py:72
  31.6 24.3 %copy-start.1 = (f32[16,5,4,4,1,320]{5,4,3,2,1,0:T(1,128)S(1)}, f32[16,5,4,4,1,320]{5,4,3,2,1,0:T(1,128)}, u32[]{:S(2)}) copy-start(f32[16,5,4,4,1,320]{5,4,3,2,1,0:T(1,128)} %slice.29) | copy-start | bytes 4915204
  45.9 4.3 %collective-permute-start.4 = (bf16[3,5,16,16]{0,2,1,3:T(8,128)(2,1)S(1)}, bf16[3,5,16,16]{0,2,1,3:T(8,128)(2,1)}, u32[]{:S(2)}, u32[]{:S(2)}) collective-permute-start(bf16[3,5,16,16]{0,2,1,3:T(8,128)(2,1)S(1)} %bitcast.102), channel_id=1, source_target_pairs={{4,8},{5,9},{6,10},{7,11},{20,24},{21,25},{22,26},{23,27}} | collective-permute-start | bytes 23048 | tf_op jit(solution)/shard_map/ppermute | solution.py:57
  47.3 4.5 %collective-permute-start.5 = (bf16[3,5,16,16]{0,2,1,3:T(8,128)(2,1)S(1)}, bf16[3,5,16,16]{0,2,1,3:T(8,128)(2,1)}, u32[]{:S(2)}, u32[]{:S(2)}) collective-permute-start(bf16[3,5,16,16]{0,2,1,3:T(8,128)(2,1)S(1)} %bitcast.103), channel_id=1, source_target_pairs={{4,9},{5,10},{6,11},{7,8},{20,25},{21,26},{22,27},{23,24}} | collective-permute-start | bytes 23048 | tf_op jit(solution)/shard_map/ppermute | solution.py:57
  48.7 4.7 %collective-permute-start.6 = (bf16[3,5,16,16]{0,2,1,3:T(8,128)(2,1)S(1)}, bf16[3,5,16,16]{0,2,1,3:T(8,128)(2,1)S(1)}, u32[]{:S(2)}, u32[]{:S(2)}) collective-permute-start(bf16[3,5,16,16]{0,2,1,3:T(8,128)(2,1)S(1)} %bitcast.104), channel_id=1, source_target_pairs={{4,10},{5,11},{6,8},{7,9},{20,26},{21,27},{22,24},{23,25}} | collective-permute-start | bytes 23048 | tf_op jit(solution)/shard_map/ppermute | solution.py:57
  49.4 4.7 %collective-permute-start.7 = (bf16[3,5,16,16]{0,2,1,3:T(8,128)(2,1)S(1)}, bf16[3,5,16,16]{0,2,1,3:T(8,128)(2,1)S(1)}, u32[]{:S(2)}, u32[]{:S(2)}) collective-permute-start(bf16[3,5,16,16]{0,2,1,3:T(8,128)(2,1)S(1)} %bitcast.105), channel_id=1, source_target_pairs={{4,11},{5,8},{6,9},{7,10},{20,27},{21,24},{22,25},{23,26}} | collective-permute-start | bytes 23048 | tf_op jit(solution)/shard_map/ppermute | solution.py:57
  64.5 18.1 %collective-permute-start.8 = (bf16[3,5,16,16]{0,2,1,3:T(8,128)(2,1)S(1)}, bf16[3,5,16,16]{0,2,1,3:T(8,128)(2,1)S(1)}, u32[]{:S(2)}, u32[]{:S(2)}) collective-permute-start(bf16[3,5,16,16]{0,2,1,3:T(8,128)(2,1)S(1)} %bitcast.98), channel_id=1, source_target_pairs={{8,12},{9,13},{10,14},{11,15},{24,28},{25,29},{26,30},{27,31}} | collective-permute-start | bytes 23048 | tf_op jit(solution)/shard_map/ppermute | solution.py:57
  65.8 19.9 %collective-permute-start.9 = (bf16[3,5,16,16]{0,2,1,3:T(8,128)(2,1)S(1)}, bf16[3,5,16,16]{0,2,1,3:T(8,128)(2,1)S(1)}, u32[]{:S(2)}, u32[]{:S(2)}) collective-permute-start(bf16[3,5,16,16]{0,2,1,3:T(8,128)(2,1)S(1)} %bitcast.99), channel_id=1, source_target_pairs={{8,13},{9,14},{10,15},{11,12},{24,29},{25,30},{26,31},{27,28}} | collective-permute-start | bytes 23048 | tf_op jit(solution)/shard_map/ppermute | solution.py:57
  67.1 24.8 %collective-permute-start.10 = (bf16[3,5,16,16]{0,2,1,3:T(8,128)(2,1)S(1)}, bf16[3,5,16,16]{0,2,1,3:T(8,128)(2,1)S(1)}, u32[]{:S(2)}, u32[]{:S(2)}) collective-permute-start(bf16[3,5,16,16]{0,2,1,3:T(8,128)(2,1)S(1)} %bitcast.100), channel_id=1, source_target_pairs={{8,14},{9,15},{10,12},{11,13},{24,30},{25,31},{26,28},{27,29}} | collective-permute-start | bytes 23048 | tf_op jit(solution)/shard_map/ppermute | solution.py:57
  68.4 30.4 %collective-permute-start.11 = (bf16[3,5,16,16]{0,2,1,3:T(8,128)(2,1)S(1)}, bf16[3,5,16,16]{0,2,1,3:T(8,128)(2,1)S(1)}, u32[]{:S(2)}, u32[]{:S(2)}) collective-permute-start(bf16[3,5,16,16]{0,2,1,3:T(8,128)(2,1)S(1)} %bitcast.101), channel_id=1, source_target_pairs={{8,15},{9,12},{10,13},{11,14},{24,31},{25,28},{26,29},{27,30}} | collective-permute-start | bytes 23048 | tf_op jit(solution)/shard_map/ppermute | solution.py:57

commit v3 on v1

--- a/solution.py
+++ b/solution.py
@@ -37,28 +37,23 @@
     pos = shift * local + up % local
     onehot = (jnp.arange(groups * local)[None, :, None] == pos[:, None, :]).astype(jnp.bfloat16)
 
+    base = jnp.sum(inv * rhs_t[:, None, :], axis=-1)
+    lifted = jnp.einsum("erwi,kif->erwkf", inv.reshape(local, BLOCK, VARS, NODES), lift, precision=HIGH)
+    coupled_inv = jnp.einsum("erwkf,kwve->erkvf", lifted, jac, precision=HIGH).reshape(local, BLOCK, 3 * VARS * FACE)
+
     def solve(traces_in):
-        if traces_in is None:
-            x = rhs_t
-        else:
-            upstream = jnp.einsum("kvfp,kpe->kvfe", traces_in, onehot, preferred_element_type=jnp.float32)
-            mixed = jnp.einsum("kwve,kvfe->kwfe", jac, upstream, precision=HIGH)
-            coupling = jnp.einsum("kwfe,kif->ewi", mixed, lift, precision=HIGH)
-            x = rhs_t - coupling.reshape(local, BLOCK)
-        return jnp.sum(inv * x[:, None, :], axis=-1)
+        upstream = jnp.einsum("kvfp,kpe->kvfe", traces_in, onehot, preferred_element_type=jnp.float32)
+        upstream = jnp.transpose(upstream, (3, 0, 1, 2)).reshape(local, 3 * VARS * FACE)
+        return base - jnp.sum(coupled_inv * upstream[:, None, :], axis=-1)
 
-    out = jnp.zeros((local, BLOCK), jnp.float32)
-    traces = None
-    for turn in range(chains):
-        if turn > 0:
-            blocks = []
-            for d in range(groups):
-                pairs = [((turn - 1) * groups + s, turn * groups + (s + d) % groups) for s in range(groups)]
-                blocks.append(lax.ppermute(traces, ("chain", "group"), pairs))
-            traces_in = jnp.concatenate(blocks, axis=3)
-        else:
-            traces_in = None
-        sol = solve(traces_in)
+    out = base
+    traces = face_traces(base).astype(jnp.bfloat16)
+    for turn in range(1, chains):
+        blocks = []
+        for d in range(groups):
+            pairs = [((turn - 1) * groups + s, turn * groups + (s + d) % groups) for s in range(groups)]
+            blocks.append(lax.ppermute(traces, ("chain", "group"), pairs))
+        sol = solve(jnp.concatenate(blocks, axis=3))
         out = jnp.where(c == turn, sol, out)
         if turn + 1 < chains:
             traces = face_traces(sol).astype(jnp.bfloat16)

time: 52.4 us -> 79.6 us (1.52)
  matrix products: 2.87 us -> 26.5 us
  local copies, waits for them, and re-layouts: 3.09 us -> 12.4 us
  waiting for transfers between devices: 18.4 us -> 14.9 us
  other arithmetic: 16.7 us -> 14.1 us
    dot_general x6 -> x2, matrix products: 2.16 us -> 25.8 us  [the longest x1 16 us: body(): jnp.einsum('erwkf,kwve->erkvf', lifted, jac, precision=HIGH)]
    unnamed x10 -> x11, local copies, waits for them, and re-layouts: 0.05 us -> 8.7 us
    ppermute x12, waiting for transfers between devices: 18.4 us -> 14.9 us  [body(): blocks.append(lax.ppermute(traces, ('chain', 'group'), pairs))]
    reduce_sum x4 -> x3, other arithmetic: 16.5 us -> 14 us  [the longest x2 9.85 us: solve(): return base - jnp.sum(coupled_inv * upstream[:, None, :], axis=-1)]
    transpose x3, local copies, waits for them, and re-layouts: 0.06 us -> 1.1 us  [solve(): jnp.transpose(upstream, (3, 0, 1, 2)).reshape(local, 3 * VARS * FACE)]
  transfers between devices with their start and end apart: 12 -> 12, of which waited for: 2 -> 3; matrix products, arithmetic and copies ran while one was open for 0% -> 24% of each run, Pallas kernels for 0% -> 0%
where the time goes in v3:
time: 79.6 us; the launch traced here: 79 us
  matrix products  26.5 us (33%)
  waiting for transfers between devices  14.9 us (19%)
  other arithmetic  14.1 us (18%)
  local copies, waits for them, and re-layouts  12.4 us (16%)
  starting transfers between devices  10.7 us (13%)
    dot_general x1, matrix products, body(): jnp.einsum('erwkf,kwve->erkvf', lifted, jac, precision=HIGH)  16 us
    ppermute x12, waiting for transfers between devices, body(): blocks.append(lax.ppermute(traces, ('chain', 'group'), pairs))  14.9 us
    ppermute x12, starting transfers between devices, body(): blocks.append(lax.ppermute(traces, ('chain', 'group'), pairs))  10.7 us
    dot_general x1, matrix products, body(): jnp.einsum('erwi,kif->erwkf', inv.reshape(local, BLOCK, VARS, NODES), lif...  9.86 us
    reduce_sum x2, other arithmetic, solve(): return base - jnp.sum(coupled_inv * upstream[:, None, :], axis=-1)  9.85 us
    unnamed x11, local copies, waits for them, and re-layouts  8.7 us
    reduce_sum x1, other arithmetic, body(): base = jnp.sum(inv * rhs_t[:, None, :], axis=-1)  4.14 us
  transfers between devices with their start and end apart: 12, of which 3 were waited for; matrix products, arithmetic and copies ran while one was open for 24% of the time, Pallas kernels for 0%

profile of v3, /device:TPU:7, one launch (start us, length us, event | category | flops | bytes accessed | tf_op | source)
XLA Modules:
  0.0 79.0 jit_solution(13186178400969901134)
XLA Ops:
  0.0 0.8 %copy.39 = f32[16,5,64]{2,1,0:T(8,128)S(1)} copy(f32[16,5,64]{2,0,1:T(8,128)} %bitcast.107) | data formatting | bytes 40960 | tf_op jit(solution)/shard_map/transpose | solution.py:34
  0.9 4.1 %fusion.5 = f32[16,320]{1,0:T(8,128)S(1)} fusion(f32[1,16,320,320]{3,2,1,0:T(8,128)} %param.6, f32[16,320]{1,0:T(8,128)S(1)} %mul.45), kind=kLoop, calls=%fused_computation.9 | loop fusion | flops 3271680 | bytes 6594560 | tf_op jit(solution)/shard_map/reduce_sum | solution.py:40
  5.0 0.1 copy.44
  5.3 0.7 collective-permute-start
  6.0 0.7 collective-permute-start.1
  6.6 0.7 collective-permute-start.2
  7.3 0.7 collective-permute-start.3
  8.0 8.6 %copy.40 = f32[1,16,320,320]{2,3,1,0:T(8,128)} copy(f32[1,16,320,320]{3,2,1,0:T(8,128)} %param.6) | data formatting | bytes 13107200 | tf_op args[1]
  16.7 9.9 %fusion.30 = f32[16,320,5,3,16]{1,4,3,2,0:T(8,128)} fusion(f32[16,320,5,64,1]{1,3,4,2,0:T(8,128)} %bitcast.87, f32[3,64,16]{1,2,0:T(8,128)S(1)} %copy-done), kind=kOutput, calls=%fused_computation.42 | convolution fusion | flops 943718400 | bytes 11481088 | tf_op jit(solution)/shard_map/erwi,kif->erwkf/dot_general | solution.py:41
  26.6 0.2 copy.53
  26.8 0.2 convolution_bitcast_fusion.2
  27.0 0.4 copy.45
  27.4 16.0 %fusion = (f32[16,320]{1,0:T(8,128)S(1)}, f32[16,3,320,16,5]{2,4,3,1,0:T(8,128)}) fusion(f32[16,3,5,16]{2,3,1,0:T(8,128)S(1)} %copy.45, f32[3,5,5,16,1]{1,2,4,0,3:T(8,128)S(1)} %copy.53, f32[16,320,5,3,16]{1,4,3,2,0:T(8,128)} %fusion.30), kind=kOutput, calls=%fused_computation.3 | convolution fusion | flops 76180480 | bytes 9871040 | tf_op jit(solution)/shard_map/erwkf,kwve->erkvf/dot_general | solution.py:42
  43.4 0.1 copy.46
  43.6 0.7 collective-permute-start.4
  44.3 0.7 collective-permute-start.5
  45.0 0.8 %collective-permute-start.6 = (bf16[3,5,16,16]{3,2,1,0:T(8,128)(2,1)S(1)}, bf16[3,5,16,16]{3,2,1,0:T(8,128)(2,1)S(1)}, u32[]{:S(2)}, u32[]{:S(2)}) collective-permute-start(bf16[3,5,16,16]{3,2,1,0:T(8,128)(2,1)S(1)} %maximum_bitcast_fusion.1), channel_id=1, source_target_pairs={{4,10},{5,11},{6,8},{7,9},{20,26},{21,27},{22,24},{23,25}} | collective-permute-start | bytes 23048 | tf_op jit(solution)/shard_map/ppermute | solution.py:55
  45.8 0.7 collective-permute-start.7
  46.6 0.2 convolution_bitcast_fusion.1
  46.8 0.4 copy.47
  47.2 4.9 %fusion.1 = f32[16,320]{1,0:T(8,128)S(1)} fusion(f32[16,3,320,16,5]{2,4,3,1,0:T(8,128)} %get-tuple-element.6, f32[16,3,5,16]{2,3,1,0:T(8,128)S(1)} %copy.47), kind=kLoop, calls=%fused_computation.4 | loop fusion | flops 2452480 | bytes 4951040 | tf_op jit(solution)/shard_map/reduce_sum | solution.py:47
  52.4 1.3 %collective-permute-start.10 = (bf16[3,5,16,16]{3,2,1,0:T(8,128)(2,1)S(1)}, bf16[3,5,16,16]{3,2,1,0:T(8,128)(2,1)S(1)}, u32[]{:S(2)}, u32[]{:S(2)}) collective-permute-start(bf16[3,5,16,16]{3,2,1,0:T(8,128)(2,1)S(1)} %maximum_bitcast_fusion.2), channel_id=1, source_target_pairs={{8,14},{9,15},{10,12},{11,13},{24,30},{25,31},{26,28},{27,29}} | collective-permute-start | bytes 23048 | tf_op jit(solution)/shard_map/ppermute | solution.py:55
  53.7 1.3 %collective-permute-start.11 = (bf16[3,5,16,16]{3,2,1,0:T(8,128)(2,1)S(1)}, bf16[3,5,16,16]{3,2,1,0:T(8,128)(2,1)S(1)}, u32[]{:S(2)}, u32[]{:S(2)}) collective-permute-start(bf16[3,5,16,16]{3,2,1,0:T(8,128)(2,1)S(1)} %maximum_bitcast_fusion.2), channel_id=1, source_target_pairs={{8,15},{9,12},{10,13},{11,14},{24,31},{25,28},{26,29},{27,30}} | collective-permute-start | bytes 23048 | tf_op jit(solution)/shard_map/ppermute | solution.py:55
  55.0 1.3 %collective-permute-start.8 = (bf16[3,5,16,16]{3,2,1,0:T(8,128)(2,1)S(1)}, bf16[3,5,16,16]{3,2,1,0:T(8,128)(2,1)S(1)}, u32[]{:S(2)}, u32[]{:S(2)}) collective-permute-start(bf16[3,5,16,16]{3,2,1,0:T(8,128)(2,1)S(1)} %maximum_bitcast_fusion.2), channel_id=1, source_target_pairs={{8,12},{9,13},{10,14},{11,15},{24,28},{25,29},{26,30},{27,31}} | collective-permute-start | bytes 23048 | tf_op jit(solution)/shard_map/ppermute | solution.py:55
  56.3 1.3 %collective-permute-start.9 = (bf16[3,5,16,16]{3,2,1,0:T(8,128)(2,1)S(1)}, bf16[3,5,16,16]{3,2,1,0:T(8,128)(2,1)S(1)}, u32[]{:S(2)}, u32[]{:S(2)}) collective-permute-start(bf16[3,5,16,16]{3,2,1,0:T(8,128)(2,1)S(1)} %maximum_bitcast_fusion.2), channel_id=1, source_target_pairs={{8,13},{9,14},{10,15},{11,12},{24,29},{25,30},{26,31},{27,28}} | collective-permute-start | bytes 23048 | tf_op jit(solution)/shard_map/ppermute | solution.py:55
  57.8 8.5 %collective-permute-done.10 = bf16[3,5,16,16]{3,2,1,0:T(8,128)(2,1)S(1)} collective-permute-done((bf16[3,5,16,16]{3,2,1,0:T(8,128)(2,1)S(1)}, bf16[3,5,16,16]{3,2,1,0:T(8,128)(2,1)S(1)}, u32[]{:S(2)}, u32[]{:S(2)}) %collective-permute-start.10) | collective-permute-done | bytes 7712 | tf_op jit(solution)/shard_map/ppermute | solution.py:55
  66.3 1.2 %collective-permute-done.11 = bf16[3,5,16,16]{3,2,1,0:T(8,128)(2,1)S(1)} collective-permute-done((bf16[3,5,16,16]{3,2,1,0:T(8,128)(2,1)S(1)}, bf16[3,5,16,16]{3,2,1,0:T(8,128)(2,1)S(1)}, u32[]{:S(2)}, u32[]{:S(2)}) %collective-permute-start.11) | collective-permute-done | bytes 7712 | tf_op jit(solution)/shard_map/ppermute | solution.py:55
  67.4 5.3 %collective-permute-done.9 = bf16[3,5,16,16]{3,2,1,0:T(8,128)(2,1)S(1)} collective-permute-done((bf16[3,5,16,16]{3,2,1,0:T(8,128)(2,1)S(1)}, bf16[3,5,16,16]{3,2,1,0:T(8,128)(2,1)S(1)}, u32[]{:S(2)}, u32[]{:S(2)}) %collective-permute-start.9) | collective-permute-done | bytes 7712 | tf_op jit(solution)/shard_map/ppermute | solution.py:55
  72.7 0.2 convolution_bitcast_fusion
  73.0 0.4 copy.49
  73.3 4.9 %fusion.2 = f32[16,320]{1,0:T(8,128)S(1)} fusion(f32[16,3,320,16,5]{2,4,3,1,0:T(8,128)} %get-tuple-element.6, f32[16,3,5,16]{2,3,1,0:T(8,128)S(1)} %copy.49), kind=kLoop, calls=%fused_computation.5 | loop fusion | flops 2452480 | bytes 4951040 | tf_op jit(solution)/shard_map/reduce_sum | solution.py:47
  78.4 0.6 copy.50
  (42 shorter events, 0.9 us)
Async XLA Ops:
  0.0 16.6 %copy-start = (f32[3,64,16]{1,2,0:T(8,128)S(1)}, f32[3,64,16]{1,2,0:T(8,128)}, u32[]{:S(2)}) copy-start(f32[3,64,16]{1,2,0:T(8,128)} %param.9) | copy-start | bytes 36868
  5.3 21.4 %collective-permute-start = (bf16[3,5,16,16]{3,2,1,0:T(8,128)(2,1)S(1)}, bf16[3,5,16,16]{3,2,1,0:T(8,128)(2,1)S(1)}, u32[]{:S(2)}, u32[]{:S(2)}) collective-permute-start(bf16[3,5,16,16]{3,2,1,0:T(8,128)(2,1)S(1)} %maximum_bitcast_fusion), channel_id=1, source_target_pairs={{0,4},{1,5},{2,6},{3,7},{16,20},{17,21},{18,22},{19,23}} | collective-permute-start | bytes 23048 | tf_op jit(solution)/shard_map/ppermute | solution.py:55
  6.0 20.8 %collective-permute-start.1 = (bf16[3,5,16,16]{3,2,1,0:T(8,128)(2,1)S(1)}, bf16[3,5,16,16]{3,2,1,0:T(8,128)(2,1)S(1)}, u32[]{:S(2)}, u32[]{:S(2)}) collective-permute-start(bf16[3,5,16,16]{3,2,1,0:T(8,128)(2,1)S(1)} %maximum_bitcast_fusion), channel_id=1, source_target_pairs={{0,5},{1,6},{2,7},{3,4},{16,21},{17,22},{18,23},{19,20}} | collective-permute-start | bytes 23048 | tf_op jit(solution)/shard_map/ppermute | solution.py:55
  6.6 20.1 %collective-permute-start.2 = (bf16[3,5,16,16]{3,2,1,0:T(8,128)(2,1)S(1)}, bf16[3,5,16,16]{3,2,1,0:T(8,128)(2,1)S(1)}, u32[]{:S(2)}, u32[]{:S(2)}) collective-permute-start(bf16[3,5,16,16]{3,2,1,0:T(8,128)(2,1)S(1)} %maximum_bitcast_fusion), channel_id=1, source_target_pairs={{0,6},{1,7},{2,4},{3,5},{16,22},{17,23},{18,20},{19,21}} | collective-permute-start | bytes 23048 | tf_op jit(solution)/shard_map/ppermute | solution.py:55
  7.3 19.5 %collective-permute-start.3 = (bf16[3,5,16,16]{3,2,1,0:T(8,128)(2,1)S(1)}, bf16[3,5,16,16]{3,2,1,0:T(8,128)(2,1)S(1)}, u32[]{:S(2)}, u32[]{:S(2)}) collective-permute-start(bf16[3,5,16,16]{3,2,1,0:T(8,128)(2,1)S(1)} %maximum_bitcast_fusion), channel_id=1, source_target_pairs={{0,7},{1,4},{2,5},{3,6},{16,23},{17,20},{18,21},{19,22}} | collective-permute-start | bytes 23048 | tf_op jit(solution)/shard_map/ppermute | solution.py:55
  16.6 9.9 %copy-start.2 = (s32[1,3,16]{2,0,1:T(1,128)S(1)}, s32[1,3,16]{2,0,1:T(1,128)}, u32[]{:S(2)}) copy-start(s32[1,3,16]{2,0,1:T(1,128)} %param.8) | copy-start | bytes 580
  16.6 9.9 %copy-start.1 = (f32[1,3,5,5,16]{4,0,3,2,1:T(1,128)S(1)}, f32[1,3,5,5,16]{4,0,3,2,1:T(1,128)}, u32[]{:S(2)}) copy-start(f32[1,3,5,5,16]{4,0,3,2,1:T(1,128)} %param.7) | copy-start | bytes 14404
  43.6 2.9 %collective-permute-start.4 = (bf16[3,5,16,16]{3,2,1,0:T(8,128)(2,1)S(1)}, bf16[3,5,16,16]{3,2,1,0:T(8,128)(2,1)S(1)}, u32[]{:S(2)}, u32[]{:S(2)}) collective-permute-start(bf16[3,5,16,16]{3,2,1,0:T(8,128)(2,1)S(1)} %maximum_bitcast_fusion.1), channel_id=1, source_target_pairs={{4,8},{5,9},{6,10},{7,11},{20,24},{21,25},{22,26},{23,27}} | collective-permute-start | bytes 23048 | tf_op jit(solution)/shard_map/ppermute | solution.py:55
  44.3 2.2 %collective-permute-start.5 = (bf16[3,5,16,16]{3,2,1,0:T(8,128)(2,1)S(1)}, bf16[3,5,16,16]{3,2,1,0:T(8,128)(2,1)S(1)}, u32[]{:S(2)}, u32[]{:S(2)}) collective-permute-start(bf16[3,5,16,16]{3,2,1,0:T(8,128)(2,1)S(1)} %maximum_bitcast_fusion.1), channel_id=1, source_target_pairs={{4,9},{5,10},{6,11},{7,8},{20,25},{21,26},{22,27},{23,24}} | collective-permute-start | bytes 23048 | tf_op jit(solution)/shard_map/ppermute | solution.py:55
  45.0 1.5 %collective-permute-start.6 = (bf16[3,5,16,16]{3,2,1,0:T(8,128)(2,1)S(1)}, bf16[3,5,16,16]{3,2,1,0:T(8,128)(2,1)S(1)}, u32[]{:S(2)}, u32[]{:S(2)}) collective-permute-start(bf16[3,5,16,16]{3,2,1,0:T(8,128)(2,1)S(1)} %maximum_bitcast_fusion.1), channel_id=1, source_target_pairs={{4,10},{5,11},{6,8},{7,9},{20,26},{21,27},{22,24},{23,25}} | collective-permute-start | bytes 23048 | tf_op jit(solution)/shard_map/ppermute | solution.py:55
  45.8 0.7 collective-permute-start.7
  52.4 13.9 %collective-permute-start.10 = (bf16[3,5,16,16]{3,2,1,0:T(8,128)(2,1)S(1)}, bf16[3,5,16,16]{3,2,1,0:T(8,128)(2,1)S(1)}, u32[]{:S(2)}, u32[]{:S(2)}) collective-permute-start(bf16[3,5,16,16]{3,2,1,0:T(8,128)(2,1)S(1)} %maximum_bitcast_fusion.2), channel_id=1, source_target_pairs={{8,14},{9,15},{10,12},{11,13},{24,30},{25,31},{26,28},{27,29}} | collective-permute-start | bytes 23048 | tf_op jit(solution)/shard_map/ppermute | solution.py:55
  53.7 13.8 %collective-permute-start.11 = (bf16[3,5,16,16]{3,2,1,0:T(8,128)(2,1)S(1)}, bf16[3,5,16,16]{3,2,1,0:T(8,128)(2,1)S(1)}, u32[]{:S(2)}, u32[]{:S(2)}) collective-permute-start(bf16[3,5,16,16]{3,2,1,0:T(8,128)(2,1)S(1)} %maximum_bitcast_fusion.2), channel_id=1, source_target_pairs={{8,15},{9,12},{10,13},{11,14},{24,31},{25,28},{26,29},{27,30}} | collective-permute-start | bytes 23048 | tf_op jit(solution)/shard_map/ppermute | solution.py:55
  55.0 12.5 %collective-permute-start.8 = (bf16[3,5,16,16]{3,2,1,0:T(8,128)(2,1)S(1)}, bf16[3,5,16,16]{3,2,1,0:T(8,128)(2,1)S(1)}, u32[]{:S(2)}, u32[]{:S(2)}) collective-permute-start(bf16[3,5,16,16]{3,2,1,0:T(8,128)(2,1)S(1)} %maximum_bitcast_fusion.2), channel_id=1, source_target_pairs={{8,12},{9,13},{10,14},{11,15},{24,28},{25,29},{26,30},{27,31}} | collective-permute-start | bytes 23048 | tf_op jit(solution)/shard_map/ppermute | solution.py:55
  56.3 16.5 %collective-permute-start.9 = (bf16[3,5,16,16]{3,2,1,0:T(8,128)(2,1)S(1)}, bf16[3,5,16,16]{3,2,1,0:T(8,128)(2,1)S(1)}, u32[]{:S(2)}, u32[]{:S(2)}) collective-permute-start(bf16[3,5,16,16]{3,2,1,0:T(8,128)(2,1)S(1)} %maximum_bitcast_fusion.2), channel_id=1, source_target_pairs={{8,13},{9,14},{10,15},{11,12},{24,29},{25,30},{26,31},{27,28}} | collective-permute-start | bytes 23048 | tf_op jit(solution)/shard_map/ppermute | solution.py:55

commit v4 on v1

--- a/solution.py
+++ b/solution.py
@@ -35,14 +35,14 @@
 
     shift = (g - up // local) % groups
     pos = shift * local + up % local
-    onehot = (jnp.arange(groups * local)[None, :, None] == pos[:, None, :]).astype(jnp.bfloat16)
+    onehot = (jnp.arange(groups * local)[None, :, None] == pos[:, None, :]).astype(jnp.float32)
+    picked_jac = jnp.einsum("kpe,kwve->kvpwe", onehot, jac)
 
     def solve(traces_in):
         if traces_in is None:
             x = rhs_t
         else:
-            upstream = jnp.einsum("kvfp,kpe->kvfe", traces_in, onehot, preferred_element_type=jnp.float32)
-            mixed = jnp.einsum("kwve,kvfe->kwfe", jac, upstream, precision=HIGH)
+            mixed = jnp.einsum("kvfp,kvpwe->kwfe", traces_in.astype(jnp.float32), picked_jac, precision=HIGH)
             coupling = jnp.einsum("kwfe,kif->ewi", mixed, lift, precision=HIGH)
             x = rhs_t - coupling.reshape(local, BLOCK)
         return jnp.sum(inv * x[:, None, :], axis=-1)

time: 52.4 us -> 51.6 us (0.985)
  local copies, waits for them, and re-layouts: 3.09 us -> 2.53 us
    dot_general x6 -> x3, matrix products: 2.06 us -> 1.71 us  [solve(): jnp.einsum('kvfp,kvpwe->kwfe', traces_in.astype(jnp.float32), picked_jac,...]
where the time goes in v4:
time: 51.6 us; the launch traced here: 51.2 us
  waiting for transfers between devices  18.5 us (36%)
  other arithmetic  16.7 us (32%)
  starting transfers between devices  10.5 us (20%)
  local copies, waits for them, and re-layouts  2.53 us (5%)
  matrix products  2.53 us (5%)
    ppermute x12, waiting for transfers between devices, body(): blocks.append(lax.ppermute(traces, ('chain', 'group'), pairs))  18.5 us
    reduce_sum x4, other arithmetic, solve(): return jnp.sum(inv * x[:, None, :], axis=-1)  16.5 us
    ppermute x12, starting transfers between devices, body(): blocks.append(lax.ppermute(traces, ('chain', 'group'), pairs))  10.5 us
    dot_general x3, matrix products, solve(): jnp.einsum('kvfp,kvpwe->kwfe', traces_in.astype(jnp.float32), picked_jac,...  1.71 us
  transfers between devices with their start and end apart: 12, of which 2 were waited for; matrix products, arithmetic and copies ran while one was open for 0% of the time, Pallas kernels for 0%

profile of v4, /device:TPU:7, one launch (start us, length us, event | category | flops | bytes accessed | tf_op | source)
XLA Modules:
  0.0 51.2 jit_solution(729453553007291319)
XLA Ops:
  0.0 0.8 %copy.17 = f32[16,5,64]{2,1,0:T(8,128)S(1)} copy(f32[16,5,64]{2,0,1:T(8,128)} %bitcast.138) | data formatting | bytes 40960 | tf_op jit(solution)/shard_map/transpose | solution.py:34
  0.8 0.1 reshape.125
  0.9 4.1 %fusion = f32[16,320]{1,0:T(8,128)S(1)} fusion(f32[1,16,320,320]{3,2,1,0:T(8,128)} %param.6, f32[16,320]{1,0:T(8,128)S(1)} %reshape.125), kind=kLoop, calls=%fused_computation.4 | loop fusion | flops 3271680 | bytes 6594560 | tf_op jit(solution)/shard_map/reduce_sum | solution.py:48
  5.1 0.1 copy.20
  5.3 0.7 %collective-permute-start = (bf16[3,5,16,16]{3,2,1,0:T(8,128)(2,1)S(1)}, bf16[3,5,16,16]{3,2,1,0:T(8,128)(2,1)S(1)}, u32[]{:S(2)}, u32[]{:S(2)}) collective-permute-start(bf16[3,5,16,16]{3,2,1,0:T(8,128)(2,1)S(1)} %maximum_bitcast_fusion), channel_id=1, source_target_pairs={{0,4},{1,5},{2,6},{3,7},{16,20},{17,21},{18,22},{19,23}} | collective-permute-start | bytes 23048 | tf_op jit(solution)/shard_map/ppermute | solution.py:57
  6.0 0.7 %collective-permute-start.1 = (bf16[3,5,16,16]{3,2,1,0:T(8,128)(2,1)S(1)}, bf16[3,5,16,16]{3,2,1,0:T(8,128)(2,1)S(1)}, u32[]{:S(2)}, u32[]{:S(2)}) collective-permute-start(bf16[3,5,16,16]{3,2,1,0:T(8,128)(2,1)S(1)} %maximum_bitcast_fusion), channel_id=1, source_target_pairs={{0,5},{1,6},{2,7},{3,4},{16,21},{17,22},{18,23},{19,20}} | collective-permute-start | bytes 23048 | tf_op jit(solution)/shard_map/ppermute | solution.py:57
  6.7 0.7 %collective-permute-start.2 = (bf16[3,5,16,16]{3,2,1,0:T(8,128)(2,1)S(1)}, bf16[3,5,16,16]{3,2,1,0:T(8,128)(2,1)S(1)}, u32[]{:S(2)}, u32[]{:S(2)}) collective-permute-start(bf16[3,5,16,16]{3,2,1,0:T(8,128)(2,1)S(1)} %maximum_bitcast_fusion), channel_id=1, source_target_pairs={{0,6},{1,7},{2,4},{3,5},{16,22},{17,23},{18,20},{19,21}} | collective-permute-start | bytes 23048 | tf_op jit(solution)/shard_map/ppermute | solution.py:57
  7.3 0.7 %collective-permute-start.3 = (bf16[3,5,16,16]{3,2,1,0:T(8,128)(2,1)S(1)}, bf16[3,5,16,16]{3,2,1,0:T(8,128)(2,1)S(1)}, u32[]{:S(2)}, u32[]{:S(2)}) collective-permute-start(bf16[3,5,16,16]{3,2,1,0:T(8,128)(2,1)S(1)} %maximum_bitcast_fusion), channel_id=1, source_target_pairs={{0,7},{1,4},{2,5},{3,6},{16,23},{17,20},{18,21},{19,22}} | collective-permute-start | bytes 23048 | tf_op jit(solution)/shard_map/ppermute | solution.py:57
  8.1 0.1 convert_bitcast_fusion
  8.2 0.6 %convolution_bitcast_fusion.2 = f32[3,5,16,16]{2,3,0,1:T(8,128)S(1)} fusion(f32[3,16,5,5]{1,3,0,2:T(8,128)S(1)} %copy.19, f32[3,16,64]{2,1,0:T(8,128)S(1)} %convert_bitcast_fusion, bf16[3,5,16,16]{3,2,1,0:T(8,128)(2,1)S(1)} %collective-permute-done.3, bf16[3,5,16,16]{3,2,1,0:T(8,128)(2,1)S(1)} %collective-permute-done.2, ...), kind=kOutput, calls=%fused_computation.10 | convolution fusion | flops 14945280 | bytes 63168 | tf_op jit(solution)/shard_map/kvfp,kvpwe->kwfe/dot_general | solution.py:45
  8.8 0.3 convolution_bitcast_fusion.5
  9.2 4.1 %fusion.1 = f32[16,320]{1,0:T(8,128)S(1)} fusion(f32[1,16,320,320]{3,2,1,0:T(8,128)} %param.6, f32[16,320]{1,0:T(8,128)S(1)} %sub.40), kind=kLoop, calls=%fused_computation.5 | loop fusion | flops 3271680 | bytes 6594560 | tf_op jit(solution)/shard_map/reduce_sum | solution.py:48
  13.3 0.1 copy.22
  13.6 0.7 %collective-permute-start.4 = (bf16[3,5,16,16]{3,2,1,0:T(8,128)(2,1)S(1)}, bf16[3,5,16,16]{3,2,1,0:T(8,128)(2,1)S(1)}, u32[]{:S(2)}, u32[]{:S(2)}) collective-permute-start(bf16[3,5,16,16]{3,2,1,0:T(8,128)(2,1)S(1)} %maximum_bitcast_fusion.3), channel_id=1, source_target_pairs={{4,8},{5,9},{6,10},{7,11},{20,24},{21,25},{22,26},{23,27}} | collective-permute-start | bytes 23048 | tf_op jit(solution)/shard_map/ppermute | solution.py:57
  14.3 0.7 %collective-permute-start.5 = (bf16[3,5,16,16]{3,2,1,0:T(8,128)(2,1)S(1)}, bf16[3,5,16,16]{3,2,1,0:T(8,128)(2,1)S(1)}, u32[]{:S(2)}, u32[]{:S(2)}) collective-permute-start(bf16[3,5,16,16]{3,2,1,0:T(8,128)(2,1)S(1)} %maximum_bitcast_fusion.3), channel_id=1, source_target_pairs={{4,9},{5,10},{6,11},{7,8},{20,25},{21,26},{22,27},{23,24}} | collective-permute-start | bytes 23048 | tf_op jit(solution)/shard_map/ppermute | solution.py:57
  14.9 0.7 %collective-permute-start.6 = (bf16[3,5,16,16]{3,2,1,0:T(8,128)(2,1)S(1)}, bf16[3,5,16,16]{3,2,1,0:T(8,128)(2,1)S(1)}, u32[]{:S(2)}, u32[]{:S(2)}) collective-permute-start(bf16[3,5,16,16]{3,2,1,0:T(8,128)(2,1)S(1)} %maximum_bitcast_fusion.3), channel_id=1, source_target_pairs={{4,10},{5,11},{6,8},{7,9},{20,26},{21,27},{22,24},{23,25}} | collective-permute-start | bytes 23048 | tf_op jit(solution)/shard_map/ppermute | solution.py:57
  15.6 0.7 %collective-permute-start.7 = (bf16[3,5,16,16]{3,2,1,0:T(8,128)(2,1)S(1)}, bf16[3,5,16,16]{3,2,1,0:T(8,128)(2,1)S(1)}, u32[]{:S(2)}, u32[]{:S(2)}) collective-permute-start(bf16[3,5,16,16]{3,2,1,0:T(8,128)(2,1)S(1)} %maximum_bitcast_fusion.3), channel_id=1, source_target_pairs={{4,11},{5,8},{6,9},{7,10},{20,27},{21,24},{22,25},{23,26}} | collective-permute-start | bytes 23048 | tf_op jit(solution)/shard_map/ppermute | solution.py:57
  16.3 0.6 %convolution_bitcast_fusion.1 = f32[3,5,16,16]{2,3,0,1:T(8,128)S(1)} fusion(f32[3,16,5,5]{1,3,0,2:T(8,128)S(1)} %copy.19, f32[3,16,64]{2,1,0:T(8,128)S(1)} %convert_bitcast_fusion, bf16[3,5,16,16]{3,2,1,0:T(8,128)(2,1)S(1)} %collective-permute-done.7, bf16[3,5,16,16]{3,2,1,0:T(8,128)(2,1)S(1)} %collective-permute-done.6, ...), kind=kOutput, calls=%fused_computation.9 | convolution fusion | flops 14945280 | bytes 63168 | tf_op jit(solution)/shard_map/kvfp,kvpwe->kwfe/dot_general | solution.py:45
  16.9 0.3 convolution_bitcast_fusion.4
  17.3 4.1 %fusion.2 = f32[16,320]{1,0:T(8,128)S(1)} fusion(f32[1,16,320,320]{3,2,1,0:T(8,128)} %param.6, f32[16,320]{1,0:T(8,128)S(1)} %sub.41), kind=kLoop, calls=%fused_computation.6 | loop fusion | flops 3271680 | bytes 6594560 | tf_op jit(solution)/shard_map/reduce_sum | solution.py:48
  21.4 0.1 copy.24
  21.7 1.3 %collective-permute-start.10 = (bf16[3,5,16,16]{3,2,1,0:T(8,128)(2,1)S(1)}, bf16[3,5,16,16]{3,2,1,0:T(8,128)(2,1)S(1)}, u32[]{:S(2)}, u32[]{:S(2)}) collective-permute-start(bf16[3,5,16,16]{3,2,1,0:T(8,128)(2,1)S(1)} %maximum_bitcast_fusion.6), channel_id=1, source_target_pairs={{8,14},{9,15},{10,12},{11,13},{24,30},{25,31},{26,28},{27,29}} | collective-permute-start | bytes 23048 | tf_op jit(solution)/shard_map/ppermute | solution.py:57
  23.0 1.3 %collective-permute-start.11 = (bf16[3,5,16,16]{3,2,1,0:T(8,128)(2,1)S(1)}, bf16[3,5,16,16]{3,2,1,0:T(8,128)(2,1)S(1)}, u32[]{:S(2)}, u32[]{:S(2)}) collective-permute-start(bf16[3,5,16,16]{3,2,1,0:T(8,128)(2,1)S(1)} %maximum_bitcast_fusion.6), channel_id=1, source_target_pairs={{8,15},{9,12},{10,13},{11,14},{24,31},{25,28},{26,29},{27,30}} | collective-permute-start | bytes 23048 | tf_op jit(solution)/shard_map/ppermute | solution.py:57
  24.3 1.3 %collective-permute-start.8 = (bf16[3,5,16,16]{3,2,1,0:T(8,128)(2,1)S(1)}, bf16[3,5,16,16]{3,2,1,0:T(8,128)(2,1)S(1)}, u32[]{:S(2)}, u32[]{:S(2)}) collective-permute-start(bf16[3,5,16,16]{3,2,1,0:T(8,128)(2,1)S(1)} %maximum_bitcast_fusion.6), channel_id=1, source_target_pairs={{8,12},{9,13},{10,14},{11,15},{24,28},{25,29},{26,30},{27,31}} | collective-permute-start | bytes 23048 | tf_op jit(solution)/shard_map/ppermute | solution.py:57
  25.6 1.3 %collective-permute-start.9 = (bf16[3,5,16,16]{3,2,1,0:T(8,128)(2,1)S(1)}, bf16[3,5,16,16]{3,2,1,0:T(8,128)(2,1)S(1)}, u32[]{:S(2)}, u32[]{:S(2)}) collective-permute-start(bf16[3,5,16,16]{3,2,1,0:T(8,128)(2,1)S(1)} %maximum_bitcast_fusion.6), channel_id=1, source_target_pairs={{8,13},{9,14},{10,15},{11,12},{24,29},{25,30},{26,31},{27,28}} | collective-permute-start | bytes 23048 | tf_op jit(solution)/shard_map/ppermute | solution.py:57
  26.9 15.2 %collective-permute-done.10 = bf16[3,5,16,16]{3,2,1,0:T(8,128)(2,1)S(1)} collective-permute-done((bf16[3,5,16,16]{3,2,1,0:T(8,128)(2,1)S(1)}, bf16[3,5,16,16]{3,2,1,0:T(8,128)(2,1)S(1)}, u32[]{:S(2)}, u32[]{:S(2)}) %collective-permute-start.10) | collective-permute-done | bytes 7712 | tf_op jit(solution)/shard_map/ppermute | solution.py:57
  42.1 3.2 %collective-permute-done.9 = bf16[3,5,16,16]{3,2,1,0:T(8,128)(2,1)S(1)} collective-permute-done((bf16[3,5,16,16]{3,2,1,0:T(8,128)(2,1)S(1)}, bf16[3,5,16,16]{3,2,1,0:T(8,128)(2,1)S(1)}, u32[]{:S(2)}, u32[]{:S(2)}) %collective-permute-start.9) | collective-permute-done | bytes 7712 | tf_op jit(solution)/shard_map/ppermute | solution.py:57
  45.3 0.6 %convolution_bitcast_fusion = f32[3,5,16,16]{2,3,0,1:T(8,128)S(1)} fusion(f32[3,16,5,5]{1,3,0,2:T(8,128)S(1)} %copy.19, f32[3,16,64]{2,1,0:T(8,128)S(1)} %convert_bitcast_fusion, bf16[3,5,16,16]{3,2,1,0:T(8,128)(2,1)S(1)} %collective-permute-done.11, bf16[3,5,16,16]{3,2,1,0:T(8,128)(2,1)S(1)} %collective-permute-done.10, ...), kind=kOutput, calls=%fused_computation.8 | convolution fusion | flops 14945280 | bytes 63168 | tf_op jit(solution)/shard_map/kvfp,kvpwe->kwfe/dot_general | solution.py:45
  45.9 0.3 convolution_bitcast_fusion.3
  46.3 4.1 %fusion.3 = f32[16,320]{1,0:T(8,128)S(1)} fusion(f32[1,16,320,320]{3,2,1,0:T(8,128)} %param.6, f32[16,320]{1,0:T(8,128)S(1)} %sub.42), kind=kLoop, calls=%fused_computation.7 | loop fusion | flops 3271680 | bytes 6594560 | tf_op jit(solution)/shard_map/reduce_sum | solution.py:48
  50.5 0.1 select_n.75
  50.5 0.6 %copy.26 = f32[1,5,64,16]{2,3,1,0:T(8,128)} copy(f32[1,5,64,16]{2,1,3,0:T(8,128)S(1)} %bitcast.127) | data formatting | bytes 40960 | tf_op jit(solution)/shard_map/broadcast_in_dim | solution.py:65
  (47 shorter events, 0.7 us)
Async XLA Ops:
  0.0 8.8 %copy-start = (f32[3,64,16]{1,2,0:T(8,128)S(1)}, f32[3,64,16]{1,2,0:T(8,128)}, u32[]{:S(2)}) copy-start(f32[3,64,16]{1,2,0:T(8,128)} %param.9) | copy-start | bytes 36868
  0.0 8.0 %copy-start.2 = (s32[1,3,16]{2,0,1:T(1,128)S(1)}, s32[1,3,16]{2,0,1:T(1,128)}, u32[]{:S(2)}) copy-start(s32[1,3,16]{2,0,1:T(1,128)} %param.8) | copy-start | bytes 580
  0.0 8.1 %copy-start.1 = (f32[1,3,5,5,16]{4,0,3,2,1:T(1,128)S(1)}, f32[1,3,5,5,16]{4,0,3,2,1:T(1,128)}, u32[]{:S(2)}) copy-start(f32[1,3,5,5,16]{4,0,3,2,1:T(1,128)} %param.7) | copy-start | bytes 14404
  5.3 2.8 %collective-permute-start = (bf16[3,5,16,16]{3,2,1,0:T(8,128)(2,1)S(1)}, bf16[3,5,16,16]{3,2,1,0:T(8,128)(2,1)S(1)}, u32[]{:S(2)}, u32[]{:S(2)}) collective-permute-start(bf16[3,5,16,16]{3,2,1,0:T(8,128)(2,1)S(1)} %maximum_bitcast_fusion), channel_id=1, source_target_pairs={{0,4},{1,5},{2,6},{3,7},{16,20},{17,21},{18,22},{19,23}} | collective-permute-start | bytes 23048 | tf_op jit(solution)/shard_map/ppermute | solution.py:57
  6.0 2.2 %collective-permute-start.1 = (bf16[3,5,16,16]{3,2,1,0:T(8,128)(2,1)S(1)}, bf16[3,5,16,16]{3,2,1,0:T(8,128)(2,1)S(1)}, u32[]{:S(2)}, u32[]{:S(2)}) collective-permute-start(bf16[3,5,16,16]{3,2,1,0:T(8,128)(2,1)S(1)} %maximum_bitcast_fusion), channel_id=1, source_target_pairs={{0,5},{1,6},{2,7},{3,4},{16,21},{17,22},{18,23},{19,20}} | collective-permute-start | bytes 23048 | tf_op jit(solution)/shard_map/ppermute | solution.py:57
  6.7 1.5 %collective-permute-start.2 = (bf16[3,5,16,16]{3,2,1,0:T(8,128)(2,1)S(1)}, bf16[3,5,16,16]{3,2,1,0:T(8,128)(2,1)S(1)}, u32[]{:S(2)}, u32[]{:S(2)}) collective-permute-start(bf16[3,5,16,16]{3,2,1,0:T(8,128)(2,1)S(1)} %maximum_bitcast_fusion), channel_id=1, source_target_pairs={{0,6},{1,7},{2,4},{3,5},{16,22},{17,23},{18,20},{19,21}} | collective-permute-start | bytes 23048 | tf_op jit(solution)/shard_map/ppermute | solution.py:57
  7.3 0.9 %collective-permute-start.3 = (bf16[3,5,16,16]{3,2,1,0:T(8,128)(2,1)S(1)}, bf16[3,5,16,16]{3,2,1,0:T(8,128)(2,1)S(1)}, u32[]{:S(2)}, u32[]{:S(2)}) collective-permute-start(bf16[3,5,16,16]{3,2,1,0:T(8,128)(2,1)S(1)} %maximum_bitcast_fusion), channel_id=1, source_target_pairs={{0,7},{1,4},{2,5},{3,6},{16,23},{17,20},{18,21},{19,22}} | collective-permute-start | bytes 23048 | tf_op jit(solution)/shard_map/ppermute | solution.py:57
  13.6 2.7 %collective-permute-start.4 = (bf16[3,5,16,16]{3,2,1,0:T(8,128)(2,1)S(1)}, bf16[3,5,16,16]{3,2,1,0:T(8,128)(2,1)S(1)}, u32[]{:S(2)}, u32[]{:S(2)}) collective-permute-start(bf16[3,5,16,16]{3,2,1,0:T(8,128)(2,1)S(1)} %maximum_bitcast_fusion.3), channel_id=1, source_target_pairs={{4,8},{5,9},{6,10},{7,11},{20,24},{21,25},{22,26},{23,27}} | collective-permute-start | bytes 23048 | tf_op jit(solution)/shard_map/ppermute | solution.py:57
  14.3 2.0 %collective-permute-start.5 = (bf16[3,5,16,16]{3,2,1,0:T(8,128)(2,1)S(1)}, bf16[3,5,16,16]{3,2,1,0:T(8,128)(2,1)S(1)}, u32[]{:S(2)}, u32[]{:S(2)}) collective-permute-start(bf16[3,5,16,16]{3,2,1,0:T(8,128)(2,1)S(1)} %maximum_bitcast_fusion.3), channel_id=1, source_target_pairs={{4,9},{5,10},{6,11},{7,8},{20,25},{21,26},{22,27},{23,24}} | collective-permute-start | bytes 23048 | tf_op jit(solution)/shard_map/ppermute | solution.py:57
  14.9 1.4 %collective-permute-start.6 = (bf16[3,5,16,16]{3,2,1,0:T(8,128)(2,1)S(1)}, bf16[3,5,16,16]{3,2,1,0:T(8,128)(2,1)S(1)}, u32[]{:S(2)}, u32[]{:S(2)}) collective-permute-start(bf16[3,5,16,16]{3,2,1,0:T(8,128)(2,1)S(1)} %maximum_bitcast_fusion.3), channel_id=1, source_target_pairs={{4,10},{5,11},{6,8},{7,9},{20,26},{21,27},{22,24},{23,25}} | collective-permute-start | bytes 23048 | tf_op jit(solution)/shard_map/ppermute | solution.py:57
  15.6 0.7 %collective-permute-start.7 = (bf16[3,5,16,16]{3,2,1,0:T(8,128)(2,1)S(1)}, bf16[3,5,16,16]{3,2,1,0:T(8,128)(2,1)S(1)}, u32[]{:S(2)}, u32[]{:S(2)}) collective-permute-start(bf16[3,5,16,16]{3,2,1,0:T(8,128)(2,1)S(1)} %maximum_bitcast_fusion.3), channel_id=1, source_target_pairs={{4,11},{5,8},{6,9},{7,10},{20,27},{21,24},{22,25},{23,26}} | collective-permute-start | bytes 23048 | tf_op jit(solution)/shard_map/ppermute | solution.py:57
  21.7 20.4 %collective-permute-start.10 = (bf16[3,5,16,16]{3,2,1,0:T(8,128)(2,1)S(1)}, bf16[3,5,16,16]{3,2,1,0:T(8,128)(2,1)S(1)}, u32[]{:S(2)}, u32[]{:S(2)}) collective-permute-start(bf16[3,5,16,16]{3,2,1,0:T(8,128)(2,1)S(1)} %maximum_bitcast_fusion.6), channel_id=1, source_target_pairs={{8,14},{9,15},{10,12},{11,13},{24,30},{25,31},{26,28},{27,29}} | collective-permute-start | bytes 23048 | tf_op jit(solution)/shard_map/ppermute | solution.py:57
  23.0 19.1 %collective-permute-start.11 = (bf16[3,5,16,16]{3,2,1,0:T(8,128)(2,1)S(1)}, bf16[3,5,16,16]{3,2,1,0:T(8,128)(2,1)S(1)}, u32[]{:S(2)}, u32[]{:S(2)}) collective-permute-start(bf16[3,5,16,16]{3,2,1,0:T(8,128)(2,1)S(1)} %maximum_bitcast_fusion.6), channel_id=1, source_target_pairs={{8,15},{9,12},{10,13},{11,14},{24,31},{25,28},{26,29},{27,30}} | collective-permute-start | bytes 23048 | tf_op jit(solution)/shard_map/ppermute | solution.py:57
  24.3 17.8 %collective-permute-start.8 = (bf16[3,5,16,16]{3,2,1,0:T(8,128)(2,1)S(1)}, bf16[3,5,16,16]{3,2,1,0:T(8,128)(2,1)S(1)}, u32[]{:S(2)}, u32[]{:S(2)}) collective-permute-start(bf16[3,5,16,16]{3,2,1,0:T(8,128)(2,1)S(1)} %maximum_bitcast_fusion.6), channel_id=1, source_target_pairs={{8,12},{9,13},{10,14},{11,15},{24,28},{25,29},{26,30},{27,31}} | collective-permute-start | bytes 23048 | tf_op jit(solution)/shard_map/ppermute | solution.py:57
  25.6 19.7 %collective-permute-start.9 = (bf16[3,5,16,16]{3,2,1,0:T(8,128)(2,1)S(1)}, bf16[3,5,16,16]{3,2,1,0:T(8,128)(2,1)S(1)}, u32[]{:S(2)}, u32[]{:S(2)}) collective-permute-start(bf16[3,5,16,16]{3,2,1,0:T(8,128)(2,1)S(1)} %maximum_bitcast_fusion.6), channel_id=1, source_target_pairs={{8,13},{9,14},{10,15},{11,12},{24,29},{25,30},{26,31},{27,28}} | collective-permute-start | bytes 23048 | tf_op jit(solution)/shard_map/ppermute | solution.py:57

commit v5 on v3

--- a/solution.py
+++ b/solution.py
@@ -35,28 +35,29 @@
 
     shift = (g - up // local) % groups
     pos = shift * local + up % local
-    onehot = (jnp.arange(groups * local)[None, :, None] == pos[:, None, :]).astype(jnp.bfloat16)
+    onehot = (jnp.arange(groups * local)[None, :, None] == pos[:, None, :]).astype(jnp.float32)
+    picked_jac = jnp.einsum("kpe,kwve->kvpwe", onehot, jac)
+
+    def coupling_of(traces_in):
+        mixed = jnp.einsum("kvfp,kvpwe->kwfe", traces_in.astype(jnp.float32), picked_jac, precision=HIGH)
+        coupling = jnp.einsum("kwfe,kif->ewi", mixed, lift, precision=HIGH)
+        return coupling.reshape(local, BLOCK)
 
     base = jnp.sum(inv * rhs_t[:, None, :], axis=-1)
-    lifted = jnp.einsum("erwi,kif->erwkf", inv.reshape(local, BLOCK, VARS, NODES), lift, precision=HIGH)
-    coupled_inv = jnp.einsum("erwkf,kwve->erkvf", lifted, jac, precision=HIGH).reshape(local, BLOCK, 3 * VARS * FACE)
-
-    def solve(traces_in):
-        upstream = jnp.einsum("kvfp,kpe->kvfe", traces_in, onehot, preferred_element_type=jnp.float32)
-        upstream = jnp.transpose(upstream, (3, 0, 1, 2)).reshape(local, 3 * VARS * FACE)
-        return base - jnp.sum(coupled_inv * upstream[:, None, :], axis=-1)
-
-    out = base
+    inv_narrow = lax.optimization_barrier(inv.astype(jnp.bfloat16))
     traces = face_traces(base).astype(jnp.bfloat16)
+    own_coupling = jnp.zeros((local, BLOCK), jnp.float32)
     for turn in range(1, chains):
         blocks = []
         for d in range(groups):
             pairs = [((turn - 1) * groups + s, turn * groups + (s + d) % groups) for s in range(groups)]
             blocks.append(lax.ppermute(traces, ("chain", "group"), pairs))
-        sol = solve(jnp.concatenate(blocks, axis=3))
-        out = jnp.where(c == turn, sol, out)
+        coupling = coupling_of(jnp.concatenate(blocks, axis=3))
+        own_coupling = jnp.where(c == turn, coupling, own_coupling)
         if turn + 1 < chains:
-            traces = face_traces(sol).astype(jnp.bfloat16)
+            approx = base - jnp.sum(inv_narrow.astype(jnp.float32) * coupling[:, None, :], axis=-1)
+            traces = face_traces(approx).astype(jnp.bfloat16)
+    out = base - jnp.sum(inv * own_coupling[:, None, :], axis=-1)
     return jnp.transpose(out.reshape(local, VARS, NODES), (1, 2, 0))[None]
 
 

time: 79.6 us -> 52 us (0.65)
  matrix products: 26.5 us -> 2.53 us
  local copies, waits for them, and re-layouts: 12.4 us -> 2.51 us
  other arithmetic: 14.1 us -> 20.3 us
    dot_general x5 -> x6, matrix products: 26.5 us -> 2.53 us  [the longest x3 1.71 us: coupling_of(): jnp.einsum('kvfp,kvpwe->kwfe', traces_in.astype(jnp.float32), picked_jac,...]
    unnamed x11 -> x10, local copies, waits for them, and re-layouts: 8.7 us -> 0.06 us
    convert_element_type x2 -> x3, other arithmetic: 0.04 us -> 5.71 us  [the longest x1 5.67 us: body(): inv_narrow = lax.optimization_barrier(inv.astype(jnp.bfloat16))]
    transpose x3, local copies, waits for them, and re-layouts: 1.1 us -> 0.06 us  [coupling_of(): coupling = jnp.einsum('kwfe,kif->ewi', mixed, lift, precision=HIGH)]
    reduce_sum x2 -> x3, other arithmetic: 9.85 us -> 10.3 us  [the longest x2 6.2 us: body(): jnp.sum(inv_narrow.astype(jnp.float32) * coupling[:, None, :], axis=-1)]
  transfers between devices with their start and end apart: 12 -> 12, of which waited for: 3 -> 3; matrix products, arithmetic and copies ran while one was open for 24% -> 11% of each run, Pallas kernels for 0% -> 0%
where the time goes in v5:
time: 52 us; the launch traced here: 51.5 us
  other arithmetic  20.3 us (39%)
  waiting for transfers between devices  15.2 us (29%)
  starting transfers between devices  10.5 us (20%)
  matrix products  2.53 us (5%)
  local copies, waits for them, and re-layouts  2.51 us (5%)
    ppermute x12, waiting for transfers between devices, body(): blocks.append(lax.ppermute(traces, ('chain', 'group'), pairs))  15.2 us
    ppermute x12, starting transfers between devices, body(): blocks.append(lax.ppermute(traces, ('chain', 'group'), pairs))  10.5 us
    reduce_sum x2, other arithmetic, body(): jnp.sum(inv_narrow.astype(jnp.float32) * coupling[:, None, :], axis=-1)  6.2 us
    convert_element_type x1, other arithmetic, body(): inv_narrow = lax.optimization_barrier(inv.astype(jnp.bfloat16))  5.67 us
    reduce_sum x1, other arithmetic, body(): base = jnp.sum(inv * rhs_t[:, None, :], axis=-1)  4.14 us
    reduce_sum x1, other arithmetic, body(): out = base - jnp.sum(inv * own_coupling[:, None, :], axis=-1)  4.13 us
    dot_general x3, matrix products, coupling_of(): jnp.einsum('kvfp,kvpwe->kwfe', traces_in.astype(jnp.float32), picked_jac,...  1.71 us
  transfers between devices with their start and end apart: 12, of which 3 were waited for; matrix products, arithmetic and copies ran while one was open for 11% of the time, Pallas kernels for 0%

profile of v5, /device:TPU:7, one launch (start us, length us, event | category | flops | bytes accessed | tf_op | source)
XLA Modules:
  0.0 51.5 jit_solution(13942231192524296121)
XLA Ops:
  0.0 0.8 %copy.17 = f32[16,5,64]{2,1,0:T(8,128)S(1)} copy(f32[16,5,64]{2,0,1:T(8,128)} %bitcast.133) | data formatting | bytes 40960 | tf_op jit(solution)/shard_map/transpose | solution.py:34
  0.9 4.1 %fusion.2 = f32[16,320]{1,0:T(8,128)S(1)} fusion(f32[1,16,320,320]{3,2,1,0:T(8,128)} %param.6, f32[16,320]{1,0:T(8,128)S(1)} %mul.46), kind=kLoop, calls=%fused_computation.7 | loop fusion | flops 3271680 | bytes 6594560 | tf_op jit(solution)/shard_map/reduce_sum | solution.py:46
  5.1 0.1 copy.20
  5.3 0.7 %collective-permute-start = (bf16[3,5,16,16]{3,2,1,0:T(8,128)(2,1)S(1)}, bf16[3,5,16,16]{3,2,1,0:T(8,128)(2,1)S(1)}, u32[]{:S(2)}, u32[]{:S(2)}) collective-permute-start(bf16[3,5,16,16]{3,2,1,0:T(8,128)(2,1)S(1)} %maximum_bitcast_fusion), channel_id=1, source_target_pairs={{0,4},{1,5},{2,6},{3,7},{16,20},{17,21},{18,22},{19,23}} | collective-permute-start | bytes 23048 | tf_op jit(solution)/shard_map/ppermute | solution.py:54
  6.0 0.7 %collective-permute-start.1 = (bf16[3,5,16,16]{3,2,1,0:T(8,128)(2,1)S(1)}, bf16[3,5,16,16]{3,2,1,0:T(8,128)(2,1)S(1)}, u32[]{:S(2)}, u32[]{:S(2)}) collective-permute-start(bf16[3,5,16,16]{3,2,1,0:T(8,128)(2,1)S(1)} %maximum_bitcast_fusion), channel_id=1, source_target_pairs={{0,5},{1,6},{2,7},{3,4},{16,21},{17,22},{18,23},{19,20}} | collective-permute-start | bytes 23048 | tf_op jit(solution)/shard_map/ppermute | solution.py:54
  6.7 0.7 %collective-permute-start.2 = (bf16[3,5,16,16]{3,2,1,0:T(8,128)(2,1)S(1)}, bf16[3,5,16,16]{3,2,1,0:T(8,128)(2,1)S(1)}, u32[]{:S(2)}, u32[]{:S(2)}) collective-permute-start(bf16[3,5,16,16]{3,2,1,0:T(8,128)(2,1)S(1)} %maximum_bitcast_fusion), channel_id=1, source_target_pairs={{0,6},{1,7},{2,4},{3,5},{16,22},{17,23},{18,20},{19,21}} | collective-permute-start | bytes 23048 | tf_op jit(solution)/shard_map/ppermute | solution.py:54
  7.3 0.7 %collective-permute-start.3 = (bf16[3,5,16,16]{3,2,1,0:T(8,128)(2,1)S(1)}, bf16[3,5,16,16]{3,2,1,0:T(8,128)(2,1)S(1)}, u32[]{:S(2)}, u32[]{:S(2)}) collective-permute-start(bf16[3,5,16,16]{3,2,1,0:T(8,128)(2,1)S(1)} %maximum_bitcast_fusion), channel_id=1, source_target_pairs={{0,7},{1,4},{2,5},{3,6},{16,23},{17,20},{18,21},{19,22}} | collective-permute-start | bytes 23048 | tf_op jit(solution)/shard_map/ppermute | solution.py:54
  8.0 5.7 %bitcast_convert_fusion = bf16[16,320,320]{2,1,0:T(8,128)(2,1)} fusion(f32[1,16,320,320]{3,2,1,0:T(8,128)} %param.6), kind=kLoop, calls=%fused_computation.5 | loop fusion | flops 1638400 | bytes 9830400 | tf_op jit(solution)/shard_map/convert_element_type | solution.py:47
  13.9 0.6 %convolution_bitcast_fusion.2 = f32[3,5,16,16]{2,3,0,1:T(8,128)S(1)} fusion(f32[3,16,5,5]{1,3,0,2:T(8,128)S(1)} %copy.19, f32[3,16,64]{2,1,0:T(8,128)S(1)} %convert_bitcast_fusion, bf16[3,5,16,16]{3,2,1,0:T(8,128)(2,1)S(1)} %collective-permute-done.3, bf16[3,5,16,16]{3,2,1,0:T(8,128)(2,1)S(1)} %collective-permute-done.2, ...), kind=kOutput, calls=%fused_computation.11 | convolution fusion | flops 14945280 | bytes 63168 | tf_op jit(solution)/shard_map/kvfp,kvpwe->kwfe/dot_general | solution.py:42
  14.5 0.3 convolution_bitcast_fusion.5
  14.8 3.1 %fusion = f32[16,320]{1,0:T(8,128)S(1)} fusion(bf16[16,320,320]{2,1,0:T(8,128)(2,1)} %bitcast_convert_fusion, f32[16,320]{1,0:T(8,128)S(1)} %mul.50), kind=kLoop, calls=%fused_computation.2 | loop fusion | flops 4910080 | bytes 3317760 | tf_op jit(solution)/shard_map/reduce_sum | solution.py:58
  18.0 0.1 copy.22
  18.2 0.7 %collective-permute-start.4 = (bf16[3,5,16,16]{3,2,1,0:T(8,128)(2,1)S(1)}, bf16[3,5,16,16]{3,2,1,0:T(8,128)(2,1)S(1)}, u32[]{:S(2)}, u32[]{:S(2)}) collective-permute-start(bf16[3,5,16,16]{3,2,1,0:T(8,128)(2,1)S(1)} %maximum_bitcast_fusion.3), channel_id=1, source_target_pairs={{4,8},{5,9},{6,10},{7,11},{20,24},{21,25},{22,26},{23,27}} | collective-permute-start | bytes 23048 | tf_op jit(solution)/shard_map/ppermute | solution.py:54
  18.9 0.7 %collective-permute-start.5 = (bf16[3,5,16,16]{3,2,1,0:T(8,128)(2,1)S(1)}, bf16[3,5,16,16]{3,2,1,0:T(8,128)(2,1)S(1)}, u32[]{:S(2)}, u32[]{:S(2)}) collective-permute-start(bf16[3,5,16,16]{3,2,1,0:T(8,128)(2,1)S(1)} %maximum_bitcast_fusion.3), channel_id=1, source_target_pairs={{4,9},{5,10},{6,11},{7,8},{20,25},{21,26},{22,27},{23,24}} | collective-permute-start | bytes 23048 | tf_op jit(solution)/shard_map/ppermute | solution.py:54
  19.6 0.7 %collective-permute-start.6 = (bf16[3,5,16,16]{3,2,1,0:T(8,128)(2,1)S(1)}, bf16[3,5,16,16]{3,2,1,0:T(8,128)(2,1)S(1)}, u32[]{:S(2)}, u32[]{:S(2)}) collective-permute-start(bf16[3,5,16,16]{3,2,1,0:T(8,128)(2,1)S(1)} %maximum_bitcast_fusion.3), channel_id=1, source_target_pairs={{4,10},{5,11},{6,8},{7,9},{20,26},{21,27},{22,24},{23,25}} | collective-permute-start | bytes 23048 | tf_op jit(solution)/shard_map/ppermute | solution.py:54
  20.2 0.7 %collective-permute-start.7 = (bf16[3,5,16,16]{3,2,1,0:T(8,128)(2,1)S(1)}, bf16[3,5,16,16]{3,2,1,0:T(8,128)(2,1)S(1)}, u32[]{:S(2)}, u32[]{:S(2)}) collective-permute-start(bf16[3,5,16,16]{3,2,1,0:T(8,128)(2,1)S(1)} %maximum_bitcast_fusion.3), channel_id=1, source_target_pairs={{4,11},{5,8},{6,9},{7,10},{20,27},{21,24},{22,25},{23,26}} | collective-permute-start | bytes 23048 | tf_op jit(solution)/shard_map/ppermute | solution.py:54
  20.9 0.6 %convolution_bitcast_fusion.1 = f32[3,5,16,16]{2,3,0,1:T(8,128)S(1)} fusion(f32[3,16,5,5]{1,3,0,2:T(8,128)S(1)} %copy.19, f32[3,16,64]{2,1,0:T(8,128)S(1)} %convert_bitcast_fusion, bf16[3,5,16,16]{3,2,1,0:T(8,128)(2,1)S(1)} %collective-permute-done.7, bf16[3,5,16,16]{3,2,1,0:T(8,128)(2,1)S(1)} %collective-permute-done.6, ...), kind=kOutput, calls=%fused_computation.10 | convolution fusion | flops 14945280 | bytes 63168 | tf_op jit(solution)/shard_map/kvfp,kvpwe->kwfe/dot_general | solution.py:42
  21.5 0.3 convolution_bitcast_fusion.4
  21.9 3.1 %fusion.1 = f32[16,320]{1,0:T(8,128)S(1)} fusion(bf16[16,320,320]{2,1,0:T(8,128)(2,1)} %bitcast_convert_fusion, f32[16,320]{1,0:T(8,128)S(1)} %mul.53), kind=kLoop, calls=%fused_computation.3 | loop fusion | flops 4910080 | bytes 3317760 | tf_op jit(solution)/shard_map/reduce_sum | solution.py:58
  25.0 0.1 copy.24
  25.3 1.3 %collective-permute-start.10 = (bf16[3,5,16,16]{3,2,1,0:T(8,128)(2,1)S(1)}, bf16[3,5,16,16]{3,2,1,0:T(8,128)(2,1)S(1)}, u32[]{:S(2)}, u32[]{:S(2)}) collective-permute-start(bf16[3,5,16,16]{3,2,1,0:T(8,128)(2,1)S(1)} %maximum_bitcast_fusion.6), channel_id=1, source_target_pairs={{8,14},{9,15},{10,12},{11,13},{24,30},{25,31},{26,28},{27,29}} | collective-permute-start | bytes 23048 | tf_op jit(solution)/shard_map/ppermute | solution.py:54
  26.6 1.3 %collective-permute-start.11 = (bf16[3,5,16,16]{3,2,1,0:T(8,128)(2,1)S(1)}, bf16[3,5,16,16]{3,2,1,0:T(8,128)(2,1)S(1)}, u32[]{:S(2)}, u32[]{:S(2)}) collective-permute-start(bf16[3,5,16,16]{3,2,1,0:T(8,128)(2,1)S(1)} %maximum_bitcast_fusion.6), channel_id=1, source_target_pairs={{8,15},{9,12},{10,13},{11,14},{24,31},{25,28},{26,29},{27,30}} | collective-permute-start | bytes 23048 | tf_op jit(solution)/shard_map/ppermute | solution.py:54
  27.9 1.3 %collective-permute-start.8 = (bf16[3,5,16,16]{3,2,1,0:T(8,128)(2,1)S(1)}, bf16[3,5,16,16]{3,2,1,0:T(8,128)(2,1)S(1)}, u32[]{:S(2)}, u32[]{:S(2)}) collective-permute-start(bf16[3,5,16,16]{3,2,1,0:T(8,128)(2,1)S(1)} %maximum_bitcast_fusion.6), channel_id=1, source_target_pairs={{8,12},{9,13},{10,14},{11,15},{24,28},{25,29},{26,30},{27,31}} | collective-permute-start | bytes 23048 | tf_op jit(solution)/shard_map/ppermute | solution.py:54
  29.2 1.3 %collective-permute-start.9 = (bf16[3,5,16,16]{3,2,1,0:T(8,128)(2,1)S(1)}, bf16[3,5,16,16]{3,2,1,0:T(8,128)(2,1)S(1)}, u32[]{:S(2)}, u32[]{:S(2)}) collective-permute-start(bf16[3,5,16,16]{3,2,1,0:T(8,128)(2,1)S(1)} %maximum_bitcast_fusion.6), channel_id=1, source_target_pairs={{8,13},{9,14},{10,15},{11,12},{24,29},{25,30},{26,31},{27,28}} | collective-permute-start | bytes 23048 | tf_op jit(solution)/shard_map/ppermute | solution.py:54
  30.5 8.9 %collective-permute-done.10 = bf16[3,5,16,16]{3,2,1,0:T(8,128)(2,1)S(1)} collective-permute-done((bf16[3,5,16,16]{3,2,1,0:T(8,128)(2,1)S(1)}, bf16[3,5,16,16]{3,2,1,0:T(8,128)(2,1)S(1)}, u32[]{:S(2)}, u32[]{:S(2)}) %collective-permute-start.10) | collective-permute-done | bytes 7712 | tf_op jit(solution)/shard_map/ppermute | solution.py:54
  39.4 1.0 %collective-permute-done.11 = bf16[3,5,16,16]{3,2,1,0:T(8,128)(2,1)S(1)} collective-permute-done((bf16[3,5,16,16]{3,2,1,0:T(8,128)(2,1)S(1)}, bf16[3,5,16,16]{3,2,1,0:T(8,128)(2,1)S(1)}, u32[]{:S(2)}, u32[]{:S(2)}) %collective-permute-start.11) | collective-permute-done | bytes 7712 | tf_op jit(solution)/shard_map/ppermute | solution.py:54
  40.4 5.3 %collective-permute-done.9 = bf16[3,5,16,16]{3,2,1,0:T(8,128)(2,1)S(1)} collective-permute-done((bf16[3,5,16,16]{3,2,1,0:T(8,128)(2,1)S(1)}, bf16[3,5,16,16]{3,2,1,0:T(8,128)(2,1)S(1)}, u32[]{:S(2)}, u32[]{:S(2)}) %collective-permute-start.9) | collective-permute-done | bytes 7712 | tf_op jit(solution)/shard_map/ppermute | solution.py:54
  45.7 0.6 %convolution_bitcast_fusion = f32[3,5,16,16]{2,3,0,1:T(8,128)S(1)} fusion(f32[3,16,5,5]{1,3,0,2:T(8,128)S(1)} %copy.19, f32[3,16,64]{2,1,0:T(8,128)S(1)} %convert_bitcast_fusion, bf16[3,5,16,16]{3,2,1,0:T(8,128)(2,1)S(1)} %collective-permute-done.11, bf16[3,5,16,16]{3,2,1,0:T(8,128)(2,1)S(1)} %collective-permute-done.10, ...), kind=kOutput, calls=%fused_computation.9 | convolution fusion | flops 14945280 | bytes 63168 | tf_op jit(solution)/shard_map/kvfp,kvpwe->kwfe/dot_general | solution.py:42
  46.2 0.3 convolution_bitcast_fusion.3
  46.6 4.1 %fusion.3 = f32[16,320]{1,0:T(8,128)S(1)} fusion(f32[1,16,320,320]{3,2,1,0:T(8,128)} %param.6, f32[16,320]{1,0:T(8,128)S(1)} %select_select_fusion), kind=kLoop, calls=%fused_computation.8 | loop fusion | flops 3271680 | bytes 6594560 | tf_op jit(solution)/shard_map/reduce_sum | solution.py:60
  50.8 0.1 sub.37
  50.8 0.6 %copy.26 = f32[1,5,64,16]{2,3,1,0:T(8,128)} copy(f32[1,5,64,16]{2,1,3,0:T(8,128)S(1)} %bitcast.122) | data formatting | bytes 40960 | tf_op jit(solution)/shard_map/broadcast_in_dim | solution.py:61
  (46 shorter events, 0.8 us)
Async XLA Ops:
  0.0 14.5 %copy-start = (f32[3,64,16]{1,2,0:T(8,128)S(1)}, f32[3,64,16]{1,2,0:T(8,128)}, u32[]{:S(2)}) copy-start(f32[3,64,16]{1,2,0:T(8,128)} %param.9) | copy-start | bytes 36868
  5.0 8.7 %copy-start.2 = (s32[1,3,16]{2,0,1:T(1,128)S(1)}, s32[1,3,16]{2,0,1:T(1,128)}, u32[]{:S(2)}) copy-start(s32[1,3,16]{2,0,1:T(1,128)} %param.8) | copy-start | bytes 580
  5.0 8.8 %copy-start.1 = (f32[1,3,5,5,16]{4,0,3,2,1:T(1,128)S(1)}, f32[1,3,5,5,16]{4,0,3,2,1:T(1,128)}, u32[]{:S(2)}) copy-start(f32[1,3,5,5,16]{4,0,3,2,1:T(1,128)} %param.7) | copy-start | bytes 14404
  5.3 8.5 %collective-permute-start = (bf16[3,5,16,16]{3,2,1,0:T(8,128)(2,1)S(1)}, bf16[3,5,16,16]{3,2,1,0:T(8,128)(2,1)S(1)}, u32[]{:S(2)}, u32[]{:S(2)}) collective-permute-start(bf16[3,5,16,16]{3,2,1,0:T(8,128)(2,1)S(1)} %maximum_bitcast_fusion), channel_id=1, source_target_pairs={{0,4},{1,5},{2,6},{3,7},{16,20},{17,21},{18,22},{19,23}} | collective-permute-start | bytes 23048 | tf_op jit(solution)/shard_map/ppermute | solution.py:54
  6.0 7.8 %collective-permute-start.1 = (bf16[3,5,16,16]{3,2,1,0:T(8,128)(2,1)S(1)}, bf16[3,5,16,16]{3,2,1,0:T(8,128)(2,1)S(1)}, u32[]{:S(2)}, u32[]{:S(2)}) collective-permute-start(bf16[3,5,16,16]{3,2,1,0:T(8,128)(2,1)S(1)} %maximum_bitcast_fusion), channel_id=1, source_target_pairs={{0,5},{1,6},{2,7},{3,4},{16,21},{17,22},{18,23},{19,20}} | collective-permute-start | bytes 23048 | tf_op jit(solution)/shard_map/ppermute | solution.py:54
  6.7 7.2 %collective-permute-start.2 = (bf16[3,5,16,16]{3,2,1,0:T(8,128)(2,1)S(1)}, bf16[3,5,16,16]{3,2,1,0:T(8,128)(2,1)S(1)}, u32[]{:S(2)}, u32[]{:S(2)}) collective-permute-start(bf16[3,5,16,16]{3,2,1,0:T(8,128)(2,1)S(1)} %maximum_bitcast_fusion), channel_id=1, source_target_pairs={{0,6},{1,7},{2,4},{3,5},{16,22},{17,23},{18,20},{19,21}} | collective-permute-start | bytes 23048 | tf_op jit(solution)/shard_map/ppermute | solution.py:54
  7.3 6.5 %collective-permute-start.3 = (bf16[3,5,16,16]{3,2,1,0:T(8,128)(2,1)S(1)}, bf16[3,5,16,16]{3,2,1,0:T(8,128)(2,1)S(1)}, u32[]{:S(2)}, u32[]{:S(2)}) collective-permute-start(bf16[3,5,16,16]{3,2,1,0:T(8,128)(2,1)S(1)} %maximum_bitcast_fusion), channel_id=1, source_target_pairs={{0,7},{1,4},{2,5},{3,6},{16,23},{17,20},{18,21},{19,22}} | collective-permute-start | bytes 23048 | tf_op jit(solution)/shard_map/ppermute | solution.py:54
  18.2 2.7 %collective-permute-start.4 = (bf16[3,5,16,16]{3,2,1,0:T(8,128)(2,1)S(1)}, bf16[3,5,16,16]{3,2,1,0:T(8,128)(2,1)S(1)}, u32[]{:S(2)}, u32[]{:S(2)}) collective-permute-start(bf16[3,5,16,16]{3,2,1,0:T(8,128)(2,1)S(1)} %maximum_bitcast_fusion.3), channel_id=1, source_target_pairs={{4,8},{5,9},{6,10},{7,11},{20,24},{21,25},{22,26},{23,27}} | collective-permute-start | bytes 23048 | tf_op jit(solution)/shard_map/ppermute | solution.py:54
  18.9 2.0 %collective-permute-start.5 = (bf16[3,5,16,16]{3,2,1,0:T(8,128)(2,1)S(1)}, bf16[3,5,16,16]{3,2,1,0:T(8,128)(2,1)S(1)}, u32[]{:S(2)}, u32[]{:S(2)}) collective-permute-start(bf16[3,5,16,16]{3,2,1,0:T(8,128)(2,1)S(1)} %maximum_bitcast_fusion.3), channel_id=1, source_target_pairs={{4,9},{5,10},{6,11},{7,8},{20,25},{21,26},{22,27},{23,24}} | collective-permute-start | bytes 23048 | tf_op jit(solution)/shard_map/ppermute | solution.py:54
  19.6 1.4 %collective-permute-start.6 = (bf16[3,5,16,16]{3,2,1,0:T(8,128)(2,1)S(1)}, bf16[3,5,16,16]{3,2,1,0:T(8,128)(2,1)S(1)}, u32[]{:S(2)}, u32[]{:S(2)}) collective-permute-start(bf16[3,5,16,16]{3,2,1,0:T(8,128)(2,1)S(1)} %maximum_bitcast_fusion.3), channel_id=1, source_target_pairs={{4,10},{5,11},{6,8},{7,9},{20,26},{21,27},{22,24},{23,25}} | collective-permute-start | bytes 23048 | tf_op jit(solution)/shard_map/ppermute | solution.py:54
  20.2 0.7 %collective-permute-start.7 = (bf16[3,5,16,16]{3,2,1,0:T(8,128)(2,1)S(1)}, bf16[3,5,16,16]{3,2,1,0:T(8,128)(2,1)S(1)}, u32[]{:S(2)}, u32[]{:S(2)}) collective-permute-start(bf16[3,5,16,16]{3,2,1,0:T(8,128)(2,1)S(1)} %maximum_bitcast_fusion.3), channel_id=1, source_target_pairs={{4,11},{5,8},{6,9},{7,10},{20,27},{21,24},{22,25},{23,26}} | collective-permute-start | bytes 23048 | tf_op jit(solution)/shard_map/ppermute | solution.py:54
  25.3 14.1 %collective-permute-start.10 = (bf16[3,5,16,16]{3,2,1,0:T(8,128)(2,1)S(1)}, bf16[3,5,16,16]{3,2,1,0:T(8,128)(2,1)S(1)}, u32[]{:S(2)}, u32[]{:S(2)}) collective-permute-start(bf16[3,5,16,16]{3,2,1,0:T(8,128)(2,1)S(1)} %maximum_bitcast_fusion.6), channel_id=1, source_target_pairs={{8,14},{9,15},{10,12},{11,13},{24,30},{25,31},{26,28},{27,29}} | collective-permute-start | bytes 23048 | tf_op jit(solution)/shard_map/ppermute | solution.py:54
  26.6 13.8 %collective-permute-start.11 = (bf16[3,5,16,16]{3,2,1,0:T(8,128)(2,1)S(1)}, bf16[3,5,16,16]{3,2,1,0:T(8,128)(2,1)S(1)}, u32[]{:S(2)}, u32[]{:S(2)}) collective-permute-start(bf16[3,5,16,16]{3,2,1,0:T(8,128)(2,1)S(1)} %maximum_bitcast_fusion.6), channel_id=1, source_target_pairs={{8,15},{9,12},{10,13},{11,14},{24,31},{25,28},{26,29},{27,30}} | collective-permute-start | bytes 23048 | tf_op jit(solution)/shard_map/ppermute | solution.py:54
  27.9 12.5 %collective-permute-start.8 = (bf16[3,5,16,16]{3,2,1,0:T(8,128)(2,1)S(1)}, bf16[3,5,16,16]{3,2,1,0:T(8,128)(2,1)S(1)}, u32[]{:S(2)}, u32[]{:S(2)}) collective-permute-start(bf16[3,5,16,16]{3,2,1,0:T(8,128)(2,1)S(1)} %maximum_bitcast_fusion.6), channel_id=1, source_target_pairs={{8,12},{9,13},{10,14},{11,15},{24,28},{25,29},{26,30},{27,31}} | collective-permute-start | bytes 23048 | tf_op jit(solution)/shard_map/ppermute | solution.py:54
  29.2 16.5 %collective-permute-start.9 = (bf16[3,5,16,16]{3,2,1,0:T(8,128)(2,1)S(1)}, bf16[3,5,16,16]{3,2,1,0:T(8,128)(2,1)S(1)}, u32[]{:S(2)}, u32[]{:S(2)}) collective-permute-start(bf16[3,5,16,16]{3,2,1,0:T(8,128)(2,1)S(1)} %maximum_bitcast_fusion.6), channel_id=1, source_target_pairs={{8,13},{9,14},{10,15},{11,12},{24,29},{25,30},{26,31},{27,28}} | collective-permute-start | bytes 23048 | tf_op jit(solution)/shard_map/ppermute | solution.py:54

commit v6 on v4

--- a/solution.py
+++ b/solution.py
@@ -33,7 +33,8 @@
     up = up_elem[0]
     rhs_t = jnp.transpose(rhs[0], (2, 0, 1)).reshape(local, BLOCK)
 
-    shift = (g - up // local) % groups
+    xor_pairs = groups & (groups - 1) == 0
+    shift = jnp.bitwise_xor(g, up // local) if xor_pairs else (g - up // local) % groups
     pos = shift * local + up % local
     onehot = (jnp.arange(groups * local)[None, :, None] == pos[:, None, :]).astype(jnp.float32)
     picked_jac = jnp.einsum("kpe,kwve->kvpwe", onehot, jac)
@@ -51,10 +52,11 @@
     traces = None
     for turn in range(chains):
         if turn > 0:
-            blocks = []
-            for d in range(groups):
-                pairs = [((turn - 1) * groups + s, turn * groups + (s + d) % groups) for s in range(groups)]
-                blocks.append(lax.ppermute(traces, ("chain", "group"), pairs))
+            blocks = [None] * groups
+            for d in reversed(range(groups)):
+                pairs = [((turn - 1) * groups + s, turn * groups + ((s ^ d) if xor_pairs else (s + d) % groups))
+                         for s in range(groups)]
+                blocks[d] = lax.ppermute(traces, ("chain", "group"), pairs)
             traces_in = jnp.concatenate(blocks, axis=3)
         else:
             traces_in = None

time: 51.6 us -> 51.5 us (level)
  the two profiles are of different devices: /device:TPU:7 before, /device:TPU:11 now
where the time goes in v6:
time: 51.5 us; the launch traced here: 51 us
  waiting for transfers between devices  18.3 us (36%)
  other arithmetic  16.7 us (32%)
  starting transfers between devices  10.5 us (20%)
  local copies, waits for them, and re-layouts  2.53 us (5%)
  matrix products  2.53 us (5%)
    ppermute x12, waiting for transfers between devices, body(): blocks[d] = lax.ppermute(traces, ('chain', 'group'), pairs)  18.3 us
    reduce_sum x4, other arithmetic, solve(): return jnp.sum(inv * x[:, None, :], axis=-1)  16.5 us
    ppermute x12, starting transfers between devices, body(): blocks[d] = lax.ppermute(traces, ('chain', 'group'), pairs)  10.5 us
    dot_general x3, matrix products, solve(): jnp.einsum('kvfp,kvpwe->kwfe', traces_in.astype(jnp.float32), picked_jac,...  1.71 us
  transfers between devices with their start and end apart: 12, of which 3 were waited for; matrix products, arithmetic and copies ran while one was open for 0% of the time, Pallas kernels for 0%

profile of v6, /device:TPU:11, one launch (start us, length us, event | category | flops | bytes accessed | tf_op | source)
XLA Modules:
  0.0 51.0 jit_solution(9197208764088291974)
XLA Ops:
  0.0 0.8 %copy.17 = f32[16,5,64]{2,1,0:T(8,128)S(1)} copy(f32[16,5,64]{2,0,1:T(8,128)} %bitcast.136) | data formatting | bytes 40960 | tf_op jit(solution)/shard_map/transpose | solution.py:34
  0.8 0.1 reshape.114
  0.9 4.1 %fusion = f32[16,320]{1,0:T(8,128)S(1)} fusion(f32[1,16,320,320]{3,2,1,0:T(8,128)} %param.6, f32[16,320]{1,0:T(8,128)S(1)} %reshape.114), kind=kLoop, calls=%fused_computation.4 | loop fusion | flops 3271680 | bytes 6594560 | tf_op jit(solution)/shard_map/reduce_sum | solution.py:49
  5.1 0.1 copy.20
  5.3 0.7 %collective-permute-start = (bf16[3,5,16,16]{3,2,1,0:T(8,128)(2,1)S(1)}, bf16[3,5,16,16]{3,2,1,0:T(8,128)(2,1)S(1)}, u32[]{:S(2)}, u32[]{:S(2)}) collective-permute-start(bf16[3,5,16,16]{3,2,1,0:T(8,128)(2,1)S(1)} %maximum_bitcast_fusion), channel_id=1, source_target_pairs={{0,4},{1,5},{2,6},{3,7},{16,20},{17,21},{18,22},{19,23}} | collective-permute-start | bytes 23048 | tf_op jit(solution)/shard_map/ppermute | solution.py:59
  6.0 0.7 %collective-permute-start.1 = (bf16[3,5,16,16]{3,2,1,0:T(8,128)(2,1)S(1)}, bf16[3,5,16,16]{3,2,1,0:T(8,128)(2,1)S(1)}, u32[]{:S(2)}, u32[]{:S(2)}) collective-permute-start(bf16[3,5,16,16]{3,2,1,0:T(8,128)(2,1)S(1)} %maximum_bitcast_fusion), channel_id=1, source_target_pairs={{0,5},{1,4},{2,7},{3,6},{16,21},{17,20},{18,23},{19,22}} | collective-permute-start | bytes 23048 | tf_op jit(solution)/shard_map/ppermute | solution.py:59
  6.7 0.7 %collective-permute-start.2 = (bf16[3,5,16,16]{3,2,1,0:T(8,128)(2,1)S(1)}, bf16[3,5,16,16]{3,2,1,0:T(8,128)(2,1)S(1)}, u32[]{:S(2)}, u32[]{:S(2)}) collective-permute-start(bf16[3,5,16,16]{3,2,1,0:T(8,128)(2,1)S(1)} %maximum_bitcast_fusion), channel_id=1, source_target_pairs={{0,6},{1,7},{2,4},{3,5},{16,22},{17,23},{18,20},{19,21}} | collective-permute-start | bytes 23048 | tf_op jit(solution)/shard_map/ppermute | solution.py:59
  7.3 0.7 %collective-permute-start.3 = (bf16[3,5,16,16]{3,2,1,0:T(8,128)(2,1)S(1)}, bf16[3,5,16,16]{3,2,1,0:T(8,128)(2,1)S(1)}, u32[]{:S(2)}, u32[]{:S(2)}) collective-permute-start(bf16[3,5,16,16]{3,2,1,0:T(8,128)(2,1)S(1)} %maximum_bitcast_fusion), channel_id=1, source_target_pairs={{0,7},{1,6},{2,5},{3,4},{16,23},{17,22},{18,21},{19,20}} | collective-permute-start | bytes 23048 | tf_op jit(solution)/shard_map/ppermute | solution.py:59
  8.2 0.6 %convolution_bitcast_fusion.2 = f32[3,5,16,16]{2,3,0,1:T(8,128)S(1)} fusion(f32[3,16,5,5]{1,3,0,2:T(8,128)S(1)} %copy.19, f32[3,16,64]{2,1,0:T(8,128)S(1)} %convert_bitcast_fusion, bf16[3,5,16,16]{3,2,1,0:T(8,128)(2,1)S(1)} %collective-permute-done.3, bf16[3,5,16,16]{3,2,1,0:T(8,128)(2,1)S(1)} %collective-permute-done.2, ...), kind=kOutput, calls=%fused_computation.10 | convolution fusion | flops 14945280 | bytes 63168 | tf_op jit(solution)/shard_map/kvfp,kvpwe->kwfe/dot_general | solution.py:46
  8.8 0.3 convolution_bitcast_fusion.5
  9.2 4.1 %fusion.1 = f32[16,320]{1,0:T(8,128)S(1)} fusion(f32[1,16,320,320]{3,2,1,0:T(8,128)} %param.6, f32[16,320]{1,0:T(8,128)S(1)} %sub.28), kind=kLoop, calls=%fused_computation.5 | loop fusion | flops 3271680 | bytes 6594560 | tf_op jit(solution)/shard_map/reduce_sum | solution.py:49
  13.3 0.1 copy.22
  13.6 0.7 %collective-permute-start.4 = (bf16[3,5,16,16]{3,2,1,0:T(8,128)(2,1)S(1)}, bf16[3,5,16,16]{3,2,1,0:T(8,128)(2,1)S(1)}, u32[]{:S(2)}, u32[]{:S(2)}) collective-permute-start(bf16[3,5,16,16]{3,2,1,0:T(8,128)(2,1)S(1)} %maximum_bitcast_fusion.3), channel_id=1, source_target_pairs={{4,8},{5,9},{6,10},{7,11},{20,24},{21,25},{22,26},{23,27}} | collective-permute-start | bytes 23048 | tf_op jit(solution)/shard_map/ppermute | solution.py:59
  14.3 0.7 %collective-permute-start.5 = (bf16[3,5,16,16]{3,2,1,0:T(8,128)(2,1)S(1)}, bf16[3,5,16,16]{3,2,1,0:T(8,128)(2,1)S(1)}, u32[]{:S(2)}, u32[]{:S(2)}) collective-permute-start(bf16[3,5,16,16]{3,2,1,0:T(8,128)(2,1)S(1)} %maximum_bitcast_fusion.3), channel_id=1, source_target_pairs={{4,9},{5,8},{6,11},{7,10},{20,25},{21,24},{22,27},{23,26}} | collective-permute-start | bytes 23048 | tf_op jit(solution)/shard_map/ppermute | solution.py:59
  14.9 0.7 %collective-permute-start.6 = (bf16[3,5,16,16]{3,2,1,0:T(8,128)(2,1)S(1)}, bf16[3,5,16,16]{3,2,1,0:T(8,128)(2,1)S(1)}, u32[]{:S(2)}, u32[]{:S(2)}) collective-permute-start(bf16[3,5,16,16]{3,2,1,0:T(8,128)(2,1)S(1)} %maximum_bitcast_fusion.3), channel_id=1, source_target_pairs={{4,10},{5,11},{6,8},{7,9},{20,26},{21,27},{22,24},{23,25}} | collective-permute-start | bytes 23048 | tf_op jit(solution)/shard_map/ppermute | solution.py:59
  15.6 0.7 %collective-permute-start.7 = (bf16[3,5,16,16]{3,2,1,0:T(8,128)(2,1)S(1)}, bf16[3,5,16,16]{3,2,1,0:T(8,128)(2,1)S(1)}, u32[]{:S(2)}, u32[]{:S(2)}) collective-permute-start(bf16[3,5,16,16]{3,2,1,0:T(8,128)(2,1)S(1)} %maximum_bitcast_fusion.3), channel_id=1, source_target_pairs={{4,11},{5,10},{6,9},{7,8},{20,27},{21,26},{22,25},{23,24}} | collective-permute-start | bytes 23048 | tf_op jit(solution)/shard_map/ppermute | solution.py:59
  16.3 0.6 %convolution_bitcast_fusion.1 = f32[3,5,16,16]{2,3,0,1:T(8,128)S(1)} fusion(f32[3,16,5,5]{1,3,0,2:T(8,128)S(1)} %copy.19, f32[3,16,64]{2,1,0:T(8,128)S(1)} %convert_bitcast_fusion, bf16[3,5,16,16]{3,2,1,0:T(8,128)(2,1)S(1)} %collective-permute-done.7, bf16[3,5,16,16]{3,2,1,0:T(8,128)(2,1)S(1)} %collective-permute-done.6, ...), kind=kOutput, calls=%fused_computation.9 | convolution fusion | flops 14945280 | bytes 63168 | tf_op jit(solution)/shard_map/kvfp,kvpwe->kwfe/dot_general | solution.py:46
  16.9 0.3 convolution_bitcast_fusion.4
  17.3 4.1 %fusion.2 = f32[16,320]{1,0:T(8,128)S(1)} fusion(f32[1,16,320,320]{3,2,1,0:T(8,128)} %param.6, f32[16,320]{1,0:T(8,128)S(1)} %sub.29), kind=kLoop, calls=%fused_computation.6 | loop fusion | flops 3271680 | bytes 6594560 | tf_op jit(solution)/shard_map/reduce_sum | solution.py:49
  21.4 0.1 copy.24
  21.7 1.3 %collective-permute-start.10 = (bf16[3,5,16,16]{3,2,1,0:T(8,128)(2,1)S(1)}, bf16[3,5,16,16]{3,2,1,0:T(8,128)(2,1)S(1)}, u32[]{:S(2)}, u32[]{:S(2)}) collective-permute-start(bf16[3,5,16,16]{3,2,1,0:T(8,128)(2,1)S(1)} %maximum_bitcast_fusion.6), channel_id=1, source_target_pairs={{8,14},{9,15},{10,12},{11,13},{24,30},{25,31},{26,28},{27,29}} | collective-permute-start | bytes 23048 | tf_op jit(solution)/shard_map/ppermute | solution.py:59
  23.0 1.3 %collective-permute-start.11 = (bf16[3,5,16,16]{3,2,1,0:T(8,128)(2,1)S(1)}, bf16[3,5,16,16]{3,2,1,0:T(8,128)(2,1)S(1)}, u32[]{:S(2)}, u32[]{:S(2)}) collective-permute-start(bf16[3,5,16,16]{3,2,1,0:T(8,128)(2,1)S(1)} %maximum_bitcast_fusion.6), channel_id=1, source_target_pairs={{8,15},{9,14},{10,13},{11,12},{24,31},{25,30},{26,29},{27,28}} | collective-permute-start | bytes 23048 | tf_op jit(solution)/shard_map/ppermute | solution.py:59
  24.3 1.3 %collective-permute-start.8 = (bf16[3,5,16,16]{3,2,1,0:T(8,128)(2,1)S(1)}, bf16[3,5,16,16]{3,2,1,0:T(8,128)(2,1)S(1)}, u32[]{:S(2)}, u32[]{:S(2)}) collective-permute-start(bf16[3,5,16,16]{3,2,1,0:T(8,128)(2,1)S(1)} %maximum_bitcast_fusion.6), channel_id=1, source_target_pairs={{8,12},{9,13},{10,14},{11,15},{24,28},{25,29},{26,30},{27,31}} | collective-permute-start | bytes 23048 | tf_op jit(solution)/shard_map/ppermute | solution.py:59
  25.6 1.3 %collective-permute-start.9 = (bf16[3,5,16,16]{3,2,1,0:T(8,128)(2,1)S(1)}, bf16[3,5,16,16]{3,2,1,0:T(8,128)(2,1)S(1)}, u32[]{:S(2)}, u32[]{:S(2)}) collective-permute-start(bf16[3,5,16,16]{3,2,1,0:T(8,128)(2,1)S(1)} %maximum_bitcast_fusion.6), channel_id=1, source_target_pairs={{8,13},{9,12},{10,15},{11,14},{24,29},{25,28},{26,31},{27,30}} | collective-permute-start | bytes 23048 | tf_op jit(solution)/shard_map/ppermute | solution.py:59
  26.9 13.6 %collective-permute-done.10 = bf16[3,5,16,16]{3,2,1,0:T(8,128)(2,1)S(1)} collective-permute-done((bf16[3,5,16,16]{3,2,1,0:T(8,128)(2,1)S(1)}, bf16[3,5,16,16]{3,2,1,0:T(8,128)(2,1)S(1)}, u32[]{:S(2)}, u32[]{:S(2)}) %collective-permute-start.10) | collective-permute-done | bytes 7712 | tf_op jit(solution)/shard_map/ppermute | solution.py:59
  40.5 0.7 %collective-permute-done.11 = bf16[3,5,16,16]{3,2,1,0:T(8,128)(2,1)S(1)} collective-permute-done((bf16[3,5,16,16]{3,2,1,0:T(8,128)(2,1)S(1)}, bf16[3,5,16,16]{3,2,1,0:T(8,128)(2,1)S(1)}, u32[]{:S(2)}, u32[]{:S(2)}) %collective-permute-start.11) | collective-permute-done | bytes 7712 | tf_op jit(solution)/shard_map/ppermute | solution.py:59
  41.2 4.0 %collective-permute-done.9 = bf16[3,5,16,16]{3,2,1,0:T(8,128)(2,1)S(1)} collective-permute-done((bf16[3,5,16,16]{3,2,1,0:T(8,128)(2,1)S(1)}, bf16[3,5,16,16]{3,2,1,0:T(8,128)(2,1)S(1)}, u32[]{:S(2)}, u32[]{:S(2)}) %collective-permute-start.9) | collective-permute-done | bytes 7712 | tf_op jit(solution)/shard_map/ppermute | solution.py:59
  45.2 0.6 %convolution_bitcast_fusion = f32[3,5,16,16]{2,3,0,1:T(8,128)S(1)} fusion(f32[3,16,5,5]{1,3,0,2:T(8,128)S(1)} %copy.19, f32[3,16,64]{2,1,0:T(8,128)S(1)} %convert_bitcast_fusion, bf16[3,5,16,16]{3,2,1,0:T(8,128)(2,1)S(1)} %collective-permute-done.11, bf16[3,5,16,16]{3,2,1,0:T(8,128)(2,1)S(1)} %collective-permute-done.10, ...), kind=kOutput, calls=%fused_computation.8 | convolution fusion | flops 14945280 | bytes 63168 | tf_op jit(solution)/shard_map/kvfp,kvpwe->kwfe/dot_general | solution.py:46
  45.8 0.3 convolution_bitcast_fusion.3
  46.2 4.1 %fusion.3 = f32[16,320]{1,0:T(8,128)S(1)} fusion(f32[1,16,320,320]{3,2,1,0:T(8,128)} %param.6, f32[16,320]{1,0:T(8,128)S(1)} %sub.30), kind=kLoop, calls=%fused_computation.7 | loop fusion | flops 3271680 | bytes 6594560 | tf_op jit(solution)/shard_map/reduce_sum | solution.py:49
  50.3 0.1 select_n.66
  50.4 0.6 %copy.26 = f32[1,5,64,16]{2,3,1,0:T(8,128)} copy(f32[1,5,64,16]{2,1,3,0:T(8,128)S(1)} %bitcast.125) | data formatting | bytes 40960 | tf_op jit(solution)/shard_map/broadcast_in_dim | solution.py:67
  (47 shorter events, 0.8 us)
Async XLA Ops:
  0.0 8.8 %copy-start = (f32[3,64,16]{1,2,0:T(8,128)S(1)}, f32[3,64,16]{1,2,0:T(8,128)}, u32[]{:S(2)}) copy-start(f32[3,64,16]{1,2,0:T(8,128)} %param.9) | copy-start | bytes 36868
  0.0 8.0 %copy-start.2 = (s32[1,3,16]{2,0,1:T(1,128)S(1)}, s32[1,3,16]{2,0,1:T(1,128)}, u32[]{:S(2)}) copy-start(s32[1,3,16]{2,0,1:T(1,128)} %param.8) | copy-start | bytes 580
  0.0 8.1 %copy-start.1 = (f32[1,3,5,5,16]{4,0,3,2,1:T(1,128)S(1)}, f32[1,3,5,5,16]{4,0,3,2,1:T(1,128)}, u32[]{:S(2)}) copy-start(f32[1,3,5,5,16]{4,0,3,2,1:T(1,128)} %param.7) | copy-start | bytes 14404
  5.3 2.8 %collective-permute-start = (bf16[3,5,16,16]{3,2,1,0:T(8,128)(2,1)S(1)}, bf16[3,5,16,16]{3,2,1,0:T(8,128)(2,1)S(1)}, u32[]{:S(2)}, u32[]{:S(2)}) collective-permute-start(bf16[3,5,16,16]{3,2,1,0:T(8,128)(2,1)S(1)} %maximum_bitcast_fusion), channel_id=1, source_target_pairs={{0,4},{1,5},{2,6},{3,7},{16,20},{17,21},{18,22},{19,23}} | collective-permute-start | bytes 23048 | tf_op jit(solution)/shard_map/ppermute | solution.py:59
  6.0 2.2 %collective-permute-start.1 = (bf16[3,5,16,16]{3,2,1,0:T(8,128)(2,1)S(1)}, bf16[3,5,16,16]{3,2,1,0:T(8,128)(2,1)S(1)}, u32[]{:S(2)}, u32[]{:S(2)}) collective-permute-start(bf16[3,5,16,16]{3,2,1,0:T(8,128)(2,1)S(1)} %maximum_bitcast_fusion), channel_id=1, source_target_pairs={{0,5},{1,4},{2,7},{3,6},{16,21},{17,20},{18,23},{19,22}} | collective-permute-start | bytes 23048 | tf_op jit(solution)/shard_map/ppermute | solution.py:59
  6.7 1.5 %collective-permute-start.2 = (bf16[3,5,16,16]{3,2,1,0:T(8,128)(2,1)S(1)}, bf16[3,5,16,16]{3,2,1,0:T(8,128)(2,1)S(1)}, u32[]{:S(2)}, u32[]{:S(2)}) collective-permute-start(bf16[3,5,16,16]{3,2,1,0:T(8,128)(2,1)S(1)} %maximum_bitcast_fusion), channel_id=1, source_target_pairs={{0,6},{1,7},{2,4},{3,5},{16,22},{17,23},{18,20},{19,21}} | collective-permute-start | bytes 23048 | tf_op jit(solution)/shard_map/ppermute | solution.py:59
  7.3 0.9 %collective-permute-start.3 = (bf16[3,5,16,16]{3,2,1,0:T(8,128)(2,1)S(1)}, bf16[3,5,16,16]{3,2,1,0:T(8,128)(2,1)S(1)}, u32[]{:S(2)}, u32[]{:S(2)}) collective-permute-start(bf16[3,5,16,16]{3,2,1,0:T(8,128)(2,1)S(1)} %maximum_bitcast_fusion), channel_id=1, source_target_pairs={{0,7},{1,6},{2,5},{3,4},{16,23},{17,22},{18,21},{19,20}} | collective-permute-start | bytes 23048 | tf_op jit(solution)/shard_map/ppermute | solution.py:59
  13.6 2.7 %collective-permute-start.4 = (bf16[3,5,16,16]{3,2,1,0:T(8,128)(2,1)S(1)}, bf16[3,5,16,16]{3,2,1,0:T(8,128)(2,1)S(1)}, u32[]{:S(2)}, u32[]{:S(2)}) collective-permute-start(bf16[3,5,16,16]{3,2,1,0:T(8,128)(2,1)S(1)} %maximum_bitcast_fusion.3), channel_id=1, source_target_pairs={{4,8},{5,9},{6,10},{7,11},{20,24},{21,25},{22,26},{23,27}} | collective-permute-start | bytes 23048 | tf_op jit(solution)/shard_map/ppermute | solution.py:59
  14.3 2.0 %collective-permute-start.5 = (bf16[3,5,16,16]{3,2,1,0:T(8,128)(2,1)S(1)}, bf16[3,5,16,16]{3,2,1,0:T(8,128)(2,1)S(1)}, u32[]{:S(2)}, u32[]{:S(2)}) collective-permute-start(bf16[3,5,16,16]{3,2,1,0:T(8,128)(2,1)S(1)} %maximum_bitcast_fusion.3), channel_id=1, source_target_pairs={{4,9},{5,8},{6,11},{7,10},{20,25},{21,24},{22,27},{23,26}} | collective-permute-start | bytes 23048 | tf_op jit(solution)/shard_map/ppermute | solution.py:59
  14.9 1.4 %collective-permute-start.6 = (bf16[3,5,16,16]{3,2,1,0:T(8,128)(2,1)S(1)}, bf16[3,5,16,16]{3,2,1,0:T(8,128)(2,1)S(1)}, u32[]{:S(2)}, u32[]{:S(2)}) collective-permute-start(bf16[3,5,16,16]{3,2,1,0:T(8,128)(2,1)S(1)} %maximum_bitcast_fusion.3), channel_id=1, source_target_pairs={{4,10},{5,11},{6,8},{7,9},{20,26},{21,27},{22,24},{23,25}} | collective-permute-start | bytes 23048 | tf_op jit(solution)/shard_map/ppermute | solution.py:59
  15.6 0.7 %collective-permute-start.7 = (bf16[3,5,16,16]{3,2,1,0:T(8,128)(2,1)S(1)}, bf16[3,5,16,16]{3,2,1,0:T(8,128)(2,1)S(1)}, u32[]{:S(2)}, u32[]{:S(2)}) collective-permute-start(bf16[3,5,16,16]{3,2,1,0:T(8,128)(2,1)S(1)} %maximum_bitcast_fusion.3), channel_id=1, source_target_pairs={{4,11},{5,10},{6,9},{7,8},{20,27},{21,26},{22,25},{23,24}} | collective-permute-start | bytes 23048 | tf_op jit(solution)/shard_map/ppermute | solution.py:59
  21.7 18.8 %collective-permute-start.10 = (bf16[3,5,16,16]{3,2,1,0:T(8,128)(2,1)S(1)}, bf16[3,5,16,16]{3,2,1,0:T(8,128)(2,1)S(1)}, u32[]{:S(2)}, u32[]{:S(2)}) collective-permute-start(bf16[3,5,16,16]{3,2,1,0:T(8,128)(2,1)S(1)} %maximum_bitcast_fusion.6), channel_id=1, source_target_pairs={{8,14},{9,15},{10,12},{11,13},{24,30},{25,31},{26,28},{27,29}} | collective-permute-start | bytes 23048 | tf_op jit(solution)/shard_map/ppermute | solution.py:59
  23.0 18.2 %collective-permute-start.11 = (bf16[3,5,16,16]{3,2,1,0:T(8,128)(2,1)S(1)}, bf16[3,5,16,16]{3,2,1,0:T(8,128)(2,1)S(1)}, u32[]{:S(2)}, u32[]{:S(2)}) collective-permute-start(bf16[3,5,16,16]{3,2,1,0:T(8,128)(2,1)S(1)} %maximum_bitcast_fusion.6), channel_id=1, source_target_pairs={{8,15},{9,14},{10,13},{11,12},{24,31},{25,30},{26,29},{27,28}} | collective-permute-start | bytes 23048 | tf_op jit(solution)/shard_map/ppermute | solution.py:59
  24.3 16.9 %collective-permute-start.8 = (bf16[3,5,16,16]{3,2,1,0:T(8,128)(2,1)S(1)}, bf16[3,5,16,16]{3,2,1,0:T(8,128)(2,1)S(1)}, u32[]{:S(2)}, u32[]{:S(2)}) collective-permute-start(bf16[3,5,16,16]{3,2,1,0:T(8,128)(2,1)S(1)} %maximum_bitcast_fusion.6), channel_id=1, source_target_pairs={{8,12},{9,13},{10,14},{11,15},{24,28},{25,29},{26,30},{27,31}} | collective-permute-start | bytes 23048 | tf_op jit(solution)/shard_map/ppermute | solution.py:59
  25.6 19.6 %collective-permute-start.9 = (bf16[3,5,16,16]{3,2,1,0:T(8,128)(2,1)S(1)}, bf16[3,5,16,16]{3,2,1,0:T(8,128)(2,1)S(1)}, u32[]{:S(2)}, u32[]{:S(2)}) collective-permute-start(bf16[3,5,16,16]{3,2,1,0:T(8,128)(2,1)S(1)} %maximum_bitcast_fusion.6), channel_id=1, source_target_pairs={{8,13},{9,12},{10,15},{11,14},{24,29},{25,28},{26,31},{27,30}} | collective-permute-start | bytes 23048 | tf_op jit(solution)/shard_map/ppermute | solution.py:59

commit v7 on v5

--- a/solution.py
+++ b/solution.py
@@ -33,7 +33,8 @@
     up = up_elem[0]
     rhs_t = jnp.transpose(rhs[0], (2, 0, 1)).reshape(local, BLOCK)
 
-    shift = (g - up // local) % groups
+    xor_pairs = groups & (groups - 1) == 0
+    shift = jnp.bitwise_xor(g, up // local) if xor_pairs else (g - up // local) % groups
     pos = shift * local + up % local
     onehot = (jnp.arange(groups * local)[None, :, None] == pos[:, None, :]).astype(jnp.float32)
     picked_jac = jnp.einsum("kpe,kwve->kvpwe", onehot, jac)
@@ -48,10 +49,11 @@
     traces = face_traces(base).astype(jnp.bfloat16)
     own_coupling = jnp.zeros((local, BLOCK), jnp.float32)
     for turn in range(1, chains):
-        blocks = []
-        for d in range(groups):
-            pairs = [((turn - 1) * groups + s, turn * groups + (s + d) % groups) for s in range(groups)]
-            blocks.append(lax.ppermute(traces, ("chain", "group"), pairs))
+        blocks = [None] * groups
+        for d in reversed(range(groups)):
+            pairs = [((turn - 1) * groups + s, turn * groups + ((s ^ d) if xor_pairs else (s + d) % groups))
+                     for s in range(groups)]
+            blocks[d] = lax.ppermute(traces, ("chain", "group"), pairs)
         coupling = coupling_of(jnp.concatenate(blocks, axis=3))
         own_coupling = jnp.where(c == turn, coupling, own_coupling)
         if turn + 1 < chains:

time: 52 us -> 50 us (0.962)
  waiting for transfers between devices: 15.2 us -> 13.2 us
    ppermute x12, waiting for transfers between devices: 15.2 us -> 13.2 us  [body(): blocks[d] = lax.ppermute(traces, ('chain', 'group'), pairs)]
  transfers between devices with their start and end apart: 12 -> 12, of which waited for: 3 -> 3; matrix products, arithmetic and copies ran while one was open for 11% -> 12% of each run, Pallas kernels for 0% -> 0%
where the time goes in v7:
time: 50 us; the launch traced here: 49.5 us
  other arithmetic  20.3 us (41%)
  waiting for transfers between devices  13.2 us (26%)
  starting transfers between devices  10.5 us (21%)
  matrix products  2.53 us (5%)
  local copies, waits for them, and re-layouts  2.51 us (5%)
    ppermute x12, waiting for transfers between devices, body(): blocks[d] = lax.ppermute(traces, ('chain', 'group'), pairs)  13.2 us
    ppermute x12, starting transfers between devices, body(): blocks[d] = lax.ppermute(traces, ('chain', 'group'), pairs)  10.5 us
    reduce_sum x2, other arithmetic, body(): jnp.sum(inv_narrow.astype(jnp.float32) * coupling[:, None, :], axis=-1)  6.2 us
    convert_element_type x1, other arithmetic, body(): inv_narrow = lax.optimization_barrier(inv.astype(jnp.bfloat16))  5.67 us
    reduce_sum x1, other arithmetic, body(): base = jnp.sum(inv * rhs_t[:, None, :], axis=-1)  4.14 us
    reduce_sum x1, other arithmetic, body(): out = base - jnp.sum(inv * own_coupling[:, None, :], axis=-1)  4.13 us
    dot_general x3, matrix products, coupling_of(): jnp.einsum('kvfp,kvpwe->kwfe', traces_in.astype(jnp.float32), picked_jac,...  1.71 us
  transfers between devices with their start and end apart: 12, of which 3 were waited for; matrix products, arithmetic and copies ran while one was open for 12% of the time, Pallas kernels for 0%

profile of v7, /device:TPU:7, one launch (start us, length us, event | category | flops | bytes accessed | tf_op | source)
XLA Modules:
  0.0 49.5 jit_solution(4225950855680729215)
XLA Ops:
  0.0 0.8 %copy.17 = f32[16,5,64]{2,1,0:T(8,128)S(1)} copy(f32[16,5,64]{2,0,1:T(8,128)} %bitcast.131) | data formatting | bytes 40960 | tf_op jit(solution)/shard_map/transpose | solution.py:34
  0.9 4.1 %fusion.2 = f32[16,320]{1,0:T(8,128)S(1)} fusion(f32[1,16,320,320]{3,2,1,0:T(8,128)} %param.6, f32[16,320]{1,0:T(8,128)S(1)} %mul.46), kind=kLoop, calls=%fused_computation.7 | loop fusion | flops 3271680 | bytes 6594560 | tf_op jit(solution)/shard_map/reduce_sum | solution.py:47
  5.1 0.1 copy.20
  5.3 0.7 %collective-permute-start = (bf16[3,5,16,16]{3,2,1,0:T(8,128)(2,1)S(1)}, bf16[3,5,16,16]{3,2,1,0:T(8,128)(2,1)S(1)}, u32[]{:S(2)}, u32[]{:S(2)}) collective-permute-start(bf16[3,5,16,16]{3,2,1,0:T(8,128)(2,1)S(1)} %maximum_bitcast_fusion), channel_id=1, source_target_pairs={{0,4},{1,5},{2,6},{3,7},{16,20},{17,21},{18,22},{19,23}} | collective-permute-start | bytes 23048 | tf_op jit(solution)/shard_map/ppermute | solution.py:56
  6.0 0.7 %collective-permute-start.1 = (bf16[3,5,16,16]{3,2,1,0:T(8,128)(2,1)S(1)}, bf16[3,5,16,16]{3,2,1,0:T(8,128)(2,1)S(1)}, u32[]{:S(2)}, u32[]{:S(2)}) collective-permute-start(bf16[3,5,16,16]{3,2,1,0:T(8,128)(2,1)S(1)} %maximum_bitcast_fusion), channel_id=1, source_target_pairs={{0,5},{1,4},{2,7},{3,6},{16,21},{17,20},{18,23},{19,22}} | collective-permute-start | bytes 23048 | tf_op jit(solution)/shard_map/ppermute | solution.py:56
  6.7 0.7 %collective-permute-start.2 = (bf16[3,5,16,16]{3,2,1,0:T(8,128)(2,1)S(1)}, bf16[3,5,16,16]{3,2,1,0:T(8,128)(2,1)S(1)}, u32[]{:S(2)}, u32[]{:S(2)}) collective-permute-start(bf16[3,5,16,16]{3,2,1,0:T(8,128)(2,1)S(1)} %maximum_bitcast_fusion), channel_id=1, source_target_pairs={{0,6},{1,7},{2,4},{3,5},{16,22},{17,23},{18,20},{19,21}} | collective-permute-start | bytes 23048 | tf_op jit(solution)/shard_map/ppermute | solution.py:56
  7.3 0.7 %collective-permute-start.3 = (bf16[3,5,16,16]{3,2,1,0:T(8,128)(2,1)S(1)}, bf16[3,5,16,16]{3,2,1,0:T(8,128)(2,1)S(1)}, u32[]{:S(2)}, u32[]{:S(2)}) collective-permute-start(bf16[3,5,16,16]{3,2,1,0:T(8,128)(2,1)S(1)} %maximum_bitcast_fusion), channel_id=1, source_target_pairs={{0,7},{1,6},{2,5},{3,4},{16,23},{17,22},{18,21},{19,20}} | collective-permute-start | bytes 23048 | tf_op jit(solution)/shard_map/ppermute | solution.py:56
  8.0 5.7 %bitcast_convert_fusion = bf16[16,320,320]{2,1,0:T(8,128)(2,1)} fusion(f32[1,16,320,320]{3,2,1,0:T(8,128)} %param.6), kind=kLoop, calls=%fused_computation.5 | loop fusion | flops 1638400 | bytes 9830400 | tf_op jit(solution)/shard_map/convert_element_type | solution.py:48
  13.9 0.6 %convolution_bitcast_fusion.2 = f32[3,5,16,16]{2,3,0,1:T(8,128)S(1)} fusion(f32[3,16,5,5]{1,3,0,2:T(8,128)S(1)} %copy.19, f32[3,16,64]{2,1,0:T(8,128)S(1)} %convert_bitcast_fusion, bf16[3,5,16,16]{3,2,1,0:T(8,128)(2,1)S(1)} %collective-permute-done.3, bf16[3,5,16,16]{3,2,1,0:T(8,128)(2,1)S(1)} %collective-permute-done.2, ...), kind=kOutput, calls=%fused_computation.11 | convolution fusion | flops 14945280 | bytes 63168 | tf_op jit(solution)/shard_map/kvfp,kvpwe->kwfe/dot_general | solution.py:43
  14.5 0.3 convolution_bitcast_fusion.5
  14.8 3.1 %fusion = f32[16,320]{1,0:T(8,128)S(1)} fusion(bf16[16,320,320]{2,1,0:T(8,128)(2,1)} %bitcast_convert_fusion, f32[16,320]{1,0:T(8,128)S(1)} %mul.50), kind=kLoop, calls=%fused_computation.2 | loop fusion | flops 4910080 | bytes 3317760 | tf_op jit(solution)/shard_map/reduce_sum | solution.py:60
  17.9 0.1 copy.22
  18.2 0.7 %collective-permute-start.4 = (bf16[3,5,16,16]{3,2,1,0:T(8,128)(2,1)S(1)}, bf16[3,5,16,16]{3,2,1,0:T(8,128)(2,1)S(1)}, u32[]{:S(2)}, u32[]{:S(2)}) collective-permute-start(bf16[3,5,16,16]{3,2,1,0:T(8,128)(2,1)S(1)} %maximum_bitcast_fusion.3), channel_id=1, source_target_pairs={{4,8},{5,9},{6,10},{7,11},{20,24},{21,25},{22,26},{23,27}} | collective-permute-start | bytes 23048 | tf_op jit(solution)/shard_map/ppermute | solution.py:56
  18.9 0.7 %collective-permute-start.5 = (bf16[3,5,16,16]{3,2,1,0:T(8,128)(2,1)S(1)}, bf16[3,5,16,16]{3,2,1,0:T(8,128)(2,1)S(1)}, u32[]{:S(2)}, u32[]{:S(2)}) collective-permute-start(bf16[3,5,16,16]{3,2,1,0:T(8,128)(2,1)S(1)} %maximum_bitcast_fusion.3), channel_id=1, source_target_pairs={{4,9},{5,8},{6,11},{7,10},{20,25},{21,24},{22,27},{23,26}} | collective-permute-start | bytes 23048 | tf_op jit(solution)/shard_map/ppermute | solution.py:56
  19.5 0.7 %collective-permute-start.6 = (bf16[3,5,16,16]{3,2,1,0:T(8,128)(2,1)S(1)}, bf16[3,5,16,16]{3,2,1,0:T(8,128)(2,1)S(1)}, u32[]{:S(2)}, u32[]{:S(2)}) collective-permute-start(bf16[3,5,16,16]{3,2,1,0:T(8,128)(2,1)S(1)} %maximum_bitcast_fusion.3), channel_id=1, source_target_pairs={{4,10},{5,11},{6,8},{7,9},{20,26},{21,27},{22,24},{23,25}} | collective-permute-start | bytes 23048 | tf_op jit(solution)/shard_map/ppermute | solution.py:56
  20.2 0.7 %collective-permute-start.7 = (bf16[3,5,16,16]{3,2,1,0:T(8,128)(2,1)S(1)}, bf16[3,5,16,16]{3,2,1,0:T(8,128)(2,1)S(1)}, u32[]{:S(2)}, u32[]{:S(2)}) collective-permute-start(bf16[3,5,16,16]{3,2,1,0:T(8,128)(2,1)S(1)} %maximum_bitcast_fusion.3), channel_id=1, source_target_pairs={{4,11},{5,10},{6,9},{7,8},{20,27},{21,26},{22,25},{23,24}} | collective-permute-start | bytes 23048 | tf_op jit(solution)/shard_map/ppermute | solution.py:56
  20.9 0.6 %convolution_bitcast_fusion.1 = f32[3,5,16,16]{2,3,0,1:T(8,128)S(1)} fusion(f32[3,16,5,5]{1,3,0,2:T(8,128)S(1)} %copy.19, f32[3,16,64]{2,1,0:T(8,128)S(1)} %convert_bitcast_fusion, bf16[3,5,16,16]{3,2,1,0:T(8,128)(2,1)S(1)} %collective-permute-done.7, bf16[3,5,16,16]{3,2,1,0:T(8,128)(2,1)S(1)} %collective-permute-done.6, ...), kind=kOutput, calls=%fused_computation.10 | convolution fusion | flops 14945280 | bytes 63168 | tf_op jit(solution)/shard_map/kvfp,kvpwe->kwfe/dot_general | solution.py:43
  21.5 0.3 convolution_bitcast_fusion.4
  21.9 3.1 %fusion.1 = f32[16,320]{1,0:T(8,128)S(1)} fusion(bf16[16,320,320]{2,1,0:T(8,128)(2,1)} %bitcast_convert_fusion, f32[16,320]{1,0:T(8,128)S(1)} %mul.53), kind=kLoop, calls=%fused_computation.3 | loop fusion | flops 4910080 | bytes 3317760 | tf_op jit(solution)/shard_map/reduce_sum | solution.py:60
  25.0 0.1 copy.24
  25.3 1.3 %collective-permute-start.10 = (bf16[3,5,16,16]{3,2,1,0:T(8,128)(2,1)S(1)}, bf16[3,5,16,16]{3,2,1,0:T(8,128)(2,1)S(1)}, u32[]{:S(2)}, u32[]{:S(2)}) collective-permute-start(bf16[3,5,16,16]{3,2,1,0:T(8,128)(2,1)S(1)} %maximum_bitcast_fusion.6), channel_id=1, source_target_pairs={{8,14},{9,15},{10,12},{11,13},{24,30},{25,31},{26,28},{27,29}} | collective-permute-start | bytes 23048 | tf_op jit(solution)/shard_map/ppermute | solution.py:56
  26.6 1.3 %collective-permute-start.11 = (bf16[3,5,16,16]{3,2,1,0:T(8,128)(2,1)S(1)}, bf16[3,5,16,16]{3,2,1,0:T(8,128)(2,1)S(1)}, u32[]{:S(2)}, u32[]{:S(2)}) collective-permute-start(bf16[3,5,16,16]{3,2,1,0:T(8,128)(2,1)S(1)} %maximum_bitcast_fusion.6), channel_id=1, source_target_pairs={{8,15},{9,14},{10,13},{11,12},{24,31},{25,30},{26,29},{27,28}} | collective-permute-start | bytes 23048 | tf_op jit(solution)/shard_map/ppermute | solution.py:56
  27.9 1.3 %collective-permute-start.8 = (bf16[3,5,16,16]{3,2,1,0:T(8,128)(2,1)S(1)}, bf16[3,5,16,16]{3,2,1,0:T(8,128)(2,1)S(1)}, u32[]{:S(2)}, u32[]{:S(2)}) collective-permute-start(bf16[3,5,16,16]{3,2,1,0:T(8,128)(2,1)S(1)} %maximum_bitcast_fusion.6), channel_id=1, source_target_pairs={{8,12},{9,13},{10,14},{11,15},{24,28},{25,29},{26,30},{27,31}} | collective-permute-start | bytes 23048 | tf_op jit(solution)/shard_map/ppermute | solution.py:56
  29.2 1.3 %collective-permute-start.9 = (bf16[3,5,16,16]{3,2,1,0:T(8,128)(2,1)S(1)}, bf16[3,5,16,16]{3,2,1,0:T(8,128)(2,1)S(1)}, u32[]{:S(2)}, u32[]{:S(2)}) collective-permute-start(bf16[3,5,16,16]{3,2,1,0:T(8,128)(2,1)S(1)} %maximum_bitcast_fusion.6), channel_id=1, source_target_pairs={{8,13},{9,12},{10,15},{11,14},{24,29},{25,28},{26,31},{27,30}} | collective-permute-start | bytes 23048 | tf_op jit(solution)/shard_map/ppermute | solution.py:56
  30.5 9.5 %collective-permute-done.10 = bf16[3,5,16,16]{3,2,1,0:T(8,128)(2,1)S(1)} collective-permute-done((bf16[3,5,16,16]{3,2,1,0:T(8,128)(2,1)S(1)}, bf16[3,5,16,16]{3,2,1,0:T(8,128)(2,1)S(1)}, u32[]{:S(2)}, u32[]{:S(2)}) %collective-permute-start.10) | collective-permute-done | bytes 7712 | tf_op jit(solution)/shard_map/ppermute | solution.py:56
  39.9 3.1 %collective-permute-done.11 = bf16[3,5,16,16]{3,2,1,0:T(8,128)(2,1)S(1)} collective-permute-done((bf16[3,5,16,16]{3,2,1,0:T(8,128)(2,1)S(1)}, bf16[3,5,16,16]{3,2,1,0:T(8,128)(2,1)S(1)}, u32[]{:S(2)}, u32[]{:S(2)}) %collective-permute-start.11) | collective-permute-done | bytes 7712 | tf_op jit(solution)/shard_map/ppermute | solution.py:56
  43.1 0.6 %collective-permute-done.9 = bf16[3,5,16,16]{3,2,1,0:T(8,128)(2,1)S(1)} collective-permute-done((bf16[3,5,16,16]{3,2,1,0:T(8,128)(2,1)S(1)}, bf16[3,5,16,16]{3,2,1,0:T(8,128)(2,1)S(1)}, u32[]{:S(2)}, u32[]{:S(2)}) %collective-permute-start.9) | collective-permute-done | bytes 7712 | tf_op jit(solution)/shard_map/ppermute | solution.py:56
  43.7 0.6 %convolution_bitcast_fusion = f32[3,5,16,16]{2,3,0,1:T(8,128)S(1)} fusion(f32[3,16,5,5]{1,3,0,2:T(8,128)S(1)} %copy.19, f32[3,16,64]{2,1,0:T(8,128)S(1)} %convert_bitcast_fusion, bf16[3,5,16,16]{3,2,1,0:T(8,128)(2,1)S(1)} %collective-permute-done.11, bf16[3,5,16,16]{3,2,1,0:T(8,128)(2,1)S(1)} %collective-permute-done.10, ...), kind=kOutput, calls=%fused_computation.9 | convolution fusion | flops 14945280 | bytes 63168 | tf_op jit(solution)/shard_map/kvfp,kvpwe->kwfe/dot_general | solution.py:43
  44.3 0.3 convolution_bitcast_fusion.3
  44.7 4.1 %fusion.3 = f32[16,320]{1,0:T(8,128)S(1)} fusion(f32[1,16,320,320]{3,2,1,0:T(8,128)} %param.6, f32[16,320]{1,0:T(8,128)S(1)} %select_select_fusion), kind=kLoop, calls=%fused_computation.8 | loop fusion | flops 3271680 | bytes 6594560 | tf_op jit(solution)/shard_map/reduce_sum | solution.py:62
  48.8 0.1 sub.25
  48.9 0.6 %copy.26 = f32[1,5,64,16]{2,3,1,0:T(8,128)} copy(f32[1,5,64,16]{2,1,3,0:T(8,128)S(1)} %bitcast.120) | data formatting | bytes 40960 | tf_op jit(solution)/shard_map/broadcast_in_dim | solution.py:63
  (46 shorter events, 0.8 us)
Async XLA Ops:
  0.0 14.4 %copy-start = (f32[3,64,16]{1,2,0:T(8,128)S(1)}, f32[3,64,16]{1,2,0:T(8,128)}, u32[]{:S(2)}) copy-start(f32[3,64,16]{1,2,0:T(8,128)} %param.9) | copy-start | bytes 36868
  5.0 8.7 %copy-start.2 = (s32[1,3,16]{2,0,1:T(1,128)S(1)}, s32[1,3,16]{2,0,1:T(1,128)}, u32[]{:S(2)}) copy-start(s32[1,3,16]{2,0,1:T(1,128)} %param.8) | copy-start | bytes 580
  5.0 8.7 %copy-start.1 = (f32[1,3,5,5,16]{4,0,3,2,1:T(1,128)S(1)}, f32[1,3,5,5,16]{4,0,3,2,1:T(1,128)}, u32[]{:S(2)}) copy-start(f32[1,3,5,5,16]{4,0,3,2,1:T(1,128)} %param.7) | copy-start | bytes 14404
  5.3 8.5 %collective-permute-start = (bf16[3,5,16,16]{3,2,1,0:T(8,128)(2,1)S(1)}, bf16[3,5,16,16]{3,2,1,0:T(8,128)(2,1)S(1)}, u32[]{:S(2)}, u32[]{:S(2)}) collective-permute-start(bf16[3,5,16,16]{3,2,1,0:T(8,128)(2,1)S(1)} %maximum_bitcast_fusion), channel_id=1, source_target_pairs={{0,4},{1,5},{2,6},{3,7},{16,20},{17,21},{18,22},{19,23}} | collective-permute-start | bytes 23048 | tf_op jit(solution)/shard_map/ppermute | solution.py:56
  6.0 7.8 %collective-permute-start.1 = (bf16[3,5,16,16]{3,2,1,0:T(8,128)(2,1)S(1)}, bf16[3,5,16,16]{3,2,1,0:T(8,128)(2,1)S(1)}, u32[]{:S(2)}, u32[]{:S(2)}) collective-permute-start(bf16[3,5,16,16]{3,2,1,0:T(8,128)(2,1)S(1)} %maximum_bitcast_fusion), channel_id=1, source_target_pairs={{0,5},{1,4},{2,7},{3,6},{16,21},{17,20},{18,23},{19,22}} | collective-permute-start | bytes 23048 | tf_op jit(solution)/shard_map/ppermute | solution.py:56
  6.7 7.2 %collective-permute-start.2 = (bf16[3,5,16,16]{3,2,1,0:T(8,128)(2,1)S(1)}, bf16[3,5,16,16]{3,2,1,0:T(8,128)(2,1)S(1)}, u32[]{:S(2)}, u32[]{:S(2)}) collective-permute-start(bf16[3,5,16,16]{3,2,1,0:T(8,128)(2,1)S(1)} %maximum_bitcast_fusion), channel_id=1, source_target_pairs={{0,6},{1,7},{2,4},{3,5},{16,22},{17,23},{18,20},{19,21}} | collective-permute-start | bytes 23048 | tf_op jit(solution)/shard_map/ppermute | solution.py:56
  7.3 6.5 %collective-permute-start.3 = (bf16[3,5,16,16]{3,2,1,0:T(8,128)(2,1)S(1)}, bf16[3,5,16,16]{3,2,1,0:T(8,128)(2,1)S(1)}, u32[]{:S(2)}, u32[]{:S(2)}) collective-permute-start(bf16[3,5,16,16]{3,2,1,0:T(8,128)(2,1)S(1)} %maximum_bitcast_fusion), channel_id=1, source_target_pairs={{0,7},{1,6},{2,5},{3,4},{16,23},{17,22},{18,21},{19,20}} | collective-permute-start | bytes 23048 | tf_op jit(solution)/shard_map/ppermute | solution.py:56
  18.2 2.7 %collective-permute-start.4 = (bf16[3,5,16,16]{3,2,1,0:T(8,128)(2,1)S(1)}, bf16[3,5,16,16]{3,2,1,0:T(8,128)(2,1)S(1)}, u32[]{:S(2)}, u32[]{:S(2)}) collective-permute-start(bf16[3,5,16,16]{3,2,1,0:T(8,128)(2,1)S(1)} %maximum_bitcast_fusion.3), channel_id=1, source_target_pairs={{4,8},{5,9},{6,10},{7,11},{20,24},{21,25},{22,26},{23,27}} | collective-permute-start | bytes 23048 | tf_op jit(solution)/shard_map/ppermute | solution.py:56
  18.9 2.0 %collective-permute-start.5 = (bf16[3,5,16,16]{3,2,1,0:T(8,128)(2,1)S(1)}, bf16[3,5,16,16]{3,2,1,0:T(8,128)(2,1)S(1)}, u32[]{:S(2)}, u32[]{:S(2)}) collective-permute-start(bf16[3,5,16,16]{3,2,1,0:T(8,128)(2,1)S(1)} %maximum_bitcast_fusion.3), channel_id=1, source_target_pairs={{4,9},{5,8},{6,11},{7,10},{20,25},{21,24},{22,27},{23,26}} | collective-permute-start | bytes 23048 | tf_op jit(solution)/shard_map/ppermute | solution.py:56
  19.5 1.4 %collective-permute-start.6 = (bf16[3,5,16,16]{3,2,1,0:T(8,128)(2,1)S(1)}, bf16[3,5,16,16]{3,2,1,0:T(8,128)(2,1)S(1)}, u32[]{:S(2)}, u32[]{:S(2)}) collective-permute-start(bf16[3,5,16,16]{3,2,1,0:T(8,128)(2,1)S(1)} %maximum_bitcast_fusion.3), channel_id=1, source_target_pairs={{4,10},{5,11},{6,8},{7,9},{20,26},{21,27},{22,24},{23,25}} | collective-permute-start | bytes 23048 | tf_op jit(solution)/shard_map/ppermute | solution.py:56
  20.2 0.7 %collective-permute-start.7 = (bf16[3,5,16,16]{3,2,1,0:T(8,128)(2,1)S(1)}, bf16[3,5,16,16]{3,2,1,0:T(8,128)(2,1)S(1)}, u32[]{:S(2)}, u32[]{:S(2)}) collective-permute-start(bf16[3,5,16,16]{3,2,1,0:T(8,128)(2,1)S(1)} %maximum_bitcast_fusion.3), channel_id=1, source_target_pairs={{4,11},{5,10},{6,9},{7,8},{20,27},{21,26},{22,25},{23,24}} | collective-permute-start | bytes 23048 | tf_op jit(solution)/shard_map/ppermute | solution.py:56
  25.3 14.7 %collective-permute-start.10 = (bf16[3,5,16,16]{3,2,1,0:T(8,128)(2,1)S(1)}, bf16[3,5,16,16]{3,2,1,0:T(8,128)(2,1)S(1)}, u32[]{:S(2)}, u32[]{:S(2)}) collective-permute-start(bf16[3,5,16,16]{3,2,1,0:T(8,128)(2,1)S(1)} %maximum_bitcast_fusion.6), channel_id=1, source_target_pairs={{8,14},{9,15},{10,12},{11,13},{24,30},{25,31},{26,28},{27,29}} | collective-permute-start | bytes 23048 | tf_op jit(solution)/shard_map/ppermute | solution.py:56
  26.6 16.5 %collective-permute-start.11 = (bf16[3,5,16,16]{3,2,1,0:T(8,128)(2,1)S(1)}, bf16[3,5,16,16]{3,2,1,0:T(8,128)(2,1)S(1)}, u32[]{:S(2)}, u32[]{:S(2)}) collective-permute-start(bf16[3,5,16,16]{3,2,1,0:T(8,128)(2,1)S(1)} %maximum_bitcast_fusion.6), channel_id=1, source_target_pairs={{8,15},{9,14},{10,13},{11,12},{24,31},{25,30},{26,29},{27,28}} | collective-permute-start | bytes 23048 | tf_op jit(solution)/shard_map/ppermute | solution.py:56
  27.9 15.2 %collective-permute-start.8 = (bf16[3,5,16,16]{3,2,1,0:T(8,128)(2,1)S(1)}, bf16[3,5,16,16]{3,2,1,0:T(8,128)(2,1)S(1)}, u32[]{:S(2)}, u32[]{:S(2)}) collective-permute-start(bf16[3,5,16,16]{3,2,1,0:T(8,128)(2,1)S(1)} %maximum_bitcast_fusion.6), channel_id=1, source_target_pairs={{8,12},{9,13},{10,14},{11,15},{24,28},{25,29},{26,30},{27,31}} | collective-permute-start | bytes 23048 | tf_op jit(solution)/shard_map/ppermute | solution.py:56
  29.2 14.5 %collective-permute-start.9 = (bf16[3,5,16,16]{3,2,1,0:T(8,128)(2,1)S(1)}, bf16[3,5,16,16]{3,2,1,0:T(8,128)(2,1)S(1)}, u32[]{:S(2)}, u32[]{:S(2)}) collective-permute-start(bf16[3,5,16,16]{3,2,1,0:T(8,128)(2,1)S(1)} %maximum_bitcast_fusion.6), channel_id=1, source_target_pairs={{8,13},{9,12},{10,15},{11,14},{24,29},{25,28},{26,31},{27,30}} | collective-permute-start | bytes 23048 | tf_op jit(solution)/shard_map/ppermute | solution.py:56

commit v8 on v7

--- a/solution.py
+++ b/solution.py
@@ -39,8 +39,12 @@
     onehot = (jnp.arange(groups * local)[None, :, None] == pos[:, None, :]).astype(jnp.float32)
     picked_jac = jnp.einsum("kpe,kwve->kvpwe", onehot, jac)
 
-    def coupling_of(traces_in):
-        mixed = jnp.einsum("kvfp,kvpwe->kwfe", traces_in.astype(jnp.float32), picked_jac, precision=HIGH)
+    jac_blocks = [picked_jac[:, :, d * local:(d + 1) * local] for d in range(groups)]
+
+    def coupling_of(blocks):
+        mixed = [jnp.einsum("kvfp,kvpwe->kwfe", blocks[d].astype(jnp.float32), jac_blocks[d], precision=HIGH)
+                 for d in reversed(range(groups))]
+        mixed = sum(mixed[1:], mixed[0])
         coupling = jnp.einsum("kwfe,kif->ewi", mixed, lift, precision=HIGH)
         return coupling.reshape(local, BLOCK)
 
@@ -54,7 +58,7 @@
             pairs = [((turn - 1) * groups + s, turn * groups + ((s ^ d) if xor_pairs else (s + d) % groups))
                      for s in range(groups)]
             blocks[d] = lax.ppermute(traces, ("chain", "group"), pairs)
-        coupling = coupling_of(jnp.concatenate(blocks, axis=3))
+        coupling = coupling_of(blocks)
         own_coupling = jnp.where(c == turn, coupling, own_coupling)
         if turn + 1 < chains:
             approx = base - jnp.sum(inv_narrow.astype(jnp.float32) * coupling[:, None, :], axis=-1)

time: 50 us -> 53.5 us (1.070)
  matrix products: 2.53 us -> 6.67 us
  waiting for transfers between devices: 13.2 us -> 12.3 us
    dot_general x3 -> x12, matrix products: 1.71 us -> 5.86 us  [coupling_of(): jnp.einsum('kvfp,kvpwe->kwfe', blocks[d].astype(jnp.float32), jac_blocks[...]
    ppermute x12, waiting for transfers between devices: 13.2 us -> 12.3 us  [body(): blocks[d] = lax.ppermute(traces, ('chain', 'group'), pairs)]
  transfers between devices with their start and end apart: 12 -> 12, of which waited for: 3 -> 3; matrix products, arithmetic and copies ran while one was open for 12% -> 19% of each run, Pallas kernels for 0% -> 0%
where the time goes in v8:
time: 53.5 us; the launch traced here: 53 us
  other arithmetic  20.5 us (38%)
  waiting for transfers between devices  12.3 us (23%)
  starting transfers between devices  10.5 us (20%)
  matrix products  6.67 us (12%)
  local copies, waits for them, and re-layouts  2.52 us (5%)
  between operations  0.54 us (1%)
    ppermute x12, waiting for transfers between devices, body(): blocks[d] = lax.ppermute(traces, ('chain', 'group'), pairs)  12.3 us
    ppermute x12, starting transfers between devices, body(): blocks[d] = lax.ppermute(traces, ('chain', 'group'), pairs)  10.5 us
    reduce_sum x2, other arithmetic, body(): jnp.sum(inv_narrow.astype(jnp.float32) * coupling[:, None, :], axis=-1)  6.2 us
    dot_general x12, matrix products, coupling_of(): jnp.einsum('kvfp,kvpwe->kwfe', blocks[d].astype(jnp.float32), jac_blocks[...  5.86 us
    convert_element_type x1, other arithmetic, body(): inv_narrow = lax.optimization_barrier(inv.astype(jnp.bfloat16))  5.67 us
    reduce_sum x1, other arithmetic, body(): base = jnp.sum(inv * rhs_t[:, None, :], axis=-1)  4.14 us
    reduce_sum x1, other arithmetic, body(): out = base - jnp.sum(inv * own_coupling[:, None, :], axis=-1)  4.13 us
  transfers between devices with their start and end apart: 12, of which 3 were waited for; matrix products, arithmetic and copies ran while one was open for 19% of the time, Pallas kernels for 0%

profile of v8, /device:TPU:7, one launch (start us, length us, event | category | flops | bytes accessed | tf_op | source)
XLA Modules:
  0.0 53.0 jit_solution(11137538224569830466)
XLA Ops:
  0.0 0.8 %copy.17 = f32[16,5,64]{2,1,0:T(8,128)S(1)} copy(f32[16,5,64]{2,0,1:T(8,128)} %bitcast.204) | data formatting | bytes 40960 | tf_op jit(solution)/shard_map/transpose | solution.py:34
  0.9 4.1 %fusion.2 = f32[16,320]{1,0:T(8,128)S(1)} fusion(f32[1,16,320,320]{3,2,1,0:T(8,128)} %param.6, f32[16,320]{1,0:T(8,128)S(1)} %mul.46), kind=kLoop, calls=%fused_computation.7 | loop fusion | flops 3271680 | bytes 6594560 | tf_op jit(solution)/shard_map/reduce_sum | solution.py:51
  5.3 0.7 %collective-permute-start.1 = (bf16[3,5,16,16]{3,2,1,0:T(8,128)(2,1)S(1)}, bf16[3,5,16,16]{3,2,1,0:T(8,128)(2,1)S(1)}, u32[]{:S(2)}, u32[]{:S(2)}) collective-permute-start(bf16[3,5,16,16]{3,2,1,0:T(8,128)(2,1)S(1)} %maximum_bitcast_fusion), channel_id=1, source_target_pairs={{0,6},{1,7},{2,4},{3,5},{16,22},{17,23},{18,20},{19,21}} | collective-permute-start | bytes 23048 | tf_op jit(solution)/shard_map/ppermute | solution.py:60
  6.0 0.7 %collective-permute-start.3 = (bf16[3,5,16,16]{3,2,1,0:T(8,128)(2,1)S(1)}, bf16[3,5,16,16]{3,2,1,0:T(8,128)(2,1)S(1)}, u32[]{:S(2)}, u32[]{:S(2)}) collective-permute-start(bf16[3,5,16,16]{3,2,1,0:T(8,128)(2,1)S(1)} %maximum_bitcast_fusion), channel_id=1, source_target_pairs={{0,4},{1,5},{2,6},{3,7},{16,20},{17,21},{18,22},{19,23}} | collective-permute-start | bytes 23048 | tf_op jit(solution)/shard_map/ppermute | solution.py:60
  6.7 0.7 %collective-permute-start.2 = (bf16[3,5,16,16]{3,2,1,0:T(8,128)(2,1)S(1)}, bf16[3,5,16,16]{3,2,1,0:T(8,128)(2,1)S(1)}, u32[]{:S(2)}, u32[]{:S(2)}) collective-permute-start(bf16[3,5,16,16]{3,2,1,0:T(8,128)(2,1)S(1)} %maximum_bitcast_fusion), channel_id=1, source_target_pairs={{0,5},{1,4},{2,7},{3,6},{16,21},{17,20},{18,23},{19,22}} | collective-permute-start | bytes 23048 | tf_op jit(solution)/shard_map/ppermute | solution.py:60
  7.3 0.7 %collective-permute-start = (bf16[3,5,16,16]{3,2,1,0:T(8,128)(2,1)S(1)}, bf16[3,5,16,16]{3,2,1,0:T(8,128)(2,1)S(1)}, u32[]{:S(2)}, u32[]{:S(2)}) collective-permute-start(bf16[3,5,16,16]{3,2,1,0:T(8,128)(2,1)S(1)} %maximum_bitcast_fusion), channel_id=1, source_target_pairs={{0,7},{1,6},{2,5},{3,4},{16,23},{17,22},{18,21},{19,20}} | collective-permute-start | bytes 23048 | tf_op jit(solution)/shard_map/ppermute | solution.py:60
  8.0 5.7 %bitcast_convert_fusion = bf16[16,320,320]{2,1,0:T(8,128)(2,1)} fusion(f32[1,16,320,320]{3,2,1,0:T(8,128)} %param.6), kind=kLoop, calls=%fused_computation.5 | loop fusion | flops 1638400 | bytes 9830400 | tf_op jit(solution)/shard_map/convert_element_type | solution.py:52
  14.1 0.5 convolution_bitcast_fusion.10
  14.6 0.4 convolution_bitcast_fusion.8
  15.0 0.5 convolution_bitcast_fusion.9
  15.6 0.5 fusion.7
  16.5 3.1 %fusion = f32[16,320]{1,0:T(8,128)S(1)} fusion(bf16[16,320,320]{2,1,0:T(8,128)(2,1)} %bitcast_convert_fusion, f32[16,320]{1,0:T(8,128)S(1)} %mul.50), kind=kLoop, calls=%fused_computation.2 | loop fusion | flops 4910080 | bytes 3317760 | tf_op jit(solution)/shard_map/reduce_sum | solution.py:64
  19.9 0.7 %collective-permute-start.5 = (bf16[3,5,16,16]{3,2,1,0:T(8,128)(2,1)S(1)}, bf16[3,5,16,16]{3,2,1,0:T(8,128)(2,1)S(1)}, u32[]{:S(2)}, u32[]{:S(2)}) collective-permute-start(bf16[3,5,16,16]{3,2,1,0:T(8,128)(2,1)S(1)} %maximum_bitcast_fusion.1), channel_id=1, source_target_pairs={{4,10},{5,11},{6,8},{7,9},{20,26},{21,27},{22,24},{23,25}} | collective-permute-start | bytes 23048 | tf_op jit(solution)/shard_map/ppermute | solution.py:60
  20.5 0.7 %collective-permute-start.6 = (bf16[3,5,16,16]{3,2,1,0:T(8,128)(2,1)S(1)}, bf16[3,5,16,16]{3,2,1,0:T(8,128)(2,1)S(1)}, u32[]{:S(2)}, u32[]{:S(2)}) collective-permute-start(bf16[3,5,16,16]{3,2,1,0:T(8,128)(2,1)S(1)} %maximum_bitcast_fusion.1), channel_id=1, source_target_pairs={{4,9},{5,8},{6,11},{7,10},{20,25},{21,24},{22,27},{23,26}} | collective-permute-start | bytes 23048 | tf_op jit(solution)/shard_map/ppermute | solution.py:60
  21.2 0.7 %collective-permute-start.7 = (bf16[3,5,16,16]{3,2,1,0:T(8,128)(2,1)S(1)}, bf16[3,5,16,16]{3,2,1,0:T(8,128)(2,1)S(1)}, u32[]{:S(2)}, u32[]{:S(2)}) collective-permute-start(bf16[3,5,16,16]{3,2,1,0:T(8,128)(2,1)S(1)} %maximum_bitcast_fusion.1), channel_id=1, source_target_pairs={{4,8},{5,9},{6,10},{7,11},{20,24},{21,25},{22,26},{23,27}} | collective-permute-start | bytes 23048 | tf_op jit(solution)/shard_map/ppermute | solution.py:60
  21.9 0.7 %collective-permute-start.4 = (bf16[3,5,16,16]{3,2,1,0:T(8,128)(2,1)S(1)}, bf16[3,5,16,16]{3,2,1,0:T(8,128)(2,1)S(1)}, u32[]{:S(2)}, u32[]{:S(2)}) collective-permute-start(bf16[3,5,16,16]{3,2,1,0:T(8,128)(2,1)S(1)} %maximum_bitcast_fusion.1), channel_id=1, source_target_pairs={{4,11},{5,10},{6,9},{7,8},{20,27},{21,26},{22,25},{23,24}} | collective-permute-start | bytes 23048 | tf_op jit(solution)/shard_map/ppermute | solution.py:60
  22.6 0.5 convolution_bitcast_fusion.6
  23.1 0.5 convolution_bitcast_fusion.5
  24.1 0.5 fusion.11
  25.0 3.1 %fusion.1 = f32[16,320]{1,0:T(8,128)S(1)} fusion(bf16[16,320,320]{2,1,0:T(8,128)(2,1)} %bitcast_convert_fusion, f32[16,320]{1,0:T(8,128)S(1)} %mul.53), kind=kLoop, calls=%fused_computation.3 | loop fusion | flops 4910080 | bytes 3317760 | tf_op jit(solution)/shard_map/reduce_sum | solution.py:64
  28.3 1.3 %collective-permute-start.9 = (bf16[3,5,16,16]{3,2,1,0:T(8,128)(2,1)S(1)}, bf16[3,5,16,16]{3,2,1,0:T(8,128)(2,1)S(1)}, u32[]{:S(2)}, u32[]{:S(2)}) collective-permute-start(bf16[3,5,16,16]{3,2,1,0:T(8,128)(2,1)S(1)} %maximum_bitcast_fusion.2), channel_id=1, source_target_pairs={{8,14},{9,15},{10,12},{11,13},{24,30},{25,31},{26,28},{27,29}} | collective-permute-start | bytes 23048 | tf_op jit(solution)/shard_map/ppermute | solution.py:60
  29.6 1.3 %collective-permute-start.10 = (bf16[3,5,16,16]{3,2,1,0:T(8,128)(2,1)S(1)}, bf16[3,5,16,16]{3,2,1,0:T(8,128)(2,1)S(1)}, u32[]{:S(2)}, u32[]{:S(2)}) collective-permute-start(bf16[3,5,16,16]{3,2,1,0:T(8,128)(2,1)S(1)} %maximum_bitcast_fusion.2), channel_id=1, source_target_pairs={{8,13},{9,12},{10,15},{11,14},{24,29},{25,28},{26,31},{27,30}} | collective-permute-start | bytes 23048 | tf_op jit(solution)/shard_map/ppermute | solution.py:60
  30.9 1.3 %collective-permute-start.11 = (bf16[3,5,16,16]{3,2,1,0:T(8,128)(2,1)S(1)}, bf16[3,5,16,16]{3,2,1,0:T(8,128)(2,1)S(1)}, u32[]{:S(2)}, u32[]{:S(2)}) collective-permute-start(bf16[3,5,16,16]{3,2,1,0:T(8,128)(2,1)S(1)} %maximum_bitcast_fusion.2), channel_id=1, source_target_pairs={{8,12},{9,13},{10,14},{11,15},{24,28},{25,29},{26,30},{27,31}} | collective-permute-start | bytes 23048 | tf_op jit(solution)/shard_map/ppermute | solution.py:60
  32.2 1.3 %collective-permute-start.8 = (bf16[3,5,16,16]{3,2,1,0:T(8,128)(2,1)S(1)}, bf16[3,5,16,16]{3,2,1,0:T(8,128)(2,1)S(1)}, u32[]{:S(2)}, u32[]{:S(2)}) collective-permute-start(bf16[3,5,16,16]{3,2,1,0:T(8,128)(2,1)S(1)} %maximum_bitcast_fusion.2), channel_id=1, source_target_pairs={{8,15},{9,14},{10,13},{11,12},{24,31},{25,30},{26,29},{27,28}} | collective-permute-start | bytes 23048 | tf_op jit(solution)/shard_map/ppermute | solution.py:60
  33.5 8.0 %collective-permute-done.9 = bf16[3,5,16,16]{3,2,1,0:T(8,128)(2,1)S(1)} collective-permute-done((bf16[3,5,16,16]{3,2,1,0:T(8,128)(2,1)S(1)}, bf16[3,5,16,16]{3,2,1,0:T(8,128)(2,1)S(1)}, u32[]{:S(2)}, u32[]{:S(2)}) %collective-permute-start.9) | collective-permute-done | bytes 7712 | tf_op jit(solution)/shard_map/ppermute | solution.py:60
  41.5 0.5 convolution_bitcast_fusion.2
  42.1 0.6 %collective-permute-done.10 = bf16[3,5,16,16]{3,2,1,0:T(8,128)(2,1)S(1)} collective-permute-done((bf16[3,5,16,16]{3,2,1,0:T(8,128)(2,1)S(1)}, bf16[3,5,16,16]{3,2,1,0:T(8,128)(2,1)S(1)}, u32[]{:S(2)}, u32[]{:S(2)}) %collective-permute-start.10) | collective-permute-done | bytes 7712 | tf_op jit(solution)/shard_map/ppermute | solution.py:60
  42.6 0.5 convolution_bitcast_fusion.1
  43.6 3.7 %collective-permute-done.8 = bf16[3,5,16,16]{3,2,1,0:T(8,128)(2,1)S(1)} collective-permute-done((bf16[3,5,16,16]{3,2,1,0:T(8,128)(2,1)S(1)}, bf16[3,5,16,16]{3,2,1,0:T(8,128)(2,1)S(1)}, u32[]{:S(2)}, u32[]{:S(2)}) %collective-permute-start.8) | collective-permute-done | bytes 7712 | tf_op jit(solution)/shard_map/ppermute | solution.py:60
  47.3 0.5 fusion.15
  48.2 4.1 %fusion.3 = f32[16,320]{1,0:T(8,128)S(1)} fusion(f32[1,16,320,320]{3,2,1,0:T(8,128)} %param.6, f32[16,320]{1,0:T(8,128)S(1)} %select_select_fusion), kind=kLoop, calls=%fused_computation.8 | loop fusion | flops 3271680 | bytes 6594560 | tf_op jit(solution)/shard_map/reduce_sum | solution.py:66
  52.4 0.6 %copy.26 = f32[1,5,64,16]{2,3,1,0:T(8,128)} copy(f32[1,5,64,16]{2,1,3,0:T(8,128)S(1)} %bitcast.193) | data formatting | bytes 40960 | tf_op jit(solution)/shard_map/broadcast_in_dim | solution.py:67
  (56 shorter events, 3.2 us)
Async XLA Ops:
  0.0 16.1 %copy-start = (f32[3,64,16]{1,2,0:T(8,128)S(1)}, f32[3,64,16]{1,2,0:T(8,128)}, u32[]{:S(2)}) copy-start(f32[3,64,16]{1,2,0:T(8,128)} %param.9) | copy-start | bytes 36868
  5.0 8.7 %copy-start.2 = (s32[1,3,16]{2,0,1:T(1,128)S(1)}, s32[1,3,16]{2,0,1:T(1,128)}, u32[]{:S(2)}) copy-start(s32[1,3,16]{2,0,1:T(1,128)} %param.8) | copy-start | bytes 580
  5.0 8.8 %copy-start.1 = (f32[1,3,5,5,16]{4,0,3,2,1:T(1,128)S(1)}, f32[1,3,5,5,16]{4,0,3,2,1:T(1,128)}, u32[]{:S(2)}) copy-start(f32[1,3,5,5,16]{4,0,3,2,1:T(1,128)} %param.7) | copy-start | bytes 14404
  5.3 8.7 %collective-permute-start.1 = (bf16[3,5,16,16]{3,2,1,0:T(8,128)(2,1)S(1)}, bf16[3,5,16,16]{3,2,1,0:T(8,128)(2,1)S(1)}, u32[]{:S(2)}, u32[]{:S(2)}) collective-permute-start(bf16[3,5,16,16]{3,2,1,0:T(8,128)(2,1)S(1)} %maximum_bitcast_fusion), channel_id=1, source_target_pairs={{0,6},{1,7},{2,4},{3,5},{16,22},{17,23},{18,20},{19,21}} | collective-permute-start | bytes 23048 | tf_op jit(solution)/shard_map/ppermute | solution.py:60
  6.0 8.6 %collective-permute-start.3 = (bf16[3,5,16,16]{3,2,1,0:T(8,128)(2,1)S(1)}, bf16[3,5,16,16]{3,2,1,0:T(8,128)(2,1)S(1)}, u32[]{:S(2)}, u32[]{:S(2)}) collective-permute-start(bf16[3,5,16,16]{3,2,1,0:T(8,128)(2,1)S(1)} %maximum_bitcast_fusion), channel_id=1, source_target_pairs={{0,4},{1,5},{2,6},{3,7},{16,20},{17,21},{18,22},{19,23}} | collective-permute-start | bytes 23048 | tf_op jit(solution)/shard_map/ppermute | solution.py:60
  6.7 8.4 %collective-permute-start.2 = (bf16[3,5,16,16]{3,2,1,0:T(8,128)(2,1)S(1)}, bf16[3,5,16,16]{3,2,1,0:T(8,128)(2,1)S(1)}, u32[]{:S(2)}, u32[]{:S(2)}) collective-permute-start(bf16[3,5,16,16]{3,2,1,0:T(8,128)(2,1)S(1)} %maximum_bitcast_fusion), channel_id=1, source_target_pairs={{0,5},{1,4},{2,7},{3,6},{16,21},{17,20},{18,23},{19,22}} | collective-permute-start | bytes 23048 | tf_op jit(solution)/shard_map/ppermute | solution.py:60
  7.3 8.2 %collective-permute-start = (bf16[3,5,16,16]{3,2,1,0:T(8,128)(2,1)S(1)}, bf16[3,5,16,16]{3,2,1,0:T(8,128)(2,1)S(1)}, u32[]{:S(2)}, u32[]{:S(2)}) collective-permute-start(bf16[3,5,16,16]{3,2,1,0:T(8,128)(2,1)S(1)} %maximum_bitcast_fusion), channel_id=1, source_target_pairs={{0,7},{1,6},{2,5},{3,4},{16,23},{17,22},{18,21},{19,20}} | collective-permute-start | bytes 23048 | tf_op jit(solution)/shard_map/ppermute | solution.py:60
  19.9 2.7 %collective-permute-start.5 = (bf16[3,5,16,16]{3,2,1,0:T(8,128)(2,1)S(1)}, bf16[3,5,16,16]{3,2,1,0:T(8,128)(2,1)S(1)}, u32[]{:S(2)}, u32[]{:S(2)}) collective-permute-start(bf16[3,5,16,16]{3,2,1,0:T(8,128)(2,1)S(1)} %maximum_bitcast_fusion.1), channel_id=1, source_target_pairs={{4,10},{5,11},{6,8},{7,9},{20,26},{21,27},{22,24},{23,25}} | collective-permute-start | bytes 23048 | tf_op jit(solution)/shard_map/ppermute | solution.py:60
  20.5 2.5 %collective-permute-start.6 = (bf16[3,5,16,16]{3,2,1,0:T(8,128)(2,1)S(1)}, bf16[3,5,16,16]{3,2,1,0:T(8,128)(2,1)S(1)}, u32[]{:S(2)}, u32[]{:S(2)}) collective-permute-start(bf16[3,5,16,16]{3,2,1,0:T(8,128)(2,1)S(1)} %maximum_bitcast_fusion.1), channel_id=1, source_target_pairs={{4,9},{5,8},{6,11},{7,10},{20,25},{21,24},{22,27},{23,26}} | collective-permute-start | bytes 23048 | tf_op jit(solution)/shard_map/ppermute | solution.py:60
  21.2 2.4 %collective-permute-start.7 = (bf16[3,5,16,16]{3,2,1,0:T(8,128)(2,1)S(1)}, bf16[3,5,16,16]{3,2,1,0:T(8,128)(2,1)S(1)}, u32[]{:S(2)}, u32[]{:S(2)}) collective-permute-start(bf16[3,5,16,16]{3,2,1,0:T(8,128)(2,1)S(1)} %maximum_bitcast_fusion.1), channel_id=1, source_target_pairs={{4,8},{5,9},{6,10},{7,11},{20,24},{21,25},{22,26},{23,27}} | collective-permute-start | bytes 23048 | tf_op jit(solution)/shard_map/ppermute | solution.py:60
  21.9 2.2 %collective-permute-start.4 = (bf16[3,5,16,16]{3,2,1,0:T(8,128)(2,1)S(1)}, bf16[3,5,16,16]{3,2,1,0:T(8,128)(2,1)S(1)}, u32[]{:S(2)}, u32[]{:S(2)}) collective-permute-start(bf16[3,5,16,16]{3,2,1,0:T(8,128)(2,1)S(1)} %maximum_bitcast_fusion.1), channel_id=1, source_target_pairs={{4,11},{5,10},{6,9},{7,8},{20,27},{21,26},{22,25},{23,24}} | collective-permute-start | bytes 23048 | tf_op jit(solution)/shard_map/ppermute | solution.py:60
  28.3 13.2 %collective-permute-start.9 = (bf16[3,5,16,16]{3,2,1,0:T(8,128)(2,1)S(1)}, bf16[3,5,16,16]{3,2,1,0:T(8,128)(2,1)S(1)}, u32[]{:S(2)}, u32[]{:S(2)}) collective-permute-start(bf16[3,5,16,16]{3,2,1,0:T(8,128)(2,1)S(1)} %maximum_bitcast_fusion.2), channel_id=1, source_target_pairs={{8,14},{9,15},{10,12},{11,13},{24,30},{25,31},{26,28},{27,29}} | collective-permute-start | bytes 23048 | tf_op jit(solution)/shard_map/ppermute | solution.py:60
  29.6 13.0 %collective-permute-start.10 = (bf16[3,5,16,16]{3,2,1,0:T(8,128)(2,1)S(1)}, bf16[3,5,16,16]{3,2,1,0:T(8,128)(2,1)S(1)}, u32[]{:S(2)}, u32[]{:S(2)}) collective-permute-start(bf16[3,5,16,16]{3,2,1,0:T(8,128)(2,1)S(1)} %maximum_bitcast_fusion.2), channel_id=1, source_target_pairs={{8,13},{9,12},{10,15},{11,14},{24,29},{25,28},{26,31},{27,30}} | collective-permute-start | bytes 23048 | tf_op jit(solution)/shard_map/ppermute | solution.py:60
  30.9 12.2 %collective-permute-start.11 = (bf16[3,5,16,16]{3,2,1,0:T(8,128)(2,1)S(1)}, bf16[3,5,16,16]{3,2,1,0:T(8,128)(2,1)S(1)}, u32[]{:S(2)}, u32[]{:S(2)}) collective-permute-start(bf16[3,5,16,16]{3,2,1,0:T(8,128)(2,1)S(1)} %maximum_bitcast_fusion.2), channel_id=1, source_target_pairs={{8,12},{9,13},{10,14},{11,15},{24,28},{25,29},{26,30},{27,31}} | collective-permute-start | bytes 23048 | tf_op jit(solution)/shard_map/ppermute | solution.py:60
  32.2 15.0 %collective-permute-start.8 = (bf16[3,5,16,16]{3,2,1,0:T(8,128)(2,1)S(1)}, bf16[3,5,16,16]{3,2,1,0:T(8,128)(2,1)S(1)}, u32[]{:S(2)}, u32[]{:S(2)}) collective-permute-start(bf16[3,5,16,16]{3,2,1,0:T(8,128)(2,1)S(1)} %maximum_bitcast_fusion.2), channel_id=1, source_target_pairs={{8,15},{9,14},{10,13},{11,12},{24,31},{25,30},{26,29},{27,28}} | collective-permute-start | bytes 23048 | tf_op jit(solution)/shard_map/ppermute | solution.py:60

commit v9 on v7

--- a/solution.py
+++ b/solution.py
@@ -40,13 +40,13 @@
     picked_jac = jnp.einsum("kpe,kwve->kvpwe", onehot, jac)
 
     def coupling_of(traces_in):
-        mixed = jnp.einsum("kvfp,kvpwe->kwfe", traces_in.astype(jnp.float32), picked_jac, precision=HIGH)
+        mixed = jnp.einsum("kvfp,kvpwe->kwfe", traces_in, picked_jac, precision=HIGH)
         coupling = jnp.einsum("kwfe,kif->ewi", mixed, lift, precision=HIGH)
         return coupling.reshape(local, BLOCK)
 
     base = jnp.sum(inv * rhs_t[:, None, :], axis=-1)
     inv_narrow = lax.optimization_barrier(inv.astype(jnp.bfloat16))
-    traces = face_traces(base).astype(jnp.bfloat16)
+    traces = face_traces(base)
     own_coupling = jnp.zeros((local, BLOCK), jnp.float32)
     for turn in range(1, chains):
         blocks = [None] * groups
@@ -58,8 +58,8 @@
         own_coupling = jnp.where(c == turn, coupling, own_coupling)
         if turn + 1 < chains:
             approx = base - jnp.sum(inv_narrow.astype(jnp.float32) * coupling[:, None, :], axis=-1)
-            traces = face_traces(approx).astype(jnp.bfloat16)
-    out = base - jnp.sum(inv * own_coupling[:, None, :], axis=-1)
+            traces = face_traces(approx)
+    out = base - jnp.sum(inv_narrow.astype(jnp.float32) * own_coupling[:, None, :], axis=-1)
     return jnp.transpose(out.reshape(local, VARS, NODES), (1, 2, 0))[None]
 
 

time: 50 us -> 54.4 us (1.088)
  waiting for transfers between devices: 13.2 us -> 17.8 us
  other arithmetic: 20.3 us -> 19.4 us
  matrix products: 2.53 us -> 3.33 us
    ppermute x12, waiting for transfers between devices: 13.2 us -> 17.8 us  [body(): blocks[d] = lax.ppermute(traces, ('chain', 'group'), pairs)]
    reduce_sum x1, other arithmetic: 4.13 us -> 3.11 us  [body(): jnp.sum(inv_narrow.astype(jnp.float32) * own_coupling[:, None, :], axis=-1)]
    dot_general x3, matrix products: 1.71 us -> 2.52 us  [coupling_of(): jnp.einsum('kvfp,kvpwe->kwfe', traces_in, picked_jac, precision=HIGH)]
  transfers between devices with their start and end apart: 12 -> 12, of which waited for: 3 -> 2; matrix products, arithmetic and copies ran while one was open for 12% -> 11% of each run, Pallas kernels for 0% -> 0%
where the time goes in v9:
time: 54.4 us; the launch traced here: 53.8 us
  other arithmetic  19.4 us (36%)
  waiting for transfers between devices  17.8 us (33%)
  starting transfers between devices  10.5 us (19%)
  matrix products  3.33 us (6%)
  local copies, waits for them, and re-layouts  2.4 us (4%)
    ppermute x12, waiting for transfers between devices, body(): blocks[d] = lax.ppermute(traces, ('chain', 'group'), pairs)  17.8 us
    ppermute x12, starting transfers between devices, body(): blocks[d] = lax.ppermute(traces, ('chain', 'group'), pairs)  10.5 us
    reduce_sum x2, other arithmetic, body(): jnp.sum(inv_narrow.astype(jnp.float32) * coupling[:, None, :], axis=-1)  6.2 us
    convert_element_type x1, other arithmetic, body(): inv_narrow = lax.optimization_barrier(inv.astype(jnp.bfloat16))  5.67 us
    reduce_sum x1, other arithmetic, body(): base = jnp.sum(inv * rhs_t[:, None, :], axis=-1)  4.14 us
    reduce_sum x1, other arithmetic, body(): jnp.sum(inv_narrow.astype(jnp.float32) * own_coupling[:, None, :], axis=-1)  3.11 us
    dot_general x3, matrix products, coupling_of(): jnp.einsum('kvfp,kvpwe->kwfe', traces_in, picked_jac, precision=HIGH)  2.52 us
  transfers between devices with their start and end apart: 12, of which 2 were waited for; matrix products, arithmetic and copies ran while one was open for 11% of the time, Pallas kernels for 0%

profile of v9, /device:TPU:7, one launch (start us, length us, event | category | flops | bytes accessed | tf_op | source)
XLA Modules:
  0.0 53.8 jit_solution(10552382287079567050)
XLA Ops:
  0.0 0.8 %copy.17 = f32[16,5,64]{2,1,0:T(8,128)S(1)} copy(f32[16,5,64]{2,0,1:T(8,128)} %bitcast.126) | data formatting | bytes 40960 | tf_op jit(solution)/shard_map/transpose | solution.py:34
  0.9 4.1 %fusion.3 = f32[16,320]{1,0:T(8,128)S(1)} fusion(f32[1,16,320,320]{3,2,1,0:T(8,128)} %param.6, f32[16,320]{1,0:T(8,128)S(1)} %mul.46), kind=kLoop, calls=%fused_computation.8 | loop fusion | flops 3271680 | bytes 6594560 | tf_op jit(solution)/shard_map/reduce_sum | solution.py:47
  5.1 0.1 copy.20
  5.3 0.7 %collective-permute-start = (f32[3,5,16,16]{3,2,1,0:T(8,128)S(1)}, f32[3,5,16,16]{3,2,1,0:T(8,128)S(1)}, u32[]{:S(2)}, u32[]{:S(2)}) collective-permute-start(f32[3,5,16,16]{3,2,1,0:T(8,128)S(1)} %maximum_bitcast_fusion), channel_id=1, source_target_pairs={{0,4},{1,5},{2,6},{3,7},{16,20},{17,21},{18,22},{19,23}} | collective-permute-start | bytes 46088 | tf_op jit(solution)/shard_map/ppermute | solution.py:56
  5.9 0.7 %collective-permute-start.1 = (f32[3,5,16,16]{3,2,1,0:T(8,128)S(1)}, f32[3,5,16,16]{3,2,1,0:T(8,128)S(1)}, u32[]{:S(2)}, u32[]{:S(2)}) collective-permute-start(f32[3,5,16,16]{3,2,1,0:T(8,128)S(1)} %maximum_bitcast_fusion), channel_id=1, source_target_pairs={{0,5},{1,4},{2,7},{3,6},{16,21},{17,20},{18,23},{19,22}} | collective-permute-start | bytes 46088 | tf_op jit(solution)/shard_map/ppermute | solution.py:56
  6.6 0.7 %collective-permute-start.2 = (f32[3,5,16,16]{3,2,1,0:T(8,128)S(1)}, f32[3,5,16,16]{3,2,1,0:T(8,128)S(1)}, u32[]{:S(2)}, u32[]{:S(2)}) collective-permute-start(f32[3,5,16,16]{3,2,1,0:T(8,128)S(1)} %maximum_bitcast_fusion), channel_id=1, source_target_pairs={{0,6},{1,7},{2,4},{3,5},{16,22},{17,23},{18,20},{19,21}} | collective-permute-start | bytes 46088 | tf_op jit(solution)/shard_map/ppermute | solution.py:56
  7.3 0.7 %collective-permute-start.3 = (f32[3,5,16,16]{3,2,1,0:T(8,128)S(1)}, f32[3,5,16,16]{3,2,1,0:T(8,128)S(1)}, u32[]{:S(2)}, u32[]{:S(2)}) collective-permute-start(f32[3,5,16,16]{3,2,1,0:T(8,128)S(1)} %maximum_bitcast_fusion), channel_id=1, source_target_pairs={{0,7},{1,6},{2,5},{3,4},{16,23},{17,22},{18,21},{19,20}} | collective-permute-start | bytes 46088 | tf_op jit(solution)/shard_map/ppermute | solution.py:56
  8.0 5.7 %bitcast_convert_fusion = bf16[16,320,320]{2,1,0:T(8,128)(2,1)} fusion(f32[1,16,320,320]{3,2,1,0:T(8,128)} %param.6), kind=kLoop, calls=%fused_computation.6 | loop fusion | flops 1638400 | bytes 9830400 | tf_op jit(solution)/shard_map/convert_element_type | solution.py:48
  13.7 0.1 convert_bitcast_fusion
  13.8 0.8 %convolution_bitcast_fusion.2 = f32[3,5,16,16]{2,3,0,1:T(8,128)S(1)} fusion(f32[3,16,5,5]{1,3,0,2:T(8,128)S(1)} %copy.19, f32[3,16,64]{2,1,0:T(8,128)S(1)} %convert_bitcast_fusion, f32[3,5,16,16]{3,2,1,0:T(8,128)S(1)} %collective-permute-done.3, f32[3,5,16,16]{3,2,1,0:T(8,128)S(1)} %collective-permute-done.2, ...), kind=kOutput, calls=%fused_computation.11 | convolution fusion | flops 14868480 | bytes 93888 | tf_op jit(solution)/shard_map/kvfp,kvpwe->kwfe/dot_general | solution.py:43
  14.7 0.3 convolution_bitcast_fusion.5
  15.1 3.1 %fusion = f32[16,320]{1,0:T(8,128)S(1)} fusion(bf16[16,320,320]{2,1,0:T(8,128)(2,1)} %bitcast_convert_fusion, f32[16,320]{1,0:T(8,128)S(1)} %mul.50), kind=kLoop, calls=%fused_computation.3 | loop fusion | flops 4910080 | bytes 3317760 | tf_op jit(solution)/shard_map/reduce_sum | solution.py:60
  18.2 0.1 copy.22
  18.4 0.7 %collective-permute-start.4 = (f32[3,5,16,16]{3,2,1,0:T(8,128)S(1)}, f32[3,5,16,16]{3,2,1,0:T(8,128)S(1)}, u32[]{:S(2)}, u32[]{:S(2)}) collective-permute-start(f32[3,5,16,16]{3,2,1,0:T(8,128)S(1)} %maximum_bitcast_fusion.3), channel_id=1, source_target_pairs={{4,8},{5,9},{6,10},{7,11},{20,24},{21,25},{22,26},{23,27}} | collective-permute-start | bytes 46088 | tf_op jit(solution)/shard_map/ppermute | solution.py:56
  19.1 0.7 %collective-permute-start.5 = (f32[3,5,16,16]{3,2,1,0:T(8,128)S(1)}, f32[3,5,16,16]{3,2,1,0:T(8,128)S(1)}, u32[]{:S(2)}, u32[]{:S(2)}) collective-permute-start(f32[3,5,16,16]{3,2,1,0:T(8,128)S(1)} %maximum_bitcast_fusion.3), channel_id=1, source_target_pairs={{4,9},{5,8},{6,11},{7,10},{20,25},{21,24},{22,27},{23,26}} | collective-permute-start | bytes 46088 | tf_op jit(solution)/shard_map/ppermute | solution.py:56
  19.8 0.7 %collective-permute-start.6 = (f32[3,5,16,16]{3,2,1,0:T(8,128)S(1)}, f32[3,5,16,16]{3,2,1,0:T(8,128)S(1)}, u32[]{:S(2)}, u32[]{:S(2)}) collective-permute-start(f32[3,5,16,16]{3,2,1,0:T(8,128)S(1)} %maximum_bitcast_fusion.3), channel_id=1, source_target_pairs={{4,10},{5,11},{6,8},{7,9},{20,26},{21,27},{22,24},{23,25}} | collective-permute-start | bytes 46088 | tf_op jit(solution)/shard_map/ppermute | solution.py:56
  20.5 0.7 %collective-permute-start.7 = (f32[3,5,16,16]{3,2,1,0:T(8,128)S(1)}, f32[3,5,16,16]{3,2,1,0:T(8,128)S(1)}, u32[]{:S(2)}, u32[]{:S(2)}) collective-permute-start(f32[3,5,16,16]{3,2,1,0:T(8,128)S(1)} %maximum_bitcast_fusion.3), channel_id=1, source_target_pairs={{4,11},{5,10},{6,9},{7,8},{20,27},{21,26},{22,25},{23,24}} | collective-permute-start | bytes 46088 | tf_op jit(solution)/shard_map/ppermute | solution.py:56
  21.2 0.8 %convolution_bitcast_fusion.1 = f32[3,5,16,16]{2,3,0,1:T(8,128)S(1)} fusion(f32[3,16,5,5]{1,3,0,2:T(8,128)S(1)} %copy.19, f32[3,16,64]{2,1,0:T(8,128)S(1)} %convert_bitcast_fusion, f32[3,5,16,16]{3,2,1,0:T(8,128)S(1)} %collective-permute-done.7, f32[3,5,16,16]{3,2,1,0:T(8,128)S(1)} %collective-permute-done.6, ...), kind=kOutput, calls=%fused_computation.10 | convolution fusion | flops 14868480 | bytes 93888 | tf_op jit(solution)/shard_map/kvfp,kvpwe->kwfe/dot_general | solution.py:43
  22.0 0.3 convolution_bitcast_fusion.4
  22.4 3.1 %fusion.1 = f32[16,320]{1,0:T(8,128)S(1)} fusion(bf16[16,320,320]{2,1,0:T(8,128)(2,1)} %bitcast_convert_fusion, f32[16,320]{1,0:T(8,128)S(1)} %mul.53), kind=kLoop, calls=%fused_computation.4 | loop fusion | flops 4910080 | bytes 3317760 | tf_op jit(solution)/shard_map/reduce_sum | solution.py:60
  25.5 0.1 copy.24
  25.8 1.3 %collective-permute-start.10 = (f32[3,5,16,16]{3,2,1,0:T(8,128)S(1)}, f32[3,5,16,16]{3,2,1,0:T(8,128)S(1)}, u32[]{:S(2)}, u32[]{:S(2)}) collective-permute-start(f32[3,5,16,16]{3,2,1,0:T(8,128)S(1)} %maximum_bitcast_fusion.6), channel_id=1, source_target_pairs={{8,14},{9,15},{10,12},{11,13},{24,30},{25,31},{26,28},{27,29}} | collective-permute-start | bytes 46088 | tf_op jit(solution)/shard_map/ppermute | solution.py:56
  27.1 1.3 %collective-permute-start.11 = (f32[3,5,16,16]{3,2,1,0:T(8,128)S(1)}, f32[3,5,16,16]{3,2,1,0:T(8,128)S(1)}, u32[]{:S(2)}, u32[]{:S(2)}) collective-permute-start(f32[3,5,16,16]{3,2,1,0:T(8,128)S(1)} %maximum_bitcast_fusion.6), channel_id=1, source_target_pairs={{8,15},{9,14},{10,13},{11,12},{24,31},{25,30},{26,29},{27,28}} | collective-permute-start | bytes 46088 | tf_op jit(solution)/shard_map/ppermute | solution.py:56
  28.4 1.3 %collective-permute-start.8 = (f32[3,5,16,16]{3,2,1,0:T(8,128)S(1)}, f32[3,5,16,16]{3,2,1,0:T(8,128)S(1)}, u32[]{:S(2)}, u32[]{:S(2)}) collective-permute-start(f32[3,5,16,16]{3,2,1,0:T(8,128)S(1)} %maximum_bitcast_fusion.6), channel_id=1, source_target_pairs={{8,12},{9,13},{10,14},{11,15},{24,28},{25,29},{26,30},{27,31}} | collective-permute-start | bytes 46088 | tf_op jit(solution)/shard_map/ppermute | solution.py:56
  29.7 1.3 %collective-permute-start.9 = (f32[3,5,16,16]{3,2,1,0:T(8,128)S(1)}, f32[3,5,16,16]{3,2,1,0:T(8,128)S(1)}, u32[]{:S(2)}, u32[]{:S(2)}) collective-permute-start(f32[3,5,16,16]{3,2,1,0:T(8,128)S(1)} %maximum_bitcast_fusion.6), channel_id=1, source_target_pairs={{8,13},{9,12},{10,15},{11,14},{24,29},{25,28},{26,31},{27,30}} | collective-permute-start | bytes 46088 | tf_op jit(solution)/shard_map/ppermute | solution.py:56
  31.0 16.1 %collective-permute-done.10 = f32[3,5,16,16]{3,2,1,0:T(8,128)S(1)} collective-permute-done((f32[3,5,16,16]{3,2,1,0:T(8,128)S(1)}, f32[3,5,16,16]{3,2,1,0:T(8,128)S(1)}, u32[]{:S(2)}, u32[]{:S(2)}) %collective-permute-start.10) | collective-permute-done | bytes 15392 | tf_op jit(solution)/shard_map/ppermute | solution.py:56
  47.1 1.7 %collective-permute-done.9 = f32[3,5,16,16]{3,2,1,0:T(8,128)S(1)} collective-permute-done((f32[3,5,16,16]{3,2,1,0:T(8,128)S(1)}, f32[3,5,16,16]{3,2,1,0:T(8,128)S(1)}, u32[]{:S(2)}, u32[]{:S(2)}) %collective-permute-start.9) | collective-permute-done | bytes 15392 | tf_op jit(solution)/shard_map/ppermute | solution.py:56
  48.8 0.8 %convolution_bitcast_fusion = f32[3,5,16,16]{2,3,0,1:T(8,128)S(1)} fusion(f32[3,16,5,5]{1,3,0,2:T(8,128)S(1)} %copy.19, f32[3,16,64]{2,1,0:T(8,128)S(1)} %convert_bitcast_fusion, f32[3,5,16,16]{3,2,1,0:T(8,128)S(1)} %collective-permute-done.11, f32[3,5,16,16]{3,2,1,0:T(8,128)S(1)} %collective-permute-done.10, ...), kind=kOutput, calls=%fused_computation.9 | convolution fusion | flops 14868480 | bytes 93888 | tf_op jit(solution)/shard_map/kvfp,kvpwe->kwfe/dot_general | solution.py:43
  49.6 0.3 convolution_bitcast_fusion.3
  50.0 3.1 %fusion.2 = f32[16,320]{1,0:T(8,128)S(1)} fusion(bf16[16,320,320]{2,1,0:T(8,128)(2,1)} %bitcast_convert_fusion, f32[16,320]{1,0:T(8,128)S(1)} %select_select_fusion), kind=kLoop, calls=%fused_computation.5 | loop fusion | flops 4910080 | bytes 3317760 | tf_op jit(solution)/shard_map/reduce_sum | solution.py:62
  53.1 0.1 sub.25
  53.2 0.6 %copy.26 = f32[1,5,64,16]{2,3,1,0:T(8,128)} copy(f32[1,5,64,16]{2,1,3,0:T(8,128)S(1)} %bitcast.115) | data formatting | bytes 40960 | tf_op jit(solution)/shard_map/broadcast_in_dim | solution.py:63
  (42 shorter events, 0.8 us)
Async XLA Ops:
  0.0 14.7 %copy-start = (f32[3,64,16]{1,2,0:T(8,128)S(1)}, f32[3,64,16]{1,2,0:T(8,128)}, u32[]{:S(2)}) copy-start(f32[3,64,16]{1,2,0:T(8,128)} %param.9) | copy-start | bytes 36868
  5.0 8.6 %copy-start.2 = (s32[1,3,16]{2,0,1:T(1,128)S(1)}, s32[1,3,16]{2,0,1:T(1,128)}, u32[]{:S(2)}) copy-start(s32[1,3,16]{2,0,1:T(1,128)} %param.8) | copy-start | bytes 580
  5.0 8.7 %copy-start.1 = (f32[1,3,5,5,16]{4,0,3,2,1:T(1,128)S(1)}, f32[1,3,5,5,16]{4,0,3,2,1:T(1,128)}, u32[]{:S(2)}) copy-start(f32[1,3,5,5,16]{4,0,3,2,1:T(1,128)} %param.7) | copy-start | bytes 14404
  5.3 8.5 %collective-permute-start = (f32[3,5,16,16]{3,2,1,0:T(8,128)S(1)}, f32[3,5,16,16]{3,2,1,0:T(8,128)S(1)}, u32[]{:S(2)}, u32[]{:S(2)}) collective-permute-start(f32[3,5,16,16]{3,2,1,0:T(8,128)S(1)} %maximum_bitcast_fusion), channel_id=1, source_target_pairs={{0,4},{1,5},{2,6},{3,7},{16,20},{17,21},{18,22},{19,23}} | collective-permute-start | bytes 46088 | tf_op jit(solution)/shard_map/ppermute | solution.py:56
  5.9 7.9 %collective-permute-start.1 = (f32[3,5,16,16]{3,2,1,0:T(8,128)S(1)}, f32[3,5,16,16]{3,2,1,0:T(8,128)S(1)}, u32[]{:S(2)}, u32[]{:S(2)}) collective-permute-start(f32[3,5,16,16]{3,2,1,0:T(8,128)S(1)} %maximum_bitcast_fusion), channel_id=1, source_target_pairs={{0,5},{1,4},{2,7},{3,6},{16,21},{17,20},{18,23},{19,22}} | collective-permute-start | bytes 46088 | tf_op jit(solution)/shard_map/ppermute | solution.py:56
  6.6 7.2 %collective-permute-start.2 = (f32[3,5,16,16]{3,2,1,0:T(8,128)S(1)}, f32[3,5,16,16]{3,2,1,0:T(8,128)S(1)}, u32[]{:S(2)}, u32[]{:S(2)}) collective-permute-start(f32[3,5,16,16]{3,2,1,0:T(8,128)S(1)} %maximum_bitcast_fusion), channel_id=1, source_target_pairs={{0,6},{1,7},{2,4},{3,5},{16,22},{17,23},{18,20},{19,21}} | collective-permute-start | bytes 46088 | tf_op jit(solution)/shard_map/ppermute | solution.py:56
  7.3 6.5 %collective-permute-start.3 = (f32[3,5,16,16]{3,2,1,0:T(8,128)S(1)}, f32[3,5,16,16]{3,2,1,0:T(8,128)S(1)}, u32[]{:S(2)}, u32[]{:S(2)}) collective-permute-start(f32[3,5,16,16]{3,2,1,0:T(8,128)S(1)} %maximum_bitcast_fusion), channel_id=1, source_target_pairs={{0,7},{1,6},{2,5},{3,4},{16,23},{17,22},{18,21},{19,20}} | collective-permute-start | bytes 46088 | tf_op jit(solution)/shard_map/ppermute | solution.py:56
  18.4 2.7 %collective-permute-start.4 = (f32[3,5,16,16]{3,2,1,0:T(8,128)S(1)}, f32[3,5,16,16]{3,2,1,0:T(8,128)S(1)}, u32[]{:S(2)}, u32[]{:S(2)}) collective-permute-start(f32[3,5,16,16]{3,2,1,0:T(8,128)S(1)} %maximum_bitcast_fusion.3), channel_id=1, source_target_pairs={{4,8},{5,9},{6,10},{7,11},{20,24},{21,25},{22,26},{23,27}} | collective-permute-start | bytes 46088 | tf_op jit(solution)/shard_map/ppermute | solution.py:56
  19.1 2.0 %collective-permute-start.5 = (f32[3,5,16,16]{3,2,1,0:T(8,128)S(1)}, f32[3,5,16,16]{3,2,1,0:T(8,128)S(1)}, u32[]{:S(2)}, u32[]{:S(2)}) collective-permute-start(f32[3,5,16,16]{3,2,1,0:T(8,128)S(1)} %maximum_bitcast_fusion.3), channel_id=1, source_target_pairs={{4,9},{5,8},{6,11},{7,10},{20,25},{21,24},{22,27},{23,26}} | collective-permute-start | bytes 46088 | tf_op jit(solution)/shard_map/ppermute | solution.py:56
  19.8 1.4 %collective-permute-start.6 = (f32[3,5,16,16]{3,2,1,0:T(8,128)S(1)}, f32[3,5,16,16]{3,2,1,0:T(8,128)S(1)}, u32[]{:S(2)}, u32[]{:S(2)}) collective-permute-start(f32[3,5,16,16]{3,2,1,0:T(8,128)S(1)} %maximum_bitcast_fusion.3), channel_id=1, source_target_pairs={{4,10},{5,11},{6,8},{7,9},{20,26},{21,27},{22,24},{23,25}} | collective-permute-start | bytes 46088 | tf_op jit(solution)/shard_map/ppermute | solution.py:56
  20.5 0.7 %collective-permute-start.7 = (f32[3,5,16,16]{3,2,1,0:T(8,128)S(1)}, f32[3,5,16,16]{3,2,1,0:T(8,128)S(1)}, u32[]{:S(2)}, u32[]{:S(2)}) collective-permute-start(f32[3,5,16,16]{3,2,1,0:T(8,128)S(1)} %maximum_bitcast_fusion.3), channel_id=1, source_target_pairs={{4,11},{5,10},{6,9},{7,8},{20,27},{21,26},{22,25},{23,24}} | collective-permute-start | bytes 46088 | tf_op jit(solution)/shard_map/ppermute | solution.py:56
  25.8 21.3 %collective-permute-start.10 = (f32[3,5,16,16]{3,2,1,0:T(8,128)S(1)}, f32[3,5,16,16]{3,2,1,0:T(8,128)S(1)}, u32[]{:S(2)}, u32[]{:S(2)}) collective-permute-start(f32[3,5,16,16]{3,2,1,0:T(8,128)S(1)} %maximum_bitcast_fusion.6), channel_id=1, source_target_pairs={{8,14},{9,15},{10,12},{11,13},{24,30},{25,31},{26,28},{27,29}} | collective-permute-start | bytes 46088 | tf_op jit(solution)/shard_map/ppermute | solution.py:56
  27.1 20.0 %collective-permute-start.11 = (f32[3,5,16,16]{3,2,1,0:T(8,128)S(1)}, f32[3,5,16,16]{3,2,1,0:T(8,128)S(1)}, u32[]{:S(2)}, u32[]{:S(2)}) collective-permute-start(f32[3,5,16,16]{3,2,1,0:T(8,128)S(1)} %maximum_bitcast_fusion.6), channel_id=1, source_target_pairs={{8,15},{9,14},{10,13},{11,12},{24,31},{25,30},{26,29},{27,28}} | collective-permute-start | bytes 46088 | tf_op jit(solution)/shard_map/ppermute | solution.py:56
  28.4 18.7 %collective-permute-start.8 = (f32[3,5,16,16]{3,2,1,0:T(8,128)S(1)}, f32[3,5,16,16]{3,2,1,0:T(8,128)S(1)}, u32[]{:S(2)}, u32[]{:S(2)}) collective-permute-start(f32[3,5,16,16]{3,2,1,0:T(8,128)S(1)} %maximum_bitcast_fusion.6), channel_id=1, source_target_pairs={{8,12},{9,13},{10,14},{11,15},{24,28},{25,29},{26,30},{27,31}} | collective-permute-start | bytes 46088 | tf_op jit(solution)/shard_map/ppermute | solution.py:56
  29.7 19.1 %collective-permute-start.9 = (f32[3,5,16,16]{3,2,1,0:T(8,128)S(1)}, f32[3,5,16,16]{3,2,1,0:T(8,128)S(1)}, u32[]{:S(2)}, u32[]{:S(2)}) collective-permute-start(f32[3,5,16,16]{3,2,1,0:T(8,128)S(1)} %maximum_bitcast_fusion.6), channel_id=1, source_target_pairs={{8,13},{9,12},{10,15},{11,14},{24,29},{25,28},{26,31},{27,30}} | collective-permute-start | bytes 46088 | tf_op jit(solution)/shard_map/ppermute | solution.py:56

commit v10 on v7

--- a/solution.py
+++ b/solution.py
@@ -59,7 +59,7 @@
         if turn + 1 < chains:
             approx = base - jnp.sum(inv_narrow.astype(jnp.float32) * coupling[:, None, :], axis=-1)
             traces = face_traces(approx).astype(jnp.bfloat16)
-    out = base - jnp.sum(inv * own_coupling[:, None, :], axis=-1)
+    out = base - jnp.sum(inv_narrow.astype(jnp.float32) * own_coupling[:, None, :], axis=-1)
     return jnp.transpose(out.reshape(local, VARS, NODES), (1, 2, 0))[None]
 
 

time: 50 us -> 49 us (0.980)
  other arithmetic: 20.3 us -> 19.3 us
    reduce_sum x1, other arithmetic: 4.13 us -> 3.1 us  [body(): jnp.sum(inv_narrow.astype(jnp.float32) * own_coupling[:, None, :], axis=-1)]
where the time goes in v10:
time: 49 us; the launch traced here: 48.5 us
  other arithmetic  19.3 us (39%)
  waiting for transfers between devices  13.2 us (27%)
  starting transfers between devices  10.5 us (21%)
  matrix products  2.53 us (5%)
  local copies, waits for them, and re-layouts  2.51 us (5%)
    ppermute x12, waiting for transfers between devices, body(): blocks[d] = lax.ppermute(traces, ('chain', 'group'), pairs)  13.2 us
    ppermute x12, starting transfers between devices, body(): blocks[d] = lax.ppermute(traces, ('chain', 'group'), pairs)  10.5 us
    reduce_sum x2, other arithmetic, body(): jnp.sum(inv_narrow.astype(jnp.float32) * coupling[:, None, :], axis=-1)  6.2 us
    convert_element_type x1, other arithmetic, body(): inv_narrow = lax.optimization_barrier(inv.astype(jnp.bfloat16))  5.67 us
    reduce_sum x1, other arithmetic, body(): base = jnp.sum(inv * rhs_t[:, None, :], axis=-1)  4.14 us
    reduce_sum x1, other arithmetic, body(): jnp.sum(inv_narrow.astype(jnp.float32) * own_coupling[:, None, :], axis=-1)  3.1 us
    dot_general x3, matrix products, coupling_of(): jnp.einsum('kvfp,kvpwe->kwfe', traces_in.astype(jnp.float32), picked_jac,...  1.71 us
  transfers between devices with their start and end apart: 12, of which 3 were waited for; matrix products, arithmetic and copies ran while one was open for 12% of the time, Pallas kernels for 0%

profile of v10, /device:TPU:7, one launch (start us, length us, event | category | flops | bytes accessed | tf_op | source)
XLA Modules:
  0.0 48.5 jit_solution(2411849919924702694)
XLA Ops:
  0.0 0.8 %copy.17 = f32[16,5,64]{2,1,0:T(8,128)S(1)} copy(f32[16,5,64]{2,0,1:T(8,128)} %bitcast.128) | data formatting | bytes 40960 | tf_op jit(solution)/shard_map/transpose | solution.py:34
  0.9 4.1 %fusion.3 = f32[16,320]{1,0:T(8,128)S(1)} fusion(f32[1,16,320,320]{3,2,1,0:T(8,128)} %param.6, f32[16,320]{1,0:T(8,128)S(1)} %mul.46), kind=kLoop, calls=%fused_computation.8 | loop fusion | flops 3271680 | bytes 6594560 | tf_op jit(solution)/shard_map/reduce_sum | solution.py:47
  5.1 0.1 copy.20
  5.3 0.7 %collective-permute-start = (bf16[3,5,16,16]{3,2,1,0:T(8,128)(2,1)S(1)}, bf16[3,5,16,16]{3,2,1,0:T(8,128)(2,1)S(1)}, u32[]{:S(2)}, u32[]{:S(2)}) collective-permute-start(bf16[3,5,16,16]{3,2,1,0:T(8,128)(2,1)S(1)} %maximum_bitcast_fusion), channel_id=1, source_target_pairs={{0,4},{1,5},{2,6},{3,7},{16,20},{17,21},{18,22},{19,23}} | collective-permute-start | bytes 23048 | tf_op jit(solution)/shard_map/ppermute | solution.py:56
  6.0 0.7 %collective-permute-start.1 = (bf16[3,5,16,16]{3,2,1,0:T(8,128)(2,1)S(1)}, bf16[3,5,16,16]{3,2,1,0:T(8,128)(2,1)S(1)}, u32[]{:S(2)}, u32[]{:S(2)}) collective-permute-start(bf16[3,5,16,16]{3,2,1,0:T(8,128)(2,1)S(1)} %maximum_bitcast_fusion), channel_id=1, source_target_pairs={{0,5},{1,4},{2,7},{3,6},{16,21},{17,20},{18,23},{19,22}} | collective-permute-start | bytes 23048 | tf_op jit(solution)/shard_map/ppermute | solution.py:56
  6.7 0.7 %collective-permute-start.2 = (bf16[3,5,16,16]{3,2,1,0:T(8,128)(2,1)S(1)}, bf16[3,5,16,16]{3,2,1,0:T(8,128)(2,1)S(1)}, u32[]{:S(2)}, u32[]{:S(2)}) collective-permute-start(bf16[3,5,16,16]{3,2,1,0:T(8,128)(2,1)S(1)} %maximum_bitcast_fusion), channel_id=1, source_target_pairs={{0,6},{1,7},{2,4},{3,5},{16,22},{17,23},{18,20},{19,21}} | collective-permute-start | bytes 23048 | tf_op jit(solution)/shard_map/ppermute | solution.py:56
  7.3 0.7 %collective-permute-start.3 = (bf16[3,5,16,16]{3,2,1,0:T(8,128)(2,1)S(1)}, bf16[3,5,16,16]{3,2,1,0:T(8,128)(2,1)S(1)}, u32[]{:S(2)}, u32[]{:S(2)}) collective-permute-start(bf16[3,5,16,16]{3,2,1,0:T(8,128)(2,1)S(1)} %maximum_bitcast_fusion), channel_id=1, source_target_pairs={{0,7},{1,6},{2,5},{3,4},{16,23},{17,22},{18,21},{19,20}} | collective-permute-start | bytes 23048 | tf_op jit(solution)/shard_map/ppermute | solution.py:56
  8.0 5.7 %bitcast_convert_fusion = bf16[16,320,320]{2,1,0:T(8,128)(2,1)} fusion(f32[1,16,320,320]{3,2,1,0:T(8,128)} %param.6), kind=kLoop, calls=%fused_computation.6 | loop fusion | flops 1638400 | bytes 9830400 | tf_op jit(solution)/shard_map/convert_element_type | solution.py:48
  13.9 0.6 %convolution_bitcast_fusion.2 = f32[3,5,16,16]{2,3,0,1:T(8,128)S(1)} fusion(f32[3,16,5,5]{1,3,0,2:T(8,128)S(1)} %copy.19, f32[3,16,64]{2,1,0:T(8,128)S(1)} %convert_bitcast_fusion, bf16[3,5,16,16]{3,2,1,0:T(8,128)(2,1)S(1)} %collective-permute-done.3, bf16[3,5,16,16]{3,2,1,0:T(8,128)(2,1)S(1)} %collective-permute-done.2, ...), kind=kOutput, calls=%fused_computation.11 | convolution fusion | flops 14945280 | bytes 63168 | tf_op jit(solution)/shard_map/kvfp,kvpwe->kwfe/dot_general | solution.py:43
  14.5 0.3 convolution_bitcast_fusion.5
  14.8 3.1 %fusion = f32[16,320]{1,0:T(8,128)S(1)} fusion(bf16[16,320,320]{2,1,0:T(8,128)(2,1)} %bitcast_convert_fusion, f32[16,320]{1,0:T(8,128)S(1)} %mul.50), kind=kLoop, calls=%fused_computation.3 | loop fusion | flops 4910080 | bytes 3317760 | tf_op jit(solution)/shard_map/reduce_sum | solution.py:60
  17.9 0.1 copy.22
  18.2 0.7 %collective-permute-start.4 = (bf16[3,5,16,16]{3,2,1,0:T(8,128)(2,1)S(1)}, bf16[3,5,16,16]{3,2,1,0:T(8,128)(2,1)S(1)}, u32[]{:S(2)}, u32[]{:S(2)}) collective-permute-start(bf16[3,5,16,16]{3,2,1,0:T(8,128)(2,1)S(1)} %maximum_bitcast_fusion.3), channel_id=1, source_target_pairs={{4,8},{5,9},{6,10},{7,11},{20,24},{21,25},{22,26},{23,27}} | collective-permute-start | bytes 23048 | tf_op jit(solution)/shard_map/ppermute | solution.py:56
  18.9 0.7 %collective-permute-start.5 = (bf16[3,5,16,16]{3,2,1,0:T(8,128)(2,1)S(1)}, bf16[3,5,16,16]{3,2,1,0:T(8,128)(2,1)S(1)}, u32[]{:S(2)}, u32[]{:S(2)}) collective-permute-start(bf16[3,5,16,16]{3,2,1,0:T(8,128)(2,1)S(1)} %maximum_bitcast_fusion.3), channel_id=1, source_target_pairs={{4,9},{5,8},{6,11},{7,10},{20,25},{21,24},{22,27},{23,26}} | collective-permute-start | bytes 23048 | tf_op jit(solution)/shard_map/ppermute | solution.py:56
  19.5 0.7 %collective-permute-start.6 = (bf16[3,5,16,16]{3,2,1,0:T(8,128)(2,1)S(1)}, bf16[3,5,16,16]{3,2,1,0:T(8,128)(2,1)S(1)}, u32[]{:S(2)}, u32[]{:S(2)}) collective-permute-start(bf16[3,5,16,16]{3,2,1,0:T(8,128)(2,1)S(1)} %maximum_bitcast_fusion.3), channel_id=1, source_target_pairs={{4,10},{5,11},{6,8},{7,9},{20,26},{21,27},{22,24},{23,25}} | collective-permute-start | bytes 23048 | tf_op jit(solution)/shard_map/ppermute | solution.py:56
  20.2 0.7 %collective-permute-start.7 = (bf16[3,5,16,16]{3,2,1,0:T(8,128)(2,1)S(1)}, bf16[3,5,16,16]{3,2,1,0:T(8,128)(2,1)S(1)}, u32[]{:S(2)}, u32[]{:S(2)}) collective-permute-start(bf16[3,5,16,16]{3,2,1,0:T(8,128)(2,1)S(1)} %maximum_bitcast_fusion.3), channel_id=1, source_target_pairs={{4,11},{5,10},{6,9},{7,8},{20,27},{21,26},{22,25},{23,24}} | collective-permute-start | bytes 23048 | tf_op jit(solution)/shard_map/ppermute | solution.py:56
  20.9 0.6 %convolution_bitcast_fusion.1 = f32[3,5,16,16]{2,3,0,1:T(8,128)S(1)} fusion(f32[3,16,5,5]{1,3,0,2:T(8,128)S(1)} %copy.19, f32[3,16,64]{2,1,0:T(8,128)S(1)} %convert_bitcast_fusion, bf16[3,5,16,16]{3,2,1,0:T(8,128)(2,1)S(1)} %collective-permute-done.7, bf16[3,5,16,16]{3,2,1,0:T(8,128)(2,1)S(1)} %collective-permute-done.6, ...), kind=kOutput, calls=%fused_computation.10 | convolution fusion | flops 14945280 | bytes 63168 | tf_op jit(solution)/shard_map/kvfp,kvpwe->kwfe/dot_general | solution.py:43
  21.5 0.3 convolution_bitcast_fusion.4
  21.9 3.1 %fusion.1 = f32[16,320]{1,0:T(8,128)S(1)} fusion(bf16[16,320,320]{2,1,0:T(8,128)(2,1)} %bitcast_convert_fusion, f32[16,320]{1,0:T(8,128)S(1)} %mul.53), kind=kLoop, calls=%fused_computation.4 | loop fusion | flops 4910080 | bytes 3317760 | tf_op jit(solution)/shard_map/reduce_sum | solution.py:60
  25.0 0.1 copy.24
  25.3 1.3 %collective-permute-start.10 = (bf16[3,5,16,16]{3,2,1,0:T(8,128)(2,1)S(1)}, bf16[3,5,16,16]{3,2,1,0:T(8,128)(2,1)S(1)}, u32[]{:S(2)}, u32[]{:S(2)}) collective-permute-start(bf16[3,5,16,16]{3,2,1,0:T(8,128)(2,1)S(1)} %maximum_bitcast_fusion.6), channel_id=1, source_target_pairs={{8,14},{9,15},{10,12},{11,13},{24,30},{25,31},{26,28},{27,29}} | collective-permute-start | bytes 23048 | tf_op jit(solution)/shard_map/ppermute | solution.py:56
  26.6 1.3 %collective-permute-start.11 = (bf16[3,5,16,16]{3,2,1,0:T(8,128)(2,1)S(1)}, bf16[3,5,16,16]{3,2,1,0:T(8,128)(2,1)S(1)}, u32[]{:S(2)}, u32[]{:S(2)}) collective-permute-start(bf16[3,5,16,16]{3,2,1,0:T(8,128)(2,1)S(1)} %maximum_bitcast_fusion.6), channel_id=1, source_target_pairs={{8,15},{9,14},{10,13},{11,12},{24,31},{25,30},{26,29},{27,28}} | collective-permute-start | bytes 23048 | tf_op jit(solution)/shard_map/ppermute | solution.py:56
  27.9 1.3 %collective-permute-start.8 = (bf16[3,5,16,16]{3,2,1,0:T(8,128)(2,1)S(1)}, bf16[3,5,16,16]{3,2,1,0:T(8,128)(2,1)S(1)}, u32[]{:S(2)}, u32[]{:S(2)}) collective-permute-start(bf16[3,5,16,16]{3,2,1,0:T(8,128)(2,1)S(1)} %maximum_bitcast_fusion.6), channel_id=1, source_target_pairs={{8,12},{9,13},{10,14},{11,15},{24,28},{25,29},{26,30},{27,31}} | collective-permute-start | bytes 23048 | tf_op jit(solution)/shard_map/ppermute | solution.py:56
  29.2 1.3 %collective-permute-start.9 = (bf16[3,5,16,16]{3,2,1,0:T(8,128)(2,1)S(1)}, bf16[3,5,16,16]{3,2,1,0:T(8,128)(2,1)S(1)}, u32[]{:S(2)}, u32[]{:S(2)}) collective-permute-start(bf16[3,5,16,16]{3,2,1,0:T(8,128)(2,1)S(1)} %maximum_bitcast_fusion.6), channel_id=1, source_target_pairs={{8,13},{9,12},{10,15},{11,14},{24,29},{25,28},{26,31},{27,30}} | collective-permute-start | bytes 23048 | tf_op jit(solution)/shard_map/ppermute | solution.py:56
  30.5 9.5 %collective-permute-done.10 = bf16[3,5,16,16]{3,2,1,0:T(8,128)(2,1)S(1)} collective-permute-done((bf16[3,5,16,16]{3,2,1,0:T(8,128)(2,1)S(1)}, bf16[3,5,16,16]{3,2,1,0:T(8,128)(2,1)S(1)}, u32[]{:S(2)}, u32[]{:S(2)}) %collective-permute-start.10) | collective-permute-done | bytes 7712 | tf_op jit(solution)/shard_map/ppermute | solution.py:56
  39.9 3.1 %collective-permute-done.11 = bf16[3,5,16,16]{3,2,1,0:T(8,128)(2,1)S(1)} collective-permute-done((bf16[3,5,16,16]{3,2,1,0:T(8,128)(2,1)S(1)}, bf16[3,5,16,16]{3,2,1,0:T(8,128)(2,1)S(1)}, u32[]{:S(2)}, u32[]{:S(2)}) %collective-permute-start.11) | collective-permute-done | bytes 7712 | tf_op jit(solution)/shard_map/ppermute | solution.py:56
  43.1 0.6 %collective-permute-done.9 = bf16[3,5,16,16]{3,2,1,0:T(8,128)(2,1)S(1)} collective-permute-done((bf16[3,5,16,16]{3,2,1,0:T(8,128)(2,1)S(1)}, bf16[3,5,16,16]{3,2,1,0:T(8,128)(2,1)S(1)}, u32[]{:S(2)}, u32[]{:S(2)}) %collective-permute-start.9) | collective-permute-done | bytes 7712 | tf_op jit(solution)/shard_map/ppermute | solution.py:56
  43.7 0.6 %convolution_bitcast_fusion = f32[3,5,16,16]{2,3,0,1:T(8,128)S(1)} fusion(f32[3,16,5,5]{1,3,0,2:T(8,128)S(1)} %copy.19, f32[3,16,64]{2,1,0:T(8,128)S(1)} %convert_bitcast_fusion, bf16[3,5,16,16]{3,2,1,0:T(8,128)(2,1)S(1)} %collective-permute-done.11, bf16[3,5,16,16]{3,2,1,0:T(8,128)(2,1)S(1)} %collective-permute-done.10, ...), kind=kOutput, calls=%fused_computation.9 | convolution fusion | flops 14945280 | bytes 63168 | tf_op jit(solution)/shard_map/kvfp,kvpwe->kwfe/dot_general | solution.py:43
  44.3 0.3 convolution_bitcast_fusion.3
  44.7 3.1 %fusion.2 = f32[16,320]{1,0:T(8,128)S(1)} fusion(bf16[16,320,320]{2,1,0:T(8,128)(2,1)} %bitcast_convert_fusion, f32[16,320]{1,0:T(8,128)S(1)} %select_select_fusion), kind=kLoop, calls=%fused_computation.5 | loop fusion | flops 4910080 | bytes 3317760 | tf_op jit(solution)/shard_map/reduce_sum | solution.py:62
  47.8 0.1 sub.25
  47.9 0.6 %copy.26 = f32[1,5,64,16]{2,3,1,0:T(8,128)} copy(f32[1,5,64,16]{2,1,3,0:T(8,128)S(1)} %bitcast.117) | data formatting | bytes 40960 | tf_op jit(solution)/shard_map/broadcast_in_dim | solution.py:63
  (46 shorter events, 0.8 us)
Async XLA Ops:
  0.0 14.4 %copy-start = (f32[3,64,16]{1,2,0:T(8,128)S(1)}, f32[3,64,16]{1,2,0:T(8,128)}, u32[]{:S(2)}) copy-start(f32[3,64,16]{1,2,0:T(8,128)} %param.9) | copy-start | bytes 36868
  5.0 8.7 %copy-start.2 = (s32[1,3,16]{2,0,1:T(1,128)S(1)}, s32[1,3,16]{2,0,1:T(1,128)}, u32[]{:S(2)}) copy-start(s32[1,3,16]{2,0,1:T(1,128)} %param.8) | copy-start | bytes 580
  5.0 8.7 %copy-start.1 = (f32[1,3,5,5,16]{4,0,3,2,1:T(1,128)S(1)}, f32[1,3,5,5,16]{4,0,3,2,1:T(1,128)}, u32[]{:S(2)}) copy-start(f32[1,3,5,5,16]{4,0,3,2,1:T(1,128)} %param.7) | copy-start | bytes 14404
  5.3 8.5 %collective-permute-start = (bf16[3,5,16,16]{3,2,1,0:T(8,128)(2,1)S(1)}, bf16[3,5,16,16]{3,2,1,0:T(8,128)(2,1)S(1)}, u32[]{:S(2)}, u32[]{:S(2)}) collective-permute-start(bf16[3,5,16,16]{3,2,1,0:T(8,128)(2,1)S(1)} %maximum_bitcast_fusion), channel_id=1, source_target_pairs={{0,4},{1,5},{2,6},{3,7},{16,20},{17,21},{18,22},{19,23}} | collective-permute-start | bytes 23048 | tf_op jit(solution)/shard_map/ppermute | solution.py:56
  6.0 7.8 %collective-permute-start.1 = (bf16[3,5,16,16]{3,2,1,0:T(8,128)(2,1)S(1)}, bf16[3,5,16,16]{3,2,1,0:T(8,128)(2,1)S(1)}, u32[]{:S(2)}, u32[]{:S(2)}) collective-permute-start(bf16[3,5,16,16]{3,2,1,0:T(8,128)(2,1)S(1)} %maximum_bitcast_fusion), channel_id=1, source_target_pairs={{0,5},{1,4},{2,7},{3,6},{16,21},{17,20},{18,23},{19,22}} | collective-permute-start | bytes 23048 | tf_op jit(solution)/shard_map/ppermute | solution.py:56
  6.7 7.2 %collective-permute-start.2 = (bf16[3,5,16,16]{3,2,1,0:T(8,128)(2,1)S(1)}, bf16[3,5,16,16]{3,2,1,0:T(8,128)(2,1)S(1)}, u32[]{:S(2)}, u32[]{:S(2)}) collective-permute-start(bf16[3,5,16,16]{3,2,1,0:T(8,128)(2,1)S(1)} %maximum_bitcast_fusion), channel_id=1, source_target_pairs={{0,6},{1,7},{2,4},{3,5},{16,22},{17,23},{18,20},{19,21}} | collective-permute-start | bytes 23048 | tf_op jit(solution)/shard_map/ppermute | solution.py:56
  7.3 6.5 %collective-permute-start.3 = (bf16[3,5,16,16]{3,2,1,0:T(8,128)(2,1)S(1)}, bf16[3,5,16,16]{3,2,1,0:T(8,128)(2,1)S(1)}, u32[]{:S(2)}, u32[]{:S(2)}) collective-permute-start(bf16[3,5,16,16]{3,2,1,0:T(8,128)(2,1)S(1)} %maximum_bitcast_fusion), channel_id=1, source_target_pairs={{0,7},{1,6},{2,5},{3,4},{16,23},{17,22},{18,21},{19,20}} | collective-permute-start | bytes 23048 | tf_op jit(solution)/shard_map/ppermute | solution.py:56
  18.2 2.7 %collective-permute-start.4 = (bf16[3,5,16,16]{3,2,1,0:T(8,128)(2,1)S(1)}, bf16[3,5,16,16]{3,2,1,0:T(8,128)(2,1)S(1)}, u32[]{:S(2)}, u32[]{:S(2)}) collective-permute-start(bf16[3,5,16,16]{3,2,1,0:T(8,128)(2,1)S(1)} %maximum_bitcast_fusion.3), channel_id=1, source_target_pairs={{4,8},{5,9},{6,10},{7,11},{20,24},{21,25},{22,26},{23,27}} | collective-permute-start | bytes 23048 | tf_op jit(solution)/shard_map/ppermute | solution.py:56
  18.9 2.0 %collective-permute-start.5 = (bf16[3,5,16,16]{3,2,1,0:T(8,128)(2,1)S(1)}, bf16[3,5,16,16]{3,2,1,0:T(8,128)(2,1)S(1)}, u32[]{:S(2)}, u32[]{:S(2)}) collective-permute-start(bf16[3,5,16,16]{3,2,1,0:T(8,128)(2,1)S(1)} %maximum_bitcast_fusion.3), channel_id=1, source_target_pairs={{4,9},{5,8},{6,11},{7,10},{20,25},{21,24},{22,27},{23,26}} | collective-permute-start | bytes 23048 | tf_op jit(solution)/shard_map/ppermute | solution.py:56
  19.5 1.4 %collective-permute-start.6 = (bf16[3,5,16,16]{3,2,1,0:T(8,128)(2,1)S(1)}, bf16[3,5,16,16]{3,2,1,0:T(8,128)(2,1)S(1)}, u32[]{:S(2)}, u32[]{:S(2)}) collective-permute-start(bf16[3,5,16,16]{3,2,1,0:T(8,128)(2,1)S(1)} %maximum_bitcast_fusion.3), channel_id=1, source_target_pairs={{4,10},{5,11},{6,8},{7,9},{20,26},{21,27},{22,24},{23,25}} | collective-permute-start | bytes 23048 | tf_op jit(solution)/shard_map/ppermute | solution.py:56
  20.2 0.7 %collective-permute-start.7 = (bf16[3,5,16,16]{3,2,1,0:T(8,128)(2,1)S(1)}, bf16[3,5,16,16]{3,2,1,0:T(8,128)(2,1)S(1)}, u32[]{:S(2)}, u32[]{:S(2)}) collective-permute-start(bf16[3,5,16,16]{3,2,1,0:T(8,128)(2,1)S(1)} %maximum_bitcast_fusion.3), channel_id=1, source_target_pairs={{4,11},{5,10},{6,9},{7,8},{20,27},{21,26},{22,25},{23,24}} | collective-permute-start | bytes 23048 | tf_op jit(solution)/shard_map/ppermute | solution.py:56
  25.3 14.7 %collective-permute-start.10 = (bf16[3,5,16,16]{3,2,1,0:T(8,128)(2,1)S(1)}, bf16[3,5,16,16]{3,2,1,0:T(8,128)(2,1)S(1)}, u32[]{:S(2)}, u32[]{:S(2)}) collective-permute-start(bf16[3,5,16,16]{3,2,1,0:T(8,128)(2,1)S(1)} %maximum_bitcast_fusion.6), channel_id=1, source_target_pairs={{8,14},{9,15},{10,12},{11,13},{24,30},{25,31},{26,28},{27,29}} | collective-permute-start | bytes 23048 | tf_op jit(solution)/shard_map/ppermute | solution.py:56
  26.6 16.5 %collective-permute-start.11 = (bf16[3,5,16,16]{3,2,1,0:T(8,128)(2,1)S(1)}, bf16[3,5,16,16]{3,2,1,0:T(8,128)(2,1)S(1)}, u32[]{:S(2)}, u32[]{:S(2)}) collective-permute-start(bf16[3,5,16,16]{3,2,1,0:T(8,128)(2,1)S(1)} %maximum_bitcast_fusion.6), channel_id=1, source_target_pairs={{8,15},{9,14},{10,13},{11,12},{24,31},{25,30},{26,29},{27,28}} | collective-permute-start | bytes 23048 | tf_op jit(solution)/shard_map/ppermute | solution.py:56
  27.9 15.2 %collective-permute-start.8 = (bf16[3,5,16,16]{3,2,1,0:T(8,128)(2,1)S(1)}, bf16[3,5,16,16]{3,2,1,0:T(8,128)(2,1)S(1)}, u32[]{:S(2)}, u32[]{:S(2)}) collective-permute-start(bf16[3,5,16,16]{3,2,1,0:T(8,128)(2,1)S(1)} %maximum_bitcast_fusion.6), channel_id=1, source_target_pairs={{8,12},{9,13},{10,14},{11,15},{24,28},{25,29},{26,30},{27,31}} | collective-permute-start | bytes 23048 | tf_op jit(solution)/shard_map/ppermute | solution.py:56
  29.2 14.5 %collective-permute-start.9 = (bf16[3,5,16,16]{3,2,1,0:T(8,128)(2,1)S(1)}, bf16[3,5,16,16]{3,2,1,0:T(8,128)(2,1)S(1)}, u32[]{:S(2)}, u32[]{:S(2)}) collective-permute-start(bf16[3,5,16,16]{3,2,1,0:T(8,128)(2,1)S(1)} %maximum_bitcast_fusion.6), channel_id=1, source_target_pairs={{8,13},{9,12},{10,15},{11,14},{24,29},{25,28},{26,31},{27,30}} | collective-permute-start | bytes 23048 | tf_op jit(solution)/shard_map/ppermute | solution.py:56

commit v11 on v10

--- a/solution.py
+++ b/solution.py
@@ -10,6 +10,7 @@
 BLOCK = VARS * NODES
 
 HIGH = lax.Precision.HIGHEST
+HIGHEST = lax.Precision.HIGHEST
 
 
 def face_traces(sol):
@@ -32,6 +33,7 @@
     jac = flux_jac[0]
     up = up_elem[0]
     rhs_t = jnp.transpose(rhs[0], (2, 0, 1)).reshape(local, BLOCK)
+    eye = jnp.eye(local, dtype=jnp.float32)
 
     xor_pairs = groups & (groups - 1) == 0
     shift = jnp.bitwise_xor(g, up // local) if xor_pairs else (g - up // local) % groups
@@ -60,7 +62,8 @@
             approx = base - jnp.sum(inv_narrow.astype(jnp.float32) * coupling[:, None, :], axis=-1)
             traces = face_traces(approx).astype(jnp.bfloat16)
     out = base - jnp.sum(inv_narrow.astype(jnp.float32) * own_coupling[:, None, :], axis=-1)
-    return jnp.transpose(out.reshape(local, VARS, NODES), (1, 2, 0))[None]
+    out = jnp.einsum("evi,ef->vfi", out.reshape(local, VARS, NODES), eye, precision=HIGHEST)
+    return jnp.transpose(out, (0, 2, 1))[None]
 
 
 def solution(mesh):

time: 49 us -> 49.2 us (level)
  matrix products: 2.53 us -> 3.29 us
  local copies, waits for them, and re-layouts: 2.51 us -> 1.88 us
    dot_general x0 -> x1, matrix products: none -> 0.77 us  [body(): jnp.einsum('evi,ef->vfi', out.reshape(local, VARS, NODES), eye, precision...]
    broadcast_in_dim x1 -> x0, local copies, waits for them, and re-layouts: 0.63 us -> none  [body(): return jnp.transpose(out.reshape(local, VARS, NODES), (1, 2, 0))[None]]
where the time goes in v11:
time: 49.2 us; the launch traced here: 48.6 us
  other arithmetic  19.3 us (39%)
  waiting for transfers between devices  13.2 us (27%)
  starting transfers between devices  10.5 us (21%)
  matrix products  3.29 us (7%)
  local copies, waits for them, and re-layouts  1.88 us (4%)
    ppermute x12, waiting for transfers between devices, body(): blocks[d] = lax.ppermute(traces, ('chain', 'group'), pairs)  13.2 us
    ppermute x12, starting transfers between devices, body(): blocks[d] = lax.ppermute(traces, ('chain', 'group'), pairs)  10.5 us
    reduce_sum x2, other arithmetic, body(): jnp.sum(inv_narrow.astype(jnp.float32) * coupling[:, None, :], axis=-1)  6.2 us
    convert_element_type x1, other arithmetic, body(): inv_narrow = lax.optimization_barrier(inv.astype(jnp.bfloat16))  5.67 us
    reduce_sum x1, other arithmetic, body(): base = jnp.sum(inv * rhs_t[:, None, :], axis=-1)  4.14 us
    reduce_sum x1, other arithmetic, body(): jnp.sum(inv_narrow.astype(jnp.float32) * own_coupling[:, None, :], axis=-1)  3.1 us
    dot_general x3, matrix products, coupling_of(): jnp.einsum('kvfp,kvpwe->kwfe', traces_in.astype(jnp.float32), picked_jac,...  1.71 us
  transfers between devices with their start and end apart: 12, of which 3 were waited for; matrix products, arithmetic and copies ran while one was open for 12% of the time, Pallas kernels for 0%

profile of v11, /device:TPU:7, one launch (start us, length us, event | category | flops | bytes accessed | tf_op | source)
XLA Modules:
  0.0 48.6 jit_solution(14894346544913926832)
XLA Ops:
  0.0 0.8 %copy.17 = f32[16,5,64]{2,1,0:T(8,128)S(1)} copy(f32[16,5,64]{2,0,1:T(8,128)} %bitcast.129) | data formatting | bytes 40960 | tf_op jit(solution)/shard_map/transpose | solution.py:35
  0.9 4.1 %fusion.3 = f32[16,320]{1,0:T(8,128)S(1)} fusion(f32[1,16,320,320]{3,2,1,0:T(8,128)} %param.6, f32[16,320]{1,0:T(8,128)S(1)} %mul.46), kind=kLoop, calls=%fused_computation.8 | loop fusion | flops 3271680 | bytes 6594560 | tf_op jit(solution)/shard_map/reduce_sum | solution.py:49
  5.1 0.1 copy.20
  5.3 0.7 %collective-permute-start = (bf16[3,5,16,16]{3,2,1,0:T(8,128)(2,1)S(1)}, bf16[3,5,16,16]{3,2,1,0:T(8,128)(2,1)S(1)}, u32[]{:S(2)}, u32[]{:S(2)}) collective-permute-start(bf16[3,5,16,16]{3,2,1,0:T(8,128)(2,1)S(1)} %maximum_bitcast_fusion), channel_id=1, source_target_pairs={{0,4},{1,5},{2,6},{3,7},{16,20},{17,21},{18,22},{19,23}} | collective-permute-start | bytes 23048 | tf_op jit(solution)/shard_map/ppermute | solution.py:58
  6.0 0.7 %collective-permute-start.1 = (bf16[3,5,16,16]{3,2,1,0:T(8,128)(2,1)S(1)}, bf16[3,5,16,16]{3,2,1,0:T(8,128)(2,1)S(1)}, u32[]{:S(2)}, u32[]{:S(2)}) collective-permute-start(bf16[3,5,16,16]{3,2,1,0:T(8,128)(2,1)S(1)} %maximum_bitcast_fusion), channel_id=1, source_target_pairs={{0,5},{1,4},{2,7},{3,6},{16,21},{17,20},{18,23},{19,22}} | collective-permute-start | bytes 23048 | tf_op jit(solution)/shard_map/ppermute | solution.py:58
  6.7 0.7 %collective-permute-start.2 = (bf16[3,5,16,16]{3,2,1,0:T(8,128)(2,1)S(1)}, bf16[3,5,16,16]{3,2,1,0:T(8,128)(2,1)S(1)}, u32[]{:S(2)}, u32[]{:S(2)}) collective-permute-start(bf16[3,5,16,16]{3,2,1,0:T(8,128)(2,1)S(1)} %maximum_bitcast_fusion), channel_id=1, source_target_pairs={{0,6},{1,7},{2,4},{3,5},{16,22},{17,23},{18,20},{19,21}} | collective-permute-start | bytes 23048 | tf_op jit(solution)/shard_map/ppermute | solution.py:58
  7.3 0.7 %collective-permute-start.3 = (bf16[3,5,16,16]{3,2,1,0:T(8,128)(2,1)S(1)}, bf16[3,5,16,16]{3,2,1,0:T(8,128)(2,1)S(1)}, u32[]{:S(2)}, u32[]{:S(2)}) collective-permute-start(bf16[3,5,16,16]{3,2,1,0:T(8,128)(2,1)S(1)} %maximum_bitcast_fusion), channel_id=1, source_target_pairs={{0,7},{1,6},{2,5},{3,4},{16,23},{17,22},{18,21},{19,20}} | collective-permute-start | bytes 23048 | tf_op jit(solution)/shard_map/ppermute | solution.py:58
  8.0 5.7 %bitcast_convert_fusion = bf16[16,320,320]{2,1,0:T(8,128)(2,1)} fusion(f32[1,16,320,320]{3,2,1,0:T(8,128)} %param.6), kind=kLoop, calls=%fused_computation.6 | loop fusion | flops 1638400 | bytes 9830400 | tf_op jit(solution)/shard_map/convert_element_type | solution.py:50
  13.9 0.6 %convolution_bitcast_fusion.2 = f32[3,5,16,16]{2,3,0,1:T(8,128)S(1)} fusion(f32[3,16,5,5]{1,3,0,2:T(8,128)S(1)} %copy.19, f32[3,16,64]{2,1,0:T(8,128)S(1)} %convert_bitcast_fusion, bf16[3,5,16,16]{3,2,1,0:T(8,128)(2,1)S(1)} %collective-permute-done.3, bf16[3,5,16,16]{3,2,1,0:T(8,128)(2,1)S(1)} %collective-permute-done.2, ...), kind=kOutput, calls=%fused_computation.11 | convolution fusion | flops 14945280 | bytes 63168 | tf_op jit(solution)/shard_map/kvfp,kvpwe->kwfe/dot_general | solution.py:45
  14.5 0.3 convolution_bitcast_fusion.6
  14.8 3.1 %fusion = f32[16,320]{1,0:T(8,128)S(1)} fusion(bf16[16,320,320]{2,1,0:T(8,128)(2,1)} %bitcast_convert_fusion, f32[16,320]{1,0:T(8,128)S(1)} %mul.50), kind=kLoop, calls=%fused_computation.3 | loop fusion | flops 4910080 | bytes 3317760 | tf_op jit(solution)/shard_map/reduce_sum | solution.py:62
  17.9 0.1 copy.22
  18.2 0.7 %collective-permute-start.4 = (bf16[3,5,16,16]{3,2,1,0:T(8,128)(2,1)S(1)}, bf16[3,5,16,16]{3,2,1,0:T(8,128)(2,1)S(1)}, u32[]{:S(2)}, u32[]{:S(2)}) collective-permute-start(bf16[3,5,16,16]{3,2,1,0:T(8,128)(2,1)S(1)} %maximum_bitcast_fusion.3), channel_id=1, source_target_pairs={{4,8},{5,9},{6,10},{7,11},{20,24},{21,25},{22,26},{23,27}} | collective-permute-start | bytes 23048 | tf_op jit(solution)/shard_map/ppermute | solution.py:58
  18.9 0.7 %collective-permute-start.5 = (bf16[3,5,16,16]{3,2,1,0:T(8,128)(2,1)S(1)}, bf16[3,5,16,16]{3,2,1,0:T(8,128)(2,1)S(1)}, u32[]{:S(2)}, u32[]{:S(2)}) collective-permute-start(bf16[3,5,16,16]{3,2,1,0:T(8,128)(2,1)S(1)} %maximum_bitcast_fusion.3), channel_id=1, source_target_pairs={{4,9},{5,8},{6,11},{7,10},{20,25},{21,24},{22,27},{23,26}} | collective-permute-start | bytes 23048 | tf_op jit(solution)/shard_map/ppermute | solution.py:58
  19.5 0.7 %collective-permute-start.6 = (bf16[3,5,16,16]{3,2,1,0:T(8,128)(2,1)S(1)}, bf16[3,5,16,16]{3,2,1,0:T(8,128)(2,1)S(1)}, u32[]{:S(2)}, u32[]{:S(2)}) collective-permute-start(bf16[3,5,16,16]{3,2,1,0:T(8,128)(2,1)S(1)} %maximum_bitcast_fusion.3), channel_id=1, source_target_pairs={{4,10},{5,11},{6,8},{7,9},{20,26},{21,27},{22,24},{23,25}} | collective-permute-start | bytes 23048 | tf_op jit(solution)/shard_map/ppermute | solution.py:58
  20.2 0.7 %collective-permute-start.7 = (bf16[3,5,16,16]{3,2,1,0:T(8,128)(2,1)S(1)}, bf16[3,5,16,16]{3,2,1,0:T(8,128)(2,1)S(1)}, u32[]{:S(2)}, u32[]{:S(2)}) collective-permute-start(bf16[3,5,16,16]{3,2,1,0:T(8,128)(2,1)S(1)} %maximum_bitcast_fusion.3), channel_id=1, source_target_pairs={{4,11},{5,10},{6,9},{7,8},{20,27},{21,26},{22,25},{23,24}} | collective-permute-start | bytes 23048 | tf_op jit(solution)/shard_map/ppermute | solution.py:58
  20.9 0.6 %convolution_bitcast_fusion.1 = f32[3,5,16,16]{2,3,0,1:T(8,128)S(1)} fusion(f32[3,16,5,5]{1,3,0,2:T(8,128)S(1)} %copy.19, f32[3,16,64]{2,1,0:T(8,128)S(1)} %convert_bitcast_fusion, bf16[3,5,16,16]{3,2,1,0:T(8,128)(2,1)S(1)} %collective-permute-done.7, bf16[3,5,16,16]{3,2,1,0:T(8,128)(2,1)S(1)} %collective-permute-done.6, ...), kind=kOutput, calls=%fused_computation.10 | convolution fusion | flops 14945280 | bytes 63168 | tf_op jit(solution)/shard_map/kvfp,kvpwe->kwfe/dot_general | solution.py:45
  21.5 0.3 convolution_bitcast_fusion.5
  21.9 3.1 %fusion.1 = f32[16,320]{1,0:T(8,128)S(1)} fusion(bf16[16,320,320]{2,1,0:T(8,128)(2,1)} %bitcast_convert_fusion, f32[16,320]{1,0:T(8,128)S(1)} %mul.53), kind=kLoop, calls=%fused_computation.4 | loop fusion | flops 4910080 | bytes 3317760 | tf_op jit(solution)/shard_map/reduce_sum | solution.py:62
  25.0 0.1 copy.24
  25.3 1.3 %collective-permute-start.10 = (bf16[3,5,16,16]{3,2,1,0:T(8,128)(2,1)S(1)}, bf16[3,5,16,16]{3,2,1,0:T(8,128)(2,1)S(1)}, u32[]{:S(2)}, u32[]{:S(2)}) collective-permute-start(bf16[3,5,16,16]{3,2,1,0:T(8,128)(2,1)S(1)} %maximum_bitcast_fusion.6), channel_id=1, source_target_pairs={{8,14},{9,15},{10,12},{11,13},{24,30},{25,31},{26,28},{27,29}} | collective-permute-start | bytes 23048 | tf_op jit(solution)/shard_map/ppermute | solution.py:58
  26.6 1.3 %collective-permute-start.11 = (bf16[3,5,16,16]{3,2,1,0:T(8,128)(2,1)S(1)}, bf16[3,5,16,16]{3,2,1,0:T(8,128)(2,1)S(1)}, u32[]{:S(2)}, u32[]{:S(2)}) collective-permute-start(bf16[3,5,16,16]{3,2,1,0:T(8,128)(2,1)S(1)} %maximum_bitcast_fusion.6), channel_id=1, source_target_pairs={{8,15},{9,14},{10,13},{11,12},{24,31},{25,30},{26,29},{27,28}} | collective-permute-start | bytes 23048 | tf_op jit(solution)/shard_map/ppermute | solution.py:58
  27.9 1.3 %collective-permute-start.8 = (bf16[3,5,16,16]{3,2,1,0:T(8,128)(2,1)S(1)}, bf16[3,5,16,16]{3,2,1,0:T(8,128)(2,1)S(1)}, u32[]{:S(2)}, u32[]{:S(2)}) collective-permute-start(bf16[3,5,16,16]{3,2,1,0:T(8,128)(2,1)S(1)} %maximum_bitcast_fusion.6), channel_id=1, source_target_pairs={{8,12},{9,13},{10,14},{11,15},{24,28},{25,29},{26,30},{27,31}} | collective-permute-start | bytes 23048 | tf_op jit(solution)/shard_map/ppermute | solution.py:58
  29.2 1.3 %collective-permute-start.9 = (bf16[3,5,16,16]{3,2,1,0:T(8,128)(2,1)S(1)}, bf16[3,5,16,16]{3,2,1,0:T(8,128)(2,1)S(1)}, u32[]{:S(2)}, u32[]{:S(2)}) collective-permute-start(bf16[3,5,16,16]{3,2,1,0:T(8,128)(2,1)S(1)} %maximum_bitcast_fusion.6), channel_id=1, source_target_pairs={{8,13},{9,12},{10,15},{11,14},{24,29},{25,28},{26,31},{27,30}} | collective-permute-start | bytes 23048 | tf_op jit(solution)/shard_map/ppermute | solution.py:58
  30.5 9.5 %collective-permute-done.10 = bf16[3,5,16,16]{3,2,1,0:T(8,128)(2,1)S(1)} collective-permute-done((bf16[3,5,16,16]{3,2,1,0:T(8,128)(2,1)S(1)}, bf16[3,5,16,16]{3,2,1,0:T(8,128)(2,1)S(1)}, u32[]{:S(2)}, u32[]{:S(2)}) %collective-permute-start.10) | collective-permute-done | bytes 7712 | tf_op jit(solution)/shard_map/ppermute | solution.py:58
  39.9 3.1 %collective-permute-done.11 = bf16[3,5,16,16]{3,2,1,0:T(8,128)(2,1)S(1)} collective-permute-done((bf16[3,5,16,16]{3,2,1,0:T(8,128)(2,1)S(1)}, bf16[3,5,16,16]{3,2,1,0:T(8,128)(2,1)S(1)}, u32[]{:S(2)}, u32[]{:S(2)}) %collective-permute-start.11) | collective-permute-done | bytes 7712 | tf_op jit(solution)/shard_map/ppermute | solution.py:58
  43.1 0.6 %collective-permute-done.9 = bf16[3,5,16,16]{3,2,1,0:T(8,128)(2,1)S(1)} collective-permute-done((bf16[3,5,16,16]{3,2,1,0:T(8,128)(2,1)S(1)}, bf16[3,5,16,16]{3,2,1,0:T(8,128)(2,1)S(1)}, u32[]{:S(2)}, u32[]{:S(2)}) %collective-permute-start.9) | collective-permute-done | bytes 7712 | tf_op jit(solution)/shard_map/ppermute | solution.py:58
  43.7 0.6 %convolution_bitcast_fusion = f32[3,5,16,16]{2,3,0,1:T(8,128)S(1)} fusion(f32[3,16,5,5]{1,3,0,2:T(8,128)S(1)} %copy.19, f32[3,16,64]{2,1,0:T(8,128)S(1)} %convert_bitcast_fusion, bf16[3,5,16,16]{3,2,1,0:T(8,128)(2,1)S(1)} %collective-permute-done.11, bf16[3,5,16,16]{3,2,1,0:T(8,128)(2,1)S(1)} %collective-permute-done.10, ...), kind=kOutput, calls=%fused_computation.9 | convolution fusion | flops 14945280 | bytes 63168 | tf_op jit(solution)/shard_map/kvfp,kvpwe->kwfe/dot_general | solution.py:45
  44.3 0.3 convolution_bitcast_fusion.4
  44.7 3.1 %fusion.2 = f32[16,320]{1,0:T(8,128)S(1)} fusion(bf16[16,320,320]{2,1,0:T(8,128)(2,1)} %bitcast_convert_fusion, f32[16,320]{1,0:T(8,128)S(1)} %select_select_fusion), kind=kLoop, calls=%fused_computation.5 | loop fusion | flops 4910080 | bytes 3317760 | tf_op jit(solution)/shard_map/reduce_sum | solution.py:64
  47.8 0.1 sub.25
  47.9 0.8 %convolution_bitcast_fusion.3 = f32[1,5,64,16]{2,3,1,0:T(8,128)} fusion(f32[16,5,64]{2,1,0:T(8,128)S(1)} %sub.25), kind=kOutput, calls=%fused_computation.12 | convolution fusion | flops 983296 | bytes 40960 | tf_op jit(solution)/shard_map/evi,ef->vfi/dot_general | solution.py:65
  (46 shorter events, 0.8 us)
Async XLA Ops:
  0.0 14.4 %copy-start = (f32[3,64,16]{1,2,0:T(8,128)S(1)}, f32[3,64,16]{1,2,0:T(8,128)}, u32[]{:S(2)}) copy-start(f32[3,64,16]{1,2,0:T(8,128)} %param.9) | copy-start | bytes 36868
  5.0 8.7 %copy-start.2 = (s32[1,3,16]{2,0,1:T(1,128)S(1)}, s32[1,3,16]{2,0,1:T(1,128)}, u32[]{:S(2)}) copy-start(s32[1,3,16]{2,0,1:T(1,128)} %param.8) | copy-start | bytes 580
  5.0 8.7 %copy-start.1 = (f32[1,3,5,5,16]{4,0,3,2,1:T(1,128)S(1)}, f32[1,3,5,5,16]{4,0,3,2,1:T(1,128)}, u32[]{:S(2)}) copy-start(f32[1,3,5,5,16]{4,0,3,2,1:T(1,128)} %param.7) | copy-start | bytes 14404
  5.3 8.5 %collective-permute-start = (bf16[3,5,16,16]{3,2,1,0:T(8,128)(2,1)S(1)}, bf16[3,5,16,16]{3,2,1,0:T(8,128)(2,1)S(1)}, u32[]{:S(2)}, u32[]{:S(2)}) collective-permute-start(bf16[3,5,16,16]{3,2,1,0:T(8,128)(2,1)S(1)} %maximum_bitcast_fusion), channel_id=1, source_target_pairs={{0,4},{1,5},{2,6},{3,7},{16,20},{17,21},{18,22},{19,23}} | collective-permute-start | bytes 23048 | tf_op jit(solution)/shard_map/ppermute | solution.py:58
  6.0 7.8 %collective-permute-start.1 = (bf16[3,5,16,16]{3,2,1,0:T(8,128)(2,1)S(1)}, bf16[3,5,16,16]{3,2,1,0:T(8,128)(2,1)S(1)}, u32[]{:S(2)}, u32[]{:S(2)}) collective-permute-start(bf16[3,5,16,16]{3,2,1,0:T(8,128)(2,1)S(1)} %maximum_bitcast_fusion), channel_id=1, source_target_pairs={{0,5},{1,4},{2,7},{3,6},{16,21},{17,20},{18,23},{19,22}} | collective-permute-start | bytes 23048 | tf_op jit(solution)/shard_map/ppermute | solution.py:58
  6.7 7.2 %collective-permute-start.2 = (bf16[3,5,16,16]{3,2,1,0:T(8,128)(2,1)S(1)}, bf16[3,5,16,16]{3,2,1,0:T(8,128)(2,1)S(1)}, u32[]{:S(2)}, u32[]{:S(2)}) collective-permute-start(bf16[3,5,16,16]{3,2,1,0:T(8,128)(2,1)S(1)} %maximum_bitcast_fusion), channel_id=1, source_target_pairs={{0,6},{1,7},{2,4},{3,5},{16,22},{17,23},{18,20},{19,21}} | collective-permute-start | bytes 23048 | tf_op jit(solution)/shard_map/ppermute | solution.py:58
  7.3 6.5 %collective-permute-start.3 = (bf16[3,5,16,16]{3,2,1,0:T(8,128)(2,1)S(1)}, bf16[3,5,16,16]{3,2,1,0:T(8,128)(2,1)S(1)}, u32[]{:S(2)}, u32[]{:S(2)}) collective-permute-start(bf16[3,5,16,16]{3,2,1,0:T(8,128)(2,1)S(1)} %maximum_bitcast_fusion), channel_id=1, source_target_pairs={{0,7},{1,6},{2,5},{3,4},{16,23},{17,22},{18,21},{19,20}} | collective-permute-start | bytes 23048 | tf_op jit(solution)/shard_map/ppermute | solution.py:58
  18.2 2.7 %collective-permute-start.4 = (bf16[3,5,16,16]{3,2,1,0:T(8,128)(2,1)S(1)}, bf16[3,5,16,16]{3,2,1,0:T(8,128)(2,1)S(1)}, u32[]{:S(2)}, u32[]{:S(2)}) collective-permute-start(bf16[3,5,16,16]{3,2,1,0:T(8,128)(2,1)S(1)} %maximum_bitcast_fusion.3), channel_id=1, source_target_pairs={{4,8},{5,9},{6,10},{7,11},{20,24},{21,25},{22,26},{23,27}} | collective-permute-start | bytes 23048 | tf_op jit(solution)/shard_map/ppermute | solution.py:58
  18.9 2.0 %collective-permute-start.5 = (bf16[3,5,16,16]{3,2,1,0:T(8,128)(2,1)S(1)}, bf16[3,5,16,16]{3,2,1,0:T(8,128)(2,1)S(1)}, u32[]{:S(2)}, u32[]{:S(2)}) collective-permute-start(bf16[3,5,16,16]{3,2,1,0:T(8,128)(2,1)S(1)} %maximum_bitcast_fusion.3), channel_id=1, source_target_pairs={{4,9},{5,8},{6,11},{7,10},{20,25},{21,24},{22,27},{23,26}} | collective-permute-start | bytes 23048 | tf_op jit(solution)/shard_map/ppermute | solution.py:58
  19.5 1.4 %collective-permute-start.6 = (bf16[3,5,16,16]{3,2,1,0:T(8,128)(2,1)S(1)}, bf16[3,5,16,16]{3,2,1,0:T(8,128)(2,1)S(1)}, u32[]{:S(2)}, u32[]{:S(2)}) collective-permute-start(bf16[3,5,16,16]{3,2,1,0:T(8,128)(2,1)S(1)} %maximum_bitcast_fusion.3), channel_id=1, source_target_pairs={{4,10},{5,11},{6,8},{7,9},{20,26},{21,27},{22,24},{23,25}} | collective-permute-start | bytes 23048 | tf_op jit(solution)/shard_map/ppermute | solution.py:58
  20.2 0.7 %collective-permute-start.7 = (bf16[3,5,16,16]{3,2,1,0:T(8,128)(2,1)S(1)}, bf16[3,5,16,16]{3,2,1,0:T(8,128)(2,1)S(1)}, u32[]{:S(2)}, u32[]{:S(2)}) collective-permute-start(bf16[3,5,16,16]{3,2,1,0:T(8,128)(2,1)S(1)} %maximum_bitcast_fusion.3), channel_id=1, source_target_pairs={{4,11},{5,10},{6,9},{7,8},{20,27},{21,26},{22,25},{23,24}} | collective-permute-start | bytes 23048 | tf_op jit(solution)/shard_map/ppermute | solution.py:58
  25.3 14.7 %collective-permute-start.10 = (bf16[3,5,16,16]{3,2,1,0:T(8,128)(2,1)S(1)}, bf16[3,5,16,16]{3,2,1,0:T(8,128)(2,1)S(1)}, u32[]{:S(2)}, u32[]{:S(2)}) collective-permute-start(bf16[3,5,16,16]{3,2,1,0:T(8,128)(2,1)S(1)} %maximum_bitcast_fusion.6), channel_id=1, source_target_pairs={{8,14},{9,15},{10,12},{11,13},{24,30},{25,31},{26,28},{27,29}} | collective-permute-start | bytes 23048 | tf_op jit(solution)/shard_map/ppermute | solution.py:58
  26.6 16.5 %collective-permute-start.11 = (bf16[3,5,16,16]{3,2,1,0:T(8,128)(2,1)S(1)}, bf16[3,5,16,16]{3,2,1,0:T(8,128)(2,1)S(1)}, u32[]{:S(2)}, u32[]{:S(2)}) collective-permute-start(bf16[3,5,16,16]{3,2,1,0:T(8,128)(2,1)S(1)} %maximum_bitcast_fusion.6), channel_id=1, source_target_pairs={{8,15},{9,14},{10,13},{11,12},{24,31},{25,30},{26,29},{27,28}} | collective-permute-start | bytes 23048 | tf_op jit(solution)/shard_map/ppermute | solution.py:58
  27.9 15.2 %collective-permute-start.8 = (bf16[3,5,16,16]{3,2,1,0:T(8,128)(2,1)S(1)}, bf16[3,5,16,16]{3,2,1,0:T(8,128)(2,1)S(1)}, u32[]{:S(2)}, u32[]{:S(2)}) collective-permute-start(bf16[3,5,16,16]{3,2,1,0:T(8,128)(2,1)S(1)} %maximum_bitcast_fusion.6), channel_id=1, source_target_pairs={{8,12},{9,13},{10,14},{11,15},{24,28},{25,29},{26,30},{27,31}} | collective-permute-start | bytes 23048 | tf_op jit(solution)/shard_map/ppermute | solution.py:58
  29.2 14.5 %collective-permute-start.9 = (bf16[3,5,16,16]{3,2,1,0:T(8,128)(2,1)S(1)}, bf16[3,5,16,16]{3,2,1,0:T(8,128)(2,1)S(1)}, u32[]{:S(2)}, u32[]{:S(2)}) collective-permute-start(bf16[3,5,16,16]{3,2,1,0:T(8,128)(2,1)S(1)} %maximum_bitcast_fusion.6), channel_id=1, source_target_pairs={{8,13},{9,12},{10,15},{11,14},{24,29},{25,28},{26,31},{27,30}} | collective-permute-start | bytes 23048 | tf_op jit(solution)/shard_map/ppermute | solution.py:58

commit v12 on v10

--- a/solution.py
+++ b/solution.py
@@ -1,4 +1,5 @@
 import jax
+import numpy as np
 import jax.numpy as jnp
 from jax import lax
 from jax.sharding import PartitionSpec as P
@@ -46,6 +47,11 @@
 
     base = jnp.sum(inv * rhs_t[:, None, :], axis=-1)
     inv_narrow = lax.optimization_barrier(inv.astype(jnp.bfloat16))
+    f = np.arange(FACE)
+    face_nodes = np.stack([48 + f, (f // 4) * 16 + 12 + f % 4, (f // 4) * 16 + (f % 4) * 4 + 3])
+    face_rows = (np.arange(VARS)[None, :, None] * NODES + face_nodes[:, None, :]).reshape(-1)
+    face_inv = lax.optimization_barrier(jnp.take(inv, face_rows, axis=1).astype(jnp.bfloat16))
+    face_base = jnp.take(base, face_rows, axis=1)
     traces = face_traces(base).astype(jnp.bfloat16)
     own_coupling = jnp.zeros((local, BLOCK), jnp.float32)
     for turn in range(1, chains):
@@ -57,8 +63,8 @@
         coupling = coupling_of(jnp.concatenate(blocks, axis=3))
         own_coupling = jnp.where(c == turn, coupling, own_coupling)
         if turn + 1 < chains:
-            approx = base - jnp.sum(inv_narrow.astype(jnp.float32) * coupling[:, None, :], axis=-1)
-            traces = face_traces(approx).astype(jnp.bfloat16)
+            approx = face_base - jnp.sum(face_inv.astype(jnp.float32) * coupling[:, None, :], axis=-1)
+            traces = jnp.transpose(approx.reshape(local, 3, VARS, FACE), (1, 2, 3, 0)).astype(jnp.bfloat16)
     out = base - jnp.sum(inv_narrow.astype(jnp.float32) * own_coupling[:, None, :], axis=-1)
     return jnp.transpose(out.reshape(local, VARS, NODES), (1, 2, 0))[None]
 

time: 49 us -> 57.7 us (1.18)
  local copies, waits for them, and re-layouts: 2.51 us -> 15.6 us
  other arithmetic: 19.3 us -> 12.3 us
  starting transfers between devices: 10.5 us -> 12.3 us
  matrix products: 2.53 us -> 3.41 us
    unnamed x10 -> x11, local copies, waits for them, and re-layouts: 0.06 us -> 9.43 us
    convert_element_type x3 -> x2, other arithmetic: 5.71 us -> 0.04 us  [body(): jnp.transpose(approx.reshape(local, 3, VARS, FACE), (1, 2, 3, 0))]
    reduce_sum x2, other arithmetic: 6.2 us -> 1.37 us  [body(): jnp.sum(face_inv.astype(jnp.float32) * coupling[:, None, :], axis=-1)]
    gather x0 -> x2, local copies, waits for them, and re-layouts: none -> 4.22 us  [the longest x1 3.5 us: body(): jnp.take(inv, face_rows, axis=1).astype(jnp.bfloat16)]
    reduce_sum x1, other arithmetic: 4.14 us -> 7.63 us  [body(): base = jnp.sum(inv * rhs_t[:, None, :], axis=-1)]
    ppermute x12, starting transfers between devices: 10.5 us -> 12.3 us  [body(): blocks[d] = lax.ppermute(traces, ('chain', 'group'), pairs)]
    dot_general x3, matrix products: 1.71 us -> 2.6 us  [coupling_of(): jnp.einsum('kvfp,kvpwe->kwfe', traces_in.astype(jnp.float32), picked_jac,...]
    sub x1, local copies, waits for them, and re-layouts: 0.08 us -> 0.72 us  [body(): base - jnp.sum(inv_narrow.astype(jnp.float32) * own_coupling[:, None, :],...]
  transfers between devices with their start and end apart: 12 -> 12, of which waited for: 3 -> 3; matrix products, arithmetic and copies ran while one was open for 12% -> 24% of each run, Pallas kernels for 0% -> 0%
where the time goes in v12:
time: 57.7 us; the launch traced here: 57.2 us
  local copies, waits for them, and re-layouts  15.6 us (27%)
  waiting for transfers between devices  13.2 us (23%)
  other arithmetic  12.3 us (21%)
  starting transfers between devices  12.3 us (21%)
  matrix products  3.41 us (6%)
    ppermute x12, waiting for transfers between devices, body(): blocks[d] = lax.ppermute(traces, ('chain', 'group'), pairs)  13.2 us
    ppermute x12, starting transfers between devices, body(): blocks[d] = lax.ppermute(traces, ('chain', 'group'), pairs)  12.3 us
    unnamed x11, local copies, waits for them, and re-layouts  9.43 us
    reduce_sum x1, other arithmetic, body(): base = jnp.sum(inv * rhs_t[:, None, :], axis=-1)  7.63 us
    gather x1, local copies, waits for them, and re-layouts, body(): jnp.take(inv, face_rows, axis=1).astype(jnp.bfloat16)  3.5 us
    reduce_sum x1, other arithmetic, body(): jnp.sum(inv_narrow.astype(jnp.float32) * own_coupling[:, None, :], axis=-1)  3.05 us
    dot_general x3, matrix products, coupling_of(): jnp.einsum('kvfp,kvpwe->kwfe', traces_in.astype(jnp.float32), picked_jac,...  2.6 us
    reduce_sum x2, other arithmetic, body(): jnp.sum(face_inv.astype(jnp.float32) * coupling[:, None, :], axis=-1)  1.37 us
  transfers between devices with their start and end apart: 12, of which 3 were waited for; matrix products, arithmetic and copies ran while one was open for 24% of the time, Pallas kernels for 0%

profile of v12, /device:TPU:7, one launch (start us, length us, event | category | flops | bytes accessed | tf_op | source)
XLA Modules:
  0.0 57.2 jit_solution(17678426384975376283)
XLA Ops:
  0.0 0.8 %copy.21 = f32[16,5,64]{2,1,0:T(8,128)S(1)} copy(f32[16,5,64]{2,0,1:T(8,128)} %bitcast.140) | data formatting | bytes 40960 | tf_op jit(solution)/shard_map/transpose | solution.py:35
  0.8 0.1 mul.46
  0.9 7.6 %multiply_reduce_fusion.1 = f32[16,320]{0,1:T(8,128)S(1)} fusion(f32[16,320]{1,0:T(8,128)S(1)} %mul.46, f32[1,16,320,320]{3,2,1,0:T(8,128)} %param.7), kind=kLoop, calls=%fused_computation.4 | loop fusion | flops 3271680 | bytes 6594560 | tf_op jit(solution)/shard_map/reduce_sum | solution.py:48
  8.7 0.7 %collective-permute-start = (bf16[3,5,16,16]{3,2,1,0:T(8,128)(2,1)S(1)}, bf16[3,5,16,16]{3,2,1,0:T(8,128)(2,1)S(1)}, u32[]{:S(2)}, u32[]{:S(2)}) collective-permute-start(bf16[3,5,16,16]{3,2,1,0:T(8,128)(2,1)S(1)} %maximum_bitcast_fusion), channel_id=1, source_target_pairs={{0,4},{1,5},{2,6},{3,7},{16,20},{17,21},{18,22},{19,23}} | collective-permute-start | bytes 23048 | tf_op jit(solution)/shard_map/ppermute | solution.py:62
  9.4 1.3 %collective-permute-start.1 = (bf16[3,5,16,16]{3,2,1,0:T(8,128)(2,1)S(1)}, bf16[3,5,16,16]{3,2,1,0:T(8,128)(2,1)}, u32[]{:S(2)}, u32[]{:S(2)}) collective-permute-start(bf16[3,5,16,16]{3,2,1,0:T(8,128)(2,1)S(1)} %maximum_bitcast_fusion), channel_id=1, source_target_pairs={{0,5},{1,4},{2,7},{3,6},{16,21},{17,20},{18,23},{19,22}} | collective-permute-start | bytes 23048 | tf_op jit(solution)/shard_map/ppermute | solution.py:62
  10.7 1.3 %collective-permute-start.2 = (bf16[3,5,16,16]{3,2,1,0:T(8,128)(2,1)S(1)}, bf16[3,5,16,16]{3,2,1,0:T(8,128)(2,1)}, u32[]{:S(2)}, u32[]{:S(2)}) collective-permute-start(bf16[3,5,16,16]{3,2,1,0:T(8,128)(2,1)S(1)} %maximum_bitcast_fusion), channel_id=1, source_target_pairs={{0,6},{1,7},{2,4},{3,5},{16,22},{17,23},{18,20},{19,21}} | collective-permute-start | bytes 23048 | tf_op jit(solution)/shard_map/ppermute | solution.py:62
  12.0 1.3 %collective-permute-start.3 = (bf16[3,5,16,16]{3,2,1,0:T(8,128)(2,1)S(1)}, bf16[3,5,16,16]{3,2,1,0:T(8,128)(2,1)}, u32[]{:S(2)}, u32[]{:S(2)}) collective-permute-start(bf16[3,5,16,16]{3,2,1,0:T(8,128)(2,1)S(1)} %maximum_bitcast_fusion), channel_id=1, source_target_pairs={{0,7},{1,6},{2,5},{3,4},{16,23},{17,22},{18,21},{19,20}} | collective-permute-start | bytes 23048 | tf_op jit(solution)/shard_map/ppermute | solution.py:62
  13.2 0.1 convert_bitcast_fusion.1
  13.3 9.4 %copy.71 = bf16[1,16,320,320]{3,1,2,0:T(8,128)(2,1)} copy(f32[1,16,320,320]{3,2,1,0:T(8,128)} %param.7) | data formatting | bytes 9830400 | tf_op args[1]
  22.8 0.7 %gather_fusion = f32[240,16]{1,0:T(8,128)S(1)} fusion(f32[16,320]{0,1:T(8,128)S(1)} %multiply_reduce_fusion.1, s32[1024]{0:T(1024)S(1)} %pad_clamp_fusion), kind=kCustom, calls=%fused_computation | custom fusion | bytes 31680 | tf_op jit(solution)/shard_map/jit(_take)/gather | solution.py:54
  23.5 3.5 %gather_fusion.1 = bf16[240,16,320]{2,1,0:T(8,128)(2,1)S(1)} fusion(bf16[16,320,320]{2,0,1:T(8,128)(2,1)} %bitcast.120, s32[1024]{0:T(1024)S(1)} %pad_clamp_fusion), kind=kCustom, calls=%fused_computation.1 | custom fusion | bytes 4916160 | tf_op jit(solution)/shard_map/jit(_take)/gather | solution.py:53
  27.0 1.5 %convolution_bitcast_fusion.2 = f32[3,5,16,16]{2,3,0,1:T(8,128)S(1)} fusion(bf16[3,5,16,16]{3,2,1,0:T(8,128)(2,1)} %collective-permute-done.3, bf16[3,5,16,16]{3,2,1,0:T(8,128)(2,1)} %collective-permute-done.2, bf16[3,5,16,16]{3,2,1,0:T(8,128)(2,1)} %collective-permute-done.1, bf16[3,5,16,16]{3,2,1,0:T(8,128)(2,1)S(1)} %collective-permute-done, ...), kind=kOutput, calls=%fused_computation.12 | convolution fusion | flops 14945280 | bytes 63168 | tf_op jit(solution)/shard_map/kvfp,kvpwe->kwfe/dot_general | solution.py:44
  28.5 0.3 convolution_bitcast_fusion.5
  28.9 0.7 %fusion = f32[16,240]{0,1:T(8,128)S(1)} fusion(bf16[16,240,320]{2,0,1:T(8,128)(2,1)S(1)} %bitcast.122, f32[16,320]{1,0:T(8,128)S(1)} %mul.50), kind=kLoop, calls=%fused_computation.7 | loop fusion | flops 3682560 | bytes 2493440 | tf_op jit(solution)/shard_map/reduce_sum | solution.py:66
  29.6 0.7 %collective-permute-start.4 = (bf16[3,5,16,16]{3,2,1,0:T(8,128)(2,1)S(1)}, bf16[3,5,16,16]{3,2,1,0:T(8,128)(2,1)S(1)}, u32[]{:S(2)}, u32[]{:S(2)}) collective-permute-start(bf16[3,5,16,16]{3,2,1,0:T(8,128)(2,1)S(1)} %bitcast.136), channel_id=1, source_target_pairs={{4,8},{5,9},{6,10},{7,11},{20,24},{21,25},{22,26},{23,27}} | collective-permute-start | bytes 23048 | tf_op jit(solution)/shard_map/ppermute | solution.py:62
  30.3 0.7 %collective-permute-start.5 = (bf16[3,5,16,16]{3,2,1,0:T(8,128)(2,1)S(1)}, bf16[3,5,16,16]{3,2,1,0:T(8,128)(2,1)S(1)}, u32[]{:S(2)}, u32[]{:S(2)}) collective-permute-start(bf16[3,5,16,16]{3,2,1,0:T(8,128)(2,1)S(1)} %bitcast.137), channel_id=1, source_target_pairs={{4,9},{5,8},{6,11},{7,10},{20,25},{21,24},{22,27},{23,26}} | collective-permute-start | bytes 23048 | tf_op jit(solution)/shard_map/ppermute | solution.py:62
  31.0 0.7 %collective-permute-start.6 = (bf16[3,5,16,16]{3,2,1,0:T(8,128)(2,1)S(1)}, bf16[3,5,16,16]{3,2,1,0:T(8,128)(2,1)S(1)}, u32[]{:S(2)}, u32[]{:S(2)}) collective-permute-start(bf16[3,5,16,16]{3,2,1,0:T(8,128)(2,1)S(1)} %bitcast.138), channel_id=1, source_target_pairs={{4,10},{5,11},{6,8},{7,9},{20,26},{21,27},{22,24},{23,25}} | collective-permute-start | bytes 23048 | tf_op jit(solution)/shard_map/ppermute | solution.py:62
  31.6 0.7 %collective-permute-start.7 = (bf16[3,5,16,16]{3,2,1,0:T(8,128)(2,1)S(1)}, bf16[3,5,16,16]{3,2,1,0:T(8,128)(2,1)S(1)}, u32[]{:S(2)}, u32[]{:S(2)}) collective-permute-start(bf16[3,5,16,16]{3,2,1,0:T(8,128)(2,1)S(1)} %bitcast.139), channel_id=1, source_target_pairs={{4,11},{5,10},{6,9},{7,8},{20,27},{21,26},{22,25},{23,24}} | collective-permute-start | bytes 23048 | tf_op jit(solution)/shard_map/ppermute | solution.py:62
  32.3 0.6 %convolution_bitcast_fusion.1 = f32[3,5,16,16]{2,3,0,1:T(8,128)S(1)} fusion(bf16[3,5,16,16]{3,2,1,0:T(8,128)(2,1)S(1)} %collective-permute-done.7, bf16[3,5,16,16]{3,2,1,0:T(8,128)(2,1)S(1)} %collective-permute-done.6, bf16[3,5,16,16]{3,2,1,0:T(8,128)(2,1)S(1)} %collective-permute-done.5, bf16[3,5,16,16]{3,2,1,0:T(8,128)(2,1)S(1)} %collective-permute-done.4, ...), kind=kOutput, calls=%fused_computation.11 | convolution fusion | flops 14945280 | bytes 63168 | tf_op jit(solution)/shard_map/kvfp,kvpwe->kwfe/dot_general | solution.py:44
  32.9 0.3 convolution_bitcast_fusion.4
  33.3 0.7 %fusion.1 = f32[16,240]{0,1:T(8,128)S(1)} fusion(bf16[16,240,320]{2,0,1:T(8,128)(2,1)S(1)} %bitcast.123, f32[16,320]{1,0:T(8,128)S(1)} %mul.53), kind=kLoop, calls=%fused_computation.8 | loop fusion | flops 3682560 | bytes 2493440 | tf_op jit(solution)/shard_map/reduce_sum | solution.py:66
  34.0 1.3 %collective-permute-start.10 = (bf16[3,5,16,16]{3,2,1,0:T(8,128)(2,1)S(1)}, bf16[3,5,16,16]{3,2,1,0:T(8,128)(2,1)S(1)}, u32[]{:S(2)}, u32[]{:S(2)}) collective-permute-start(bf16[3,5,16,16]{3,2,1,0:T(8,128)(2,1)S(1)} %bitcast.132), channel_id=1, source_target_pairs={{8,14},{9,15},{10,12},{11,13},{24,30},{25,31},{26,28},{27,29}} | collective-permute-start | bytes 23048 | tf_op jit(solution)/shard_map/ppermute | solution.py:62
  35.3 1.3 %collective-permute-start.11 = (bf16[3,5,16,16]{3,2,1,0:T(8,128)(2,1)S(1)}, bf16[3,5,16,16]{3,2,1,0:T(8,128)(2,1)S(1)}, u32[]{:S(2)}, u32[]{:S(2)}) collective-permute-start(bf16[3,5,16,16]{3,2,1,0:T(8,128)(2,1)S(1)} %bitcast.133), channel_id=1, source_target_pairs={{8,15},{9,14},{10,13},{11,12},{24,31},{25,30},{26,29},{27,28}} | collective-permute-start | bytes 23048 | tf_op jit(solution)/shard_map/ppermute | solution.py:62
  36.6 1.3 %collective-permute-start.8 = (bf16[3,5,16,16]{3,2,1,0:T(8,128)(2,1)S(1)}, bf16[3,5,16,16]{3,2,1,0:T(8,128)(2,1)S(1)}, u32[]{:S(2)}, u32[]{:S(2)}) collective-permute-start(bf16[3,5,16,16]{3,2,1,0:T(8,128)(2,1)S(1)} %bitcast.134), channel_id=1, source_target_pairs={{8,12},{9,13},{10,14},{11,15},{24,28},{25,29},{26,30},{27,31}} | collective-permute-start | bytes 23048 | tf_op jit(solution)/shard_map/ppermute | solution.py:62
  37.9 1.3 %collective-permute-start.9 = (bf16[3,5,16,16]{3,2,1,0:T(8,128)(2,1)S(1)}, bf16[3,5,16,16]{3,2,1,0:T(8,128)(2,1)S(1)}, u32[]{:S(2)}, u32[]{:S(2)}) collective-permute-start(bf16[3,5,16,16]{3,2,1,0:T(8,128)(2,1)S(1)} %bitcast.135), channel_id=1, source_target_pairs={{8,13},{9,12},{10,15},{11,14},{24,29},{25,28},{26,31},{27,30}} | collective-permute-start | bytes 23048 | tf_op jit(solution)/shard_map/ppermute | solution.py:62
  39.2 9.5 %collective-permute-done.10 = bf16[3,5,16,16]{3,2,1,0:T(8,128)(2,1)S(1)} collective-permute-done((bf16[3,5,16,16]{3,2,1,0:T(8,128)(2,1)S(1)}, bf16[3,5,16,16]{3,2,1,0:T(8,128)(2,1)S(1)}, u32[]{:S(2)}, u32[]{:S(2)}) %collective-permute-start.10) | collective-permute-done | bytes 7712 | tf_op jit(solution)/shard_map/ppermute | solution.py:62
  48.7 3.1 %collective-permute-done.11 = bf16[3,5,16,16]{3,2,1,0:T(8,128)(2,1)S(1)} collective-permute-done((bf16[3,5,16,16]{3,2,1,0:T(8,128)(2,1)S(1)}, bf16[3,5,16,16]{3,2,1,0:T(8,128)(2,1)S(1)}, u32[]{:S(2)}, u32[]{:S(2)}) %collective-permute-start.11) | collective-permute-done | bytes 7712 | tf_op jit(solution)/shard_map/ppermute | solution.py:62
  51.8 0.6 %collective-permute-done.9 = bf16[3,5,16,16]{3,2,1,0:T(8,128)(2,1)S(1)} collective-permute-done((bf16[3,5,16,16]{3,2,1,0:T(8,128)(2,1)S(1)}, bf16[3,5,16,16]{3,2,1,0:T(8,128)(2,1)S(1)}, u32[]{:S(2)}, u32[]{:S(2)}) %collective-permute-start.9) | collective-permute-done | bytes 7712 | tf_op jit(solution)/shard_map/ppermute | solution.py:62
  52.4 0.6 convolution_bitcast_fusion
  53.0 0.3 convolution_bitcast_fusion.3
  53.4 3.1 %multiply_reduce_fusion = f32[16,320]{0,1:T(8,128)S(1)} fusion(bf16[16,320,320]{2,0,1:T(8,128)(2,1)} %bitcast.121, f32[16,320]{1,0:T(8,128)S(1)} %select_select_fusion), kind=kLoop, calls=%fused_computation.3 | loop fusion | flops 4910080 | bytes 3317760 | tf_op jit(solution)/shard_map/reduce_sum | solution.py:68
  56.5 0.7 %copy.33 = f32[16,5,64]{2,0,1:T(8,128)} copy(f32[16,5,64]{0,2,1:T(8,128)S(1)} %bitcast.124) | data formatting | bytes 40960 | tf_op jit(solution)/shard_map/sub | solution.py:68
  (37 shorter events, 0.6 us)
Async XLA Ops:
  0.0 28.5 %copy-start = (f32[3,64,16]{1,2,0:T(8,128)S(1)}, f32[3,64,16]{1,2,0:T(8,128)}, u32[]{:S(2)}) copy-start(f32[3,64,16]{1,2,0:T(8,128)} %param.10) | copy-start | bytes 36868
  0.0 13.3 %copy-start.3 = (s32[240]{0:T(256)S(1)}, s32[240]{0:T(256)}, u32[]{:S(2)}) copy-start(s32[240]{0:T(256)} %constant.88) | copy-start | bytes 2884
  0.0 13.2 %copy-start.2 = (s32[1,3,16]{2,0,1:T(1,128)S(1)}, s32[1,3,16]{2,0,1:T(1,128)}, u32[]{:S(2)}) copy-start(s32[1,3,16]{2,0,1:T(1,128)} %param.9) | copy-start | bytes 580
  8.7 18.3 %collective-permute-start = (bf16[3,5,16,16]{3,2,1,0:T(8,128)(2,1)S(1)}, bf16[3,5,16,16]{3,2,1,0:T(8,128)(2,1)S(1)}, u32[]{:S(2)}, u32[]{:S(2)}) collective-permute-start(bf16[3,5,16,16]{3,2,1,0:T(8,128)(2,1)S(1)} %maximum_bitcast_fusion), channel_id=1, source_target_pairs={{0,4},{1,5},{2,6},{3,7},{16,20},{17,21},{18,22},{19,23}} | collective-permute-start | bytes 23048 | tf_op jit(solution)/shard_map/ppermute | solution.py:62
  9.4 17.6 %collective-permute-start.1 = (bf16[3,5,16,16]{3,2,1,0:T(8,128)(2,1)S(1)}, bf16[3,5,16,16]{3,2,1,0:T(8,128)(2,1)}, u32[]{:S(2)}, u32[]{:S(2)}) collective-permute-start(bf16[3,5,16,16]{3,2,1,0:T(8,128)(2,1)S(1)} %maximum_bitcast_fusion), channel_id=1, source_target_pairs={{0,5},{1,4},{2,7},{3,6},{16,21},{17,20},{18,23},{19,22}} | collective-permute-start | bytes 23048 | tf_op jit(solution)/shard_map/ppermute | solution.py:62
  10.7 16.4 %collective-permute-start.2 = (bf16[3,5,16,16]{3,2,1,0:T(8,128)(2,1)S(1)}, bf16[3,5,16,16]{3,2,1,0:T(8,128)(2,1)}, u32[]{:S(2)}, u32[]{:S(2)}) collective-permute-start(bf16[3,5,16,16]{3,2,1,0:T(8,128)(2,1)S(1)} %maximum_bitcast_fusion), channel_id=1, source_target_pairs={{0,6},{1,7},{2,4},{3,5},{16,22},{17,23},{18,20},{19,21}} | collective-permute-start | bytes 23048 | tf_op jit(solution)/shard_map/ppermute | solution.py:62
  12.0 15.1 %collective-permute-start.3 = (bf16[3,5,16,16]{3,2,1,0:T(8,128)(2,1)S(1)}, bf16[3,5,16,16]{3,2,1,0:T(8,128)(2,1)}, u32[]{:S(2)}, u32[]{:S(2)}) collective-permute-start(bf16[3,5,16,16]{3,2,1,0:T(8,128)(2,1)S(1)} %maximum_bitcast_fusion), channel_id=1, source_target_pairs={{0,7},{1,6},{2,5},{3,4},{16,23},{17,22},{18,21},{19,20}} | collective-permute-start | bytes 23048 | tf_op jit(solution)/shard_map/ppermute | solution.py:62
  13.3 9.4 %copy-start.1 = (f32[1,3,5,5,16]{4,0,3,2,1:T(1,128)S(1)}, f32[1,3,5,5,16]{4,0,3,2,1:T(1,128)}, u32[]{:S(2)}) copy-start(f32[1,3,5,5,16]{4,0,3,2,1:T(1,128)} %param.8) | copy-start | bytes 14404
  29.6 2.7 %collective-permute-start.4 = (bf16[3,5,16,16]{3,2,1,0:T(8,128)(2,1)S(1)}, bf16[3,5,16,16]{3,2,1,0:T(8,128)(2,1)S(1)}, u32[]{:S(2)}, u32[]{:S(2)}) collective-permute-start(bf16[3,5,16,16]{3,2,1,0:T(8,128)(2,1)S(1)} %bitcast.136), channel_id=1, source_target_pairs={{4,8},{5,9},{6,10},{7,11},{20,24},{21,25},{22,26},{23,27}} | collective-permute-start | bytes 23048 | tf_op jit(solution)/shard_map/ppermute | solution.py:62
  30.3 2.0 %collective-permute-start.5 = (bf16[3,5,16,16]{3,2,1,0:T(8,128)(2,1)S(1)}, bf16[3,5,16,16]{3,2,1,0:T(8,128)(2,1)S(1)}, u32[]{:S(2)}, u32[]{:S(2)}) collective-permute-start(bf16[3,5,16,16]{3,2,1,0:T(8,128)(2,1)S(1)} %bitcast.137), channel_id=1, source_target_pairs={{4,9},{5,8},{6,11},{7,10},{20,25},{21,24},{22,27},{23,26}} | collective-permute-start | bytes 23048 | tf_op jit(solution)/shard_map/ppermute | solution.py:62
  31.0 1.4 %collective-permute-start.6 = (bf16[3,5,16,16]{3,2,1,0:T(8,128)(2,1)S(1)}, bf16[3,5,16,16]{3,2,1,0:T(8,128)(2,1)S(1)}, u32[]{:S(2)}, u32[]{:S(2)}) collective-permute-start(bf16[3,5,16,16]{3,2,1,0:T(8,128)(2,1)S(1)} %bitcast.138), channel_id=1, source_target_pairs={{4,10},{5,11},{6,8},{7,9},{20,26},{21,27},{22,24},{23,25}} | collective-permute-start | bytes 23048 | tf_op jit(solution)/shard_map/ppermute | solution.py:62
  31.6 0.7 %collective-permute-start.7 = (bf16[3,5,16,16]{3,2,1,0:T(8,128)(2,1)S(1)}, bf16[3,5,16,16]{3,2,1,0:T(8,128)(2,1)S(1)}, u32[]{:S(2)}, u32[]{:S(2)}) collective-permute-start(bf16[3,5,16,16]{3,2,1,0:T(8,128)(2,1)S(1)} %bitcast.139), channel_id=1, source_target_pairs={{4,11},{5,10},{6,9},{7,8},{20,27},{21,26},{22,25},{23,24}} | collective-permute-start | bytes 23048 | tf_op jit(solution)/shard_map/ppermute | solution.py:62
  34.0 14.7 %collective-permute-start.10 = (bf16[3,5,16,16]{3,2,1,0:T(8,128)(2,1)S(1)}, bf16[3,5,16,16]{3,2,1,0:T(8,128)(2,1)S(1)}, u32[]{:S(2)}, u32[]{:S(2)}) collective-permute-start(bf16[3,5,16,16]{3,2,1,0:T(8,128)(2,1)S(1)} %bitcast.132), channel_id=1, source_target_pairs={{8,14},{9,15},{10,12},{11,13},{24,30},{25,31},{26,28},{27,29}} | collective-permute-start | bytes 23048 | tf_op jit(solution)/shard_map/ppermute | solution.py:62
  35.3 16.5 %collective-permute-start.11 = (bf16[3,5,16,16]{3,2,1,0:T(8,128)(2,1)S(1)}, bf16[3,5,16,16]{3,2,1,0:T(8,128)(2,1)S(1)}, u32[]{:S(2)}, u32[]{:S(2)}) collective-permute-start(bf16[3,5,16,16]{3,2,1,0:T(8,128)(2,1)S(1)} %bitcast.133), channel_id=1, source_target_pairs={{8,15},{9,14},{10,13},{11,12},{24,31},{25,30},{26,29},{27,28}} | collective-permute-start | bytes 23048 | tf_op jit(solution)/shard_map/ppermute | solution.py:62
  36.6 15.2 %collective-permute-start.8 = (bf16[3,5,16,16]{3,2,1,0:T(8,128)(2,1)S(1)}, bf16[3,5,16,16]{3,2,1,0:T(8,128)(2,1)S(1)}, u32[]{:S(2)}, u32[]{:S(2)}) collective-permute-start(bf16[3,5,16,16]{3,2,1,0:T(8,128)(2,1)S(1)} %bitcast.134), channel_id=1, source_target_pairs={{8,12},{9,13},{10,14},{11,15},{24,28},{25,29},{26,30},{27,31}} | collective-permute-start | bytes 23048 | tf_op jit(solution)/shard_map/ppermute | solution.py:62
  37.9 14.5 %collective-permute-start.9 = (bf16[3,5,16,16]{3,2,1,0:T(8,128)(2,1)S(1)}, bf16[3,5,16,16]{3,2,1,0:T(8,128)(2,1)S(1)}, u32[]{:S(2)}, u32[]{:S(2)}) collective-permute-start(bf16[3,5,16,16]{3,2,1,0:T(8,128)(2,1)S(1)} %bitcast.135), channel_id=1, source_target_pairs={{8,13},{9,12},{10,15},{11,14},{24,29},{25,28},{26,31},{27,30}} | collective-permute-start | bytes 23048 | tf_op jit(solution)/shard_map/ppermute | solution.py:62

commit v13 on v10

--- a/solution.py
+++ b/solution.py
@@ -45,7 +45,12 @@
         return coupling.reshape(local, BLOCK)
 
     base = jnp.sum(inv * rhs_t[:, None, :], axis=-1)
-    inv_narrow = lax.optimization_barrier(inv.astype(jnp.bfloat16))
+    inv_narrow = lax.optimization_barrier(
+        jnp.transpose(inv, (1, 0, 2)).astype(jnp.bfloat16).reshape(BLOCK * local, BLOCK))
+
+    def narrow_solve(x):
+        rows = inv_narrow.reshape(BLOCK, local, BLOCK).astype(jnp.float32)
+        return jnp.transpose(jnp.sum(rows * x[None, :, :], axis=-1))
     traces = face_traces(base).astype(jnp.bfloat16)
     own_coupling = jnp.zeros((local, BLOCK), jnp.float32)
     for turn in range(1, chains):
@@ -57,9 +62,9 @@
         coupling = coupling_of(jnp.concatenate(blocks, axis=3))
         own_coupling = jnp.where(c == turn, coupling, own_coupling)
         if turn + 1 < chains:
-            approx = base - jnp.sum(inv_narrow.astype(jnp.float32) * coupling[:, None, :], axis=-1)
+            approx = base - narrow_solve(coupling)
             traces = face_traces(approx).astype(jnp.bfloat16)
-    out = base - jnp.sum(inv_narrow.astype(jnp.float32) * own_coupling[:, None, :], axis=-1)
+    out = base - narrow_solve(own_coupling)
     return jnp.transpose(out.reshape(local, VARS, NODES), (1, 2, 0))[None]
 
 

time: 49 us -> 54.1 us (1.10)
  local copies, waits for them, and re-layouts: 2.51 us -> 9.46 us
  waiting for transfers between devices: 13.2 us -> 11.4 us
    convert_element_type x0 -> x1, local copies, waits for them, and re-layouts: none -> 6.33 us  [body(): jnp.transpose(inv, (1, 0, 2)).astype(jnp.bfloat16)]
    ppermute x12, waiting for transfers between devices: 13.2 us -> 11.4 us  [body(): blocks[d] = lax.ppermute(traces, ('chain', 'group'), pairs)]
    reduce_sum x0 -> x6, local copies, waits for them, and re-layouts: none -> 0.54 us  [narrow_solve(): return jnp.transpose(jnp.sum(rows * x[None, :, :], axis=-1))]
  transfers between devices with their start and end apart: 12 -> 12, of which waited for: 3 -> 3; matrix products, arithmetic and copies ran while one was open for 12% -> 23% of each run, Pallas kernels for 0% -> 0%
where the time goes in v13:
time: 54.1 us; the launch traced here: 53.5 us
  other arithmetic  19.2 us (35%)
  waiting for transfers between devices  11.4 us (21%)
  starting transfers between devices  10.5 us (19%)
  local copies, waits for them, and re-layouts  9.46 us (17%)
  matrix products  2.53 us (5%)
    ppermute x12, waiting for transfers between devices, body(): blocks[d] = lax.ppermute(traces, ('chain', 'group'), pairs)  11.4 us
    ppermute x12, starting transfers between devices, body(): blocks[d] = lax.ppermute(traces, ('chain', 'group'), pairs)  10.5 us
    reduce_sum x3, other arithmetic, narrow_solve(): return jnp.transpose(jnp.sum(rows * x[None, :, :], axis=-1))  9.16 us
    convert_element_type x1, local copies, waits for them, and re-layouts, body(): jnp.transpose(inv, (1, 0, 2)).astype(jnp.bfloat16)  6.33 us
    convert_element_type x1, other arithmetic, body(): jnp.transpose(inv, (1, 0, 2)).astype(jnp.bfloat16)  5.67 us
    reduce_sum x1, other arithmetic, body(): base = jnp.sum(inv * rhs_t[:, None, :], axis=-1)  4.14 us
    dot_general x3, matrix products, coupling_of(): jnp.einsum('kvfp,kvpwe->kwfe', traces_in.astype(jnp.float32), picked_jac,...  1.71 us
  transfers between devices with their start and end apart: 12, of which 3 were waited for; matrix products, arithmetic and copies ran while one was open for 23% of the time, Pallas kernels for 0%

profile of v13, /device:TPU:7, one launch (start us, length us, event | category | flops | bytes accessed | tf_op | source)
XLA Modules:
  0.0 53.5 jit_solution(11820280610326937900)
XLA Ops:
  0.0 0.8 %copy.18 = f32[16,5,64]{2,1,0:T(8,128)S(1)} copy(f32[16,5,64]{2,0,1:T(8,128)} %bitcast.152) | data formatting | bytes 40960 | tf_op jit(solution)/shard_map/transpose | solution.py:34
  0.9 4.1 %fusion.3 = f32[16,320]{1,0:T(8,128)S(1)} fusion(f32[1,16,320,320]{3,2,1,0:T(8,128)} %param.6, f32[16,320]{1,0:T(8,128)S(1)} %mul.55), kind=kLoop, calls=%fused_computation.8 | loop fusion | flops 3271680 | bytes 6594560 | tf_op jit(solution)/shard_map/reduce_sum | solution.py:47
  5.1 0.1 copy.22
  5.3 0.7 %collective-permute-start.3 = (bf16[3,5,16,16]{3,2,1,0:T(8,128)(2,1)S(1)}, bf16[3,5,16,16]{3,2,1,0:T(8,128)(2,1)S(1)}, u32[]{:S(2)}, u32[]{:S(2)}) collective-permute-start(bf16[3,5,16,16]{3,2,1,0:T(8,128)(2,1)S(1)} %maximum_bitcast_fusion), channel_id=1, source_target_pairs={{0,7},{1,6},{2,5},{3,4},{16,23},{17,22},{18,21},{19,20}} | collective-permute-start | bytes 23048 | tf_op jit(solution)/shard_map/ppermute | solution.py:61
  6.0 0.7 %collective-permute-start.2 = (bf16[3,5,16,16]{3,2,1,0:T(8,128)(2,1)S(1)}, bf16[3,5,16,16]{3,2,1,0:T(8,128)(2,1)S(1)}, u32[]{:S(2)}, u32[]{:S(2)}) collective-permute-start(bf16[3,5,16,16]{3,2,1,0:T(8,128)(2,1)S(1)} %maximum_bitcast_fusion), channel_id=1, source_target_pairs={{0,6},{1,7},{2,4},{3,5},{16,22},{17,23},{18,20},{19,21}} | collective-permute-start | bytes 23048 | tf_op jit(solution)/shard_map/ppermute | solution.py:61
  6.7 0.7 %collective-permute-start.1 = (bf16[3,5,16,16]{3,2,1,0:T(8,128)(2,1)S(1)}, bf16[3,5,16,16]{3,2,1,0:T(8,128)(2,1)S(1)}, u32[]{:S(2)}, u32[]{:S(2)}) collective-permute-start(bf16[3,5,16,16]{3,2,1,0:T(8,128)(2,1)S(1)} %maximum_bitcast_fusion), channel_id=1, source_target_pairs={{0,5},{1,4},{2,7},{3,6},{16,21},{17,20},{18,23},{19,22}} | collective-permute-start | bytes 23048 | tf_op jit(solution)/shard_map/ppermute | solution.py:61
  7.3 0.7 %collective-permute-start = (bf16[3,5,16,16]{3,2,1,0:T(8,128)(2,1)S(1)}, bf16[3,5,16,16]{3,2,1,0:T(8,128)(2,1)S(1)}, u32[]{:S(2)}, u32[]{:S(2)}) collective-permute-start(bf16[3,5,16,16]{3,2,1,0:T(8,128)(2,1)S(1)} %maximum_bitcast_fusion), channel_id=1, source_target_pairs={{0,4},{1,5},{2,6},{3,7},{16,20},{17,21},{18,22},{19,23}} | collective-permute-start | bytes 23048 | tf_op jit(solution)/shard_map/ppermute | solution.py:61
  8.0 5.7 %fusion.4 = bf16[320,16,320]{2,0,1:T(8,128)(2,1)} fusion(f32[1,16,320,320]{3,2,1,0:T(8,128)} %param.6), kind=kLoop, calls=%fused_computation.9 | loop fusion | flops 1638400 | bytes 9830400 | tf_op jit(solution)/shard_map/convert_element_type | solution.py:49
  13.8 6.3 %copy.19 = bf16[320,16,320]{2,1,0:T(8,128)(2,1)} copy(bf16[320,16,320]{2,0,1:T(8,128)(2,1)} %fusion.4) | data formatting | bytes 6553600 | tf_op jit(solution)/shard_map/convert_element_type | solution.py:49
  20.2 0.6 %convolution_bitcast_fusion.2 = f32[3,5,16,16]{2,3,0,1:T(8,128)S(1)} fusion(f32[3,16,5,5]{1,3,0,2:T(8,128)S(1)} %copy.21, f32[3,16,64]{2,1,0:T(8,128)S(1)} %convert_bitcast_fusion, bf16[3,5,16,16]{3,2,1,0:T(8,128)(2,1)S(1)} %collective-permute-done.3, bf16[3,5,16,16]{3,2,1,0:T(8,128)(2,1)S(1)} %collective-permute-done.2, ...), kind=kOutput, calls=%fused_computation.12 | convolution fusion | flops 14945280 | bytes 63168 | tf_op jit(solution)/shard_map/kvfp,kvpwe->kwfe/dot_general | solution.py:43
  20.8 0.3 convolution_bitcast_fusion.5
  21.2 3.0 %fusion = f32[5120]{0:T(1024)S(1)} fusion(bf16[5120,320]{1,0:T(8,128)(2,1)} %bitcast.129, f32[16,320]{1,0:T(8,128)S(1)} %mul.59), kind=kLoop, calls=%fused_computation.3 | loop fusion | flops 4910080 | bytes 3317760 | tf_op jit(solution)/shard_map/reduce_sum | solution.py:53
  24.4 0.1 copy.25
  24.7 0.7 %collective-permute-start.7 = (bf16[3,5,16,16]{3,2,1,0:T(8,128)(2,1)S(1)}, bf16[3,5,16,16]{3,2,1,0:T(8,128)(2,1)S(1)}, u32[]{:S(2)}, u32[]{:S(2)}) collective-permute-start(bf16[3,5,16,16]{3,2,1,0:T(8,128)(2,1)S(1)} %maximum_bitcast_fusion.3), channel_id=1, source_target_pairs={{4,11},{5,10},{6,9},{7,8},{20,27},{21,26},{22,25},{23,24}} | collective-permute-start | bytes 23048 | tf_op jit(solution)/shard_map/ppermute | solution.py:61
  25.4 0.7 %collective-permute-start.6 = (bf16[3,5,16,16]{3,2,1,0:T(8,128)(2,1)S(1)}, bf16[3,5,16,16]{3,2,1,0:T(8,128)(2,1)S(1)}, u32[]{:S(2)}, u32[]{:S(2)}) collective-permute-start(bf16[3,5,16,16]{3,2,1,0:T(8,128)(2,1)S(1)} %maximum_bitcast_fusion.3), channel_id=1, source_target_pairs={{4,10},{5,11},{6,8},{7,9},{20,26},{21,27},{22,24},{23,25}} | collective-permute-start | bytes 23048 | tf_op jit(solution)/shard_map/ppermute | solution.py:61
  26.0 0.7 %collective-permute-start.5 = (bf16[3,5,16,16]{3,2,1,0:T(8,128)(2,1)S(1)}, bf16[3,5,16,16]{3,2,1,0:T(8,128)(2,1)S(1)}, u32[]{:S(2)}, u32[]{:S(2)}) collective-permute-start(bf16[3,5,16,16]{3,2,1,0:T(8,128)(2,1)S(1)} %maximum_bitcast_fusion.3), channel_id=1, source_target_pairs={{4,9},{5,8},{6,11},{7,10},{20,25},{21,24},{22,27},{23,26}} | collective-permute-start | bytes 23048 | tf_op jit(solution)/shard_map/ppermute | solution.py:61
  26.7 0.7 %collective-permute-start.4 = (bf16[3,5,16,16]{3,2,1,0:T(8,128)(2,1)S(1)}, bf16[3,5,16,16]{3,2,1,0:T(8,128)(2,1)S(1)}, u32[]{:S(2)}, u32[]{:S(2)}) collective-permute-start(bf16[3,5,16,16]{3,2,1,0:T(8,128)(2,1)S(1)} %maximum_bitcast_fusion.3), channel_id=1, source_target_pairs={{4,8},{5,9},{6,10},{7,11},{20,24},{21,25},{22,26},{23,27}} | collective-permute-start | bytes 23048 | tf_op jit(solution)/shard_map/ppermute | solution.py:61
  27.4 0.6 %convolution_bitcast_fusion.1 = f32[3,5,16,16]{2,3,0,1:T(8,128)S(1)} fusion(f32[3,16,5,5]{1,3,0,2:T(8,128)S(1)} %copy.21, f32[3,16,64]{2,1,0:T(8,128)S(1)} %convert_bitcast_fusion, bf16[3,5,16,16]{3,2,1,0:T(8,128)(2,1)S(1)} %collective-permute-done.7, bf16[3,5,16,16]{3,2,1,0:T(8,128)(2,1)S(1)} %collective-permute-done.6, ...), kind=kOutput, calls=%fused_computation.11 | convolution fusion | flops 14945280 | bytes 63168 | tf_op jit(solution)/shard_map/kvfp,kvpwe->kwfe/dot_general | solution.py:43
  28.0 0.3 convolution_bitcast_fusion.4
  28.4 3.1 %fusion.1 = f32[5120]{0:T(1024)S(1)} fusion(bf16[5120,320]{1,0:T(8,128)(2,1)} %bitcast.130, f32[16,320]{1,0:T(8,128)S(1)} %mul.63), kind=kLoop, calls=%fused_computation.4 | loop fusion | flops 4910080 | bytes 3317760 | tf_op jit(solution)/shard_map/reduce_sum | solution.py:53
  31.7 0.1 copy.28
  31.9 1.3 %collective-permute-start.11 = (bf16[3,5,16,16]{3,2,1,0:T(8,128)(2,1)S(1)}, bf16[3,5,16,16]{3,2,1,0:T(8,128)(2,1)S(1)}, u32[]{:S(2)}, u32[]{:S(2)}) collective-permute-start(bf16[3,5,16,16]{3,2,1,0:T(8,128)(2,1)S(1)} %maximum_bitcast_fusion.6), channel_id=1, source_target_pairs={{8,15},{9,14},{10,13},{11,12},{24,31},{25,30},{26,29},{27,28}} | collective-permute-start | bytes 23048 | tf_op jit(solution)/shard_map/ppermute | solution.py:61
  33.2 1.3 %collective-permute-start.10 = (bf16[3,5,16,16]{3,2,1,0:T(8,128)(2,1)S(1)}, bf16[3,5,16,16]{3,2,1,0:T(8,128)(2,1)S(1)}, u32[]{:S(2)}, u32[]{:S(2)}) collective-permute-start(bf16[3,5,16,16]{3,2,1,0:T(8,128)(2,1)S(1)} %maximum_bitcast_fusion.6), channel_id=1, source_target_pairs={{8,14},{9,15},{10,12},{11,13},{24,30},{25,31},{26,28},{27,29}} | collective-permute-start | bytes 23048 | tf_op jit(solution)/shard_map/ppermute | solution.py:61
  34.5 1.3 %collective-permute-start.9 = (bf16[3,5,16,16]{3,2,1,0:T(8,128)(2,1)S(1)}, bf16[3,5,16,16]{3,2,1,0:T(8,128)(2,1)S(1)}, u32[]{:S(2)}, u32[]{:S(2)}) collective-permute-start(bf16[3,5,16,16]{3,2,1,0:T(8,128)(2,1)S(1)} %maximum_bitcast_fusion.6), channel_id=1, source_target_pairs={{8,13},{9,12},{10,15},{11,14},{24,29},{25,28},{26,31},{27,30}} | collective-permute-start | bytes 23048 | tf_op jit(solution)/shard_map/ppermute | solution.py:61
  35.8 1.3 %collective-permute-start.8 = (bf16[3,5,16,16]{3,2,1,0:T(8,128)(2,1)S(1)}, bf16[3,5,16,16]{3,2,1,0:T(8,128)(2,1)S(1)}, u32[]{:S(2)}, u32[]{:S(2)}) collective-permute-start(bf16[3,5,16,16]{3,2,1,0:T(8,128)(2,1)S(1)} %maximum_bitcast_fusion.6), channel_id=1, source_target_pairs={{8,12},{9,13},{10,14},{11,15},{24,28},{25,29},{26,30},{27,31}} | collective-permute-start | bytes 23048 | tf_op jit(solution)/shard_map/ppermute | solution.py:61
  37.2 9.4 %collective-permute-done.11 = bf16[3,5,16,16]{3,2,1,0:T(8,128)(2,1)S(1)} collective-permute-done((bf16[3,5,16,16]{3,2,1,0:T(8,128)(2,1)S(1)}, bf16[3,5,16,16]{3,2,1,0:T(8,128)(2,1)S(1)}, u32[]{:S(2)}, u32[]{:S(2)}) %collective-permute-start.11) | collective-permute-done | bytes 7712 | tf_op jit(solution)/shard_map/ppermute | solution.py:61
  46.5 0.7 %collective-permute-done.10 = bf16[3,5,16,16]{3,2,1,0:T(8,128)(2,1)S(1)} collective-permute-done((bf16[3,5,16,16]{3,2,1,0:T(8,128)(2,1)S(1)}, bf16[3,5,16,16]{3,2,1,0:T(8,128)(2,1)S(1)}, u32[]{:S(2)}, u32[]{:S(2)}) %collective-permute-start.10) | collective-permute-done | bytes 7712 | tf_op jit(solution)/shard_map/ppermute | solution.py:61
  47.2 1.4 %collective-permute-done.9 = bf16[3,5,16,16]{3,2,1,0:T(8,128)(2,1)S(1)} collective-permute-done((bf16[3,5,16,16]{3,2,1,0:T(8,128)(2,1)S(1)}, bf16[3,5,16,16]{3,2,1,0:T(8,128)(2,1)S(1)}, u32[]{:S(2)}, u32[]{:S(2)}) %collective-permute-start.9) | collective-permute-done | bytes 7712 | tf_op jit(solution)/shard_map/ppermute | solution.py:61
  48.6 0.6 %convolution_bitcast_fusion = f32[3,5,16,16]{2,3,0,1:T(8,128)S(1)} fusion(f32[3,16,5,5]{1,3,0,2:T(8,128)S(1)} %copy.21, f32[3,16,64]{2,1,0:T(8,128)S(1)} %convert_bitcast_fusion, bf16[3,5,16,16]{3,2,1,0:T(8,128)(2,1)S(1)} %collective-permute-done.11, bf16[3,5,16,16]{3,2,1,0:T(8,128)(2,1)S(1)} %collective-permute-done.10, ...), kind=kOutput, calls=%fused_computation.10 | convolution fusion | flops 14945280 | bytes 63168 | tf_op jit(solution)/shard_map/kvfp,kvpwe->kwfe/dot_general | solution.py:43
  49.2 0.3 convolution_bitcast_fusion.3
  49.5 3.1 %fusion.2 = f32[5120]{0:T(1024)S(1)} fusion(bf16[5120,320]{1,0:T(8,128)(2,1)} %bitcast.131, f32[16,320]{1,0:T(8,128)S(1)} %select_select_fusion), kind=kLoop, calls=%fused_computation.5 | loop fusion | flops 4910080 | bytes 3317760 | tf_op jit(solution)/shard_map/reduce_sum | solution.py:53
  52.9 0.6 %copy.31 = f32[1,5,64,16]{2,3,1,0:T(8,128)} copy(f32[1,5,64,16]{2,1,3,0:T(8,128)S(1)} %bitcast.141) | data formatting | bytes 40960 | tf_op jit(solution)/shard_map/broadcast_in_dim | solution.py:68
  (53 shorter events, 1.5 us)
Async XLA Ops:
  0.0 20.8 %copy-start = (f32[3,64,16]{1,2,0:T(8,128)S(1)}, f32[3,64,16]{1,2,0:T(8,128)}, u32[]{:S(2)}) copy-start(f32[3,64,16]{1,2,0:T(8,128)} %param.9) | copy-start | bytes 36868
  5.0 8.7 %copy-start.2 = (s32[1,3,16]{2,0,1:T(1,128)S(1)}, s32[1,3,16]{2,0,1:T(1,128)}, u32[]{:S(2)}) copy-start(s32[1,3,16]{2,0,1:T(1,128)} %param.8) | copy-start | bytes 580
  5.3 14.8 %copy-start.1 = (f32[1,3,5,5,16]{4,0,3,2,1:T(1,128)S(1)}, f32[1,3,5,5,16]{4,0,3,2,1:T(1,128)}, u32[]{:S(2)}) copy-start(f32[1,3,5,5,16]{4,0,3,2,1:T(1,128)} %param.7) | copy-start | bytes 14404
  5.3 14.8 %collective-permute-start.3 = (bf16[3,5,16,16]{3,2,1,0:T(8,128)(2,1)S(1)}, bf16[3,5,16,16]{3,2,1,0:T(8,128)(2,1)S(1)}, u32[]{:S(2)}, u32[]{:S(2)}) collective-permute-start(bf16[3,5,16,16]{3,2,1,0:T(8,128)(2,1)S(1)} %maximum_bitcast_fusion), channel_id=1, source_target_pairs={{0,7},{1,6},{2,5},{3,4},{16,23},{17,22},{18,21},{19,20}} | collective-permute-start | bytes 23048 | tf_op jit(solution)/shard_map/ppermute | solution.py:61
  6.0 14.2 %collective-permute-start.2 = (bf16[3,5,16,16]{3,2,1,0:T(8,128)(2,1)S(1)}, bf16[3,5,16,16]{3,2,1,0:T(8,128)(2,1)S(1)}, u32[]{:S(2)}, u32[]{:S(2)}) collective-permute-start(bf16[3,5,16,16]{3,2,1,0:T(8,128)(2,1)S(1)} %maximum_bitcast_fusion), channel_id=1, source_target_pairs={{0,6},{1,7},{2,4},{3,5},{16,22},{17,23},{18,20},{19,21}} | collective-permute-start | bytes 23048 | tf_op jit(solution)/shard_map/ppermute | solution.py:61
  6.7 13.5 %collective-permute-start.1 = (bf16[3,5,16,16]{3,2,1,0:T(8,128)(2,1)S(1)}, bf16[3,5,16,16]{3,2,1,0:T(8,128)(2,1)S(1)}, u32[]{:S(2)}, u32[]{:S(2)}) collective-permute-start(bf16[3,5,16,16]{3,2,1,0:T(8,128)(2,1)S(1)} %maximum_bitcast_fusion), channel_id=1, source_target_pairs={{0,5},{1,4},{2,7},{3,6},{16,21},{17,20},{18,23},{19,22}} | collective-permute-start | bytes 23048 | tf_op jit(solution)/shard_map/ppermute | solution.py:61
  7.3 12.8 %collective-permute-start = (bf16[3,5,16,16]{3,2,1,0:T(8,128)(2,1)S(1)}, bf16[3,5,16,16]{3,2,1,0:T(8,128)(2,1)S(1)}, u32[]{:S(2)}, u32[]{:S(2)}) collective-permute-start(bf16[3,5,16,16]{3,2,1,0:T(8,128)(2,1)S(1)} %maximum_bitcast_fusion), channel_id=1, source_target_pairs={{0,4},{1,5},{2,6},{3,7},{16,20},{17,21},{18,22},{19,23}} | collective-permute-start | bytes 23048 | tf_op jit(solution)/shard_map/ppermute | solution.py:61
  24.7 2.7 %collective-permute-start.7 = (bf16[3,5,16,16]{3,2,1,0:T(8,128)(2,1)S(1)}, bf16[3,5,16,16]{3,2,1,0:T(8,128)(2,1)S(1)}, u32[]{:S(2)}, u32[]{:S(2)}) collective-permute-start(bf16[3,5,16,16]{3,2,1,0:T(8,128)(2,1)S(1)} %maximum_bitcast_fusion.3), channel_id=1, source_target_pairs={{4,11},{5,10},{6,9},{7,8},{20,27},{21,26},{22,25},{23,24}} | collective-permute-start | bytes 23048 | tf_op jit(solution)/shard_map/ppermute | solution.py:61
  25.4 2.0 %collective-permute-start.6 = (bf16[3,5,16,16]{3,2,1,0:T(8,128)(2,1)S(1)}, bf16[3,5,16,16]{3,2,1,0:T(8,128)(2,1)S(1)}, u32[]{:S(2)}, u32[]{:S(2)}) collective-permute-start(bf16[3,5,16,16]{3,2,1,0:T(8,128)(2,1)S(1)} %maximum_bitcast_fusion.3), channel_id=1, source_target_pairs={{4,10},{5,11},{6,8},{7,9},{20,26},{21,27},{22,24},{23,25}} | collective-permute-start | bytes 23048 | tf_op jit(solution)/shard_map/ppermute | solution.py:61
  26.0 1.4 %collective-permute-start.5 = (bf16[3,5,16,16]{3,2,1,0:T(8,128)(2,1)S(1)}, bf16[3,5,16,16]{3,2,1,0:T(8,128)(2,1)S(1)}, u32[]{:S(2)}, u32[]{:S(2)}) collective-permute-start(bf16[3,5,16,16]{3,2,1,0:T(8,128)(2,1)S(1)} %maximum_bitcast_fusion.3), channel_id=1, source_target_pairs={{4,9},{5,8},{6,11},{7,10},{20,25},{21,24},{22,27},{23,26}} | collective-permute-start | bytes 23048 | tf_op jit(solution)/shard_map/ppermute | solution.py:61
  26.7 0.7 %collective-permute-start.4 = (bf16[3,5,16,16]{3,2,1,0:T(8,128)(2,1)S(1)}, bf16[3,5,16,16]{3,2,1,0:T(8,128)(2,1)S(1)}, u32[]{:S(2)}, u32[]{:S(2)}) collective-permute-start(bf16[3,5,16,16]{3,2,1,0:T(8,128)(2,1)S(1)} %maximum_bitcast_fusion.3), channel_id=1, source_target_pairs={{4,8},{5,9},{6,10},{7,11},{20,24},{21,25},{22,26},{23,27}} | collective-permute-start | bytes 23048 | tf_op jit(solution)/shard_map/ppermute | solution.py:61
  31.9 14.6 %collective-permute-start.11 = (bf16[3,5,16,16]{3,2,1,0:T(8,128)(2,1)S(1)}, bf16[3,5,16,16]{3,2,1,0:T(8,128)(2,1)S(1)}, u32[]{:S(2)}, u32[]{:S(2)}) collective-permute-start(bf16[3,5,16,16]{3,2,1,0:T(8,128)(2,1)S(1)} %maximum_bitcast_fusion.6), channel_id=1, source_target_pairs={{8,15},{9,14},{10,13},{11,12},{24,31},{25,30},{26,29},{27,28}} | collective-permute-start | bytes 23048 | tf_op jit(solution)/shard_map/ppermute | solution.py:61
  33.2 13.9 %collective-permute-start.10 = (bf16[3,5,16,16]{3,2,1,0:T(8,128)(2,1)S(1)}, bf16[3,5,16,16]{3,2,1,0:T(8,128)(2,1)S(1)}, u32[]{:S(2)}, u32[]{:S(2)}) collective-permute-start(bf16[3,5,16,16]{3,2,1,0:T(8,128)(2,1)S(1)} %maximum_bitcast_fusion.6), channel_id=1, source_target_pairs={{8,14},{9,15},{10,12},{11,13},{24,30},{25,31},{26,28},{27,29}} | collective-permute-start | bytes 23048 | tf_op jit(solution)/shard_map/ppermute | solution.py:61
  34.5 14.0 %collective-permute-start.9 = (bf16[3,5,16,16]{3,2,1,0:T(8,128)(2,1)S(1)}, bf16[3,5,16,16]{3,2,1,0:T(8,128)(2,1)S(1)}, u32[]{:S(2)}, u32[]{:S(2)}) collective-permute-start(bf16[3,5,16,16]{3,2,1,0:T(8,128)(2,1)S(1)} %maximum_bitcast_fusion.6), channel_id=1, source_target_pairs={{8,13},{9,12},{10,15},{11,14},{24,29},{25,28},{26,31},{27,30}} | collective-permute-start | bytes 23048 | tf_op jit(solution)/shard_map/ppermute | solution.py:61
  35.8 12.7 %collective-permute-start.8 = (bf16[3,5,16,16]{3,2,1,0:T(8,128)(2,1)S(1)}, bf16[3,5,16,16]{3,2,1,0:T(8,128)(2,1)S(1)}, u32[]{:S(2)}, u32[]{:S(2)}) collective-permute-start(bf16[3,5,16,16]{3,2,1,0:T(8,128)(2,1)S(1)} %maximum_bitcast_fusion.6), channel_id=1, source_target_pairs={{8,12},{9,13},{10,14},{11,15},{24,28},{25,29},{26,30},{27,31}} | collective-permute-start | bytes 23048 | tf_op jit(solution)/shard_map/ppermute | solution.py:61

commit v14 on v10

--- a/solution.py
+++ b/solution.py
@@ -1,4 +1,5 @@
 import jax
+import numpy as np
 import jax.numpy as jnp
 from jax import lax
 from jax.sharding import PartitionSpec as P
@@ -48,7 +49,15 @@
     inv_narrow = lax.optimization_barrier(inv.astype(jnp.bfloat16))
     traces = face_traces(base).astype(jnp.bfloat16)
     own_coupling = jnp.zeros((local, BLOCK), jnp.float32)
+    f = np.arange(FACE)
+    face_nodes = np.stack([48 + f, (f // 4) * 16 + 12 + f % 4, (f // 4) * 16 + (f % 4) * 4 + 3])
+    face_rows = (np.arange(VARS)[None, :, None] * NODES + face_nodes[:, None, :]).reshape(-1)
+    face_base = jnp.transpose(face_traces(base), (3, 0, 1, 2)).reshape(local, 3 * VARS * FACE)
+    face_inv = None
     for turn in range(1, chains):
+        if face_inv is None and turn >= 2 and turn + 1 < chains:
+            narrow_now, _ = lax.optimization_barrier((inv_narrow, traces))
+            face_inv = lax.optimization_barrier(jnp.take(narrow_now, face_rows, axis=1))
         blocks = [None] * groups
         for d in reversed(range(groups)):
             pairs = [((turn - 1) * groups + s, turn * groups + ((s ^ d) if xor_pairs else (s + d) % groups))
@@ -57,8 +66,12 @@
         coupling = coupling_of(jnp.concatenate(blocks, axis=3))
         own_coupling = jnp.where(c == turn, coupling, own_coupling)
         if turn + 1 < chains:
-            approx = base - jnp.sum(inv_narrow.astype(jnp.float32) * coupling[:, None, :], axis=-1)
-            traces = face_traces(approx).astype(jnp.bfloat16)
+            if face_inv is None:
+                approx = base - jnp.sum(inv_narrow.astype(jnp.float32) * coupling[:, None, :], axis=-1)
+                traces = face_traces(approx).astype(jnp.bfloat16)
+            else:
+                approx = face_base - jnp.sum(face_inv.astype(jnp.float32) * coupling[:, None, :], axis=-1)
+                traces = jnp.transpose(approx.reshape(local, 3, VARS, FACE), (1, 2, 3, 0)).astype(jnp.bfloat16)
     out = base - jnp.sum(inv_narrow.astype(jnp.float32) * own_coupling[:, None, :], axis=-1)
     return jnp.transpose(out.reshape(local, VARS, NODES), (1, 2, 0))[None]
 

time: 49 us -> 55.4 us (1.13)
  local copies, waits for them, and re-layouts: 2.51 us -> 15 us
  other arithmetic: 19.3 us -> 14.6 us
  waiting for transfers between devices: 13.2 us -> 9.12 us
  starting transfers between devices: 10.5 us -> 12.3 us
  matrix products: 2.53 us -> 3.41 us
    unnamed x10 -> x11, local copies, waits for them, and re-layouts: 0.06 us -> 9.43 us
    convert_element_type x1, other arithmetic: 5.67 us -> 0.02 us  [body(): jnp.transpose(approx.reshape(local, 3, VARS, FACE), (1, 2, 3, 0))]
    ppermute x12, waiting for transfers between devices: 13.2 us -> 9.12 us  [body(): blocks[d] = lax.ppermute(traces, ('chain', 'group'), pairs)]
    gather x0 -> x1, local copies, waits for them, and re-layouts: none -> 3.5 us  [body(): face_inv = lax.optimization_barrier(jnp.take(narrow_now, face_rows, axis=1))]
    reduce_sum x1, other arithmetic: 4.14 us -> 7.63 us  [body(): base = jnp.sum(inv * rhs_t[:, None, :], axis=-1)]
    reduce_sum x2 -> x1, other arithmetic: 6.2 us -> 3.04 us  [body(): jnp.sum(inv_narrow.astype(jnp.float32) * coupling[:, None, :], axis=-1)]
    ppermute x12, starting transfers between devices: 10.5 us -> 12.3 us  [body(): blocks[d] = lax.ppermute(traces, ('chain', 'group'), pairs)]
    dot_general x3, matrix products: 1.71 us -> 2.59 us  [coupling_of(): jnp.einsum('kvfp,kvpwe->kwfe', traces_in.astype(jnp.float32), picked_jac,...]
  transfers between devices with their start and end apart: 12 -> 12, of which waited for: 3 -> 3; matrix products, arithmetic and copies ran while one was open for 12% -> 24% of each run, Pallas kernels for 0% -> 0%
where the time goes in v14:
time: 55.4 us; the launch traced here: 54.9 us
  local copies, waits for them, and re-layouts  15 us (27%)
  other arithmetic  14.6 us (26%)
  starting transfers between devices  12.3 us (22%)
  waiting for transfers between devices  9.12 us (16%)
  matrix products  3.41 us (6%)
    ppermute x12, starting transfers between devices, body(): blocks[d] = lax.ppermute(traces, ('chain', 'group'), pairs)  12.3 us
    unnamed x11, local copies, waits for them, and re-layouts  9.43 us
    ppermute x12, waiting for transfers between devices, body(): blocks[d] = lax.ppermute(traces, ('chain', 'group'), pairs)  9.12 us
    reduce_sum x1, other arithmetic, body(): base = jnp.sum(inv * rhs_t[:, None, :], axis=-1)  7.63 us
    gather x1, local copies, waits for them, and re-layouts, body(): face_inv = lax.optimization_barrier(jnp.take(narrow_now, face_rows, axis=1))  3.5 us
    reduce_sum x1, other arithmetic, body(): jnp.sum(inv_narrow.astype(jnp.float32) * own_coupling[:, None, :], axis=-1)  3.05 us
    reduce_sum x1, other arithmetic, body(): jnp.sum(inv_narrow.astype(jnp.float32) * coupling[:, None, :], axis=-1)  3.04 us
    dot_general x3, matrix products, coupling_of(): jnp.einsum('kvfp,kvpwe->kwfe', traces_in.astype(jnp.float32), picked_jac,...  2.59 us
  transfers between devices with their start and end apart: 12, of which 3 were waited for; matrix products, arithmetic and copies ran while one was open for 24% of the time, Pallas kernels for 0%

profile of v14, /device:TPU:7, one launch (start us, length us, event | category | flops | bytes accessed | tf_op | source)
XLA Modules:
  0.0 54.9 jit_solution(13537028996130125386)
XLA Ops:
  0.0 0.8 %copy.21 = f32[16,5,64]{2,1,0:T(8,128)S(1)} copy(f32[16,5,64]{2,0,1:T(8,128)} %bitcast.136) | data formatting | bytes 40960 | tf_op jit(solution)/shard_map/transpose | solution.py:35
  0.8 0.1 mul.46
  0.9 7.6 %fusion.2 = f32[16,320]{0,1:T(8,128)S(1)} fusion(f32[1,16,320,320]{3,2,1,0:T(8,128)} %param.7, f32[16,320]{1,0:T(8,128)S(1)} %mul.46), kind=kLoop, calls=%fused_computation.7 | loop fusion | flops 3271680 | bytes 6594560 | tf_op jit(solution)/shard_map/reduce_sum | solution.py:48
  8.7 0.7 %collective-permute-start = (bf16[3,5,16,16]{3,2,1,0:T(8,128)(2,1)S(1)}, bf16[3,5,16,16]{3,2,1,0:T(8,128)(2,1)S(1)}, u32[]{:S(2)}, u32[]{:S(2)}) collective-permute-start(bf16[3,5,16,16]{3,2,1,0:T(8,128)(2,1)S(1)} %fusion.17), channel_id=1, source_target_pairs={{0,4},{1,5},{2,6},{3,7},{16,20},{17,21},{18,22},{19,23}} | collective-permute-start | bytes 23048 | tf_op jit(solution)/shard_map/ppermute | solution.py:65
  9.3 0.7 %collective-permute-start.1 = (bf16[3,5,16,16]{3,2,1,0:T(8,128)(2,1)S(1)}, bf16[3,5,16,16]{3,2,1,0:T(8,128)(2,1)S(1)}, u32[]{:S(2)}, u32[]{:S(2)}) collective-permute-start(bf16[3,5,16,16]{3,2,1,0:T(8,128)(2,1)S(1)} %fusion.17), channel_id=1, source_target_pairs={{0,5},{1,4},{2,7},{3,6},{16,21},{17,20},{18,23},{19,22}} | collective-permute-start | bytes 23048 | tf_op jit(solution)/shard_map/ppermute | solution.py:65
  10.0 0.7 %collective-permute-start.2 = (bf16[3,5,16,16]{3,2,1,0:T(8,128)(2,1)S(1)}, bf16[3,5,16,16]{3,2,1,0:T(8,128)(2,1)S(1)}, u32[]{:S(2)}, u32[]{:S(2)}) collective-permute-start(bf16[3,5,16,16]{3,2,1,0:T(8,128)(2,1)S(1)} %fusion.17), channel_id=1, source_target_pairs={{0,6},{1,7},{2,4},{3,5},{16,22},{17,23},{18,20},{19,21}} | collective-permute-start | bytes 23048 | tf_op jit(solution)/shard_map/ppermute | solution.py:65
  10.7 0.7 %collective-permute-start.3 = (bf16[3,5,16,16]{3,2,1,0:T(8,128)(2,1)S(1)}, bf16[3,5,16,16]{3,2,1,0:T(8,128)(2,1)S(1)}, u32[]{:S(2)}, u32[]{:S(2)}) collective-permute-start(bf16[3,5,16,16]{3,2,1,0:T(8,128)(2,1)S(1)} %fusion.17), channel_id=1, source_target_pairs={{0,7},{1,6},{2,5},{3,4},{16,23},{17,22},{18,21},{19,20}} | collective-permute-start | bytes 23048 | tf_op jit(solution)/shard_map/ppermute | solution.py:65
  11.4 9.4 %copy.59 = bf16[1,16,320,320]{3,1,2,0:T(8,128)(2,1)} copy(f32[1,16,320,320]{3,2,1,0:T(8,128)} %param.7) | data formatting | bytes 9830400 | tf_op args[1]
  20.9 0.6 %convolution_bitcast_fusion.2 = f32[3,5,16,16]{2,3,0,1:T(8,128)S(1)} fusion(f32[3,16,5,5]{1,3,0,2:T(8,128)S(1)} %copy.23, f32[3,16,64]{2,1,0:T(8,128)S(1)} %convert_bitcast_fusion, bf16[3,5,16,16]{3,2,1,0:T(8,128)(2,1)S(1)} %collective-permute-done.3, bf16[3,5,16,16]{3,2,1,0:T(8,128)(2,1)S(1)} %collective-permute-done.2, ...), kind=kOutput, calls=%fused_computation.11 | convolution fusion | flops 14945280 | bytes 63168 | tf_op jit(solution)/shard_map/kvfp,kvpwe->kwfe/dot_general | solution.py:44
  21.5 0.3 convolution_bitcast_fusion.5
  21.9 3.0 %fusion = f32[16,320]{0,1:T(8,128)S(1)} fusion(bf16[16,320,320]{2,0,1:T(8,128)(2,1)} %bitcast.114, f32[16,320]{1,0:T(8,128)S(1)} %mul.50), kind=kLoop, calls=%fused_computation.3 | loop fusion | flops 4910080 | bytes 3317760 | tf_op jit(solution)/shard_map/reduce_sum | solution.py:70
  25.1 0.7 %collective-permute-start.4 = (bf16[3,5,16,16]{3,2,1,0:T(8,128)(2,1)S(1)}, bf16[3,5,16,16]{3,2,1,0:T(8,128)(2,1)S(1)}, u32[]{:S(2)}, u32[]{:S(2)}) collective-permute-start(bf16[3,5,16,16]{3,2,1,0:T(8,128)(2,1)S(1)} %maximum_bitcast_fusion.2), channel_id=1, source_target_pairs={{4,8},{5,9},{6,10},{7,11},{20,24},{21,25},{22,26},{23,27}} | collective-permute-start | bytes 23048 | tf_op jit(solution)/shard_map/ppermute | solution.py:65
  25.8 1.3 %collective-permute-start.5 = (bf16[3,5,16,16]{3,2,1,0:T(8,128)(2,1)S(1)}, bf16[3,5,16,16]{3,2,1,0:T(8,128)(2,1)}, u32[]{:S(2)}, u32[]{:S(2)}) collective-permute-start(bf16[3,5,16,16]{3,2,1,0:T(8,128)(2,1)S(1)} %maximum_bitcast_fusion.2), channel_id=1, source_target_pairs={{4,9},{5,8},{6,11},{7,10},{20,25},{21,24},{22,27},{23,26}} | collective-permute-start | bytes 23048 | tf_op jit(solution)/shard_map/ppermute | solution.py:65
  27.1 1.3 %collective-permute-start.6 = (bf16[3,5,16,16]{3,2,1,0:T(8,128)(2,1)S(1)}, bf16[3,5,16,16]{3,2,1,0:T(8,128)(2,1)}, u32[]{:S(2)}, u32[]{:S(2)}) collective-permute-start(bf16[3,5,16,16]{3,2,1,0:T(8,128)(2,1)S(1)} %maximum_bitcast_fusion.2), channel_id=1, source_target_pairs={{4,10},{5,11},{6,8},{7,9},{20,26},{21,27},{22,24},{23,25}} | collective-permute-start | bytes 23048 | tf_op jit(solution)/shard_map/ppermute | solution.py:65
  28.4 1.3 %collective-permute-start.7 = (bf16[3,5,16,16]{3,2,1,0:T(8,128)(2,1)S(1)}, bf16[3,5,16,16]{3,2,1,0:T(8,128)(2,1)}, u32[]{:S(2)}, u32[]{:S(2)}) collective-permute-start(bf16[3,5,16,16]{3,2,1,0:T(8,128)(2,1)S(1)} %maximum_bitcast_fusion.2), channel_id=1, source_target_pairs={{4,11},{5,10},{6,9},{7,8},{20,27},{21,26},{22,25},{23,24}} | collective-permute-start | bytes 23048 | tf_op jit(solution)/shard_map/ppermute | solution.py:65
  29.6 3.5 %gather_fusion = bf16[240,16,320]{2,1,0:T(8,128)(2,1)S(1)} fusion(bf16[16,320,320]{2,0,1:T(8,128)(2,1)} %bitcast.115, s32[1024]{0:T(1024)S(1)} %pad_clamp_fusion), kind=kCustom, calls=%fused_computation | custom fusion | bytes 4916160 | tf_op jit(solution)/shard_map/jit(_take)/gather | solution.py:60
  33.2 1.5 %convolution_bitcast_fusion.1 = f32[3,5,16,16]{2,3,0,1:T(8,128)S(1)} fusion(f32[3,16,5,5]{1,3,0,2:T(8,128)S(1)} %copy.23, f32[3,16,64]{2,1,0:T(8,128)S(1)} %convert_bitcast_fusion, bf16[3,5,16,16]{3,2,1,0:T(8,128)(2,1)} %collective-permute-done.7, bf16[3,5,16,16]{3,2,1,0:T(8,128)(2,1)} %collective-permute-done.6, ...), kind=kOutput, calls=%fused_computation.10 | convolution fusion | flops 14945280 | bytes 63168 | tf_op jit(solution)/shard_map/kvfp,kvpwe->kwfe/dot_general | solution.py:44
  34.7 0.3 convolution_bitcast_fusion.4
  35.0 0.1 mul.53
  35.0 0.7 %multiply_reduce_fusion = f32[16,240]{0,1:T(8,128)S(1)} fusion(bf16[16,240,320]{2,0,1:T(8,128)(2,1)S(1)} %bitcast.117, f32[16,320]{1,0:T(8,128)S(1)} %mul.53), kind=kLoop, calls=%fused_computation.8 | loop fusion | flops 3682560 | bytes 2493440 | tf_op jit(solution)/shard_map/reduce_sum | solution.py:73
  35.7 1.3 %collective-permute-start.10 = (bf16[3,5,16,16]{3,2,1,0:T(8,128)(2,1)S(1)}, bf16[3,5,16,16]{3,2,1,0:T(8,128)(2,1)S(1)}, u32[]{:S(2)}, u32[]{:S(2)}) collective-permute-start(bf16[3,5,16,16]{3,2,1,0:T(8,128)(2,1)S(1)} %fusion.18), channel_id=1, source_target_pairs={{8,14},{9,15},{10,12},{11,13},{24,30},{25,31},{26,28},{27,29}} | collective-permute-start | bytes 23048 | tf_op jit(solution)/shard_map/ppermute | solution.py:65
  37.0 1.3 %collective-permute-start.11 = (bf16[3,5,16,16]{3,2,1,0:T(8,128)(2,1)S(1)}, bf16[3,5,16,16]{3,2,1,0:T(8,128)(2,1)S(1)}, u32[]{:S(2)}, u32[]{:S(2)}) collective-permute-start(bf16[3,5,16,16]{3,2,1,0:T(8,128)(2,1)S(1)} %fusion.18), channel_id=1, source_target_pairs={{8,15},{9,14},{10,13},{11,12},{24,31},{25,30},{26,29},{27,28}} | collective-permute-start | bytes 23048 | tf_op jit(solution)/shard_map/ppermute | solution.py:65
  38.3 1.3 %collective-permute-start.8 = (bf16[3,5,16,16]{3,2,1,0:T(8,128)(2,1)S(1)}, bf16[3,5,16,16]{3,2,1,0:T(8,128)(2,1)S(1)}, u32[]{:S(2)}, u32[]{:S(2)}) collective-permute-start(bf16[3,5,16,16]{3,2,1,0:T(8,128)(2,1)S(1)} %fusion.18), channel_id=1, source_target_pairs={{8,12},{9,13},{10,14},{11,15},{24,28},{25,29},{26,30},{27,31}} | collective-permute-start | bytes 23048 | tf_op jit(solution)/shard_map/ppermute | solution.py:65
  39.6 1.3 %collective-permute-start.9 = (bf16[3,5,16,16]{3,2,1,0:T(8,128)(2,1)S(1)}, bf16[3,5,16,16]{3,2,1,0:T(8,128)(2,1)S(1)}, u32[]{:S(2)}, u32[]{:S(2)}) collective-permute-start(bf16[3,5,16,16]{3,2,1,0:T(8,128)(2,1)S(1)} %fusion.18), channel_id=1, source_target_pairs={{8,13},{9,12},{10,15},{11,14},{24,29},{25,28},{26,31},{27,30}} | collective-permute-start | bytes 23048 | tf_op jit(solution)/shard_map/ppermute | solution.py:65
  41.0 5.5 %collective-permute-done.10 = bf16[3,5,16,16]{3,2,1,0:T(8,128)(2,1)S(1)} collective-permute-done((bf16[3,5,16,16]{3,2,1,0:T(8,128)(2,1)S(1)}, bf16[3,5,16,16]{3,2,1,0:T(8,128)(2,1)S(1)}, u32[]{:S(2)}, u32[]{:S(2)}) %collective-permute-start.10) | collective-permute-done | bytes 7712 | tf_op jit(solution)/shard_map/ppermute | solution.py:65
  46.5 2.0 %collective-permute-done.11 = bf16[3,5,16,16]{3,2,1,0:T(8,128)(2,1)S(1)} collective-permute-done((bf16[3,5,16,16]{3,2,1,0:T(8,128)(2,1)S(1)}, bf16[3,5,16,16]{3,2,1,0:T(8,128)(2,1)S(1)}, u32[]{:S(2)}, u32[]{:S(2)}) %collective-permute-start.11) | collective-permute-done | bytes 7712 | tf_op jit(solution)/shard_map/ppermute | solution.py:65
  48.4 1.6 %collective-permute-done.9 = bf16[3,5,16,16]{3,2,1,0:T(8,128)(2,1)S(1)} collective-permute-done((bf16[3,5,16,16]{3,2,1,0:T(8,128)(2,1)S(1)}, bf16[3,5,16,16]{3,2,1,0:T(8,128)(2,1)S(1)}, u32[]{:S(2)}, u32[]{:S(2)}) %collective-permute-start.9) | collective-permute-done | bytes 7712 | tf_op jit(solution)/shard_map/ppermute | solution.py:65
  50.1 0.6 %convolution_bitcast_fusion = f32[3,5,16,16]{2,3,0,1:T(8,128)S(1)} fusion(f32[3,16,5,5]{1,3,0,2:T(8,128)S(1)} %copy.23, f32[3,16,64]{2,1,0:T(8,128)S(1)} %convert_bitcast_fusion, bf16[3,5,16,16]{3,2,1,0:T(8,128)(2,1)S(1)} %collective-permute-done.11, bf16[3,5,16,16]{3,2,1,0:T(8,128)(2,1)S(1)} %collective-permute-done.10, ...), kind=kOutput, calls=%fused_computation.9 | convolution fusion | flops 14945280 | bytes 63168 | tf_op jit(solution)/shard_map/kvfp,kvpwe->kwfe/dot_general | solution.py:44
  50.6 0.3 convolution_bitcast_fusion.3
  51.0 3.1 %fusion.1 = f32[16,320]{0,1:T(8,128)S(1)} fusion(bf16[16,320,320]{2,0,1:T(8,128)(2,1)} %bitcast.116, f32[16,320]{1,0:T(8,128)S(1)} %select_select_fusion), kind=kLoop, calls=%fused_computation.4 | loop fusion | flops 4910080 | bytes 3317760 | tf_op jit(solution)/shard_map/reduce_sum | solution.py:75
  54.1 0.1 copy.38
  54.2 0.6 %copy.30 = f32[1,5,64,16]{2,3,1,0:T(8,128)} copy(f32[1,5,64,16]{2,1,3,0:T(8,128)S(1)} %bitcast.131) | data formatting | bytes 40960 | tf_op jit(solution)/shard_map/broadcast_in_dim | solution.py:76
  (40 shorter events, 0.6 us)
Async XLA Ops:
  0.0 21.5 %copy-start = (f32[3,64,16]{1,2,0:T(8,128)S(1)}, f32[3,64,16]{1,2,0:T(8,128)}, u32[]{:S(2)}) copy-start(f32[3,64,16]{1,2,0:T(8,128)} %param.10) | copy-start | bytes 36868
  0.0 11.3 %copy-start.2 = (s32[1,3,16]{2,0,1:T(1,128)S(1)}, s32[1,3,16]{2,0,1:T(1,128)}, u32[]{:S(2)}) copy-start(s32[1,3,16]{2,0,1:T(1,128)} %param.9) | copy-start | bytes 580
  8.7 12.2 %collective-permute-start = (bf16[3,5,16,16]{3,2,1,0:T(8,128)(2,1)S(1)}, bf16[3,5,16,16]{3,2,1,0:T(8,128)(2,1)S(1)}, u32[]{:S(2)}, u32[]{:S(2)}) collective-permute-start(bf16[3,5,16,16]{3,2,1,0:T(8,128)(2,1)S(1)} %fusion.17), channel_id=1, source_target_pairs={{0,4},{1,5},{2,6},{3,7},{16,20},{17,21},{18,22},{19,23}} | collective-permute-start | bytes 23048 | tf_op jit(solution)/shard_map/ppermute | solution.py:65
  9.3 11.6 %collective-permute-start.1 = (bf16[3,5,16,16]{3,2,1,0:T(8,128)(2,1)S(1)}, bf16[3,5,16,16]{3,2,1,0:T(8,128)(2,1)S(1)}, u32[]{:S(2)}, u32[]{:S(2)}) collective-permute-start(bf16[3,5,16,16]{3,2,1,0:T(8,128)(2,1)S(1)} %fusion.17), channel_id=1, source_target_pairs={{0,5},{1,4},{2,7},{3,6},{16,21},{17,20},{18,23},{19,22}} | collective-permute-start | bytes 23048 | tf_op jit(solution)/shard_map/ppermute | solution.py:65
  10.0 10.9 %collective-permute-start.2 = (bf16[3,5,16,16]{3,2,1,0:T(8,128)(2,1)S(1)}, bf16[3,5,16,16]{3,2,1,0:T(8,128)(2,1)S(1)}, u32[]{:S(2)}, u32[]{:S(2)}) collective-permute-start(bf16[3,5,16,16]{3,2,1,0:T(8,128)(2,1)S(1)} %fusion.17), channel_id=1, source_target_pairs={{0,6},{1,7},{2,4},{3,5},{16,22},{17,23},{18,20},{19,21}} | collective-permute-start | bytes 23048 | tf_op jit(solution)/shard_map/ppermute | solution.py:65
  10.7 10.2 %collective-permute-start.3 = (bf16[3,5,16,16]{3,2,1,0:T(8,128)(2,1)S(1)}, bf16[3,5,16,16]{3,2,1,0:T(8,128)(2,1)S(1)}, u32[]{:S(2)}, u32[]{:S(2)}) collective-permute-start(bf16[3,5,16,16]{3,2,1,0:T(8,128)(2,1)S(1)} %fusion.17), channel_id=1, source_target_pairs={{0,7},{1,6},{2,5},{3,4},{16,23},{17,22},{18,21},{19,20}} | collective-permute-start | bytes 23048 | tf_op jit(solution)/shard_map/ppermute | solution.py:65
  11.4 9.4 %copy-start.1 = (f32[1,3,5,5,16]{4,0,3,2,1:T(1,128)S(1)}, f32[1,3,5,5,16]{4,0,3,2,1:T(1,128)}, u32[]{:S(2)}) copy-start(f32[1,3,5,5,16]{4,0,3,2,1:T(1,128)} %param.8) | copy-start | bytes 14404
  20.8 8.8 %copy-start.3 = (s32[240]{0:T(256)S(1)}, s32[240]{0:T(256)}, u32[]{:S(2)}) copy-start(s32[240]{0:T(256)} %constant.74) | copy-start | bytes 2884
  25.1 8.0 %collective-permute-start.4 = (bf16[3,5,16,16]{3,2,1,0:T(8,128)(2,1)S(1)}, bf16[3,5,16,16]{3,2,1,0:T(8,128)(2,1)S(1)}, u32[]{:S(2)}, u32[]{:S(2)}) collective-permute-start(bf16[3,5,16,16]{3,2,1,0:T(8,128)(2,1)S(1)} %maximum_bitcast_fusion.2), channel_id=1, source_target_pairs={{4,8},{5,9},{6,10},{7,11},{20,24},{21,25},{22,26},{23,27}} | collective-permute-start | bytes 23048 | tf_op jit(solution)/shard_map/ppermute | solution.py:65
  25.8 7.4 %collective-permute-start.5 = (bf16[3,5,16,16]{3,2,1,0:T(8,128)(2,1)S(1)}, bf16[3,5,16,16]{3,2,1,0:T(8,128)(2,1)}, u32[]{:S(2)}, u32[]{:S(2)}) collective-permute-start(bf16[3,5,16,16]{3,2,1,0:T(8,128)(2,1)S(1)} %maximum_bitcast_fusion.2), channel_id=1, source_target_pairs={{4,9},{5,8},{6,11},{7,10},{20,25},{21,24},{22,27},{23,26}} | collective-permute-start | bytes 23048 | tf_op jit(solution)/shard_map/ppermute | solution.py:65
  27.1 6.1 %collective-permute-start.6 = (bf16[3,5,16,16]{3,2,1,0:T(8,128)(2,1)S(1)}, bf16[3,5,16,16]{3,2,1,0:T(8,128)(2,1)}, u32[]{:S(2)}, u32[]{:S(2)}) collective-permute-start(bf16[3,5,16,16]{3,2,1,0:T(8,128)(2,1)S(1)} %maximum_bitcast_fusion.2), channel_id=1, source_target_pairs={{4,10},{5,11},{6,8},{7,9},{20,26},{21,27},{22,24},{23,25}} | collective-permute-start | bytes 23048 | tf_op jit(solution)/shard_map/ppermute | solution.py:65
  28.4 4.8 %collective-permute-start.7 = (bf16[3,5,16,16]{3,2,1,0:T(8,128)(2,1)S(1)}, bf16[3,5,16,16]{3,2,1,0:T(8,128)(2,1)}, u32[]{:S(2)}, u32[]{:S(2)}) collective-permute-start(bf16[3,5,16,16]{3,2,1,0:T(8,128)(2,1)S(1)} %maximum_bitcast_fusion.2), channel_id=1, source_target_pairs={{4,11},{5,10},{6,9},{7,8},{20,27},{21,26},{22,25},{23,24}} | collective-permute-start | bytes 23048 | tf_op jit(solution)/shard_map/ppermute | solution.py:65
  35.7 10.7 %collective-permute-start.10 = (bf16[3,5,16,16]{3,2,1,0:T(8,128)(2,1)S(1)}, bf16[3,5,16,16]{3,2,1,0:T(8,128)(2,1)S(1)}, u32[]{:S(2)}, u32[]{:S(2)}) collective-permute-start(bf16[3,5,16,16]{3,2,1,0:T(8,128)(2,1)S(1)} %fusion.18), channel_id=1, source_target_pairs={{8,14},{9,15},{10,12},{11,13},{24,30},{25,31},{26,28},{27,29}} | collective-permute-start | bytes 23048 | tf_op jit(solution)/shard_map/ppermute | solution.py:65
  37.0 11.4 %collective-permute-start.11 = (bf16[3,5,16,16]{3,2,1,0:T(8,128)(2,1)S(1)}, bf16[3,5,16,16]{3,2,1,0:T(8,128)(2,1)S(1)}, u32[]{:S(2)}, u32[]{:S(2)}) collective-permute-start(bf16[3,5,16,16]{3,2,1,0:T(8,128)(2,1)S(1)} %fusion.18), channel_id=1, source_target_pairs={{8,15},{9,14},{10,13},{11,12},{24,31},{25,30},{26,29},{27,28}} | collective-permute-start | bytes 23048 | tf_op jit(solution)/shard_map/ppermute | solution.py:65
  38.3 10.1 %collective-permute-start.8 = (bf16[3,5,16,16]{3,2,1,0:T(8,128)(2,1)S(1)}, bf16[3,5,16,16]{3,2,1,0:T(8,128)(2,1)S(1)}, u32[]{:S(2)}, u32[]{:S(2)}) collective-permute-start(bf16[3,5,16,16]{3,2,1,0:T(8,128)(2,1)S(1)} %fusion.18), channel_id=1, source_target_pairs={{8,12},{9,13},{10,14},{11,15},{24,28},{25,29},{26,30},{27,31}} | collective-permute-start | bytes 23048 | tf_op jit(solution)/shard_map/ppermute | solution.py:65
  39.6 10.4 %collective-permute-start.9 = (bf16[3,5,16,16]{3,2,1,0:T(8,128)(2,1)S(1)}, bf16[3,5,16,16]{3,2,1,0:T(8,128)(2,1)S(1)}, u32[]{:S(2)}, u32[]{:S(2)}) collective-permute-start(bf16[3,5,16,16]{3,2,1,0:T(8,128)(2,1)S(1)} %fusion.18), channel_id=1, source_target_pairs={{8,13},{9,12},{10,15},{11,14},{24,29},{25,28},{26,31},{27,30}} | collective-permute-start | bytes 23048 | tf_op jit(solution)/shard_map/ppermute | solution.py:65

commit v15 on v10

--- a/solution.py
+++ b/solution.py
@@ -40,8 +40,8 @@
     picked_jac = jnp.einsum("kpe,kwve->kvpwe", onehot, jac)
 
     def coupling_of(traces_in):
-        mixed = jnp.einsum("kvfp,kvpwe->kwfe", traces_in.astype(jnp.float32), picked_jac, precision=HIGH)
-        coupling = jnp.einsum("kwfe,kif->ewi", mixed, lift, precision=HIGH)
+        mixed = jnp.einsum("kvfp,kvpwe->kwfe", traces_in.astype(jnp.float32), picked_jac, precision=lax.Precision.HIGH)
+        coupling = jnp.einsum("kwfe,kif->ewi", mixed, lift, precision=lax.Precision.HIGH)
         return coupling.reshape(local, BLOCK)
 
     base = jnp.sum(inv * rhs_t[:, None, :], axis=-1)

time: 49 us -> 48.6 us (level)
  no operation moved by 1% of the time
where the time goes in v15:
time: 48.6 us; the launch traced here: 48.1 us
  other arithmetic  19.3 us (40%)
  waiting for transfers between devices  13.2 us (27%)
  starting transfers between devices  10.5 us (22%)
  local copies, waits for them, and re-layouts  2.51 us (5%)
  matrix products  2.1 us (4%)
    ppermute x12, waiting for transfers between devices, body(): blocks[d] = lax.ppermute(traces, ('chain', 'group'), pairs)  13.2 us
    ppermute x12, starting transfers between devices, body(): blocks[d] = lax.ppermute(traces, ('chain', 'group'), pairs)  10.5 us
    reduce_sum x2, other arithmetic, body(): jnp.sum(inv_narrow.astype(jnp.float32) * coupling[:, None, :], axis=-1)  6.2 us
    convert_element_type x1, other arithmetic, body(): inv_narrow = lax.optimization_barrier(inv.astype(jnp.bfloat16))  5.67 us
    reduce_sum x1, other arithmetic, body(): base = jnp.sum(inv * rhs_t[:, None, :], axis=-1)  4.14 us
    reduce_sum x1, other arithmetic, body(): jnp.sum(inv_narrow.astype(jnp.float32) * own_coupling[:, None, :], axis=-1)  3.1 us
    dot_general x3, matrix products, coupling_of(): jnp.einsum('kvfp,kvpwe->kwfe', traces_in.astype(jnp.float32), picked_jac,...  1.39 us
  transfers between devices with their start and end apart: 12, of which 3 were waited for; matrix products, arithmetic and copies ran while one was open for 12% of the time, Pallas kernels for 0%

profile of v15, /device:TPU:7, one launch (start us, length us, event | category | flops | bytes accessed | tf_op | source)
XLA Modules:
  0.0 48.1 jit_solution(14792903273194331117)
XLA Ops:
  0.0 0.8 %copy.17 = f32[16,5,64]{2,1,0:T(8,128)S(1)} copy(f32[16,5,64]{2,0,1:T(8,128)} %bitcast.128) | data formatting | bytes 40960 | tf_op jit(solution)/shard_map/transpose | solution.py:34
  0.9 4.1 %fusion.3 = f32[16,320]{1,0:T(8,128)S(1)} fusion(f32[1,16,320,320]{3,2,1,0:T(8,128)} %param.6, f32[16,320]{1,0:T(8,128)S(1)} %mul.46), kind=kLoop, calls=%fused_computation.8 | loop fusion | flops 3271680 | bytes 6594560 | tf_op jit(solution)/shard_map/reduce_sum | solution.py:47
  5.1 0.1 copy.20
  5.3 0.7 %collective-permute-start = (bf16[3,5,16,16]{3,2,1,0:T(8,128)(2,1)S(1)}, bf16[3,5,16,16]{3,2,1,0:T(8,128)(2,1)S(1)}, u32[]{:S(2)}, u32[]{:S(2)}) collective-permute-start(bf16[3,5,16,16]{3,2,1,0:T(8,128)(2,1)S(1)} %maximum_bitcast_fusion), channel_id=1, source_target_pairs={{0,4},{1,5},{2,6},{3,7},{16,20},{17,21},{18,22},{19,23}} | collective-permute-start | bytes 23048 | tf_op jit(solution)/shard_map/ppermute | solution.py:56
  6.0 0.7 %collective-permute-start.1 = (bf16[3,5,16,16]{3,2,1,0:T(8,128)(2,1)S(1)}, bf16[3,5,16,16]{3,2,1,0:T(8,128)(2,1)S(1)}, u32[]{:S(2)}, u32[]{:S(2)}) collective-permute-start(bf16[3,5,16,16]{3,2,1,0:T(8,128)(2,1)S(1)} %maximum_bitcast_fusion), channel_id=1, source_target_pairs={{0,5},{1,4},{2,7},{3,6},{16,21},{17,20},{18,23},{19,22}} | collective-permute-start | bytes 23048 | tf_op jit(solution)/shard_map/ppermute | solution.py:56
  6.7 0.7 %collective-permute-start.2 = (bf16[3,5,16,16]{3,2,1,0:T(8,128)(2,1)S(1)}, bf16[3,5,16,16]{3,2,1,0:T(8,128)(2,1)S(1)}, u32[]{:S(2)}, u32[]{:S(2)}) collective-permute-start(bf16[3,5,16,16]{3,2,1,0:T(8,128)(2,1)S(1)} %maximum_bitcast_fusion), channel_id=1, source_target_pairs={{0,6},{1,7},{2,4},{3,5},{16,22},{17,23},{18,20},{19,21}} | collective-permute-start | bytes 23048 | tf_op jit(solution)/shard_map/ppermute | solution.py:56
  7.3 0.7 %collective-permute-start.3 = (bf16[3,5,16,16]{3,2,1,0:T(8,128)(2,1)S(1)}, bf16[3,5,16,16]{3,2,1,0:T(8,128)(2,1)S(1)}, u32[]{:S(2)}, u32[]{:S(2)}) collective-permute-start(bf16[3,5,16,16]{3,2,1,0:T(8,128)(2,1)S(1)} %maximum_bitcast_fusion), channel_id=1, source_target_pairs={{0,7},{1,6},{2,5},{3,4},{16,23},{17,22},{18,21},{19,20}} | collective-permute-start | bytes 23048 | tf_op jit(solution)/shard_map/ppermute | solution.py:56
  8.0 5.7 %bitcast_convert_fusion = bf16[16,320,320]{2,1,0:T(8,128)(2,1)} fusion(f32[1,16,320,320]{3,2,1,0:T(8,128)} %param.6), kind=kLoop, calls=%fused_computation.6 | loop fusion | flops 1638400 | bytes 9830400 | tf_op jit(solution)/shard_map/convert_element_type | solution.py:48
  13.9 0.5 convolution_bitcast_fusion.2
  14.3 0.2 convolution_bitcast_fusion.5
  14.7 3.1 %fusion = f32[16,320]{1,0:T(8,128)S(1)} fusion(bf16[16,320,320]{2,1,0:T(8,128)(2,1)} %bitcast_convert_fusion, f32[16,320]{1,0:T(8,128)S(1)} %mul.50), kind=kLoop, calls=%fused_computation.3 | loop fusion | flops 4910080 | bytes 3317760 | tf_op jit(solution)/shard_map/reduce_sum | solution.py:60
  17.8 0.1 copy.22
  18.1 0.7 %collective-permute-start.4 = (bf16[3,5,16,16]{3,2,1,0:T(8,128)(2,1)S(1)}, bf16[3,5,16,16]{3,2,1,0:T(8,128)(2,1)S(1)}, u32[]{:S(2)}, u32[]{:S(2)}) collective-permute-start(bf16[3,5,16,16]{3,2,1,0:T(8,128)(2,1)S(1)} %maximum_bitcast_fusion.3), channel_id=1, source_target_pairs={{4,8},{5,9},{6,10},{7,11},{20,24},{21,25},{22,26},{23,27}} | collective-permute-start | bytes 23048 | tf_op jit(solution)/shard_map/ppermute | solution.py:56
  18.7 0.7 %collective-permute-start.5 = (bf16[3,5,16,16]{3,2,1,0:T(8,128)(2,1)S(1)}, bf16[3,5,16,16]{3,2,1,0:T(8,128)(2,1)S(1)}, u32[]{:S(2)}, u32[]{:S(2)}) collective-permute-start(bf16[3,5,16,16]{3,2,1,0:T(8,128)(2,1)S(1)} %maximum_bitcast_fusion.3), channel_id=1, source_target_pairs={{4,9},{5,8},{6,11},{7,10},{20,25},{21,24},{22,27},{23,26}} | collective-permute-start | bytes 23048 | tf_op jit(solution)/shard_map/ppermute | solution.py:56
  19.4 0.7 %collective-permute-start.6 = (bf16[3,5,16,16]{3,2,1,0:T(8,128)(2,1)S(1)}, bf16[3,5,16,16]{3,2,1,0:T(8,128)(2,1)S(1)}, u32[]{:S(2)}, u32[]{:S(2)}) collective-permute-start(bf16[3,5,16,16]{3,2,1,0:T(8,128)(2,1)S(1)} %maximum_bitcast_fusion.3), channel_id=1, source_target_pairs={{4,10},{5,11},{6,8},{7,9},{20,26},{21,27},{22,24},{23,25}} | collective-permute-start | bytes 23048 | tf_op jit(solution)/shard_map/ppermute | solution.py:56
  20.1 0.7 %collective-permute-start.7 = (bf16[3,5,16,16]{3,2,1,0:T(8,128)(2,1)S(1)}, bf16[3,5,16,16]{3,2,1,0:T(8,128)(2,1)S(1)}, u32[]{:S(2)}, u32[]{:S(2)}) collective-permute-start(bf16[3,5,16,16]{3,2,1,0:T(8,128)(2,1)S(1)} %maximum_bitcast_fusion.3), channel_id=1, source_target_pairs={{4,11},{5,10},{6,9},{7,8},{20,27},{21,26},{22,25},{23,24}} | collective-permute-start | bytes 23048 | tf_op jit(solution)/shard_map/ppermute | solution.py:56
  20.8 0.5 convolution_bitcast_fusion.1
  21.3 0.2 convolution_bitcast_fusion.4
  21.6 3.1 %fusion.1 = f32[16,320]{1,0:T(8,128)S(1)} fusion(bf16[16,320,320]{2,1,0:T(8,128)(2,1)} %bitcast_convert_fusion, f32[16,320]{1,0:T(8,128)S(1)} %mul.53), kind=kLoop, calls=%fused_computation.4 | loop fusion | flops 4910080 | bytes 3317760 | tf_op jit(solution)/shard_map/reduce_sum | solution.py:60
  24.7 0.1 copy.24
  25.0 1.3 %collective-permute-start.10 = (bf16[3,5,16,16]{3,2,1,0:T(8,128)(2,1)S(1)}, bf16[3,5,16,16]{3,2,1,0:T(8,128)(2,1)S(1)}, u32[]{:S(2)}, u32[]{:S(2)}) collective-permute-start(bf16[3,5,16,16]{3,2,1,0:T(8,128)(2,1)S(1)} %maximum_bitcast_fusion.6), channel_id=1, source_target_pairs={{8,14},{9,15},{10,12},{11,13},{24,30},{25,31},{26,28},{27,29}} | collective-permute-start | bytes 23048 | tf_op jit(solution)/shard_map/ppermute | solution.py:56
  26.3 1.3 %collective-permute-start.11 = (bf16[3,5,16,16]{3,2,1,0:T(8,128)(2,1)S(1)}, bf16[3,5,16,16]{3,2,1,0:T(8,128)(2,1)S(1)}, u32[]{:S(2)}, u32[]{:S(2)}) collective-permute-start(bf16[3,5,16,16]{3,2,1,0:T(8,128)(2,1)S(1)} %maximum_bitcast_fusion.6), channel_id=1, source_target_pairs={{8,15},{9,14},{10,13},{11,12},{24,31},{25,30},{26,29},{27,28}} | collective-permute-start | bytes 23048 | tf_op jit(solution)/shard_map/ppermute | solution.py:56
  27.6 1.3 %collective-permute-start.8 = (bf16[3,5,16,16]{3,2,1,0:T(8,128)(2,1)S(1)}, bf16[3,5,16,16]{3,2,1,0:T(8,128)(2,1)S(1)}, u32[]{:S(2)}, u32[]{:S(2)}) collective-permute-start(bf16[3,5,16,16]{3,2,1,0:T(8,128)(2,1)S(1)} %maximum_bitcast_fusion.6), channel_id=1, source_target_pairs={{8,12},{9,13},{10,14},{11,15},{24,28},{25,29},{26,30},{27,31}} | collective-permute-start | bytes 23048 | tf_op jit(solution)/shard_map/ppermute | solution.py:56
  28.9 1.3 %collective-permute-start.9 = (bf16[3,5,16,16]{3,2,1,0:T(8,128)(2,1)S(1)}, bf16[3,5,16,16]{3,2,1,0:T(8,128)(2,1)S(1)}, u32[]{:S(2)}, u32[]{:S(2)}) collective-permute-start(bf16[3,5,16,16]{3,2,1,0:T(8,128)(2,1)S(1)} %maximum_bitcast_fusion.6), channel_id=1, source_target_pairs={{8,13},{9,12},{10,15},{11,14},{24,29},{25,28},{26,31},{27,30}} | collective-permute-start | bytes 23048 | tf_op jit(solution)/shard_map/ppermute | solution.py:56
  30.2 9.5 %collective-permute-done.10 = bf16[3,5,16,16]{3,2,1,0:T(8,128)(2,1)S(1)} collective-permute-done((bf16[3,5,16,16]{3,2,1,0:T(8,128)(2,1)S(1)}, bf16[3,5,16,16]{3,2,1,0:T(8,128)(2,1)S(1)}, u32[]{:S(2)}, u32[]{:S(2)}) %collective-permute-start.10) | collective-permute-done | bytes 7712 | tf_op jit(solution)/shard_map/ppermute | solution.py:56
  39.7 3.1 %collective-permute-done.11 = bf16[3,5,16,16]{3,2,1,0:T(8,128)(2,1)S(1)} collective-permute-done((bf16[3,5,16,16]{3,2,1,0:T(8,128)(2,1)S(1)}, bf16[3,5,16,16]{3,2,1,0:T(8,128)(2,1)S(1)}, u32[]{:S(2)}, u32[]{:S(2)}) %collective-permute-start.11) | collective-permute-done | bytes 7712 | tf_op jit(solution)/shard_map/ppermute | solution.py:56
  42.8 0.6 %collective-permute-done.9 = bf16[3,5,16,16]{3,2,1,0:T(8,128)(2,1)S(1)} collective-permute-done((bf16[3,5,16,16]{3,2,1,0:T(8,128)(2,1)S(1)}, bf16[3,5,16,16]{3,2,1,0:T(8,128)(2,1)S(1)}, u32[]{:S(2)}, u32[]{:S(2)}) %collective-permute-start.9) | collective-permute-done | bytes 7712 | tf_op jit(solution)/shard_map/ppermute | solution.py:56
  43.4 0.5 convolution_bitcast_fusion
  43.9 0.2 convolution_bitcast_fusion.3
  44.2 3.1 %fusion.2 = f32[16,320]{1,0:T(8,128)S(1)} fusion(bf16[16,320,320]{2,1,0:T(8,128)(2,1)} %bitcast_convert_fusion, f32[16,320]{1,0:T(8,128)S(1)} %select_select_fusion), kind=kLoop, calls=%fused_computation.5 | loop fusion | flops 4910080 | bytes 3317760 | tf_op jit(solution)/shard_map/reduce_sum | solution.py:62
  47.4 0.1 sub.25
  47.4 0.6 %copy.26 = f32[1,5,64,16]{2,3,1,0:T(8,128)} copy(f32[1,5,64,16]{2,1,3,0:T(8,128)S(1)} %bitcast.117) | data formatting | bytes 40960 | tf_op jit(solution)/shard_map/broadcast_in_dim | solution.py:63
  (46 shorter events, 0.8 us)
Async XLA Ops:
  0.0 14.3 %copy-start = (f32[3,64,16]{1,2,0:T(8,128)S(1)}, f32[3,64,16]{1,2,0:T(8,128)}, u32[]{:S(2)}) copy-start(f32[3,64,16]{1,2,0:T(8,128)} %param.9) | copy-start | bytes 36868
  5.0 8.7 %copy-start.2 = (s32[1,3,16]{2,0,1:T(1,128)S(1)}, s32[1,3,16]{2,0,1:T(1,128)}, u32[]{:S(2)}) copy-start(s32[1,3,16]{2,0,1:T(1,128)} %param.8) | copy-start | bytes 580
  5.0 8.7 %copy-start.1 = (f32[1,3,5,5,16]{4,0,3,2,1:T(1,128)S(1)}, f32[1,3,5,5,16]{4,0,3,2,1:T(1,128)}, u32[]{:S(2)}) copy-start(f32[1,3,5,5,16]{4,0,3,2,1:T(1,128)} %param.7) | copy-start | bytes 14404
  5.3 8.5 %collective-permute-start = (bf16[3,5,16,16]{3,2,1,0:T(8,128)(2,1)S(1)}, bf16[3,5,16,16]{3,2,1,0:T(8,128)(2,1)S(1)}, u32[]{:S(2)}, u32[]{:S(2)}) collective-permute-start(bf16[3,5,16,16]{3,2,1,0:T(8,128)(2,1)S(1)} %maximum_bitcast_fusion), channel_id=1, source_target_pairs={{0,4},{1,5},{2,6},{3,7},{16,20},{17,21},{18,22},{19,23}} | collective-permute-start | bytes 23048 | tf_op jit(solution)/shard_map/ppermute | solution.py:56
  6.0 7.8 %collective-permute-start.1 = (bf16[3,5,16,16]{3,2,1,0:T(8,128)(2,1)S(1)}, bf16[3,5,16,16]{3,2,1,0:T(8,128)(2,1)S(1)}, u32[]{:S(2)}, u32[]{:S(2)}) collective-permute-start(bf16[3,5,16,16]{3,2,1,0:T(8,128)(2,1)S(1)} %maximum_bitcast_fusion), channel_id=1, source_target_pairs={{0,5},{1,4},{2,7},{3,6},{16,21},{17,20},{18,23},{19,22}} | collective-permute-start | bytes 23048 | tf_op jit(solution)/shard_map/ppermute | solution.py:56
  6.7 7.2 %collective-permute-start.2 = (bf16[3,5,16,16]{3,2,1,0:T(8,128)(2,1)S(1)}, bf16[3,5,16,16]{3,2,1,0:T(8,128)(2,1)S(1)}, u32[]{:S(2)}, u32[]{:S(2)}) collective-permute-start(bf16[3,5,16,16]{3,2,1,0:T(8,128)(2,1)S(1)} %maximum_bitcast_fusion), channel_id=1, source_target_pairs={{0,6},{1,7},{2,4},{3,5},{16,22},{17,23},{18,20},{19,21}} | collective-permute-start | bytes 23048 | tf_op jit(solution)/shard_map/ppermute | solution.py:56
  7.3 6.5 %collective-permute-start.3 = (bf16[3,5,16,16]{3,2,1,0:T(8,128)(2,1)S(1)}, bf16[3,5,16,16]{3,2,1,0:T(8,128)(2,1)S(1)}, u32[]{:S(2)}, u32[]{:S(2)}) collective-permute-start(bf16[3,5,16,16]{3,2,1,0:T(8,128)(2,1)S(1)} %maximum_bitcast_fusion), channel_id=1, source_target_pairs={{0,7},{1,6},{2,5},{3,4},{16,23},{17,22},{18,21},{19,20}} | collective-permute-start | bytes 23048 | tf_op jit(solution)/shard_map/ppermute | solution.py:56
  18.1 2.7 %collective-permute-start.4 = (bf16[3,5,16,16]{3,2,1,0:T(8,128)(2,1)S(1)}, bf16[3,5,16,16]{3,2,1,0:T(8,128)(2,1)S(1)}, u32[]{:S(2)}, u32[]{:S(2)}) collective-permute-start(bf16[3,5,16,16]{3,2,1,0:T(8,128)(2,1)S(1)} %maximum_bitcast_fusion.3), channel_id=1, source_target_pairs={{4,8},{5,9},{6,10},{7,11},{20,24},{21,25},{22,26},{23,27}} | collective-permute-start | bytes 23048 | tf_op jit(solution)/shard_map/ppermute | solution.py:56
  18.7 2.0 %collective-permute-start.5 = (bf16[3,5,16,16]{3,2,1,0:T(8,128)(2,1)S(1)}, bf16[3,5,16,16]{3,2,1,0:T(8,128)(2,1)S(1)}, u32[]{:S(2)}, u32[]{:S(2)}) collective-permute-start(bf16[3,5,16,16]{3,2,1,0:T(8,128)(2,1)S(1)} %maximum_bitcast_fusion.3), channel_id=1, source_target_pairs={{4,9},{5,8},{6,11},{7,10},{20,25},{21,24},{22,27},{23,26}} | collective-permute-start | bytes 23048 | tf_op jit(solution)/shard_map/ppermute | solution.py:56
  19.4 1.4 %collective-permute-start.6 = (bf16[3,5,16,16]{3,2,1,0:T(8,128)(2,1)S(1)}, bf16[3,5,16,16]{3,2,1,0:T(8,128)(2,1)S(1)}, u32[]{:S(2)}, u32[]{:S(2)}) collective-permute-start(bf16[3,5,16,16]{3,2,1,0:T(8,128)(2,1)S(1)} %maximum_bitcast_fusion.3), channel_id=1, source_target_pairs={{4,10},{5,11},{6,8},{7,9},{20,26},{21,27},{22,24},{23,25}} | collective-permute-start | bytes 23048 | tf_op jit(solution)/shard_map/ppermute | solution.py:56
  20.1 0.7 %collective-permute-start.7 = (bf16[3,5,16,16]{3,2,1,0:T(8,128)(2,1)S(1)}, bf16[3,5,16,16]{3,2,1,0:T(8,128)(2,1)S(1)}, u32[]{:S(2)}, u32[]{:S(2)}) collective-permute-start(bf16[3,5,16,16]{3,2,1,0:T(8,128)(2,1)S(1)} %maximum_bitcast_fusion.3), channel_id=1, source_target_pairs={{4,11},{5,10},{6,9},{7,8},{20,27},{21,26},{22,25},{23,24}} | collective-permute-start | bytes 23048 | tf_op jit(solution)/shard_map/ppermute | solution.py:56
  25.0 14.7 %collective-permute-start.10 = (bf16[3,5,16,16]{3,2,1,0:T(8,128)(2,1)S(1)}, bf16[3,5,16,16]{3,2,1,0:T(8,128)(2,1)S(1)}, u32[]{:S(2)}, u32[]{:S(2)}) collective-permute-start(bf16[3,5,16,16]{3,2,1,0:T(8,128)(2,1)S(1)} %maximum_bitcast_fusion.6), channel_id=1, source_target_pairs={{8,14},{9,15},{10,12},{11,13},{24,30},{25,31},{26,28},{27,29}} | collective-permute-start | bytes 23048 | tf_op jit(solution)/shard_map/ppermute | solution.py:56
  26.3 16.5 %collective-permute-start.11 = (bf16[3,5,16,16]{3,2,1,0:T(8,128)(2,1)S(1)}, bf16[3,5,16,16]{3,2,1,0:T(8,128)(2,1)S(1)}, u32[]{:S(2)}, u32[]{:S(2)}) collective-permute-start(bf16[3,5,16,16]{3,2,1,0:T(8,128)(2,1)S(1)} %maximum_bitcast_fusion.6), channel_id=1, source_target_pairs={{8,15},{9,14},{10,13},{11,12},{24,31},{25,30},{26,29},{27,28}} | collective-permute-start | bytes 23048 | tf_op jit(solution)/shard_map/ppermute | solution.py:56
  27.6 15.2 %collective-permute-start.8 = (bf16[3,5,16,16]{3,2,1,0:T(8,128)(2,1)S(1)}, bf16[3,5,16,16]{3,2,1,0:T(8,128)(2,1)S(1)}, u32[]{:S(2)}, u32[]{:S(2)}) collective-permute-start(bf16[3,5,16,16]{3,2,1,0:T(8,128)(2,1)S(1)} %maximum_bitcast_fusion.6), channel_id=1, source_target_pairs={{8,12},{9,13},{10,14},{11,15},{24,28},{25,29},{26,30},{27,31}} | collective-permute-start | bytes 23048 | tf_op jit(solution)/shard_map/ppermute | solution.py:56
  28.9 14.5 %collective-permute-start.9 = (bf16[3,5,16,16]{3,2,1,0:T(8,128)(2,1)S(1)}, bf16[3,5,16,16]{3,2,1,0:T(8,128)(2,1)S(1)}, u32[]{:S(2)}, u32[]{:S(2)}) collective-permute-start(bf16[3,5,16,16]{3,2,1,0:T(8,128)(2,1)S(1)} %maximum_bitcast_fusion.6), channel_id=1, source_target_pairs={{8,13},{9,12},{10,15},{11,14},{24,29},{25,28},{26,31},{27,30}} | collective-permute-start | bytes 23048 | tf_op jit(solution)/shard_map/ppermute | solution.py:56

commit v16 on v15

--- a/solution.py
+++ b/solution.py
@@ -38,9 +38,13 @@
     pos = shift * local + up % local
     onehot = (jnp.arange(groups * local)[None, :, None] == pos[:, None, :]).astype(jnp.float32)
     picked_jac = jnp.einsum("kpe,kwve->kvpwe", onehot, jac)
+    jac_high = picked_jac.astype(jnp.bfloat16).astype(jnp.float32)
+    jac_low = (picked_jac - jac_high).astype(jnp.bfloat16).astype(jnp.float32)
+    jac_split = jnp.concatenate([jac_high, jac_low], axis=2)
 
     def coupling_of(traces_in):
-        mixed = jnp.einsum("kvfp,kvpwe->kwfe", traces_in.astype(jnp.float32), picked_jac, precision=lax.Precision.HIGH)
+        doubled = jnp.concatenate([traces_in, traces_in], axis=3).astype(jnp.float32)
+        mixed = jnp.einsum("kvfp,kvpwe->kwfe", doubled, jac_split, precision=lax.Precision.DEFAULT)
         coupling = jnp.einsum("kwfe,kif->ewi", mixed, lift, precision=lax.Precision.HIGH)
         return coupling.reshape(local, BLOCK)
 

time: 48.6 us -> 49.1 us (1.010)
  matrix products: 2.1 us -> 1.37 us
  local copies, waits for them, and re-layouts: 2.51 us -> 3.17 us
  other arithmetic: 19.3 us -> 19.9 us
    dot_general x3, matrix products: 1.39 us -> 0.66 us  [coupling_of(): jnp.einsum('kvfp,kvpwe->kwfe', doubled, jac_split, precision=lax.Precisio...]
    concatenate x0 -> x3, local copies, waits for them, and re-layouts: none -> 0.65 us  [coupling_of(): jnp.concatenate([traces_in, traces_in], axis=3).astype(jnp.float32)]
  transfers between devices with their start and end apart: 12 -> 12, of which waited for: 3 -> 3; matrix products, arithmetic and copies ran while one was open for 12% -> 13% of each run, Pallas kernels for 0% -> 0%
where the time goes in v16:
time: 49.1 us; the launch traced here: 48.6 us
  other arithmetic  19.9 us (41%)
  waiting for transfers between devices  13.2 us (27%)
  starting transfers between devices  10.5 us (21%)
  local copies, waits for them, and re-layouts  3.17 us (6%)
  matrix products  1.37 us (3%)
    ppermute x12, waiting for transfers between devices, body(): blocks[d] = lax.ppermute(traces, ('chain', 'group'), pairs)  13.2 us
    ppermute x12, starting transfers between devices, body(): blocks[d] = lax.ppermute(traces, ('chain', 'group'), pairs)  10.5 us
    reduce_sum x2, other arithmetic, body(): jnp.sum(inv_narrow.astype(jnp.float32) * coupling[:, None, :], axis=-1)  6.2 us
    convert_element_type x1, other arithmetic, body(): inv_narrow = lax.optimization_barrier(inv.astype(jnp.bfloat16))  5.67 us
    reduce_sum x1, other arithmetic, body(): base = jnp.sum(inv * rhs_t[:, None, :], axis=-1)  4.14 us
    reduce_sum x1, other arithmetic, body(): jnp.sum(inv_narrow.astype(jnp.float32) * own_coupling[:, None, :], axis=-1)  3.1 us
  transfers between devices with their start and end apart: 12, of which 3 were waited for; matrix products, arithmetic and copies ran while one was open for 13% of the time, Pallas kernels for 0%

profile of v16, /device:TPU:7, one launch (start us, length us, event | category | flops | bytes accessed | tf_op | source)
XLA Modules:
  0.0 48.6 jit_solution(9782273028863355567)
XLA Ops:
  0.0 0.8 %copy.17 = f32[16,5,64]{2,1,0:T(8,128)S(1)} copy(f32[16,5,64]{2,0,1:T(8,128)} %bitcast.132) | data formatting | bytes 40960 | tf_op jit(solution)/shard_map/transpose | solution.py:34
  0.9 4.1 %fusion.3 = f32[16,320]{1,0:T(8,128)S(1)} fusion(f32[1,16,320,320]{3,2,1,0:T(8,128)} %param.6, f32[16,320]{1,0:T(8,128)S(1)} %mul.46), kind=kLoop, calls=%fused_computation.8 | loop fusion | flops 3271680 | bytes 6594560 | tf_op jit(solution)/shard_map/reduce_sum | solution.py:51
  5.3 0.7 %collective-permute-start = (bf16[3,5,16,16]{3,2,1,0:T(8,128)(2,1)S(1)}, bf16[3,5,16,16]{3,2,1,0:T(8,128)(2,1)S(1)}, u32[]{:S(2)}, u32[]{:S(2)}) collective-permute-start(bf16[3,5,16,16]{3,2,1,0:T(8,128)(2,1)S(1)} %maximum_bitcast_fusion), channel_id=1, source_target_pairs={{0,4},{1,5},{2,6},{3,7},{16,20},{17,21},{18,22},{19,23}} | collective-permute-start | bytes 23048 | tf_op jit(solution)/shard_map/ppermute | solution.py:60
  6.0 0.7 %collective-permute-start.1 = (bf16[3,5,16,16]{3,2,1,0:T(8,128)(2,1)S(1)}, bf16[3,5,16,16]{3,2,1,0:T(8,128)(2,1)S(1)}, u32[]{:S(2)}, u32[]{:S(2)}) collective-permute-start(bf16[3,5,16,16]{3,2,1,0:T(8,128)(2,1)S(1)} %maximum_bitcast_fusion), channel_id=1, source_target_pairs={{0,5},{1,4},{2,7},{3,6},{16,21},{17,20},{18,23},{19,22}} | collective-permute-start | bytes 23048 | tf_op jit(solution)/shard_map/ppermute | solution.py:60
  6.7 0.7 %collective-permute-start.2 = (bf16[3,5,16,16]{3,2,1,0:T(8,128)(2,1)S(1)}, bf16[3,5,16,16]{3,2,1,0:T(8,128)(2,1)S(1)}, u32[]{:S(2)}, u32[]{:S(2)}) collective-permute-start(bf16[3,5,16,16]{3,2,1,0:T(8,128)(2,1)S(1)} %maximum_bitcast_fusion), channel_id=1, source_target_pairs={{0,6},{1,7},{2,4},{3,5},{16,22},{17,23},{18,20},{19,21}} | collective-permute-start | bytes 23048 | tf_op jit(solution)/shard_map/ppermute | solution.py:60
  7.3 0.7 %collective-permute-start.3 = (bf16[3,5,16,16]{3,2,1,0:T(8,128)(2,1)S(1)}, bf16[3,5,16,16]{3,2,1,0:T(8,128)(2,1)S(1)}, u32[]{:S(2)}, u32[]{:S(2)}) collective-permute-start(bf16[3,5,16,16]{3,2,1,0:T(8,128)(2,1)S(1)} %maximum_bitcast_fusion), channel_id=1, source_target_pairs={{0,7},{1,6},{2,5},{3,4},{16,23},{17,22},{18,21},{19,20}} | collective-permute-start | bytes 23048 | tf_op jit(solution)/shard_map/ppermute | solution.py:60
  8.2 0.2 fusion.8
  8.4 0.2 fusion.9
  8.6 5.7 %bitcast_convert_fusion = bf16[16,320,320]{2,1,0:T(8,128)(2,1)} fusion(f32[1,16,320,320]{3,2,1,0:T(8,128)} %param.6), kind=kLoop, calls=%fused_computation.6 | loop fusion | flops 1638400 | bytes 9830400 | tf_op jit(solution)/shard_map/convert_element_type | solution.py:52
  14.5 0.2 concatenate.19
  14.7 0.2 convolution_bitcast_fusion.2
  15.0 0.2 convolution_bitcast_fusion.5
  15.3 3.1 %fusion = f32[16,320]{1,0:T(8,128)S(1)} fusion(bf16[16,320,320]{2,1,0:T(8,128)(2,1)} %bitcast_convert_fusion, f32[16,320]{1,0:T(8,128)S(1)} %mul.50), kind=kLoop, calls=%fused_computation.3 | loop fusion | flops 4910080 | bytes 3317760 | tf_op jit(solution)/shard_map/reduce_sum | solution.py:64
  18.7 0.7 %collective-permute-start.4 = (bf16[3,5,16,16]{3,2,1,0:T(8,128)(2,1)S(1)}, bf16[3,5,16,16]{3,2,1,0:T(8,128)(2,1)S(1)}, u32[]{:S(2)}, u32[]{:S(2)}) collective-permute-start(bf16[3,5,16,16]{3,2,1,0:T(8,128)(2,1)S(1)} %maximum_bitcast_fusion.1), channel_id=1, source_target_pairs={{4,8},{5,9},{6,10},{7,11},{20,24},{21,25},{22,26},{23,27}} | collective-permute-start | bytes 23048 | tf_op jit(solution)/shard_map/ppermute | solution.py:60
  19.4 0.7 %collective-permute-start.5 = (bf16[3,5,16,16]{3,2,1,0:T(8,128)(2,1)S(1)}, bf16[3,5,16,16]{3,2,1,0:T(8,128)(2,1)S(1)}, u32[]{:S(2)}, u32[]{:S(2)}) collective-permute-start(bf16[3,5,16,16]{3,2,1,0:T(8,128)(2,1)S(1)} %maximum_bitcast_fusion.1), channel_id=1, source_target_pairs={{4,9},{5,8},{6,11},{7,10},{20,25},{21,24},{22,27},{23,26}} | collective-permute-start | bytes 23048 | tf_op jit(solution)/shard_map/ppermute | solution.py:60
  20.0 0.7 %collective-permute-start.6 = (bf16[3,5,16,16]{3,2,1,0:T(8,128)(2,1)S(1)}, bf16[3,5,16,16]{3,2,1,0:T(8,128)(2,1)S(1)}, u32[]{:S(2)}, u32[]{:S(2)}) collective-permute-start(bf16[3,5,16,16]{3,2,1,0:T(8,128)(2,1)S(1)} %maximum_bitcast_fusion.1), channel_id=1, source_target_pairs={{4,10},{5,11},{6,8},{7,9},{20,26},{21,27},{22,24},{23,25}} | collective-permute-start | bytes 23048 | tf_op jit(solution)/shard_map/ppermute | solution.py:60
  20.7 0.7 %collective-permute-start.7 = (bf16[3,5,16,16]{3,2,1,0:T(8,128)(2,1)S(1)}, bf16[3,5,16,16]{3,2,1,0:T(8,128)(2,1)S(1)}, u32[]{:S(2)}, u32[]{:S(2)}) collective-permute-start(bf16[3,5,16,16]{3,2,1,0:T(8,128)(2,1)S(1)} %maximum_bitcast_fusion.1), channel_id=1, source_target_pairs={{4,11},{5,10},{6,9},{7,8},{20,27},{21,26},{22,25},{23,24}} | collective-permute-start | bytes 23048 | tf_op jit(solution)/shard_map/ppermute | solution.py:60
  21.4 0.2 concatenate.20
  21.6 0.2 convolution_bitcast_fusion.1
  21.9 0.2 convolution_bitcast_fusion.4
  22.2 3.1 %fusion.1 = f32[16,320]{1,0:T(8,128)S(1)} fusion(bf16[16,320,320]{2,1,0:T(8,128)(2,1)} %bitcast_convert_fusion, f32[16,320]{1,0:T(8,128)S(1)} %mul.53), kind=kLoop, calls=%fused_computation.4 | loop fusion | flops 4910080 | bytes 3317760 | tf_op jit(solution)/shard_map/reduce_sum | solution.py:64
  25.6 1.3 %collective-permute-start.10 = (bf16[3,5,16,16]{3,2,1,0:T(8,128)(2,1)S(1)}, bf16[3,5,16,16]{3,2,1,0:T(8,128)(2,1)S(1)}, u32[]{:S(2)}, u32[]{:S(2)}) collective-permute-start(bf16[3,5,16,16]{3,2,1,0:T(8,128)(2,1)S(1)} %maximum_bitcast_fusion.2), channel_id=1, source_target_pairs={{8,14},{9,15},{10,12},{11,13},{24,30},{25,31},{26,28},{27,29}} | collective-permute-start | bytes 23048 | tf_op jit(solution)/shard_map/ppermute | solution.py:60
  26.9 1.3 %collective-permute-start.11 = (bf16[3,5,16,16]{3,2,1,0:T(8,128)(2,1)S(1)}, bf16[3,5,16,16]{3,2,1,0:T(8,128)(2,1)S(1)}, u32[]{:S(2)}, u32[]{:S(2)}) collective-permute-start(bf16[3,5,16,16]{3,2,1,0:T(8,128)(2,1)S(1)} %maximum_bitcast_fusion.2), channel_id=1, source_target_pairs={{8,15},{9,14},{10,13},{11,12},{24,31},{25,30},{26,29},{27,28}} | collective-permute-start | bytes 23048 | tf_op jit(solution)/shard_map/ppermute | solution.py:60
  28.2 1.3 %collective-permute-start.8 = (bf16[3,5,16,16]{3,2,1,0:T(8,128)(2,1)S(1)}, bf16[3,5,16,16]{3,2,1,0:T(8,128)(2,1)S(1)}, u32[]{:S(2)}, u32[]{:S(2)}) collective-permute-start(bf16[3,5,16,16]{3,2,1,0:T(8,128)(2,1)S(1)} %maximum_bitcast_fusion.2), channel_id=1, source_target_pairs={{8,12},{9,13},{10,14},{11,15},{24,28},{25,29},{26,30},{27,31}} | collective-permute-start | bytes 23048 | tf_op jit(solution)/shard_map/ppermute | solution.py:60
  29.5 1.3 %collective-permute-start.9 = (bf16[3,5,16,16]{3,2,1,0:T(8,128)(2,1)S(1)}, bf16[3,5,16,16]{3,2,1,0:T(8,128)(2,1)S(1)}, u32[]{:S(2)}, u32[]{:S(2)}) collective-permute-start(bf16[3,5,16,16]{3,2,1,0:T(8,128)(2,1)S(1)} %maximum_bitcast_fusion.2), channel_id=1, source_target_pairs={{8,13},{9,12},{10,15},{11,14},{24,29},{25,28},{26,31},{27,30}} | collective-permute-start | bytes 23048 | tf_op jit(solution)/shard_map/ppermute | solution.py:60
  30.8 9.5 %collective-permute-done.10 = bf16[3,5,16,16]{3,2,1,0:T(8,128)(2,1)S(1)} collective-permute-done((bf16[3,5,16,16]{3,2,1,0:T(8,128)(2,1)S(1)}, bf16[3,5,16,16]{3,2,1,0:T(8,128)(2,1)S(1)}, u32[]{:S(2)}, u32[]{:S(2)}) %collective-permute-start.10) | collective-permute-done | bytes 7712 | tf_op jit(solution)/shard_map/ppermute | solution.py:60
  40.3 3.1 %collective-permute-done.11 = bf16[3,5,16,16]{3,2,1,0:T(8,128)(2,1)S(1)} collective-permute-done((bf16[3,5,16,16]{3,2,1,0:T(8,128)(2,1)S(1)}, bf16[3,5,16,16]{3,2,1,0:T(8,128)(2,1)S(1)}, u32[]{:S(2)}, u32[]{:S(2)}) %collective-permute-start.11) | collective-permute-done | bytes 7712 | tf_op jit(solution)/shard_map/ppermute | solution.py:60
  43.4 0.6 %collective-permute-done.9 = bf16[3,5,16,16]{3,2,1,0:T(8,128)(2,1)S(1)} collective-permute-done((bf16[3,5,16,16]{3,2,1,0:T(8,128)(2,1)S(1)}, bf16[3,5,16,16]{3,2,1,0:T(8,128)(2,1)S(1)}, u32[]{:S(2)}, u32[]{:S(2)}) %collective-permute-start.9) | collective-permute-done | bytes 7712 | tf_op jit(solution)/shard_map/ppermute | solution.py:60
  44.2 0.2 convolution_bitcast_fusion
  44.5 0.2 convolution_bitcast_fusion.3
  44.8 3.1 %fusion.2 = f32[16,320]{1,0:T(8,128)S(1)} fusion(bf16[16,320,320]{2,1,0:T(8,128)(2,1)} %bitcast_convert_fusion, f32[16,320]{1,0:T(8,128)S(1)} %select_select_fusion), kind=kLoop, calls=%fused_computation.5 | loop fusion | flops 4910080 | bytes 3317760 | tf_op jit(solution)/shard_map/reduce_sum | solution.py:66
  48.0 0.6 %copy.29 = f32[1,5,64,16]{2,3,1,0:T(8,128)} copy(f32[1,5,64,16]{2,1,3,0:T(8,128)S(1)} %bitcast.121) | data formatting | bytes 40960 | tf_op jit(solution)/shard_map/broadcast_in_dim | solution.py:67
  (52 shorter events, 1.7 us)
Async XLA Ops:
  0.0 15.0 %copy-start = (f32[3,64,16]{1,2,0:T(8,128)S(1)}, f32[3,64,16]{1,2,0:T(8,128)}, u32[]{:S(2)}) copy-start(f32[3,64,16]{1,2,0:T(8,128)} %param.9) | copy-start | bytes 36868
  0.0 8.0 %copy-start.2 = (s32[1,3,16]{2,0,1:T(1,128)S(1)}, s32[1,3,16]{2,0,1:T(1,128)}, u32[]{:S(2)}) copy-start(s32[1,3,16]{2,0,1:T(1,128)} %param.8) | copy-start | bytes 580
  0.0 8.1 %copy-start.1 = (f32[1,3,5,5,16]{4,0,3,2,1:T(1,128)S(1)}, f32[1,3,5,5,16]{4,0,3,2,1:T(1,128)}, u32[]{:S(2)}) copy-start(f32[1,3,5,5,16]{4,0,3,2,1:T(1,128)} %param.7) | copy-start | bytes 14404
  5.3 9.2 %collective-permute-start = (bf16[3,5,16,16]{3,2,1,0:T(8,128)(2,1)S(1)}, bf16[3,5,16,16]{3,2,1,0:T(8,128)(2,1)S(1)}, u32[]{:S(2)}, u32[]{:S(2)}) collective-permute-start(bf16[3,5,16,16]{3,2,1,0:T(8,128)(2,1)S(1)} %maximum_bitcast_fusion), channel_id=1, source_target_pairs={{0,4},{1,5},{2,6},{3,7},{16,20},{17,21},{18,22},{19,23}} | collective-permute-start | bytes 23048 | tf_op jit(solution)/shard_map/ppermute | solution.py:60
  6.0 8.5 %collective-permute-start.1 = (bf16[3,5,16,16]{3,2,1,0:T(8,128)(2,1)S(1)}, bf16[3,5,16,16]{3,2,1,0:T(8,128)(2,1)S(1)}, u32[]{:S(2)}, u32[]{:S(2)}) collective-permute-start(bf16[3,5,16,16]{3,2,1,0:T(8,128)(2,1)S(1)} %maximum_bitcast_fusion), channel_id=1, source_target_pairs={{0,5},{1,4},{2,7},{3,6},{16,21},{17,20},{18,23},{19,22}} | collective-permute-start | bytes 23048 | tf_op jit(solution)/shard_map/ppermute | solution.py:60
  6.7 7.8 %collective-permute-start.2 = (bf16[3,5,16,16]{3,2,1,0:T(8,128)(2,1)S(1)}, bf16[3,5,16,16]{3,2,1,0:T(8,128)(2,1)S(1)}, u32[]{:S(2)}, u32[]{:S(2)}) collective-permute-start(bf16[3,5,16,16]{3,2,1,0:T(8,128)(2,1)S(1)} %maximum_bitcast_fusion), channel_id=1, source_target_pairs={{0,6},{1,7},{2,4},{3,5},{16,22},{17,23},{18,20},{19,21}} | collective-permute-start | bytes 23048 | tf_op jit(solution)/shard_map/ppermute | solution.py:60
  7.3 7.2 %collective-permute-start.3 = (bf16[3,5,16,16]{3,2,1,0:T(8,128)(2,1)S(1)}, bf16[3,5,16,16]{3,2,1,0:T(8,128)(2,1)S(1)}, u32[]{:S(2)}, u32[]{:S(2)}) collective-permute-start(bf16[3,5,16,16]{3,2,1,0:T(8,128)(2,1)S(1)} %maximum_bitcast_fusion), channel_id=1, source_target_pairs={{0,7},{1,6},{2,5},{3,4},{16,23},{17,22},{18,21},{19,20}} | collective-permute-start | bytes 23048 | tf_op jit(solution)/shard_map/ppermute | solution.py:60
  18.7 2.7 %collective-permute-start.4 = (bf16[3,5,16,16]{3,2,1,0:T(8,128)(2,1)S(1)}, bf16[3,5,16,16]{3,2,1,0:T(8,128)(2,1)S(1)}, u32[]{:S(2)}, u32[]{:S(2)}) collective-permute-start(bf16[3,5,16,16]{3,2,1,0:T(8,128)(2,1)S(1)} %maximum_bitcast_fusion.1), channel_id=1, source_target_pairs={{4,8},{5,9},{6,10},{7,11},{20,24},{21,25},{22,26},{23,27}} | collective-permute-start | bytes 23048 | tf_op jit(solution)/shard_map/ppermute | solution.py:60
  19.4 2.0 %collective-permute-start.5 = (bf16[3,5,16,16]{3,2,1,0:T(8,128)(2,1)S(1)}, bf16[3,5,16,16]{3,2,1,0:T(8,128)(2,1)S(1)}, u32[]{:S(2)}, u32[]{:S(2)}) collective-permute-start(bf16[3,5,16,16]{3,2,1,0:T(8,128)(2,1)S(1)} %maximum_bitcast_fusion.1), channel_id=1, source_target_pairs={{4,9},{5,8},{6,11},{7,10},{20,25},{21,24},{22,27},{23,26}} | collective-permute-start | bytes 23048 | tf_op jit(solution)/shard_map/ppermute | solution.py:60
  20.0 1.4 %collective-permute-start.6 = (bf16[3,5,16,16]{3,2,1,0:T(8,128)(2,1)S(1)}, bf16[3,5,16,16]{3,2,1,0:T(8,128)(2,1)S(1)}, u32[]{:S(2)}, u32[]{:S(2)}) collective-permute-start(bf16[3,5,16,16]{3,2,1,0:T(8,128)(2,1)S(1)} %maximum_bitcast_fusion.1), channel_id=1, source_target_pairs={{4,10},{5,11},{6,8},{7,9},{20,26},{21,27},{22,24},{23,25}} | collective-permute-start | bytes 23048 | tf_op jit(solution)/shard_map/ppermute | solution.py:60
  20.7 0.7 %collective-permute-start.7 = (bf16[3,5,16,16]{3,2,1,0:T(8,128)(2,1)S(1)}, bf16[3,5,16,16]{3,2,1,0:T(8,128)(2,1)S(1)}, u32[]{:S(2)}, u32[]{:S(2)}) collective-permute-start(bf16[3,5,16,16]{3,2,1,0:T(8,128)(2,1)S(1)} %maximum_bitcast_fusion.1), channel_id=1, source_target_pairs={{4,11},{5,10},{6,9},{7,8},{20,27},{21,26},{22,25},{23,24}} | collective-permute-start | bytes 23048 | tf_op jit(solution)/shard_map/ppermute | solution.py:60
  25.6 14.7 %collective-permute-start.10 = (bf16[3,5,16,16]{3,2,1,0:T(8,128)(2,1)S(1)}, bf16[3,5,16,16]{3,2,1,0:T(8,128)(2,1)S(1)}, u32[]{:S(2)}, u32[]{:S(2)}) collective-permute-start(bf16[3,5,16,16]{3,2,1,0:T(8,128)(2,1)S(1)} %maximum_bitcast_fusion.2), channel_id=1, source_target_pairs={{8,14},{9,15},{10,12},{11,13},{24,30},{25,31},{26,28},{27,29}} | collective-permute-start | bytes 23048 | tf_op jit(solution)/shard_map/ppermute | solution.py:60
  26.9 16.5 %collective-permute-start.11 = (bf16[3,5,16,16]{3,2,1,0:T(8,128)(2,1)S(1)}, bf16[3,5,16,16]{3,2,1,0:T(8,128)(2,1)S(1)}, u32[]{:S(2)}, u32[]{:S(2)}) collective-permute-start(bf16[3,5,16,16]{3,2,1,0:T(8,128)(2,1)S(1)} %maximum_bitcast_fusion.2), channel_id=1, source_target_pairs={{8,15},{9,14},{10,13},{11,12},{24,31},{25,30},{26,29},{27,28}} | collective-permute-start | bytes 23048 | tf_op jit(solution)/shard_map/ppermute | solution.py:60
  28.2 15.2 %collective-permute-start.8 = (bf16[3,5,16,16]{3,2,1,0:T(8,128)(2,1)S(1)}, bf16[3,5,16,16]{3,2,1,0:T(8,128)(2,1)S(1)}, u32[]{:S(2)}, u32[]{:S(2)}) collective-permute-start(bf16[3,5,16,16]{3,2,1,0:T(8,128)(2,1)S(1)} %maximum_bitcast_fusion.2), channel_id=1, source_target_pairs={{8,12},{9,13},{10,14},{11,15},{24,28},{25,29},{26,30},{27,31}} | collective-permute-start | bytes 23048 | tf_op jit(solution)/shard_map/ppermute | solution.py:60
  29.5 14.5 %collective-permute-start.9 = (bf16[3,5,16,16]{3,2,1,0:T(8,128)(2,1)S(1)}, bf16[3,5,16,16]{3,2,1,0:T(8,128)(2,1)S(1)}, u32[]{:S(2)}, u32[]{:S(2)}) collective-permute-start(bf16[3,5,16,16]{3,2,1,0:T(8,128)(2,1)S(1)} %maximum_bitcast_fusion.2), channel_id=1, source_target_pairs={{8,13},{9,12},{10,15},{11,14},{24,29},{25,28},{26,31},{27,30}} | collective-permute-start | bytes 23048 | tf_op jit(solution)/shard_map/ppermute | solution.py:60
